TPU v7x, 512 devices: a whole 4x8x8 slice. The times are simulated.
512 devices in a mesh: seq: 64 (over z_hi, y, x), tp: 8 (over z_lo, core).
Axes of the slice: x: 4, y: 8, z: 8 (z_hi: 2, z_lo: 4; z = z_hi * 4 + z_lo), core: 2. Of those that a mesh axis runs over, the one named last changes fastest.
Arguments:
- residual: bfloat16 [16384, 5376], P('seq', 'tp'), may hold values from -10.5 to 10.5
- input_gain: float32 [5376], replicated, may hold values from 0.25 to 1.75
- w_query: bfloat16 [5376, 4096], P('seq', 'tp'), may hold values from -0.078125 to 0.078125
- key_weight: bfloat16 [5376, 2048], P('seq', 'tp'), may hold values from -0.078125 to 0.078125
- value_weight: bfloat16 [5376, 2048], P('seq', 'tp'), may hold values from -0.078125 to 0.078125
- query_gain: float32 [128], replicated, may hold values from 0.25 to 1.75
- key_gain: float32 [128], replicated, may hold values from 0.25 to 1.75
- w_out: bfloat16 [4096, 5376], P('tp', 'seq'), may hold values from -0.1640625 to 0.1640625
- post_gain: float32 [5376], replicated, may hold values from 0.25 to 1.75
- positions: int32 [16384], replicated, may hold values from 0 to 24063, as said below
Outputs:
- mixed: bfloat16 [16384, 5376], P('seq', 'tp')
Inputs may be any that keep to these rules, and one draw needn't show every extreme that they name: positions start at 0 and rise by 1 over the first 1024 tokens; after that they rise by 1 or 2 from each token to the next, by 2 at exactly (15360) // 2 tokens.
All inputs are finite; a program needn't handle non-finite values.
Results may differ from a plain program's by a relative error of at most 0.017.
Values may be sent and summed in bfloat16 or wider, within the bound.
No kernel may reach another device: no remote copies, remote signals or barrier semaphores. Data moves between devices by JAX's collectives and lax.ppermute only.
A program may use at most 128 MiB of HBM per device.

v0:
```python
import jax
import jax.numpy as jnp
from jax import lax
from jax.sharding import PartitionSpec as P

LOOKBACK_SPAN = 1024


epsilon = 1e-06
score_scale = 168.0 ** (-0.5)
rotary_base = 10000.0


def from_behind(block, axis, distance):
    devices = range(lax.axis_size(axis))
    route = [(i - distance, i) for i in devices if i - distance in devices]
    return lax.ppermute(block, axis, route)


def norm_scale(value_matrix, gain):
    mean_square = jnp.mean(value_matrix * value_matrix, axis=-1, keepdims=True)
    return value_matrix * lax.rsqrt(mean_square + epsilon) * gain


def rotary(value_matrix, places):
    half_dim = value_matrix.shape[-1] // 2
    inverse = rotary_base ** (-jnp.arange(half_dim, dtype=jnp.float32) / half_dim)
    angles = places.astype(jnp.float32)[:, None] * inverse[None, :]
    cosine = jnp.cos(angles)[:, None, :]
    sine = jnp.sin(angles)[:, None, :]
    first = value_matrix[..., :half_dim]
    second = value_matrix[..., half_dim:]
    return jnp.concatenate(
        [first * cosine - second * sine, second * cosine + first * sine], axis=-1
    )


def local(
    residual,
    input_gain,
    w_query,
    key_weight,
    value_weight,
    query_gain,
    key_gain,
    w_out,
    post_gain,
    positions,
):
    tok_rows = residual.shape[0]
    seq_at = lax.axis_index("seq")
    tp_at = lax.axis_index("tp")
    head_dim = query_gain.shape[0]
    local_kv = key_weight.shape[1] // head_dim
    query_group = w_query.shape[1] // key_weight.shape[1]
    gathered = lax.all_gather(residual, "tp", axis=1, tiled=True)
    normalized_input = norm_scale(gathered.astype(jnp.float32), input_gain).astype(jnp.bfloat16)
    own_places = lax.dynamic_slice_in_dim(positions, seq_at * tok_rows, tok_rows, 0)
    reach = (LOOKBACK_SPAN - 2) // tok_rows + 1

    def attend(query_matrix, stacked, key_places, valid):
        key_matrix = stacked[0].reshape(-1, local_kv, head_dim)
        value_matrix = stacked[1].reshape(-1, local_kv, head_dim)
        scores = (
            jnp.einsum(
                "qkgd,skd->kgqs", query_matrix, key_matrix, preferred_element_type=jnp.float32
            )
            * score_scale
        )
        distance = own_places[:, None] - key_places[None, :]
        allowed = valid[None, :] & (distance >= 0) & (distance < LOOKBACK_SPAN)
        weights = jnp.where(allowed[None, None], jnp.exp(scores), jnp.zeros_like(scores))
        total = jnp.sum(weights, axis=-1)
        summed = jnp.einsum(
            "kgqs,skd->qkgd",
            weights.astype(jnp.bfloat16),
            value_matrix,
            preferred_element_type=jnp.float32,
        )
        return (total, summed)

    pieces = (
        lax.all_gather(w_query, "seq", axis=0, tiled=True),
        lax.all_gather(key_weight, "seq", axis=0, tiled=True),
        lax.all_gather(value_weight, "seq", axis=0, tiled=True),
    )
    queries_raw, unrotated_keys, projected_values = tuple(
        (jnp.dot(normalized_input, piece, preferred_element_type=jnp.float32) for piece in pieces)
    )
    key_matrix = rotary(
        norm_scale(unrotated_keys.reshape(tok_rows, local_kv, head_dim), key_gain), own_places
    )
    stacked = jnp.stack(
        [key_matrix.reshape(tok_rows, local_kv * head_dim), projected_values]
    ).astype(jnp.bfloat16)
    pieces = []
    for distance in range(reach, 0, -1):
        pieces.append(from_behind(stacked, "seq", distance))
    halo = jnp.concatenate(pieces, axis=1)
    query_matrix = rotary(
        norm_scale(queries_raw.reshape(tok_rows, local_kv * query_group, head_dim), query_gain),
        own_places,
    )
    query_matrix = query_matrix.astype(jnp.bfloat16).reshape(
        tok_rows, local_kv, query_group, head_dim
    )
    inner_total, inner_sum = attend(
        query_matrix, stacked, own_places, jnp.ones((tok_rows,), jnp.bool_)
    )
    span = halo.shape[1]
    padded_places = jnp.concatenate([jnp.zeros((span,), jnp.int32), positions])
    halo_places = lax.dynamic_slice_in_dim(padded_places, seq_at * tok_rows, span, 0)
    halo_valid = seq_at * tok_rows - span + jnp.arange(span, dtype=jnp.int32) >= 0
    outer_total, outer_sum = attend(query_matrix, halo, halo_places, halo_valid)
    total = jnp.transpose(inner_total + outer_total, (2, 0, 1))
    merged = (inner_sum + outer_sum) / total[..., None]
    attended = merged.astype(jnp.bfloat16).reshape(tok_rows, local_kv * query_group * head_dim)
    partial_out = jnp.dot(
        attended,
        lax.all_gather(w_out, "seq", axis=1, tiled=True),
        preferred_element_type=jnp.float32,
    )
    summed_cols = lax.psum_scatter(
        partial_out.astype(jnp.bfloat16), "tp", scatter_dimension=1, tiled=True
    ).astype(jnp.float32)
    full_width = post_gain.shape[0]
    squares = lax.psum(jnp.sum(summed_cols * summed_cols, axis=1), "tp")
    inverse_rms = lax.rsqrt(squares / full_width + epsilon)
    gain_part = lax.dynamic_slice_in_dim(
        post_gain, tp_at * summed_cols.shape[1], summed_cols.shape[1], 0
    )
    return (residual.astype(jnp.float32) + summed_cols * inverse_rms[:, None] * gain_part).astype(
        jnp.bfloat16
    )


def solution(mesh):
    in_specs = (
        P("seq", "tp"),
        P(),
        P("seq", "tp"),
        P("seq", "tp"),
        P("seq", "tp"),
        P(),
        P(),
        P("tp", "seq"),
        P(),
        P(),
    )
    out_specs = P("seq", "tp")
    return jax.shard_map(local, mesh=mesh, in_specs=in_specs, out_specs=out_specs, check_vma=False)
```

profile of v0, /device:TPU:6, one launch (start us, length us, event | category | flops | bytes accessed | tf_op | source)
XLA Modules:
  0.0 810.6 jit_solution(6384950764701939511)
XLA Ops:
  12.1 46.5 %all-gather.10.cloned.1.call-done = bf16[256,5376]{0,1:T(8,128)(2,1)} async-done(((bf16[256,672]{0,1:T(8,128)(2,1)}), bf16[256,5376]{0,1:T(8,128)(2,1)}) %all-gather.10.cloned.1.call-update) | async-done | bytes 2752528 | tf_op jit(solution)/shard_map/all_gather | solution.py:56
  58.6 2.7 fusion
  61.2 147.3 %all-gather.14.cloned.1.call-done = bf16[64,84,256]{2,1,0:T(8,128)(2,1)} async-done(((bf16[1,84,256]{2,1,0:T(8,128)(2,1)}), bf16[64,84,256]{2,1,0:T(8,128)(2,1)}) %all-gather.14.cloned.1.call-update) | async-done | bytes 2752528 | tf_op jit(solution)/shard_map/all_gather | solution.py:84
  208.5 5.2 reshape.181
  213.7 3.5 multiply_reduce_fusion.1
  218.5 134.0 %all-gather.12.cloned.1.call-done = bf16[64,84,256]{2,1,0:T(8,128)(2,1)} async-done(((bf16[1,84,256]{2,1,0:T(8,128)(2,1)}), bf16[64,84,256]{2,1,0:T(8,128)(2,1)}) %all-gather.12.cloned.1.call-update) | async-done | bytes 2752528 | tf_op jit(solution)/shard_map/all_gather | solution.py:85
  352.5 5.2 reshape.179
  357.7 3.5 convolution_convert_fusion.1
  361.2 2.5 collective-permute-start
  364.6 3.6 collective-permute-start.1
  368.1 4.0 collective-permute-start.2
  372.9 4.2 collective-permute-start.3
  377.1 1.5 collective-permute-done.1
  378.6 3.5 collective-permute-done.2
  382.1 3.1 collective-permute-done.3
  386.3 172.0 %all-gather.16.cloned.1.call-done = bf16[64,84,512]{2,1,0:T(8,128)(2,1)} async-done(((bf16[1,84,512]{2,1,0:T(8,128)(2,1)}), bf16[64,84,512]{2,1,0:T(8,128)(2,1)}) %all-gather.16.cloned.1.call-update) | async-done | bytes 5505040 | tf_op jit(solution)/shard_map/all_gather | solution.py:83
  558.2 8.9 %reshape.183 = bf16[5376,512]{1,0:T(8,128)(2,1)} reshape(bf16[64,84,512]{2,1,0:T(8,128)(2,1)} %all-gather.16.cloned.1.call-done) | data formatting | bytes 11010048
  567.1 6.5 fusion.40
  579.3 151.3 %all-gather.18.cloned.1.call-done = bf16[64,84,512]{2,1,0:T(8,128)(2,1)} async-done(((bf16[1,84,512]{2,1,0:T(8,128)(2,1)}), bf16[64,84,512]{2,1,0:T(8,128)(2,1)}) %all-gather.18.cloned.1.call-update) | async-done | bytes 5505040 | tf_op jit(solution)/shard_map/all_gather | solution.py:120
  730.6 8.9 %reshape.185 = bf16[5376,512]{1,0:T(8,128)(2,1)} reshape(bf16[64,84,512]{2,1,0:T(8,128)(2,1)} %all-gather.18.cloned.1.call-done) | data formatting | bytes 11010048
  739.5 5.7 convolution_convert_fusion
  746.0 39.7 %reduce-scatter.2.cloned.1.call-done = bf16[256,672]{0,1:T(8,128)(2,1)} async-done(((bf16[256,5376]{0,1:T(8,128)(2,1)}), bf16[256,672]{0,1:T(8,128)(2,1)}) %reduce-scatter.2.cloned.1.call-update) | async-done | bytes 344080 | tf_op jit(solution)/shard_map/reduce_scatter | solution.py:123
  786.8 15.0 %psum.7 = f32[256]{0:T(256)S(1)} all-reduce(f32[256]{0:T(256)S(1)} %fusion.27), channel_id=1, replica_groups=mesh['seq'=64,'tp'=8] {'tp'}, use_global_device_ids=true, to_apply=%region_7.8 | all-reduce | flops 256 | bytes 2048 | tf_op jit(solution)/shard_map/psum | solution.py:127
  801.8 1.9 fusion.30
  (70 shorter events, 17.0 us)
Async XLA Ops:
  6.5 52.0 %all-gather.10.cloned.1.call-start = ((), (), s32[]{:S(2)}) async-start(), calls=%async_computation.1 | async-start | bytes 3096576 | tf_op jit(solution)/shard_map/all_gather | solution.py:56
  7.3 201.2 %all-gather.14.cloned.1.call-start = ((), (), s32[]{:S(2)}) async-start(), calls=%async_computation.4 | async-start | bytes 2928640 | tf_op jit(solution)/shard_map/all_gather | solution.py:84
  8.0 344.5 %all-gather.12.cloned.1.call-start = ((), (), s32[]{:S(2)}) async-start(), calls=%async_computation.3 | async-start | bytes 2928640 | tf_op jit(solution)/shard_map/all_gather | solution.py:85
  8.7 549.5 %all-gather.16.cloned.1.call-start = ((), (), s32[]{:S(2)}) async-start(), calls=%async_computation.5 | async-start | bytes 5857280 | tf_op jit(solution)/shard_map/all_gather | solution.py:83
  9.3 721.3 %all-gather.18.cloned.1.call-start = ((), (), s32[]{:S(2)}) async-start(), calls=%async_computation.6 | async-start | bytes 5857280 | tf_op jit(solution)/shard_map/all_gather | solution.py:120
  9.9 775.8 %reduce-scatter.2.cloned.1.call-start = ((), (), s32[]{:S(2)}) async-start(), calls=%async_computation.2 | async-start | bytes 3096576 | tf_op jit(solution)/shard_map/reduce_scatter | solution.py:123
  12.1 201.6 %copy-start.9 = (f32[5376]{0:T(1024)S(1)}, f32[5376]{0:T(1024)}, u32[]{:S(2)}) copy-start(f32[5376]{0:T(1024)} %param.11) | copy-start | bytes 64516
  58.6 155.1 %copy-start = (bf16[256,5376]{0,1:T(8,128)(2,1)S(1)}, bf16[256,5376]{0,1:T(8,128)(2,1)}, u32[]{:S(2)}) copy-start(bf16[256,5376]{0,1:T(8,128)(2,1)} %all-gather.10.cloned.1.call-done) | copy-start | bytes 8257540
  61.2 155.9 %copy-start.5 = (f32[256]{0:T(256)}, f32[256]{0:T(256)S(1)}, u32[]{:S(2)}) copy-start(f32[256]{0:T(256)S(1)} %add_rsqrt_fusion.3) | copy-start | bytes 3076
  217.3 140.4 %copy-start.6 = (f32[256]{0:T(256)S(1)}, f32[256]{0:T(256)}, u32[]{:S(2)}) copy-start(f32[256]{0:T(256)} %copy-done.5) | copy-start | bytes 3076
  217.3 140.3 %copy-start.10 = (f32[5376]{0:T(1024)S(1)}, f32[5376]{0:T(1024)}, u32[]{:S(2)}) copy-start(f32[5376]{0:T(1024)} %param.11) | copy-start | bytes 64516
  361.2 15.8 %collective-permute-start = (bf16[2,256,256]{1,2,0:T(8,128)(2,1)S(1)}, bf16[2,256,256]{1,2,0:T(8,128)(2,1)S(1)}, u32[]{:S(2)}, u32[]{:S(2)}) collective-permute-start(bf16[2,256,256]{1,2,0:T(8,128)(2,1)S(1)} %pad_maximum_fusion.1), channel_id=1, source_target_pairs={{0,32},{8,40},{16,48},{24,56},{32,64},{40,72},{48,80},{56,88},{64,... | collective-permute-start | bytes 786440 | tf_op jit(solution)/shard_map/ppermute | solution.py:17
  364.6 14.0 %collective-permute-start.1 = (bf16[2,256,256]{1,2,0:T(8,128)(2,1)S(1)}, bf16[2,256,256]{1,2,0:T(8,128)(2,1)S(1)}, u32[]{:S(2)}, u32[]{:S(2)}) collective-permute-start(bf16[2,256,256]{1,2,0:T(8,128)(2,1)S(1)} %pad_maximum_fusion.1), channel_id=1, source_target_pairs={{0,24},{8,32},{16,40},{24,48},{32,56},{40,64},{48,72},{56,80},{64,... | collective-permute-start | bytes 786440 | tf_op jit(solution)/shard_map/ppermute | solution.py:17
  368.1 13.9 %collective-permute-start.2 = (bf16[2,256,256]{1,2,0:T(8,128)(2,1)S(1)}, bf16[2,256,256]{1,2,0:T(8,128)(2,1)S(1)}, u32[]{:S(2)}, u32[]{:S(2)}) collective-permute-start(bf16[2,256,256]{1,2,0:T(8,128)(2,1)S(1)} %pad_maximum_fusion.1), channel_id=1, source_target_pairs={{0,16},{8,24},{16,32},{24,40},{32,48},{40,56},{48,64},{56,72},{64,... | collective-permute-start | bytes 786440 | tf_op jit(solution)/shard_map/ppermute | solution.py:17
  372.9 12.3 %collective-permute-start.3 = (bf16[2,256,256]{1,2,0:T(8,128)(2,1)S(1)}, bf16[2,256,256]{1,2,0:T(8,128)(2,1)S(1)}, u32[]{:S(2)}, u32[]{:S(2)}) collective-permute-start(bf16[2,256,256]{1,2,0:T(8,128)(2,1)S(1)} %pad_maximum_fusion.1), channel_id=1, source_target_pairs={{0,8},{8,16},{16,24},{24,32},{32,40},{40,48},{48,56},{56,64},{64,7... | collective-permute-start | bytes 786440 | tf_op jit(solution)/shard_map/ppermute | solution.py:17
  386.2 180.9 %copy-start.7 = (f32[256]{0:T(256)S(1)}, f32[256]{0:T(256)}, u32[]{:S(2)}) copy-start(f32[256]{0:T(256)} %copy-done.5) | copy-start | bytes 3076
  567.1 8.2 %copy-start.8 = (f32[128]{0:T(128)S(1)}, f32[128]{0:T(128)}, u32[]{:S(2)}) copy-start(f32[128]{0:T(128)} %param.15) | copy-start | bytes 1540
  573.6 2.6 copy-start.4
  573.6 3.1 copy-start.3
  576.8 1.6 copy-start.2
  739.5 62.4 %copy-start.1 = (bf16[256,672]{0,1:T(8,128)(2,1)S(1)}, bf16[256,672]{0,1:T(8,128)(2,1)}, u32[]{:S(2)}) copy-start(bf16[256,672]{0,1:T(8,128)(2,1)} %param.10) | copy-start | bytes 1032196
Sparse Core Ops, SparseCore 0:
  9.4 49.0 all-gather.9
  63.1 145.3 all-gather.13
  213.1 139.3 all-gather.11
  356.9 201.2 all-gather.15
  562.6 167.9 all-gather.17
  745.4 40.2 reduce-scatter.1
where the time goes:
time: 812 us; the launch traced here: 811 us
  waiting for transfers between devices  702 us (86%)
  local copies, waits for them, and re-layouts  32.4 us (4%)
  matrix products  22.3 us (3%)
  blocking collectives  15 us (2%)
  starting transfers between devices  14.4 us (2%)
  between operations  13.8 us (2%)
  other arithmetic  10.9 us (1%)
    all_gather x1, waiting for transfers between devices, local(): lax.all_gather(w_query, 'seq', axis=0, tiled=True)  172 us
    all_gather x1, waiting for transfers between devices, local(): lax.all_gather(w_out, 'seq', axis=1, tiled=True)  151 us
    all_gather x1, waiting for transfers between devices, local(): lax.all_gather(key_weight, 'seq', axis=0, tiled=True)  147 us
    all_gather x1, waiting for transfers between devices, local(): lax.all_gather(value_weight, 'seq', axis=0, tiled=True)  134 us
    all_gather x1, waiting for transfers between devices, local(): gathered = lax.all_gather(residual, 'tp', axis=1, tiled=True)  46.5 us
    reduce_scatter x1, waiting for transfers between devices, local(): lax.psum_scatter(partial_out.astype(jnp.bfloat16), 'tp', scatter_dimensio...  39.7 us
    unnamed x29, local copies, waits for them, and re-layouts  28.2 us
  transfers between devices with their start and end apart: 10, of which 9 were waited for; matrix products, arithmetic and copies ran while one was open for 6% of the time, Pallas kernels for 0%

commit v1 on v0

--- a/solution.py
+++ b/solution.py
@@ -1,20 +1,56 @@
 import jax
 import jax.numpy as jnp
+import numpy as np
 from jax import lax
+from jax.sharding import Mesh
 from jax.sharding import PartitionSpec as P
 
 LOOKBACK_SPAN = 1024
 
+SEQ_PARTS = (("zh", 2), ("y", 8), ("x", 4))
+TP_PARTS = (("zl", 4), ("c", 2))
+SEQ = tuple(name for name, _ in SEQ_PARTS)
+TP = tuple(name for name, _ in TP_PARTS)
 
 epsilon = 1e-06
 score_scale = 168.0 ** (-0.5)
 rotary_base = 10000.0
 
 
-def from_behind(block, axis, distance):
-    devices = range(lax.axis_size(axis))
-    route = [(i - distance, i) for i in devices if i - distance in devices]
+def from_behind(block, axis, n, distance):
+    route = [(i - distance, i) for i in range(n) if i - distance >= 0]
     return lax.ppermute(block, axis, route)
+
+
+def ring(block, axis, n, split_axis):
+    if n == 1:
+        return [block]
+    fwd = [(i, (i + 1) % n) for i in range(n)]
+    bwd = [(i, (i - 1) % n) for i in range(n)]
+    if n == 2:
+        return [block, lax.ppermute(block, axis, fwd)]
+    out = [None] * n
+    out[0] = block
+    left, right = block, block
+    for d in range(1, (n + 1) // 2):
+        left = lax.ppermute(left, axis, fwd)
+        right = lax.ppermute(right, axis, bwd)
+        out[n - d] = left
+        out[d] = right
+    if n % 2 == 0:
+        k = block.shape[split_axis] // 2
+        top = lax.ppermute(lax.slice_in_dim(left, 0, k, axis=split_axis), axis, fwd)
+        bottom = lax.ppermute(lax.slice_in_dim(right, k, None, axis=split_axis), axis, bwd)
+        out[n // 2] = jnp.concatenate([top, bottom], axis=split_axis)
+    return out
+
+
+def gather_axis(block, axis, n, stack_axis, split_axis):
+    parts = ring(block, axis, n, split_axis)
+    stacked = jnp.stack(parts, axis=stack_axis)
+    if n == 1:
+        return stacked
+    return jnp.roll(stacked, lax.axis_index(axis), axis=stack_axis)
 
 
 def norm_scale(value_matrix, gain):
@@ -47,14 +83,40 @@
     post_gain,
     positions,
 ):
+    sizes = dict(SEQ_PARTS)
+    n_seq = int(np.prod([n for _, n in SEQ_PARTS]))
     tok_rows = residual.shape[0]
-    seq_at = lax.axis_index("seq")
-    tp_at = lax.axis_index("tp")
+    seq_at = lax.axis_index(SEQ)
+    tp_at = lax.axis_index(TP)
     head_dim = query_gain.shape[0]
     local_kv = key_weight.shape[1] // head_dim
     query_group = w_query.shape[1] // key_weight.shape[1]
-    gathered = lax.all_gather(residual, "tp", axis=1, tiled=True)
+    q_cols = w_query.shape[1]
+    k_cols = key_weight.shape[1]
+    v_cols = value_weight.shape[1]
+    shard_rows = w_query.shape[0]
+
+    packed = jnp.concatenate([w_query, key_weight, value_weight, w_out.T], axis=1)
+    by_zh = gather_axis(packed, "zh", sizes["zh"], 0, None)
+    split = q_cols + k_cols
+    half_a = by_zh[:, :, :split]
+    half_b = by_zh[:, :, split:]
+    a_x = gather_axis(half_a, "x", sizes["x"], 0, 0)
+    a_yx = gather_axis(a_x, "y", sizes["y"], 0, 0)
+    b_y = gather_axis(half_b, "y", sizes["y"], 0, 0)
+    b_yx = gather_axis(b_y, "x", sizes["x"], 1, 0)
+    full_rows = n_seq * shard_rows
+    a_flat = a_yx.reshape(full_rows, split)
+    b_flat = b_yx.reshape(full_rows, half_b.shape[-1])
+
+    gathered = lax.all_gather(residual, TP, axis=1, tiled=True)
     normalized_input = norm_scale(gathered.astype(jnp.float32), input_gain).astype(jnp.bfloat16)
+    nz, ny, nx = sizes["zh"], sizes["y"], sizes["x"]
+    normed_perm = (
+        normalized_input.reshape(tok_rows, nz, ny, nx, shard_rows)
+        .transpose(0, 2, 3, 1, 4)
+        .reshape(tok_rows, full_rows)
+    )
     own_places = lax.dynamic_slice_in_dim(positions, seq_at * tok_rows, tok_rows, 0)
     reach = (LOOKBACK_SPAN - 2) // tok_rows + 1
 
@@ -79,14 +141,13 @@
         )
         return (total, summed)
 
-    pieces = (
-        lax.all_gather(w_query, "seq", axis=0, tiled=True),
-        lax.all_gather(key_weight, "seq", axis=0, tiled=True),
-        lax.all_gather(value_weight, "seq", axis=0, tiled=True),
-    )
-    queries_raw, unrotated_keys, projected_values = tuple(
-        (jnp.dot(normalized_input, piece, preferred_element_type=jnp.float32) for piece in pieces)
-    )
+    qk = jnp.dot(normed_perm, a_flat, preferred_element_type=jnp.float32)
+    queries_raw = qk[:, :q_cols]
+    unrotated_keys = qk[:, q_cols:]
+    projected_values = jnp.dot(
+        normed_perm, b_flat[:, :v_cols], preferred_element_type=jnp.float32
+    )
+    out_perm = b_flat[:, v_cols:]
     key_matrix = rotary(
         norm_scale(unrotated_keys.reshape(tok_rows, local_kv, head_dim), key_gain), own_places
     )
@@ -95,7 +156,7 @@
     ).astype(jnp.bfloat16)
     pieces = []
     for distance in range(reach, 0, -1):
-        pieces.append(from_behind(stacked, "seq", distance))
+        pieces.append(from_behind(stacked, SEQ, n_seq, distance))
     halo = jnp.concatenate(pieces, axis=1)
     query_matrix = rotary(
         norm_scale(queries_raw.reshape(tok_rows, local_kv * query_group, head_dim), query_gain),
@@ -115,16 +176,22 @@
     total = jnp.transpose(inner_total + outer_total, (2, 0, 1))
     merged = (inner_sum + outer_sum) / total[..., None]
     attended = merged.astype(jnp.bfloat16).reshape(tok_rows, local_kv * query_group * head_dim)
-    partial_out = jnp.dot(
+    partial_perm = lax.dot_general(
         attended,
-        lax.all_gather(w_out, "seq", axis=1, tiled=True),
+        out_perm,
+        (((1,), (1,)), ((), ())),
         preferred_element_type=jnp.float32,
     )
+    partial_out = (
+        partial_perm.reshape(tok_rows, ny, nx, nz, shard_rows)
+        .transpose(0, 3, 1, 2, 4)
+        .reshape(tok_rows, full_rows)
+    )
     summed_cols = lax.psum_scatter(
-        partial_out.astype(jnp.bfloat16), "tp", scatter_dimension=1, tiled=True
+        partial_out.astype(jnp.bfloat16), TP, scatter_dimension=1, tiled=True
     ).astype(jnp.float32)
     full_width = post_gain.shape[0]
-    squares = lax.psum(jnp.sum(summed_cols * summed_cols, axis=1), "tp")
+    squares = lax.psum(jnp.sum(summed_cols * summed_cols, axis=1), TP)
     inverse_rms = lax.rsqrt(squares / full_width + epsilon)
     gain_part = lax.dynamic_slice_in_dim(
         post_gain, tp_at * summed_cols.shape[1], summed_cols.shape[1], 0
@@ -135,17 +202,21 @@
 
 
 def solution(mesh):
+    seq_n, tp_n = mesh.devices.shape
+    shape = tuple(n for _, n in SEQ_PARTS) + tuple(n for _, n in TP_PARTS)
+    assert int(np.prod(shape[:3])) == seq_n and int(np.prod(shape[3:])) == tp_n
+    fine = Mesh(mesh.devices.reshape(shape), SEQ + TP)
+    blocked = P(SEQ, TP)
     in_specs = (
-        P("seq", "tp"),
-        P(),
-        P("seq", "tp"),
-        P("seq", "tp"),
-        P("seq", "tp"),
-        P(),
-        P(),
-        P("tp", "seq"),
-        P(),
-        P(),
-    )
-    out_specs = P("seq", "tp")
-    return jax.shard_map(local, mesh=mesh, in_specs=in_specs, out_specs=out_specs, check_vma=False)
+        blocked,
+        P(),
+        blocked,
+        blocked,
+        blocked,
+        P(),
+        P(),
+        P(TP, SEQ),
+        P(),
+        P(),
+    )
+    return jax.shard_map(local, mesh=fine, in_specs=in_specs, out_specs=blocked, check_vma=False)

time: 812 us -> 411 us (0.51)
  the two profiles are of different devices: /device:TPU:6 before, /device:TPU:12 now
where the time goes in v1:
time: 411 us; the launch traced here: 409 us
  waiting for transfers between devices  128 us (31%)
  local copies, waits for them, and re-layouts  109 us (27%)
  starting transfers between devices  105 us (26%)
  other arithmetic  23.4 us (6%)
  blocking collectives  15.2 us (4%)
  between operations  14.5 us (4%)
  matrix products  13.6 us (3%)
    reduce_scatter x1, waiting for transfers between devices, local(): lax.psum_scatter(partial_out.astype(jnp.bfloat16), TP, scatter_dimension=...  70.4 us
    unnamed x76, local copies, waits for them, and re-layouts  38.5 us
    ppermute x8, starting transfers between devices, ring(): right = lax.ppermute(right, axis, bwd)  30.7 us
    ppermute x8, waiting for transfers between devices, ring(): left = lax.ppermute(left, axis, fwd)  28.5 us
    ppermute x8, starting transfers between devices, ring(): left = lax.ppermute(left, axis, fwd)  19.7 us
    ppermute x8, waiting for transfers between devices, ring(): right = lax.ppermute(right, axis, bwd)  18.6 us
    ppermute x4, starting transfers between devices, from_behind(): return lax.ppermute(block, axis, route)  17.6 us
    ppermute x4, starting transfers between devices, ring(): lax.ppermute(lax.slice_in_dim(right, k, None, axis=split_axis), axis, bwd)  17.1 us
  transfers between devices with their start and end apart: 31, of which 12 were waited for; matrix products, arithmetic and copies ran while one was open for 25% of the time, Pallas kernels for 0%

profile of v1, /device:TPU:12, one launch (start us, length us, event | category | flops | bytes accessed | tf_op | source)
XLA Modules:
  0.0 409.0 jit_solution(11120103514381818051)
XLA Ops:
  7.6 10.9 %collective-permute-start = (bf16[84,1536]{1,0:T(8,128)(2,1)S(1)}, bf16[84,1536]{1,0:T(8,128)(2,1)S(1)}, u32[]{:S(2)}, u32[]{:S(2)}) collective-permute-start(bf16[84,1536]{1,0:T(8,128)(2,1)S(1)} %get-tuple-element.25), channel_id=1, source_target_pairs={{0,256},{256,0},{1,257},{257,1},{2,258},{258,2},{3,259},{259,3},{4... | collective-permute-start | bytes 774152 | tf_op jit(solution)/shard_map/ppermute | solution.py:31
  18.5 6.6 %collective-permute-done = bf16[84,1536]{1,0:T(8,128)(2,1)S(1)} collective-permute-done((bf16[84,1536]{1,0:T(8,128)(2,1)S(1)}, bf16[84,1536]{1,0:T(8,128)(2,1)S(1)}, u32[]{:S(2)}, u32[]{:S(2)}) %collective-permute-start) | collective-permute-done | bytes 258080 | tf_op jit(solution)/shard_map/ppermute | solution.py:31
  43.3 3.8 collective-permute-start.2
  51.6 4.5 %collective-permute-start.3 = (bf16[2,84,768]{2,1,0:T(8,128)(2,1)S(1)}, bf16[2,84,768]{2,1,0:T(8,128)(2,1)S(1)}, u32[]{:S(2)}, u32[]{:S(2)}) collective-permute-start(bf16[2,84,768]{2,1,0:T(8,128)(2,1)S(1)} %collective-permute-done.2), channel_id=1, source_target_pairs={{0,224},{32,0},{64,32},{96,64},{128,96},{160,128},{192,160},{224,1... | collective-permute-start | bytes 774152 | tf_op jit(solution)/shard_map/ppermute | solution.py:37
  58.7 7.6 %collective-permute-done.6 = bf16[2,84,768]{2,1,0:T(8,128)(2,1)S(1)} collective-permute-done((bf16[2,84,768]{2,1,0:T(8,128)(2,1)S(1)}, bf16[2,84,768]{2,1,0:T(8,128)(2,1)S(1)}, u32[]{:S(2)}, u32[]{:S(2)}) %collective-permute-start.6) | collective-permute-done | bytes 258080 | tf_op jit(solution)/shard_map/ppermute | solution.py:36
  68.2 5.1 %collective-permute-start.8 = (bf16[1,84,768]{2,1,0:T(8,128)(2,1)S(1)}, bf16[1,84,768]{2,1,0:T(8,128)(2,1)S(1)}, u32[]{:S(2)}, u32[]{:S(2)}) collective-permute-start(bf16[1,84,768]{2,1,0:T(8,128)(2,1)S(1)} %slice.84), channel_id=1, source_target_pairs={{0,224},{32,0},{64,32},{96,64},{128,96},{160,128},{192,160},{224,1... | collective-permute-start | bytes 387080 | tf_op jit(solution)/shard_map/ppermute | solution.py:43
  86.8 5.1 %collective-permute-start.17 = (bf16[4,2,84,768]{3,0,2,1:T(4,128)(2,1)S(1)}, bf16[4,2,84,768]{3,0,2,1:T(4,128)(2,1)}, u32[]{:S(2)}, u32[]{:S(2)}) collective-permute-start(bf16[4,2,84,768]{3,0,2,1:T(4,128)(2,1)S(1)} %copy.160), channel_id=1, source_target_pairs={{0,224},{32,0},{64,32},{96,64},{128,96},{160,128},{192,160},{224,1... | collective-permute-start | bytes 3096584 | tf_op jit(solution)/shard_map/ppermute | solution.py:37
  93.9 16.2 %collective-permute-done.17 = bf16[4,2,84,768]{3,0,2,1:T(4,128)(2,1)} collective-permute-done((bf16[4,2,84,768]{3,0,2,1:T(4,128)(2,1)S(1)}, bf16[4,2,84,768]{3,0,2,1:T(4,128)(2,1)}, u32[]{:S(2)}, u32[]{:S(2)}) %collective-permute-start.17) | collective-permute-done | bytes 1032224 | tf_op jit(solution)/shard_map/ppermute | solution.py:37
  110.1 4.4 %collective-permute-start.18 = (bf16[4,2,84,768]{3,0,2,1:T(4,128)(2,1)}, bf16[4,2,84,768]{3,0,2,1:T(4,128)(2,1)}, u32[]{:S(2)}, u32[]{:S(2)}) collective-permute-start(bf16[4,2,84,768]{3,0,2,1:T(4,128)(2,1)} %collective-permute-done.17), channel_id=1, source_target_pairs={{0,224},{32,0},{64,32},{96,64},{128,96},{160,128},{192,160},{224,1... | collective-permute-start | bytes 3096584 | tf_op jit(solution)/shard_map/ppermute | solution.py:37
  119.4 8.2 %collective-permute-done.10 = bf16[8,2,84,768]{3,0,2,1:T(8,128)(2,1)S(1)} collective-permute-done((bf16[8,2,84,768]{3,0,2,1:T(8,128)(2,1)}, bf16[8,2,84,768]{3,0,2,1:T(8,128)(2,1)S(1)}, u32[]{:S(2)}, u32[]{:S(2)}) %collective-permute-start.10) | collective-permute-done | bytes 2064416 | tf_op jit(solution)/shard_map/ppermute | solution.py:36
  132.1 3.7 collective-permute-start.12
  135.8 5.1 %collective-permute-start.19 = (bf16[4,2,84,768]{3,0,2,1:T(4,128)(2,1)}, bf16[4,2,84,768]{3,0,2,1:T(4,128)(2,1)S(1)}, u32[]{:S(2)}, u32[]{:S(2)}) collective-permute-start(bf16[4,2,84,768]{3,0,2,1:T(4,128)(2,1)} %collective-permute-done.18), channel_id=1, source_target_pairs={{0,224},{32,0},{64,32},{96,64},{128,96},{160,128},{192,160},{224,1... | collective-permute-start | bytes 3096584 | tf_op jit(solution)/shard_map/ppermute | solution.py:37
  151.4 11.7 %collective-permute-done.22 = bf16[4,2,84,768]{3,0,2,1:T(4,128)(2,1)S(1)} collective-permute-done((bf16[4,2,84,768]{3,0,2,1:T(4,128)(2,1)}, bf16[4,2,84,768]{3,0,2,1:T(4,128)(2,1)S(1)}, u32[]{:S(2)}, u32[]{:S(2)}) %collective-permute-start.22) | collective-permute-done | bytes 1032224 | tf_op jit(solution)/shard_map/ppermute | solution.py:36
  168.3 5.6 %collective-permute-start.24 = (bf16[2,2,84,768]{3,1,2,0:T(2,128)(2,1)}, bf16[2,2,84,768]{3,1,2,0:T(2,128)(2,1)}, u32[]{:S(2)}, u32[]{:S(2)}) collective-permute-start(bf16[2,2,84,768]{3,1,2,0:T(2,128)(2,1)} %copy.166), channel_id=1, source_target_pairs={{0,224},{32,0},{64,32},{96,64},{128,96},{160,128},{192,160},{224,1... | collective-permute-start | bytes 1548296 | tf_op jit(solution)/shard_map/ppermute | solution.py:43
  187.7 7.1 %constant_dynamic-slice_fusion.1 = bf16[8,4,2,84,768]{4,0,3,2,1:T(8,128)(2,1)} fusion(bf16[8,8,2,84,768]{4,0,3,2,1:T(8,128)(2,1)} %bitcast_dynamic-update-slice_fusion.1, s32[]{:T(128)S(6)} %select_n.67), kind=kLoop, calls=%fused_computation.129 | loop fusion | bytes 16515076 | tf_op jit(solution)/shard_map/jit(_roll_dynamic)/dynamic_slice | solution.py:53
  194.8 8.5 %copy.159 = bf16[8,4,2,84,768]{4,3,2,1,0:T(8,128)(2,1)} copy(bf16[8,4,2,84,768]{4,0,3,2,1:T(8,128)(2,1)} %constant_dynamic-slice_fusion.1) | data formatting | bytes 16515072 | tf_op jit(solution)/shard_map/jit(_roll_dynamic)/dynamic_slice | solution.py:53
  203.3 12.4 %reshape.191 = bf16[5376,768]{1,0:T(8,128)(2,1)} reshape(bf16[8,4,2,84,768]{4,3,2,1,0:T(8,128)(2,1)} %copy.159) | data formatting | bytes 16515072 | tf_op jit(solution)/shard_map/reshape | solution.py:110
  215.7 5.3 %slice.101 = bf16[5376,512]{1,0:T(8,128)(2,1)} slice(bf16[5376,768]{1,0:T(8,128)(2,1)} %reshape.191), slice={[0:5376], [256:768]} | slice | bytes 11010048 | tf_op jit(solution)/shard_map/slice | solution.py:150
  221.0 9.0 %dot_general.29 = bf16[8,4,2,84,512]{4,3,2,1,0:T(8,128)(2,1)} reshape(bf16[5376,512]{1,0:T(8,128)(2,1)} %slice.101) | data formatting | bytes 11010048 | tf_op jit(solution)/shard_map/dot_general | solution.py:179
  263.6 5.9 %fusion.19 = f32[256,768]{1,0:T(8,128)S(1)} fusion(bf16[16,4,2,84,768]{4,3,2,1,0:T(8,128)(2,1)} %bitcast_dynamic-update-slice_fusion.7, s32[]{:T(128)S(6)} %select_n.65, bf16[256,2,8,4,84]{0,4,3,2,1:T(8,128)(2,1)S(1)} %reshape.189), kind=kOutput, calls=%fused_computation.32 | convolution fusion | flops 2113929216 | bytes 12189700 | tf_op jit(solution)/shard_map/dot_general | solution.py:144
  286.2 6.4 %collective-permute-start.26 = (bf16[2,256,256]{1,2,0:T(8,128)(2,1)S(1)}, bf16[2,256,256]{1,2,0:T(8,128)(2,1)S(1)}, u32[]{:S(2)}, u32[]{:S(2)}) collective-permute-start(bf16[2,256,256]{1,2,0:T(8,128)(2,1)S(1)} %pad_maximum_fusion.2), channel_id=1, source_target_pairs={{0,24},{8,32},{16,40},{24,48},{32,56},{40,64},{48,72},{56,80},{64,... | collective-permute-start | bytes 786440 | tf_op jit(solution)/shard_map/ppermute | solution.py:22
  294.5 7.2 %collective-permute-start.28 = (bf16[2,256,256]{1,2,0:T(8,128)(2,1)S(1)}, bf16[2,256,256]{1,2,0:T(8,128)(2,1)S(1)}, u32[]{:S(2)}, u32[]{:S(2)}) collective-permute-start(bf16[2,256,256]{1,2,0:T(8,128)(2,1)S(1)} %pad_maximum_fusion.2), channel_id=1, source_target_pairs={{0,8},{8,16},{16,24},{24,32},{32,40},{40,48},{48,56},{56,64},{64,7... | collective-permute-start | bytes 786440 | tf_op jit(solution)/shard_map/ppermute | solution.py:22
  313.5 70.4 %reduce-scatter.2.cloned.1.call-done = bf16[256,672]{0,1:T(8,128)(2,1)} async-done(((bf16[256,5376]{0,1:T(8,128)(2,1)}), bf16[256,672]{0,1:T(8,128)(2,1)}) %reduce-scatter.2.cloned.1.call-update) | async-done | bytes 344080 | tf_op jit(solution)/shard_map/reduce_scatter | solution.py:190
  385.0 15.2 %psum.7 = f32[256]{0:T(256)S(1)} all-reduce(f32[256]{0:T(256)S(1)} %fusion.41), channel_id=1, replica_groups=mesh['zh'=2,'y'=8,'x'=4,'zl'=4,'c'=2] {'zl','c'}, use_global_device_ids=true, to_apply=%region_7.8 | all-reduce | flops 256 | bytes 2048 | tf_op jit(solution)/shard_map/psum | solution.py:194
  (200 shorter events, 148.6 us)
Async XLA Ops:
  6.5 247.3 %all-gather.2.cloned.1.call-start = ((), (), s32[]{:S(2)}) async-start(), calls=%async_computation.1 | async-start | bytes 3096576 | tf_op jit(solution)/shard_map/all_gather | solution.py:112
  7.6 17.5 %collective-permute-start = (bf16[84,1536]{1,0:T(8,128)(2,1)S(1)}, bf16[84,1536]{1,0:T(8,128)(2,1)S(1)}, u32[]{:S(2)}, u32[]{:S(2)}) collective-permute-start(bf16[84,1536]{1,0:T(8,128)(2,1)S(1)} %get-tuple-element.25), channel_id=1, source_target_pairs={{0,256},{256,0},{1,257},{257,1},{2,258},{258,2},{3,259},{259,3},{4... | collective-permute-start | bytes 774152 | tf_op jit(solution)/shard_map/ppermute | solution.py:31
  25.5 11.8 %collective-permute-start.14 = (bf16[2,84,768]{2,1,0:T(8,128)(2,1)S(1)}, bf16[2,84,768]{2,1,0:T(8,128)(2,1)S(1)}, u32[]{:S(2)}, u32[]{:S(2)}) collective-permute-start(bf16[2,84,768]{2,1,0:T(8,128)(2,1)S(1)} %get-tuple-element.19), channel_id=1, source_target_pairs={{0,8},{8,16},{16,24},{24,0},{1,9},{9,17},{17,25},{25,1},{2,10},{10... | collective-permute-start | bytes 774152 | tf_op jit(solution)/shard_map/ppermute | solution.py:36
  28.6 11.8 %collective-permute-start.13 = (bf16[2,84,768]{2,1,0:T(8,128)(2,1)S(1)}, bf16[2,84,768]{2,1,0:T(8,128)(2,1)S(1)}, u32[]{:S(2)}, u32[]{:S(2)}) collective-permute-start(bf16[2,84,768]{2,1,0:T(8,128)(2,1)S(1)} %get-tuple-element.19), channel_id=1, source_target_pairs={{0,24},{8,0},{16,8},{24,16},{1,25},{9,1},{17,9},{25,17},{2,26},{10... | collective-permute-start | bytes 774152 | tf_op jit(solution)/shard_map/ppermute | solution.py:37
  31.4 11.9 %collective-permute-start.1 = (bf16[2,84,768]{2,1,0:T(8,128)(2,1)S(1)}, bf16[2,84,768]{2,1,0:T(8,128)(2,1)S(1)}, u32[]{:S(2)}, u32[]{:S(2)}) collective-permute-start(bf16[2,84,768]{2,1,0:T(8,128)(2,1)S(1)} %get-tuple-element.20), channel_id=1, source_target_pairs={{0,224},{32,0},{64,32},{96,64},{128,96},{160,128},{192,160},{224,1... | collective-permute-start | bytes 774152 | tf_op jit(solution)/shard_map/ppermute | solution.py:37
  33.8 13.3 %collective-permute-start.4 = (bf16[2,84,768]{2,1,0:T(8,128)(2,1)S(1)}, bf16[2,84,768]{2,1,0:T(8,128)(2,1)S(1)}, u32[]{:S(2)}, u32[]{:S(2)}) collective-permute-start(bf16[2,84,768]{2,1,0:T(8,128)(2,1)S(1)} %get-tuple-element.20), channel_id=1, source_target_pairs={{0,32},{32,64},{64,96},{96,128},{128,160},{160,192},{192,224},{224... | collective-permute-start | bytes 774152 | tf_op jit(solution)/shard_map/ppermute | solution.py:36
  37.4 11.8 %collective-permute-start.15 = (bf16[1,84,768]{2,1,0:T(8,128)(2,1)S(1)}, bf16[1,84,768]{2,1,0:T(8,128)(2,1)S(1)}, u32[]{:S(2)}, u32[]{:S(2)}) collective-permute-start(bf16[1,84,768]{2,1,0:T(8,128)(2,1)S(1)} %slice.89), channel_id=1, source_target_pairs={{0,8},{8,16},{16,24},{24,0},{1,9},{9,17},{17,25},{25,1},{2,10},{10... | collective-permute-start | bytes 387080 | tf_op jit(solution)/shard_map/ppermute | solution.py:42
  51.6 16.6 %collective-permute-start.3 = (bf16[2,84,768]{2,1,0:T(8,128)(2,1)S(1)}, bf16[2,84,768]{2,1,0:T(8,128)(2,1)S(1)}, u32[]{:S(2)}, u32[]{:S(2)}) collective-permute-start(bf16[2,84,768]{2,1,0:T(8,128)(2,1)S(1)} %collective-permute-done.2), channel_id=1, source_target_pairs={{0,224},{32,0},{64,32},{96,64},{128,96},{160,128},{192,160},{224,1... | collective-permute-start | bytes 774152 | tf_op jit(solution)/shard_map/ppermute | solution.py:37
  79.1 50.9 %collective-permute-start.9 = (bf16[8,2,84,768]{3,0,2,1:T(8,128)(2,1)}, bf16[8,2,84,768]{3,0,2,1:T(8,128)(2,1)}, u32[]{:S(2)}, u32[]{:S(2)}) collective-permute-start(bf16[8,2,84,768]{3,0,2,1:T(8,128)(2,1)} %get-tuple-element.10), channel_id=1, source_target_pairs={{0,24},{8,0},{16,8},{24,16},{1,25},{9,1},{17,9},{25,17},{2,26},{10... | collective-permute-start | bytes 6193160 | tf_op jit(solution)/shard_map/ppermute | solution.py:37
  81.7 45.9 %collective-permute-start.10 = (bf16[8,2,84,768]{3,0,2,1:T(8,128)(2,1)}, bf16[8,2,84,768]{3,0,2,1:T(8,128)(2,1)S(1)}, u32[]{:S(2)}, u32[]{:S(2)}) collective-permute-start(bf16[8,2,84,768]{3,0,2,1:T(8,128)(2,1)} %get-tuple-element.10), channel_id=1, source_target_pairs={{0,8},{8,16},{16,24},{24,0},{1,9},{9,17},{17,25},{25,1},{2,10},{10... | collective-permute-start | bytes 6193160 | tf_op jit(solution)/shard_map/ppermute | solution.py:36
  86.8 23.3 %collective-permute-start.17 = (bf16[4,2,84,768]{3,0,2,1:T(4,128)(2,1)S(1)}, bf16[4,2,84,768]{3,0,2,1:T(4,128)(2,1)}, u32[]{:S(2)}, u32[]{:S(2)}) collective-permute-start(bf16[4,2,84,768]{3,0,2,1:T(4,128)(2,1)S(1)} %copy.160), channel_id=1, source_target_pairs={{0,224},{32,0},{64,32},{96,64},{128,96},{160,128},{192,160},{224,1... | collective-permute-start | bytes 3096584 | tf_op jit(solution)/shard_map/ppermute | solution.py:37
  92.0 23.2 %collective-permute-start.20 = (bf16[4,2,84,768]{3,0,2,1:T(4,128)(2,1)S(1)}, bf16[4,2,84,768]{3,0,2,1:T(4,128)(2,1)}, u32[]{:S(2)}, u32[]{:S(2)}) collective-permute-start(bf16[4,2,84,768]{3,0,2,1:T(4,128)(2,1)S(1)} %copy.160), channel_id=1, source_target_pairs={{0,32},{32,64},{64,96},{96,128},{128,160},{160,192},{192,224},{224... | collective-permute-start | bytes 3096584 | tf_op jit(solution)/shard_map/ppermute | solution.py:36
  110.1 25.7 %collective-permute-start.18 = (bf16[4,2,84,768]{3,0,2,1:T(4,128)(2,1)}, bf16[4,2,84,768]{3,0,2,1:T(4,128)(2,1)}, u32[]{:S(2)}, u32[]{:S(2)}) collective-permute-start(bf16[4,2,84,768]{3,0,2,1:T(4,128)(2,1)} %collective-permute-done.17), channel_id=1, source_target_pairs={{0,224},{32,0},{64,32},{96,64},{128,96},{160,128},{192,160},{224,1... | collective-permute-start | bytes 3096584 | tf_op jit(solution)/shard_map/ppermute | solution.py:37
  115.2 25.8 %collective-permute-start.21 = (bf16[4,2,84,768]{3,0,2,1:T(4,128)(2,1)}, bf16[4,2,84,768]{3,0,2,1:T(4,128)(2,1)}, u32[]{:S(2)}, u32[]{:S(2)}) collective-permute-start(bf16[4,2,84,768]{3,0,2,1:T(4,128)(2,1)} %collective-permute-done.20), channel_id=1, source_target_pairs={{0,32},{32,64},{64,96},{96,128},{128,160},{160,192},{192,224},{224... | collective-permute-start | bytes 3096584 | tf_op jit(solution)/shard_map/ppermute | solution.py:36
  117.1 266.8 %reduce-scatter.2.cloned.1.call-start = ((), (), s32[]{:S(2)}) async-start(), calls=%async_computation.2 | async-start | bytes 3096576 | tf_op jit(solution)/shard_map/reduce_scatter | solution.py:190
  127.8 46.1 %collective-permute-start.11 = (bf16[4,2,84,768]{3,0,2,1:T(4,128)(2,1)S(1)}, bf16[4,2,84,768]{3,0,2,1:T(4,128)(2,1)S(1)}, u32[]{:S(2)}, u32[]{:S(2)}) collective-permute-start(bf16[4,2,84,768]{3,0,2,1:T(4,128)(2,1)S(1)} %slice.85), channel_id=1, source_target_pairs={{0,8},{8,16},{16,24},{24,0},{1,9},{9,17},{17,25},{25,1},{2,10},{10... | collective-permute-start | bytes 3096584 | tf_op jit(solution)/shard_map/ppermute | solution.py:42
  132.1 41.8 %collective-permute-start.12 = (bf16[4,2,84,768]{3,0,2,1:T(4,128)(2,1)S(1)}, bf16[4,2,84,768]{3,0,2,1:T(4,128)(2,1)S(1)}, u32[]{:S(2)}, u32[]{:S(2)}) collective-permute-start(bf16[4,2,84,768]{3,0,2,1:T(4,128)(2,1)S(1)} %slice.86), channel_id=1, source_target_pairs={{0,24},{8,0},{16,8},{24,16},{1,25},{9,1},{17,9},{25,17},{2,26},{10... | collective-permute-start | bytes 3096584 | tf_op jit(solution)/shard_map/ppermute | solution.py:43
  135.8 30.7 %collective-permute-start.19 = (bf16[4,2,84,768]{3,0,2,1:T(4,128)(2,1)}, bf16[4,2,84,768]{3,0,2,1:T(4,128)(2,1)S(1)}, u32[]{:S(2)}, u32[]{:S(2)}) collective-permute-start(bf16[4,2,84,768]{3,0,2,1:T(4,128)(2,1)} %collective-permute-done.18), channel_id=1, source_target_pairs={{0,224},{32,0},{64,32},{96,64},{128,96},{160,128},{192,160},{224,1... | collective-permute-start | bytes 3096584 | tf_op jit(solution)/shard_map/ppermute | solution.py:37
  140.9 22.1 %collective-permute-start.22 = (bf16[4,2,84,768]{3,0,2,1:T(4,128)(2,1)}, bf16[4,2,84,768]{3,0,2,1:T(4,128)(2,1)S(1)}, u32[]{:S(2)}, u32[]{:S(2)}) collective-permute-start(bf16[4,2,84,768]{3,0,2,1:T(4,128)(2,1)} %collective-permute-done.21), channel_id=1, source_target_pairs={{0,32},{32,64},{64,96},{96,128},{128,160},{160,192},{192,224},{224... | collective-permute-start | bytes 3096584 | tf_op jit(solution)/shard_map/ppermute | solution.py:36
  164.6 66.5 %collective-permute-start.23 = (bf16[2,2,84,768]{3,1,2,0:T(2,128)(2,1)}, bf16[2,2,84,768]{3,1,2,0:T(2,128)(2,1)}, u32[]{:S(2)}, u32[]{:S(2)}) collective-permute-start(bf16[2,2,84,768]{3,1,2,0:T(2,128)(2,1)} %copy.165), channel_id=1, source_target_pairs={{0,32},{32,64},{64,96},{96,128},{128,160},{160,192},{192,224},{224... | collective-permute-start | bytes 1548296 | tf_op jit(solution)/shard_map/ppermute | solution.py:42
  168.3 63.9 %collective-permute-start.24 = (bf16[2,2,84,768]{3,1,2,0:T(2,128)(2,1)}, bf16[2,2,84,768]{3,1,2,0:T(2,128)(2,1)}, u32[]{:S(2)}, u32[]{:S(2)}) collective-permute-start(bf16[2,2,84,768]{3,1,2,0:T(2,128)(2,1)} %copy.166), channel_id=1, source_target_pairs={{0,224},{32,0},{64,32},{96,64},{128,96},{160,128},{192,160},{224,1... | collective-permute-start | bytes 1548296 | tf_op jit(solution)/shard_map/ppermute | solution.py:43
  284.1 19.9 %collective-permute-start.25 = (bf16[2,256,256]{1,2,0:T(8,128)(2,1)S(1)}, bf16[2,256,256]{1,2,0:T(8,128)(2,1)S(1)}, u32[]{:S(2)}, u32[]{:S(2)}) collective-permute-start(bf16[2,256,256]{1,2,0:T(8,128)(2,1)S(1)} %pad_maximum_fusion.2), channel_id=1, source_target_pairs={{0,32},{8,40},{16,48},{24,56},{32,64},{40,72},{48,80},{56,88},{64,... | collective-permute-start | bytes 786440 | tf_op jit(solution)/shard_map/ppermute | solution.py:22
  286.2 17.9 %collective-permute-start.26 = (bf16[2,256,256]{1,2,0:T(8,128)(2,1)S(1)}, bf16[2,256,256]{1,2,0:T(8,128)(2,1)S(1)}, u32[]{:S(2)}, u32[]{:S(2)}) collective-permute-start(bf16[2,256,256]{1,2,0:T(8,128)(2,1)S(1)} %pad_maximum_fusion.2), channel_id=1, source_target_pairs={{0,24},{8,32},{16,40},{24,48},{32,56},{40,64},{48,72},{56,80},{64,... | collective-permute-start | bytes 786440 | tf_op jit(solution)/shard_map/ppermute | solution.py:22
  292.5 11.6 %collective-permute-start.27 = (bf16[2,256,256]{1,2,0:T(8,128)(2,1)S(1)}, bf16[2,256,256]{1,2,0:T(8,128)(2,1)S(1)}, u32[]{:S(2)}, u32[]{:S(2)}) collective-permute-start(bf16[2,256,256]{1,2,0:T(8,128)(2,1)S(1)} %pad_maximum_fusion.2), channel_id=1, source_target_pairs={{0,16},{8,24},{16,32},{24,40},{32,48},{40,56},{48,64},{56,72},{64,... | collective-permute-start | bytes 786440 | tf_op jit(solution)/shard_map/ppermute | solution.py:22
  (28 other events, 365.4 us)
Sparse Core Ops, SparseCore 0:
  117.2 56.9 all-gather.1
  312.9 71.0 reduce-scatter.1

commit v2 on v1

--- a/solution.py
+++ b/solution.py
@@ -41,16 +41,28 @@
         k = block.shape[split_axis] // 2
         top = lax.ppermute(lax.slice_in_dim(left, 0, k, axis=split_axis), axis, fwd)
         bottom = lax.ppermute(lax.slice_in_dim(right, k, None, axis=split_axis), axis, bwd)
-        out[n // 2] = jnp.concatenate([top, bottom], axis=split_axis)
+        out[n // 2] = (top, bottom)
     return out
 
 
-def gather_axis(block, axis, n, stack_axis, split_axis):
+def stacked_ring(block, axis, n, split_axis):
     parts = ring(block, axis, n, split_axis)
-    stacked = jnp.stack(parts, axis=stack_axis)
-    if n == 1:
-        return stacked
-    return jnp.roll(stacked, lax.axis_index(axis), axis=stack_axis)
+    whole = [jnp.concatenate(p, axis=split_axis) if isinstance(p, tuple) else p for p in parts]
+    return jnp.stack(whole, axis=0)
+
+
+def ring_pieces(block, axis, n, split_axis):
+    parts = ring(block, axis, n, split_axis)
+    full = block.shape[split_axis]
+    pieces = []
+    for d, p in enumerate(parts):
+        if isinstance(p, tuple):
+            k = p[0].shape[split_axis]
+            pieces.append((d, 0, k, p[0]))
+            pieces.append((d, k, full, p[1]))
+        else:
+            pieces.append((d, 0, full, p))
+    return pieces
 
 
 def norm_scale(value_matrix, gain):
@@ -96,27 +108,40 @@
     v_cols = value_weight.shape[1]
     shard_rows = w_query.shape[0]
 
+    nz, ny, nx = sizes["zh"], sizes["y"], sizes["x"]
     packed = jnp.concatenate([w_query, key_weight, value_weight, w_out.T], axis=1)
-    by_zh = gather_axis(packed, "zh", sizes["zh"], 0, None)
+    by_zh = stacked_ring(packed, "zh", nz, 0)
     split = q_cols + k_cols
     half_a = by_zh[:, :, :split]
     half_b = by_zh[:, :, split:]
-    a_x = gather_axis(half_a, "x", sizes["x"], 0, 0)
-    a_yx = gather_axis(a_x, "y", sizes["y"], 0, 0)
-    b_y = gather_axis(half_b, "y", sizes["y"], 0, 0)
-    b_yx = gather_axis(b_y, "x", sizes["x"], 1, 0)
-    full_rows = n_seq * shard_rows
-    a_flat = a_yx.reshape(full_rows, split)
-    b_flat = b_yx.reshape(full_rows, half_b.shape[-1])
+    a_x = stacked_ring(half_a, "x", nx, 0)
+    a_pieces = ring_pieces(a_x, "y", ny, 0)
+    b_y = stacked_ring(half_b, "y", ny, 0)
+    b_pieces = ring_pieces(b_y, "x", nx, 0)
 
     gathered = lax.all_gather(residual, TP, axis=1, tiled=True)
     normalized_input = norm_scale(gathered.astype(jnp.float32), input_gain).astype(jnp.bfloat16)
-    nz, ny, nx = sizes["zh"], sizes["y"], sizes["x"]
-    normed_perm = (
-        normalized_input.reshape(tok_rows, nz, ny, nx, shard_rows)
-        .transpose(0, 2, 3, 1, 4)
-        .reshape(tok_rows, full_rows)
-    )
+    at_zh, at_y, at_x = (lax.axis_index(name) for name in SEQ)
+    normed_rel = normalized_input.reshape(tok_rows, nz, ny, nx, shard_rows).transpose(0, 2, 3, 1, 4)
+    normed_rel = jnp.roll(normed_rel, -at_y, axis=1)
+    normed_rel = jnp.roll(normed_rel, -at_x, axis=2)
+    normed_rel = jnp.roll(normed_rel, -at_zh, axis=3)
+
+    def contract(lhs, piece):
+        return lax.dot_general(
+            lhs, piece, (((1, 2, 3), (0, 1, 2)), ((), ())), preferred_element_type=jnp.float32
+        )
+
+    qk = None
+    for dy, lo, hi, piece in a_pieces:
+        term = contract(normed_rel[:, dy, lo:hi], piece)
+        qk = term if qk is None else qk + term
+    projected_values = None
+    for dx, lo, hi, piece in b_pieces:
+        term = contract(normed_rel[:, lo:hi, dx], piece[..., :v_cols])
+        projected_values = term if projected_values is None else projected_values + term
+    queries_raw = qk[:, :q_cols]
+    unrotated_keys = qk[:, q_cols:]
     own_places = lax.dynamic_slice_in_dim(positions, seq_at * tok_rows, tok_rows, 0)
     reach = (LOOKBACK_SPAN - 2) // tok_rows + 1
 
@@ -141,13 +166,6 @@
         )
         return (total, summed)
 
-    qk = jnp.dot(normed_perm, a_flat, preferred_element_type=jnp.float32)
-    queries_raw = qk[:, :q_cols]
-    unrotated_keys = qk[:, q_cols:]
-    projected_values = jnp.dot(
-        normed_perm, b_flat[:, :v_cols], preferred_element_type=jnp.float32
-    )
-    out_perm = b_flat[:, v_cols:]
     key_matrix = rotary(
         norm_scale(unrotated_keys.reshape(tok_rows, local_kv, head_dim), key_gain), own_places
     )
@@ -176,19 +194,21 @@
     total = jnp.transpose(inner_total + outer_total, (2, 0, 1))
     merged = (inner_sum + outer_sum) / total[..., None]
     attended = merged.astype(jnp.bfloat16).reshape(tok_rows, local_kv * query_group * head_dim)
-    partial_perm = lax.dot_general(
-        attended,
-        out_perm,
-        (((1,), (1,)), ((), ())),
-        preferred_element_type=jnp.float32,
-    )
-    partial_out = (
-        partial_perm.reshape(tok_rows, ny, nx, nz, shard_rows)
-        .transpose(0, 3, 1, 2, 4)
-        .reshape(tok_rows, full_rows)
-    )
+    out_rel = jnp.zeros((tok_rows, ny, nx, nz, shard_rows), jnp.bfloat16)
+    for dx, lo, hi, piece in b_pieces:
+        cols = lax.dot_general(
+            attended,
+            piece[..., v_cols:],
+            (((1,), (3,)), ((), ())),
+            preferred_element_type=jnp.float32,
+        )
+        out_rel = out_rel.at[:, lo:hi, dx].set(cols.astype(jnp.bfloat16))
+    out_abs = jnp.roll(out_rel, at_y, axis=1)
+    out_abs = jnp.roll(out_abs, at_x, axis=2)
+    out_abs = jnp.roll(out_abs, at_zh, axis=3)
+    partial_out = out_abs.transpose(0, 3, 1, 2, 4).reshape(tok_rows, n_seq * shard_rows)
     summed_cols = lax.psum_scatter(
-        partial_out.astype(jnp.bfloat16), TP, scatter_dimension=1, tiled=True
+        partial_out, TP, scatter_dimension=1, tiled=True
     ).astype(jnp.float32)
     full_width = post_gain.shape[0]
     squares = lax.psum(jnp.sum(summed_cols * summed_cols, axis=1), TP)

time: 411 us -> 360 us (0.88)
  the two profiles are of different devices: /device:TPU:12 before, /device:TPU:10 now
where the time goes in v2:
time: 360 us; the launch traced here: 358 us
  waiting for transfers between devices  130 us (36%)
  starting transfers between devices  104 us (29%)
  local copies, waits for them, and re-layouts  42.6 us (12%)
  matrix products  25.8 us (7%)
  other arithmetic  25.2 us (7%)
  blocking collectives  15.2 us (4%)
  between operations  14.8 us (4%)
    reduce_scatter x1, waiting for transfers between devices, local(): lax.psum_scatter(partial_out, TP, scatter_dimension=1, tiled=True)  76.1 us
    ppermute x8, starting transfers between devices, ring(): left = lax.ppermute(left, axis, fwd)  27 us
    ppermute x8, waiting for transfers between devices, ring(): left = lax.ppermute(left, axis, fwd)  25.9 us
    ppermute x8, starting transfers between devices, ring(): right = lax.ppermute(right, axis, bwd)  23.7 us
    dot_general x14, matrix products, contract(): lax.dot_general(lhs, piece, (((1, 2, 3), (0, 1, 2)), ((), ())), preferred...  18.1 us
    ppermute x4, waiting for transfers between devices, ring(): lax.ppermute(lax.slice_in_dim(right, k, None, axis=split_axis), axis, bwd)  16.6 us
    ppermute x4, starting transfers between devices, from_behind(): return lax.ppermute(block, axis, route)  16.5 us
    psum x1, blocking collectives, local(): squares = lax.psum(jnp.sum(summed_cols * summed_cols, axis=1), TP)  15.2 us
  transfers between devices with their start and end apart: 31, of which 9 were waited for; matrix products, arithmetic and copies ran while one was open for 17% of the time, Pallas kernels for 0%

profile of v2, /device:TPU:10, one launch (start us, length us, event | category | flops | bytes accessed | tf_op | source)
XLA Modules:
  0.0 357.6 jit_solution(8039407627532864642)
XLA Ops:
  7.6 10.9 %collective-permute-start = (bf16[84,1536]{1,0:T(8,128)(2,1)S(1)}, bf16[84,1536]{1,0:T(8,128)(2,1)S(1)}, u32[]{:S(2)}, u32[]{:S(2)}) collective-permute-start(bf16[84,1536]{1,0:T(8,128)(2,1)S(1)} %get-tuple-element.81), channel_id=1, source_target_pairs={{0,256},{256,0},{1,257},{257,1},{2,258},{258,2},{3,259},{259,3},{4... | collective-permute-start | bytes 774152 | tf_op jit(solution)/shard_map/ppermute | solution.py:31
  18.5 6.6 %collective-permute-done = bf16[84,1536]{1,0:T(8,128)(2,1)S(1)} collective-permute-done((bf16[84,1536]{1,0:T(8,128)(2,1)S(1)}, bf16[84,1536]{1,0:T(8,128)(2,1)S(1)}, u32[]{:S(2)}, u32[]{:S(2)}) %collective-permute-start) | collective-permute-done | bytes 258080 | tf_op jit(solution)/shard_map/ppermute | solution.py:31
  27.6 3.4 collective-permute-start.14
  34.1 3.5 collective-permute-start.4
  37.7 3.2 collective-permute-start.16
  43.6 3.8 %collective-permute-start.2 = (bf16[2,84,768]{2,1,0:T(8,128)(2,1)}, bf16[2,84,768]{2,1,0:T(8,128)(2,1)S(1)}, u32[]{:S(2)}, u32[]{:S(2)}) collective-permute-start(bf16[2,84,768]{2,1,0:T(8,128)(2,1)} %collective-permute-done.1), channel_id=1, source_target_pairs={{0,224},{32,0},{64,32},{96,64},{128,96},{160,128},{192,160},{224,1... | collective-permute-start | bytes 774152 | tf_op jit(solution)/shard_map/ppermute | solution.py:37
  52.2 4.6 %collective-permute-start.3 = (bf16[2,84,768]{2,1,0:T(8,128)(2,1)S(1)}, bf16[2,84,768]{2,1,0:T(8,128)(2,1)S(1)}, u32[]{:S(2)}, u32[]{:S(2)}) collective-permute-start(bf16[2,84,768]{2,1,0:T(8,128)(2,1)S(1)} %collective-permute-done.2), channel_id=1, source_target_pairs={{0,224},{32,0},{64,32},{96,64},{128,96},{160,128},{192,160},{224,1... | collective-permute-start | bytes 774152 | tf_op jit(solution)/shard_map/ppermute | solution.py:37
  59.9 4.4 %collective-permute-start.20 = (bf16[4,2,84,768]{3,0,2,1:T(4,128)(2,1)S(1)}, bf16[4,2,84,768]{3,0,2,1:T(4,128)(2,1)}, u32[]{:S(2)}, u32[]{:S(2)}) collective-permute-start(bf16[4,2,84,768]{3,0,2,1:T(4,128)(2,1)S(1)} %copy.119), channel_id=1, source_target_pairs={{0,32},{32,64},{64,96},{96,128},{128,160},{160,192},{192,224},{224... | collective-permute-start | bytes 3096584 | tf_op jit(solution)/shard_map/ppermute | solution.py:36
  67.0 5.1 %collective-permute-start.8 = (bf16[1,84,768]{2,1,0:T(8,128)(2,1)S(1)}, bf16[1,84,768]{2,1,0:T(8,128)(2,1)S(1)}, u32[]{:S(2)}, u32[]{:S(2)}) collective-permute-start(bf16[1,84,768]{2,1,0:T(8,128)(2,1)S(1)} %slice.340), channel_id=1, source_target_pairs={{0,224},{32,0},{64,32},{96,64},{128,96},{160,128},{192,160},{224,1... | collective-permute-start | bytes 387080 | tf_op jit(solution)/shard_map/ppermute | solution.py:43
  74.1 16.6 %collective-permute-done.8 = bf16[1,84,768]{2,1,0:T(8,128)(2,1)S(1)} collective-permute-done((bf16[1,84,768]{2,1,0:T(8,128)(2,1)S(1)}, bf16[1,84,768]{2,1,0:T(8,128)(2,1)S(1)}, u32[]{:S(2)}, u32[]{:S(2)}) %collective-permute-start.8) | collective-permute-done | bytes 129056 | tf_op jit(solution)/shard_map/ppermute | solution.py:43
  95.1 4.2 %collective-permute-start.10 = (bf16[8,2,84,768]{3,0,2,1:T(8,128)(2,1)}, bf16[8,2,84,768]{3,0,2,1:T(8,128)(2,1)S(1)}, u32[]{:S(2)}, u32[]{:S(2)}) collective-permute-start(bf16[8,2,84,768]{3,0,2,1:T(8,128)(2,1)} %copy.113), channel_id=1, source_target_pairs={{0,8},{8,16},{16,24},{24,0},{1,9},{9,17},{17,25},{25,1},{2,10},{10... | collective-permute-start | bytes 6193160 | tf_op jit(solution)/shard_map/ppermute | solution.py:36
  101.8 3.6 %collective-permute-start.21 = (bf16[4,2,84,768]{3,0,2,1:T(4,128)(2,1)}, bf16[4,2,84,768]{3,0,2,1:T(4,128)(2,1)}, u32[]{:S(2)}, u32[]{:S(2)}) collective-permute-start(bf16[4,2,84,768]{3,0,2,1:T(4,128)(2,1)} %collective-permute-done.20), channel_id=1, source_target_pairs={{0,32},{32,64},{64,96},{96,128},{128,160},{160,192},{192,224},{224... | collective-permute-start | bytes 3096584 | tf_op jit(solution)/shard_map/ppermute | solution.py:36
  108.1 16.4 %collective-permute-done.21 = bf16[4,2,84,768]{3,0,2,1:T(4,128)(2,1)} collective-permute-done((bf16[4,2,84,768]{3,0,2,1:T(4,128)(2,1)}, bf16[4,2,84,768]{3,0,2,1:T(4,128)(2,1)}, u32[]{:S(2)}, u32[]{:S(2)}) %collective-permute-start.21) | collective-permute-done | bytes 1032224 | tf_op jit(solution)/shard_map/ppermute | solution.py:36
  124.5 4.0 %collective-permute-start.22 = (bf16[4,2,84,768]{3,0,2,1:T(4,128)(2,1)}, bf16[4,2,84,768]{3,0,2,1:T(4,128)(2,1)}, u32[]{:S(2)}, u32[]{:S(2)}) collective-permute-start(bf16[4,2,84,768]{3,0,2,1:T(4,128)(2,1)} %collective-permute-done.21), channel_id=1, source_target_pairs={{0,32},{32,64},{64,96},{96,128},{128,160},{160,192},{192,224},{224... | collective-permute-start | bytes 3096584 | tf_op jit(solution)/shard_map/ppermute | solution.py:36
  131.3 9.1 %collective-permute-done.10 = bf16[8,2,84,768]{3,0,2,1:T(8,128)(2,1)S(1)} collective-permute-done((bf16[8,2,84,768]{3,0,2,1:T(8,128)(2,1)}, bf16[8,2,84,768]{3,0,2,1:T(8,128)(2,1)S(1)}, u32[]{:S(2)}, u32[]{:S(2)}) %collective-permute-start.10) | collective-permute-done | bytes 2064416 | tf_op jit(solution)/shard_map/ppermute | solution.py:36
  141.8 3.3 collective-permute-start.11
  148.3 3.4 collective-permute-start.12
  164.1 4.1 %collective-permute-start.23 = (bf16[2,2,84,768]{3,1,2,0:T(2,128)(2,1)}, bf16[2,2,84,768]{3,1,2,0:T(2,128)(2,1)}, u32[]{:S(2)}, u32[]{:S(2)}) collective-permute-start(bf16[2,2,84,768]{3,1,2,0:T(2,128)(2,1)} %copy.124), channel_id=1, source_target_pairs={{0,32},{32,64},{64,96},{96,128},{128,160},{160,192},{192,224},{224... | collective-permute-start | bytes 1548296 | tf_op jit(solution)/shard_map/ppermute | solution.py:42
  183.1 3.6 fusion.2
  186.6 3.5 reshape.400
  222.1 7.6 %collective-permute-start.27 = (bf16[2,256,256]{1,2,0:T(8,128)(2,1)S(1)}, bf16[2,256,256]{1,2,0:T(8,128)(2,1)S(1)}, u32[]{:S(2)}, u32[]{:S(2)}) collective-permute-start(bf16[2,256,256]{1,2,0:T(8,128)(2,1)S(1)} %pad_maximum_fusion.4), channel_id=1, source_target_pairs={{0,16},{8,24},{16,32},{24,40},{32,48},{40,56},{48,64},{56,72},{64,... | collective-permute-start | bytes 786440 | tf_op jit(solution)/shard_map/ppermute | solution.py:22
  231.6 4.1 %collective-permute-start.25 = (bf16[2,256,256]{1,2,0:T(8,128)(2,1)S(1)}, bf16[2,256,256]{1,2,0:T(8,128)(2,1)S(1)}, u32[]{:S(2)}, u32[]{:S(2)}) collective-permute-start(bf16[2,256,256]{1,2,0:T(8,128)(2,1)S(1)} %pad_maximum_fusion.4), channel_id=1, source_target_pairs={{0,32},{8,40},{16,48},{24,56},{32,64},{40,72},{48,80},{56,88},{64,... | collective-permute-start | bytes 786440 | tf_op jit(solution)/shard_map/ppermute | solution.py:22
  256.4 76.1 %reduce-scatter.2.cloned.1.call-done = bf16[256,672]{0,1:T(8,128)(2,1)} async-done(((bf16[256,5376]{0,1:T(8,128)(2,1)}), bf16[256,672]{0,1:T(8,128)(2,1)}) %reduce-scatter.2.cloned.1.call-update) | async-done | bytes 344080 | tf_op jit(solution)/shard_map/reduce_scatter | solution.py:210
  333.6 15.2 %psum.7 = f32[256]{0:T(256)S(1)} all-reduce(f32[256]{0:T(256)S(1)} %fusion.93), channel_id=1, replica_groups=mesh['zh'=2,'y'=8,'x'=4,'zl'=4,'c'=2] {'zl','c'}, use_global_device_ids=true, to_apply=%region_8.12 | all-reduce | flops 256 | bytes 2048 | tf_op jit(solution)/shard_map/psum | solution.py:214
  (221 shorter events, 122.4 us)
Async XLA Ops:
  6.5 173.8 %all-gather.2.cloned.1.call-start = ((), (), s32[]{:S(2)}) async-start(), calls=%async_computation.1 | async-start | bytes 3096576 | tf_op jit(solution)/shard_map/all_gather | solution.py:122
  7.6 17.5 %collective-permute-start = (bf16[84,1536]{1,0:T(8,128)(2,1)S(1)}, bf16[84,1536]{1,0:T(8,128)(2,1)S(1)}, u32[]{:S(2)}, u32[]{:S(2)}) collective-permute-start(bf16[84,1536]{1,0:T(8,128)(2,1)S(1)} %get-tuple-element.81), channel_id=1, source_target_pairs={{0,256},{256,0},{1,257},{257,1},{2,258},{258,2},{3,259},{259,3},{4... | collective-permute-start | bytes 774152 | tf_op jit(solution)/shard_map/ppermute | solution.py:31
  27.6 13.4 %collective-permute-start.14 = (bf16[2,84,768]{2,1,0:T(8,128)(2,1)S(1)}, bf16[2,84,768]{2,1,0:T(8,128)(2,1)S(1)}, u32[]{:S(2)}, u32[]{:S(2)}) collective-permute-start(bf16[2,84,768]{2,1,0:T(8,128)(2,1)S(1)} %pad_maximum_fusion.1), channel_id=1, source_target_pairs={{0,8},{8,16},{16,24},{24,0},{1,9},{9,17},{17,25},{25,1},{2,10},{10... | collective-permute-start | bytes 774152 | tf_op jit(solution)/shard_map/ppermute | solution.py:36
  34.1 13.4 %collective-permute-start.4 = (bf16[2,84,768]{2,1,0:T(8,128)(2,1)}, bf16[2,84,768]{2,1,0:T(8,128)(2,1)}, u32[]{:S(2)}, u32[]{:S(2)}) collective-permute-start(bf16[2,84,768]{2,1,0:T(8,128)(2,1)} %get-tuple-element.71), channel_id=1, source_target_pairs={{0,32},{32,64},{64,96},{96,128},{128,160},{160,192},{192,224},{224... | collective-permute-start | bytes 774152 | tf_op jit(solution)/shard_map/ppermute | solution.py:36
  37.6 294.9 %reduce-scatter.2.cloned.1.call-start = ((), (), s32[]{:S(2)}) async-start(), calls=%async_computation.2 | async-start | bytes 3096576 | tf_op jit(solution)/shard_map/reduce_scatter | solution.py:210
  37.7 12.8 %collective-permute-start.16 = (bf16[1,84,768]{2,1,0:T(8,128)(2,1)S(1)}, bf16[1,84,768]{2,1,0:T(8,128)(2,1)S(1)}, u32[]{:S(2)}, u32[]{:S(2)}) collective-permute-start(bf16[1,84,768]{2,1,0:T(8,128)(2,1)S(1)} %slice.354), channel_id=1, source_target_pairs={{0,24},{8,0},{16,8},{24,16},{1,25},{9,1},{17,9},{25,17},{2,26},{10... | collective-permute-start | bytes 387080 | tf_op jit(solution)/shard_map/ppermute | solution.py:43
  52.2 14.8 %collective-permute-start.3 = (bf16[2,84,768]{2,1,0:T(8,128)(2,1)S(1)}, bf16[2,84,768]{2,1,0:T(8,128)(2,1)S(1)}, u32[]{:S(2)}, u32[]{:S(2)}) collective-permute-start(bf16[2,84,768]{2,1,0:T(8,128)(2,1)S(1)} %collective-permute-done.2), channel_id=1, source_target_pairs={{0,224},{32,0},{64,32},{96,64},{128,96},{160,128},{192,160},{224,1... | collective-permute-start | bytes 774152 | tf_op jit(solution)/shard_map/ppermute | solution.py:37
  57.2 14.9 %collective-permute-start.6 = (bf16[2,84,768]{2,1,0:T(8,128)(2,1)S(1)}, bf16[2,84,768]{2,1,0:T(8,128)(2,1)S(1)}, u32[]{:S(2)}, u32[]{:S(2)}) collective-permute-start(bf16[2,84,768]{2,1,0:T(8,128)(2,1)S(1)} %collective-permute-done.5), channel_id=1, source_target_pairs={{0,32},{32,64},{64,96},{96,128},{128,160},{160,192},{192,224},{224... | collective-permute-start | bytes 774152 | tf_op jit(solution)/shard_map/ppermute | solution.py:36
  59.9 41.9 %collective-permute-start.20 = (bf16[4,2,84,768]{3,0,2,1:T(4,128)(2,1)S(1)}, bf16[4,2,84,768]{3,0,2,1:T(4,128)(2,1)}, u32[]{:S(2)}, u32[]{:S(2)}) collective-permute-start(bf16[4,2,84,768]{3,0,2,1:T(4,128)(2,1)S(1)} %copy.119), channel_id=1, source_target_pairs={{0,32},{32,64},{64,96},{96,128},{128,160},{160,192},{192,224},{224... | collective-permute-start | bytes 3096584 | tf_op jit(solution)/shard_map/ppermute | solution.py:36
  64.3 41.2 %collective-permute-start.17 = (bf16[4,2,84,768]{3,0,2,1:T(4,128)(2,1)S(1)}, bf16[4,2,84,768]{3,0,2,1:T(4,128)(2,1)}, u32[]{:S(2)}, u32[]{:S(2)}) collective-permute-start(bf16[4,2,84,768]{3,0,2,1:T(4,128)(2,1)S(1)} %copy.119), channel_id=1, source_target_pairs={{0,224},{32,0},{64,32},{96,64},{128,96},{160,128},{192,160},{224,1... | collective-permute-start | bytes 3096584 | tf_op jit(solution)/shard_map/ppermute | solution.py:37
  67.0 23.7 %collective-permute-start.8 = (bf16[1,84,768]{2,1,0:T(8,128)(2,1)S(1)}, bf16[1,84,768]{2,1,0:T(8,128)(2,1)S(1)}, u32[]{:S(2)}, u32[]{:S(2)}) collective-permute-start(bf16[1,84,768]{2,1,0:T(8,128)(2,1)S(1)} %slice.340), channel_id=1, source_target_pairs={{0,224},{32,0},{64,32},{96,64},{128,96},{160,128},{192,160},{224,1... | collective-permute-start | bytes 387080 | tf_op jit(solution)/shard_map/ppermute | solution.py:43
  72.2 18.5 %collective-permute-start.7 = (bf16[1,84,768]{2,1,0:T(8,128)(2,1)S(1)}, bf16[1,84,768]{2,1,0:T(8,128)(2,1)S(1)}, u32[]{:S(2)}, u32[]{:S(2)}) collective-permute-start(bf16[1,84,768]{2,1,0:T(8,128)(2,1)S(1)} %slice.339), channel_id=1, source_target_pairs={{0,32},{32,64},{64,96},{96,128},{128,160},{160,192},{192,224},{224... | collective-permute-start | bytes 387080 | tf_op jit(solution)/shard_map/ppermute | solution.py:42
  95.1 45.3 %collective-permute-start.10 = (bf16[8,2,84,768]{3,0,2,1:T(8,128)(2,1)}, bf16[8,2,84,768]{3,0,2,1:T(8,128)(2,1)S(1)}, u32[]{:S(2)}, u32[]{:S(2)}) collective-permute-start(bf16[8,2,84,768]{3,0,2,1:T(8,128)(2,1)} %copy.113), channel_id=1, source_target_pairs={{0,8},{8,16},{16,24},{24,0},{1,9},{9,17},{17,25},{25,1},{2,10},{10... | collective-permute-start | bytes 6193160 | tf_op jit(solution)/shard_map/ppermute | solution.py:36
  99.3 45.9 %collective-permute-start.9 = (bf16[8,2,84,768]{3,0,2,1:T(8,128)(2,1)}, bf16[8,2,84,768]{3,0,2,1:T(8,128)(2,1)}, u32[]{:S(2)}, u32[]{:S(2)}) collective-permute-start(bf16[8,2,84,768]{3,0,2,1:T(8,128)(2,1)} %copy.113), channel_id=1, source_target_pairs={{0,24},{8,0},{16,8},{24,16},{1,25},{9,1},{17,9},{25,17},{2,26},{10... | collective-permute-start | bytes 6193160 | tf_op jit(solution)/shard_map/ppermute | solution.py:37
  101.8 22.7 %collective-permute-start.21 = (bf16[4,2,84,768]{3,0,2,1:T(4,128)(2,1)}, bf16[4,2,84,768]{3,0,2,1:T(4,128)(2,1)}, u32[]{:S(2)}, u32[]{:S(2)}) collective-permute-start(bf16[4,2,84,768]{3,0,2,1:T(4,128)(2,1)} %collective-permute-done.20), channel_id=1, source_target_pairs={{0,32},{32,64},{64,96},{96,128},{128,160},{160,192},{192,224},{224... | collective-permute-start | bytes 3096584 | tf_op jit(solution)/shard_map/ppermute | solution.py:36
  105.5 23.0 %collective-permute-start.18 = (bf16[4,2,84,768]{3,0,2,1:T(4,128)(2,1)}, bf16[4,2,84,768]{3,0,2,1:T(4,128)(2,1)}, u32[]{:S(2)}, u32[]{:S(2)}) collective-permute-start(bf16[4,2,84,768]{3,0,2,1:T(4,128)(2,1)} %collective-permute-done.17), channel_id=1, source_target_pairs={{0,224},{32,0},{64,32},{96,64},{128,96},{160,128},{192,160},{224,1... | collective-permute-start | bytes 3096584 | tf_op jit(solution)/shard_map/ppermute | solution.py:37
  124.5 36.8 %collective-permute-start.22 = (bf16[4,2,84,768]{3,0,2,1:T(4,128)(2,1)}, bf16[4,2,84,768]{3,0,2,1:T(4,128)(2,1)}, u32[]{:S(2)}, u32[]{:S(2)}) collective-permute-start(bf16[4,2,84,768]{3,0,2,1:T(4,128)(2,1)} %collective-permute-done.21), channel_id=1, source_target_pairs={{0,32},{32,64},{64,96},{96,128},{128,160},{160,192},{192,224},{224... | collective-permute-start | bytes 3096584 | tf_op jit(solution)/shard_map/ppermute | solution.py:36
  128.5 39.7 %collective-permute-start.19 = (bf16[4,2,84,768]{3,0,2,1:T(4,128)(2,1)}, bf16[4,2,84,768]{3,0,2,1:T(4,128)(2,1)S(1)}, u32[]{:S(2)}, u32[]{:S(2)}) collective-permute-start(bf16[4,2,84,768]{3,0,2,1:T(4,128)(2,1)} %collective-permute-done.18), channel_id=1, source_target_pairs={{0,224},{32,0},{64,32},{96,64},{128,96},{160,128},{192,160},{224,1... | collective-permute-start | bytes 3096584 | tf_op jit(solution)/shard_map/ppermute | solution.py:37
  141.8 30.4 %collective-permute-start.11 = (bf16[4,2,84,768]{3,0,2,1:T(4,128)(2,1)}, bf16[4,2,84,768]{3,0,2,1:T(4,128)(2,1)}, u32[]{:S(2)}, u32[]{:S(2)}) collective-permute-start(bf16[4,2,84,768]{3,0,2,1:T(4,128)(2,1)} %slice.345), channel_id=1, source_target_pairs={{0,8},{8,16},{16,24},{24,0},{1,9},{9,17},{17,25},{25,1},{2,10},{10... | collective-permute-start | bytes 3096584 | tf_op jit(solution)/shard_map/ppermute | solution.py:42
  148.3 28.0 %collective-permute-start.12 = (bf16[4,2,84,768]{3,0,2,1:T(4,128)(2,1)}, bf16[4,2,84,768]{3,0,2,1:T(4,128)(2,1)}, u32[]{:S(2)}, u32[]{:S(2)}) collective-permute-start(bf16[4,2,84,768]{3,0,2,1:T(4,128)(2,1)} %slice.348), channel_id=1, source_target_pairs={{0,24},{8,0},{16,8},{24,16},{1,25},{9,1},{17,9},{25,17},{2,26},{10... | collective-permute-start | bytes 3096584 | tf_op jit(solution)/shard_map/ppermute | solution.py:43
  164.1 35.5 %collective-permute-start.23 = (bf16[2,2,84,768]{3,1,2,0:T(2,128)(2,1)}, bf16[2,2,84,768]{3,1,2,0:T(2,128)(2,1)}, u32[]{:S(2)}, u32[]{:S(2)}) collective-permute-start(bf16[2,2,84,768]{3,1,2,0:T(2,128)(2,1)} %copy.124), channel_id=1, source_target_pairs={{0,32},{32,64},{64,96},{96,128},{128,160},{160,192},{192,224},{224... | collective-permute-start | bytes 1548296 | tf_op jit(solution)/shard_map/ppermute | solution.py:42
  169.9 34.6 %collective-permute-start.24 = (bf16[2,2,84,768]{3,1,2,0:T(2,128)(2,1)}, bf16[2,2,84,768]{3,1,2,0:T(2,128)(2,1)}, u32[]{:S(2)}, u32[]{:S(2)}) collective-permute-start(bf16[2,2,84,768]{3,1,2,0:T(2,128)(2,1)} %copy.126), channel_id=1, source_target_pairs={{0,224},{32,0},{64,32},{96,64},{128,96},{160,128},{192,160},{224,1... | collective-permute-start | bytes 1548296 | tf_op jit(solution)/shard_map/ppermute | solution.py:43
  219.2 21.8 %collective-permute-start.28 = (bf16[2,256,256]{1,2,0:T(8,128)(2,1)S(1)}, bf16[2,256,256]{1,2,0:T(8,128)(2,1)S(1)}, u32[]{:S(2)}, u32[]{:S(2)}) collective-permute-start(bf16[2,256,256]{1,2,0:T(8,128)(2,1)S(1)} %pad_maximum_fusion.4), channel_id=1, source_target_pairs={{0,8},{8,16},{16,24},{24,32},{32,40},{40,48},{48,56},{56,64},{64,7... | collective-permute-start | bytes 786440 | tf_op jit(solution)/shard_map/ppermute | solution.py:22
  222.1 18.9 %collective-permute-start.27 = (bf16[2,256,256]{1,2,0:T(8,128)(2,1)S(1)}, bf16[2,256,256]{1,2,0:T(8,128)(2,1)S(1)}, u32[]{:S(2)}, u32[]{:S(2)}) collective-permute-start(bf16[2,256,256]{1,2,0:T(8,128)(2,1)S(1)} %pad_maximum_fusion.4), channel_id=1, source_target_pairs={{0,16},{8,24},{16,32},{24,40},{32,48},{40,56},{48,64},{56,72},{64,... | collective-permute-start | bytes 786440 | tf_op jit(solution)/shard_map/ppermute | solution.py:22
  (44 other events, 573.3 us)
Sparse Core Ops, SparseCore 0:
  37.7 52.2 all-gather.1
  255.7 76.7 reduce-scatter.1

commit v3 on v2

--- a/solution.py
+++ b/solution.py
@@ -63,6 +63,31 @@
         else:
             pieces.append((d, 0, full, p))
     return pieces
+
+
+def reduce_scatter_tp(partial, n_chip):
+    rows = partial.shape[0]
+    block_cols = partial.shape[1] // (2 * n_chip)
+    at_c = lax.axis_index("c")
+    at_z = lax.axis_index("zl")
+    blocks = partial.reshape(rows, n_chip, 2, block_cols)
+    keep = lax.dynamic_index_in_dim(blocks, at_c, axis=2, keepdims=False)
+    give = lax.dynamic_index_in_dim(blocks, 1 - at_c, axis=2, keepdims=False)
+    got = lax.ppermute(give, "c", [(0, 1), (1, 0)])
+    chip_sum = keep.astype(jnp.float32) + got.astype(jnp.float32)
+    rightward = [(i, i + 1) for i in range(n_chip - 1)]
+    leftward = [(i + 1, i) for i in range(n_chip - 1)]
+    from_left = jnp.zeros((rows, block_cols), jnp.float32)
+    from_right = jnp.zeros((rows, block_cols), jnp.float32)
+    for step in range(1, n_chip):
+        to_right = jnp.minimum(at_z + n_chip - step, n_chip - 1)
+        to_left = jnp.maximum(at_z - n_chip + step, 0)
+        send_r = lax.dynamic_index_in_dim(chip_sum, to_right, axis=1, keepdims=False) + from_left
+        send_l = lax.dynamic_index_in_dim(chip_sum, to_left, axis=1, keepdims=False) + from_right
+        from_left = lax.ppermute(send_r.astype(jnp.bfloat16), "zl", rightward).astype(jnp.float32)
+        from_right = lax.ppermute(send_l.astype(jnp.bfloat16), "zl", leftward).astype(jnp.float32)
+    own = lax.dynamic_index_in_dim(chip_sum, at_z, axis=1, keepdims=False)
+    return own + from_left + from_right
 
 
 def norm_scale(value_matrix, gain):
@@ -207,9 +232,7 @@
     out_abs = jnp.roll(out_abs, at_x, axis=2)
     out_abs = jnp.roll(out_abs, at_zh, axis=3)
     partial_out = out_abs.transpose(0, 3, 1, 2, 4).reshape(tok_rows, n_seq * shard_rows)
-    summed_cols = lax.psum_scatter(
-        partial_out, TP, scatter_dimension=1, tiled=True
-    ).astype(jnp.float32)
+    summed_cols = reduce_scatter_tp(partial_out, dict(TP_PARTS)["zl"])
     full_width = post_gain.shape[0]
     squares = lax.psum(jnp.sum(summed_cols * summed_cols, axis=1), TP)
     inverse_rms = lax.rsqrt(squares / full_width + epsilon)

time: 360 us -> 372 us (1.033)
  the two profiles are of different devices: /device:TPU:10 before, /device:TPU:263 now
where the time goes in v3:
time: 372 us; the launch traced here: 370 us
  starting transfers between devices  152 us (41%)
  waiting for transfers between devices  81.8 us (22%)
  local copies, waits for them, and re-layouts  45 us (12%)
  other arithmetic  32.9 us (9%)
  matrix products  26.2 us (7%)
  blocking collectives  16.7 us (4%)
  between operations  14.9 us (4%)
    ppermute x8, starting transfers between devices, ring(): right = lax.ppermute(right, axis, bwd)  34.1 us
    ppermute x3, starting transfers between devices, reduce_scatter_tp(): lax.ppermute(send_r.astype(jnp.bfloat16), 'zl', rightward)  31.1 us
    ppermute x1, starting transfers between devices, reduce_scatter_tp(): got = lax.ppermute(give, 'c', [(0, 1), (1, 0)])  28.7 us
    ppermute x8, waiting for transfers between devices, ring(): left = lax.ppermute(left, axis, fwd)  19.4 us
    dot_general x14, matrix products, contract(): lax.dot_general(lhs, piece, (((1, 2, 3), (0, 1, 2)), ((), ())), preferred...  18.1 us
    ppermute x8, starting transfers between devices, ring(): left = lax.ppermute(left, axis, fwd)  17.9 us
    psum x1, blocking collectives, local(): squares = lax.psum(jnp.sum(summed_cols * summed_cols, axis=1), TP)  16.7 us
    ppermute x4, waiting for transfers between devices, ring(): lax.ppermute(lax.slice_in_dim(right, k, None, axis=split_axis), axis, bwd)  12.2 us
  transfers between devices with their start and end apart: 37, of which 12 were waited for; matrix products, arithmetic and copies ran while one was open for 17% of the time, Pallas kernels for 0%

profile of v3, /device:TPU:263, one launch (start us, length us, event | category | flops | bytes accessed | tf_op | source)
XLA Modules:
  0.0 369.9 jit_solution(4629648363512722002)
XLA Ops:
  9.5 11.4 %collective-permute-done = bf16[84,1536]{1,0:T(8,128)(2,1)S(1)} collective-permute-done((bf16[84,1536]{1,0:T(8,128)(2,1)S(1)}, bf16[84,1536]{1,0:T(8,128)(2,1)S(1)}, u32[]{:S(2)}, u32[]{:S(2)}) %collective-permute-start) | collective-permute-done | bytes 258080 | tf_op jit(solution)/shard_map/ppermute | solution.py:31
  23.4 4.0 %collective-permute-start.14 = (bf16[2,84,768]{2,1,0:T(8,128)(2,1)S(1)}, bf16[2,84,768]{2,1,0:T(8,128)(2,1)S(1)}, u32[]{:S(2)}, u32[]{:S(2)}) collective-permute-start(bf16[2,84,768]{2,1,0:T(8,128)(2,1)S(1)} %pad_maximum_fusion.1), channel_id=1, source_target_pairs={{0,8},{8,16},{16,24},{24,0},{1,9},{9,17},{17,25},{25,1},{2,10},{10... | collective-permute-start | bytes 774152 | tf_op jit(solution)/shard_map/ppermute | solution.py:36
  28.1 5.1 %collective-permute-start.1 = (bf16[2,84,768]{2,1,0:T(8,128)(2,1)}, bf16[2,84,768]{2,1,0:T(8,128)(2,1)}, u32[]{:S(2)}, u32[]{:S(2)}) collective-permute-start(bf16[2,84,768]{2,1,0:T(8,128)(2,1)} %get-tuple-element.71), channel_id=1, source_target_pairs={{0,224},{32,0},{64,32},{96,64},{128,96},{160,128},{192,160},{224,1... | collective-permute-start | bytes 774152 | tf_op jit(solution)/shard_map/ppermute | solution.py:37
  37.2 4.6 %collective-permute-start.15 = (bf16[1,84,768]{2,1,0:T(8,128)(2,1)S(1)}, bf16[1,84,768]{2,1,0:T(8,128)(2,1)S(1)}, u32[]{:S(2)}, u32[]{:S(2)}) collective-permute-start(bf16[1,84,768]{2,1,0:T(8,128)(2,1)S(1)} %slice.353), channel_id=1, source_target_pairs={{0,8},{8,16},{16,24},{24,0},{1,9},{9,17},{17,25},{25,1},{2,10},{10... | collective-permute-start | bytes 387080 | tf_op jit(solution)/shard_map/ppermute | solution.py:42
  41.8 4.6 %collective-permute-start.2 = (bf16[2,84,768]{2,1,0:T(8,128)(2,1)}, bf16[2,84,768]{2,1,0:T(8,128)(2,1)S(1)}, u32[]{:S(2)}, u32[]{:S(2)}) collective-permute-start(bf16[2,84,768]{2,1,0:T(8,128)(2,1)} %collective-permute-done.1), channel_id=1, source_target_pairs={{0,224},{32,0},{64,32},{96,64},{128,96},{160,128},{192,160},{224,1... | collective-permute-start | bytes 774152 | tf_op jit(solution)/shard_map/ppermute | solution.py:37
  50.1 5.2 %collective-permute-start.3 = (bf16[2,84,768]{2,1,0:T(8,128)(2,1)S(1)}, bf16[2,84,768]{2,1,0:T(8,128)(2,1)S(1)}, u32[]{:S(2)}, u32[]{:S(2)}) collective-permute-start(bf16[2,84,768]{2,1,0:T(8,128)(2,1)S(1)} %collective-permute-done.2), channel_id=1, source_target_pairs={{0,224},{32,0},{64,32},{96,64},{128,96},{160,128},{192,160},{224,1... | collective-permute-start | bytes 774152 | tf_op jit(solution)/shard_map/ppermute | solution.py:37
  59.9 4.6 %collective-permute-start.17 = (bf16[4,2,84,768]{3,0,2,1:T(4,128)(2,1)S(1)}, bf16[4,2,84,768]{3,0,2,1:T(4,128)(2,1)}, u32[]{:S(2)}, u32[]{:S(2)}) collective-permute-start(bf16[4,2,84,768]{3,0,2,1:T(4,128)(2,1)S(1)} %copy.119), channel_id=1, source_target_pairs={{0,224},{32,0},{64,32},{96,64},{128,96},{160,128},{192,160},{224,1... | collective-permute-start | bytes 3096584 | tf_op jit(solution)/shard_map/ppermute | solution.py:37
  69.9 12.2 %collective-permute-done.8 = bf16[1,84,768]{2,1,0:T(8,128)(2,1)S(1)} collective-permute-done((bf16[1,84,768]{2,1,0:T(8,128)(2,1)S(1)}, bf16[1,84,768]{2,1,0:T(8,128)(2,1)S(1)}, u32[]{:S(2)}, u32[]{:S(2)}) %collective-permute-start.8) | collective-permute-done | bytes 129056 | tf_op jit(solution)/shard_map/ppermute | solution.py:43
  96.2 4.6 %collective-permute-start.18 = (bf16[4,2,84,768]{3,0,2,1:T(4,128)(2,1)}, bf16[4,2,84,768]{3,0,2,1:T(4,128)(2,1)}, u32[]{:S(2)}, u32[]{:S(2)}) collective-permute-start(bf16[4,2,84,768]{3,0,2,1:T(4,128)(2,1)} %collective-permute-done.17), channel_id=1, source_target_pairs={{0,224},{32,0},{64,32},{96,64},{128,96},{160,128},{192,160},{224,1... | collective-permute-start | bytes 3096584 | tf_op jit(solution)/shard_map/ppermute | solution.py:37
  100.9 10.5 %collective-permute-done.21 = bf16[4,2,84,768]{3,0,2,1:T(4,128)(2,1)} collective-permute-done((bf16[4,2,84,768]{3,0,2,1:T(4,128)(2,1)}, bf16[4,2,84,768]{3,0,2,1:T(4,128)(2,1)}, u32[]{:S(2)}, u32[]{:S(2)}) %collective-permute-start.21) | collective-permute-done | bytes 1032224 | tf_op jit(solution)/shard_map/ppermute | solution.py:36
  113.4 4.6 %collective-permute-start.19 = (bf16[4,2,84,768]{3,0,2,1:T(4,128)(2,1)}, bf16[4,2,84,768]{3,0,2,1:T(4,128)(2,1)S(1)}, u32[]{:S(2)}, u32[]{:S(2)}) collective-permute-start(bf16[4,2,84,768]{3,0,2,1:T(4,128)(2,1)} %collective-permute-done.18), channel_id=1, source_target_pairs={{0,224},{32,0},{64,32},{96,64},{128,96},{160,128},{192,160},{224,1... | collective-permute-start | bytes 3096584 | tf_op jit(solution)/shard_map/ppermute | solution.py:37
  117.9 8.8 %collective-permute-done.10 = bf16[8,2,84,768]{3,0,2,1:T(8,128)(2,1)S(1)} collective-permute-done((bf16[8,2,84,768]{3,0,2,1:T(8,128)(2,1)}, bf16[8,2,84,768]{3,0,2,1:T(8,128)(2,1)S(1)}, u32[]{:S(2)}, u32[]{:S(2)}) %collective-permute-start.10) | collective-permute-done | bytes 2064416 | tf_op jit(solution)/shard_map/ppermute | solution.py:36
  153.3 4.6 %collective-permute-start.24 = (bf16[2,2,84,768]{3,1,2,0:T(2,128)(2,1)}, bf16[2,2,84,768]{3,1,2,0:T(2,128)(2,1)}, u32[]{:S(2)}, u32[]{:S(2)}) collective-permute-start(bf16[2,2,84,768]{3,1,2,0:T(2,128)(2,1)} %copy.126), channel_id=1, source_target_pairs={{0,224},{32,0},{64,32},{96,64},{128,96},{160,128},{192,160},{224,1... | collective-permute-start | bytes 1548296 | tf_op jit(solution)/shard_map/ppermute | solution.py:43
  212.1 3.9 %collective-permute-start.25 = (bf16[2,256,256]{1,2,0:T(8,128)(2,1)S(1)}, bf16[2,256,256]{1,2,0:T(8,128)(2,1)S(1)}, u32[]{:S(2)}, u32[]{:S(2)}) collective-permute-start(bf16[2,256,256]{1,2,0:T(8,128)(2,1)S(1)} %pad_maximum_fusion.4), channel_id=1, source_target_pairs={{0,32},{8,40},{16,48},{24,56},{32,64},{40,72},{48,80},{56,88},{64,... | collective-permute-start | bytes 786440 | tf_op jit(solution)/shard_map/ppermute | solution.py:22
  218.3 10.7 %collective-permute-done.25 = bf16[2,256,256]{1,2,0:T(8,128)(2,1)S(1)} collective-permute-done((bf16[2,256,256]{1,2,0:T(8,128)(2,1)S(1)}, bf16[2,256,256]{1,2,0:T(8,128)(2,1)S(1)}, u32[]{:S(2)}, u32[]{:S(2)}) %collective-permute-start.25) | collective-permute-done | bytes 262176 | tf_op jit(solution)/shard_map/ppermute | solution.py:22
  245.4 28.7 %collective-permute-start.29 = (bf16[256,4,672]{0,2,1:T(8,128)(2,1)S(1)}, bf16[256,4,672]{0,2,1:T(8,128)(2,1)}, u32[]{:S(2)}, u32[]{:S(2)}) collective-permute-start(bf16[256,4,672]{0,2,1:T(8,128)(2,1)S(1)} %dynamic-slice_bitcast_fusion), channel_id=1, source_target_pairs={{0,1},{1,0},{2,3},{3,2},{4,5},{5,4},{6,7},{7,6},{8,9},{9,8},{10,11... | collective-permute-start | bytes 4128776 | tf_op jit(solution)/shard_map/ppermute | solution.py:76
  279.8 21.2 %collective-permute-start.30 = (bf16[256,672]{0,1:T(8,128)(2,1)S(1)}, bf16[256,672]{0,1:T(8,128)(2,1)}, u32[]{:S(2)}, u32[]{:S(2)}) collective-permute-start(bf16[256,672]{0,1:T(8,128)(2,1)S(1)} %get-tuple-element.74), channel_id=1, source_target_pairs={{0,2},{2,4},{4,6},{1,3},{3,5},{5,7},{8,10},{10,12},{12,14},{9,11},... | collective-permute-start | bytes 1032200 | tf_op jit(solution)/shard_map/ppermute | solution.py:87
  302.3 5.0 %collective-permute-done.30 = bf16[256,672]{0,1:T(8,128)(2,1)} collective-permute-done((bf16[256,672]{0,1:T(8,128)(2,1)S(1)}, bf16[256,672]{0,1:T(8,128)(2,1)}, u32[]{:S(2)}, u32[]{:S(2)}) %collective-permute-start.30) | collective-permute-done | bytes 344096 | tf_op jit(solution)/shard_map/ppermute | solution.py:87
  309.1 5.1 %collective-permute-start.31 = (bf16[256,672]{0,1:T(8,128)(2,1)}, bf16[256,672]{0,1:T(8,128)(2,1)}, u32[]{:S(2)}, u32[]{:S(2)}) collective-permute-start(bf16[256,672]{0,1:T(8,128)(2,1)} %fusion.95), channel_id=1, source_target_pairs={{0,2},{2,4},{4,6},{1,3},{3,5},{5,7},{8,10},{10,12},{12,14},{9,11},... | collective-permute-start | bytes 1032200 | tf_op jit(solution)/shard_map/ppermute | solution.py:87
  314.2 5.7 %collective-permute-done.31 = bf16[256,672]{0,1:T(8,128)(2,1)} collective-permute-done((bf16[256,672]{0,1:T(8,128)(2,1)}, bf16[256,672]{0,1:T(8,128)(2,1)}, u32[]{:S(2)}, u32[]{:S(2)}) %collective-permute-start.31) | collective-permute-done | bytes 344096 | tf_op jit(solution)/shard_map/ppermute | solution.py:87
  323.2 4.8 %collective-permute-start.32 = (bf16[256,672]{0,1:T(8,128)(2,1)}, bf16[256,672]{0,1:T(8,128)(2,1)S(1)}, u32[]{:S(2)}, u32[]{:S(2)}) collective-permute-start(bf16[256,672]{0,1:T(8,128)(2,1)} %get-tuple-element.72), channel_id=1, source_target_pairs={{0,2},{2,4},{4,6},{1,3},{3,5},{5,7},{8,10},{10,12},{12,14},{9,11},... | collective-permute-start | bytes 1032200 | tf_op jit(solution)/shard_map/ppermute | solution.py:87
  327.9 4.6 %collective-permute-done.34 = bf16[256,672]{0,1:T(8,128)(2,1)} collective-permute-done((bf16[256,672]{0,1:T(8,128)(2,1)}, bf16[256,672]{0,1:T(8,128)(2,1)}, u32[]{:S(2)}, u32[]{:S(2)}) %collective-permute-start.34) | collective-permute-done | bytes 344096 | tf_op jit(solution)/shard_map/ppermute | solution.py:88
  336.4 6.9 %collective-permute-done.35 = bf16[256,672]{0,1:T(8,128)(2,1)} collective-permute-done((bf16[256,672]{0,1:T(8,128)(2,1)}, bf16[256,672]{0,1:T(8,128)(2,1)}, u32[]{:S(2)}, u32[]{:S(2)}) %collective-permute-start.35) | collective-permute-done | bytes 344096 | tf_op jit(solution)/shard_map/ppermute | solution.py:88
  344.5 16.7 %psum.7 = f32[256]{0:T(256)S(1)} all-reduce(f32[256]{0:T(256)S(1)} %multiply_reduce_fusion), channel_id=1, replica_groups=mesh['zh'=2,'y'=8,'x'=4,'zl'=4,'c'=2] {'zl','c'}, use_global_device_ids=true, to_apply=%region_7.11 | all-reduce | flops 256 | bytes 2048 | tf_op jit(solution)/shard_map/psum | solution.py:237
  (238 shorter events, 157.1 us)
Async XLA Ops:
  6.5 159.5 %all-gather.2.cloned.1.call-start = ((), (), s32[]{:S(2)}) async-start(), calls=%async_computation | async-start | bytes 3096576 | tf_op jit(solution)/shard_map/all_gather | solution.py:147
  20.9 14.3 %collective-permute-start.13 = (bf16[2,84,768]{2,1,0:T(8,128)(2,1)S(1)}, bf16[2,84,768]{2,1,0:T(8,128)(2,1)S(1)}, u32[]{:S(2)}, u32[]{:S(2)}) collective-permute-start(bf16[2,84,768]{2,1,0:T(8,128)(2,1)S(1)} %pad_maximum_fusion.1), channel_id=1, source_target_pairs={{0,24},{8,0},{16,8},{24,16},{1,25},{9,1},{17,9},{25,17},{2,26},{10... | collective-permute-start | bytes 774152 | tf_op jit(solution)/shard_map/ppermute | solution.py:37
  35.3 14.1 %collective-permute-start.16 = (bf16[1,84,768]{2,1,0:T(8,128)(2,1)S(1)}, bf16[1,84,768]{2,1,0:T(8,128)(2,1)S(1)}, u32[]{:S(2)}, u32[]{:S(2)}) collective-permute-start(bf16[1,84,768]{2,1,0:T(8,128)(2,1)S(1)} %slice.354), channel_id=1, source_target_pairs={{0,24},{8,0},{16,8},{24,16},{1,25},{9,1},{17,9},{25,17},{2,26},{10... | collective-permute-start | bytes 387080 | tf_op jit(solution)/shard_map/ppermute | solution.py:43
  50.1 14.4 %collective-permute-start.3 = (bf16[2,84,768]{2,1,0:T(8,128)(2,1)S(1)}, bf16[2,84,768]{2,1,0:T(8,128)(2,1)S(1)}, u32[]{:S(2)}, u32[]{:S(2)}) collective-permute-start(bf16[2,84,768]{2,1,0:T(8,128)(2,1)S(1)} %collective-permute-done.2), channel_id=1, source_target_pairs={{0,224},{32,0},{64,32},{96,64},{128,96},{160,128},{192,160},{224,1... | collective-permute-start | bytes 774152 | tf_op jit(solution)/shard_map/ppermute | solution.py:37
  58.0 36.2 %collective-permute-start.20 = (bf16[4,2,84,768]{3,0,2,1:T(4,128)(2,1)S(1)}, bf16[4,2,84,768]{3,0,2,1:T(4,128)(2,1)}, u32[]{:S(2)}, u32[]{:S(2)}) collective-permute-start(bf16[4,2,84,768]{3,0,2,1:T(4,128)(2,1)S(1)} %copy.119), channel_id=1, source_target_pairs={{0,32},{32,64},{64,96},{96,128},{128,160},{160,192},{192,224},{224... | collective-permute-start | bytes 3096584 | tf_op jit(solution)/shard_map/ppermute | solution.py:36
  59.9 36.3 %collective-permute-start.17 = (bf16[4,2,84,768]{3,0,2,1:T(4,128)(2,1)S(1)}, bf16[4,2,84,768]{3,0,2,1:T(4,128)(2,1)}, u32[]{:S(2)}, u32[]{:S(2)}) collective-permute-start(bf16[4,2,84,768]{3,0,2,1:T(4,128)(2,1)S(1)} %copy.119), channel_id=1, source_target_pairs={{0,224},{32,0},{64,32},{96,64},{128,96},{160,128},{192,160},{224,1... | collective-permute-start | bytes 3096584 | tf_op jit(solution)/shard_map/ppermute | solution.py:37
  64.6 17.5 %collective-permute-start.8 = (bf16[1,84,768]{2,1,0:T(8,128)(2,1)S(1)}, bf16[1,84,768]{2,1,0:T(8,128)(2,1)S(1)}, u32[]{:S(2)}, u32[]{:S(2)}) collective-permute-start(bf16[1,84,768]{2,1,0:T(8,128)(2,1)S(1)} %slice.340), channel_id=1, source_target_pairs={{0,224},{32,0},{64,32},{96,64},{128,96},{160,128},{192,160},{224,1... | collective-permute-start | bytes 387080 | tf_op jit(solution)/shard_map/ppermute | solution.py:43
  68.0 16.5 %collective-permute-start.7 = (bf16[1,84,768]{2,1,0:T(8,128)(2,1)S(1)}, bf16[1,84,768]{2,1,0:T(8,128)(2,1)S(1)}, u32[]{:S(2)}, u32[]{:S(2)}) collective-permute-start(bf16[1,84,768]{2,1,0:T(8,128)(2,1)S(1)} %slice.339), channel_id=1, source_target_pairs={{0,32},{32,64},{64,96},{96,128},{128,160},{160,192},{192,224},{224... | collective-permute-start | bytes 387080 | tf_op jit(solution)/shard_map/ppermute | solution.py:42
  88.8 37.9 %collective-permute-start.10 = (bf16[8,2,84,768]{3,0,2,1:T(8,128)(2,1)}, bf16[8,2,84,768]{3,0,2,1:T(8,128)(2,1)S(1)}, u32[]{:S(2)}, u32[]{:S(2)}) collective-permute-start(bf16[8,2,84,768]{3,0,2,1:T(8,128)(2,1)} %copy.113), channel_id=1, source_target_pairs={{0,8},{8,16},{16,24},{24,0},{1,9},{9,17},{17,25},{25,1},{2,10},{10... | collective-permute-start | bytes 6193160 | tf_op jit(solution)/shard_map/ppermute | solution.py:36
  91.2 40.8 %collective-permute-start.9 = (bf16[8,2,84,768]{3,0,2,1:T(8,128)(2,1)}, bf16[8,2,84,768]{3,0,2,1:T(8,128)(2,1)}, u32[]{:S(2)}, u32[]{:S(2)}) collective-permute-start(bf16[8,2,84,768]{3,0,2,1:T(8,128)(2,1)} %copy.113), channel_id=1, source_target_pairs={{0,24},{8,0},{16,8},{24,16},{1,25},{9,1},{17,9},{25,17},{2,26},{10... | collective-permute-start | bytes 6193160 | tf_op jit(solution)/shard_map/ppermute | solution.py:37
  94.2 17.2 %collective-permute-start.21 = (bf16[4,2,84,768]{3,0,2,1:T(4,128)(2,1)}, bf16[4,2,84,768]{3,0,2,1:T(4,128)(2,1)}, u32[]{:S(2)}, u32[]{:S(2)}) collective-permute-start(bf16[4,2,84,768]{3,0,2,1:T(4,128)(2,1)} %collective-permute-done.20), channel_id=1, source_target_pairs={{0,32},{32,64},{64,96},{96,128},{128,160},{160,192},{192,224},{224... | collective-permute-start | bytes 3096584 | tf_op jit(solution)/shard_map/ppermute | solution.py:36
  96.2 17.2 %collective-permute-start.18 = (bf16[4,2,84,768]{3,0,2,1:T(4,128)(2,1)}, bf16[4,2,84,768]{3,0,2,1:T(4,128)(2,1)}, u32[]{:S(2)}, u32[]{:S(2)}) collective-permute-start(bf16[4,2,84,768]{3,0,2,1:T(4,128)(2,1)} %collective-permute-done.17), channel_id=1, source_target_pairs={{0,224},{32,0},{64,32},{96,64},{128,96},{160,128},{192,160},{224,1... | collective-permute-start | bytes 3096584 | tf_op jit(solution)/shard_map/ppermute | solution.py:37
  111.4 35.4 %collective-permute-start.22 = (bf16[4,2,84,768]{3,0,2,1:T(4,128)(2,1)}, bf16[4,2,84,768]{3,0,2,1:T(4,128)(2,1)}, u32[]{:S(2)}, u32[]{:S(2)}) collective-permute-start(bf16[4,2,84,768]{3,0,2,1:T(4,128)(2,1)} %collective-permute-done.21), channel_id=1, source_target_pairs={{0,32},{32,64},{64,96},{96,128},{128,160},{160,192},{192,224},{224... | collective-permute-start | bytes 3096584 | tf_op jit(solution)/shard_map/ppermute | solution.py:36
  113.4 38.2 %collective-permute-start.19 = (bf16[4,2,84,768]{3,0,2,1:T(4,128)(2,1)}, bf16[4,2,84,768]{3,0,2,1:T(4,128)(2,1)S(1)}, u32[]{:S(2)}, u32[]{:S(2)}) collective-permute-start(bf16[4,2,84,768]{3,0,2,1:T(4,128)(2,1)} %collective-permute-done.18), channel_id=1, source_target_pairs={{0,224},{32,0},{64,32},{96,64},{128,96},{160,128},{192,160},{224,1... | collective-permute-start | bytes 3096584 | tf_op jit(solution)/shard_map/ppermute | solution.py:37
  128.2 29.7 %collective-permute-start.11 = (bf16[4,2,84,768]{3,0,2,1:T(4,128)(2,1)}, bf16[4,2,84,768]{3,0,2,1:T(4,128)(2,1)}, u32[]{:S(2)}, u32[]{:S(2)}) collective-permute-start(bf16[4,2,84,768]{3,0,2,1:T(4,128)(2,1)} %slice.345), channel_id=1, source_target_pairs={{0,8},{8,16},{16,24},{24,0},{1,9},{9,17},{17,25},{25,1},{2,10},{10... | collective-permute-start | bytes 3096584 | tf_op jit(solution)/shard_map/ppermute | solution.py:42
  135.1 26.9 %collective-permute-start.12 = (bf16[4,2,84,768]{3,0,2,1:T(4,128)(2,1)}, bf16[4,2,84,768]{3,0,2,1:T(4,128)(2,1)}, u32[]{:S(2)}, u32[]{:S(2)}) collective-permute-start(bf16[4,2,84,768]{3,0,2,1:T(4,128)(2,1)} %slice.348), channel_id=1, source_target_pairs={{0,24},{8,0},{16,8},{24,16},{1,25},{9,1},{17,9},{25,17},{2,26},{10... | collective-permute-start | bytes 3096584 | tf_op jit(solution)/shard_map/ppermute | solution.py:43
  149.6 35.6 %collective-permute-start.23 = (bf16[2,2,84,768]{3,1,2,0:T(2,128)(2,1)}, bf16[2,2,84,768]{3,1,2,0:T(2,128)(2,1)}, u32[]{:S(2)}, u32[]{:S(2)}) collective-permute-start(bf16[2,2,84,768]{3,1,2,0:T(2,128)(2,1)} %copy.124), channel_id=1, source_target_pairs={{0,32},{32,64},{64,96},{96,128},{128,160},{160,192},{192,224},{224... | collective-permute-start | bytes 1548296 | tf_op jit(solution)/shard_map/ppermute | solution.py:42
  153.3 36.9 %collective-permute-start.24 = (bf16[2,2,84,768]{3,1,2,0:T(2,128)(2,1)}, bf16[2,2,84,768]{3,1,2,0:T(2,128)(2,1)}, u32[]{:S(2)}, u32[]{:S(2)}) collective-permute-start(bf16[2,2,84,768]{3,1,2,0:T(2,128)(2,1)} %copy.126), channel_id=1, source_target_pairs={{0,224},{32,0},{64,32},{96,64},{128,96},{160,128},{192,160},{224,1... | collective-permute-start | bytes 1548296 | tf_op jit(solution)/shard_map/ppermute | solution.py:43
  204.9 24.2 %collective-permute-start.28 = (bf16[2,256,256]{1,2,0:T(8,128)(2,1)S(1)}, bf16[2,256,256]{1,2,0:T(8,128)(2,1)S(1)}, u32[]{:S(2)}, u32[]{:S(2)}) collective-permute-start(bf16[2,256,256]{1,2,0:T(8,128)(2,1)S(1)} %pad_maximum_fusion.4), channel_id=1, source_target_pairs={{0,8},{8,16},{16,24},{24,32},{32,40},{40,48},{48,56},{56,64},{64,7... | collective-permute-start | bytes 786440 | tf_op jit(solution)/shard_map/ppermute | solution.py:22
  208.1 20.9 %collective-permute-start.27 = (bf16[2,256,256]{1,2,0:T(8,128)(2,1)S(1)}, bf16[2,256,256]{1,2,0:T(8,128)(2,1)S(1)}, u32[]{:S(2)}, u32[]{:S(2)}) collective-permute-start(bf16[2,256,256]{1,2,0:T(8,128)(2,1)S(1)} %pad_maximum_fusion.4), channel_id=1, source_target_pairs={{0,16},{8,24},{16,32},{24,40},{32,48},{40,56},{48,64},{56,72},{64,... | collective-permute-start | bytes 786440 | tf_op jit(solution)/shard_map/ppermute | solution.py:22
  210.1 18.9 %collective-permute-start.26 = (bf16[2,256,256]{1,2,0:T(8,128)(2,1)S(1)}, bf16[2,256,256]{1,2,0:T(8,128)(2,1)S(1)}, u32[]{:S(2)}, u32[]{:S(2)}) collective-permute-start(bf16[2,256,256]{1,2,0:T(8,128)(2,1)S(1)} %pad_maximum_fusion.4), channel_id=1, source_target_pairs={{0,24},{8,32},{16,40},{24,48},{32,56},{40,64},{48,72},{56,80},{64,... | collective-permute-start | bytes 786440 | tf_op jit(solution)/shard_map/ppermute | solution.py:22
  212.1 16.9 %collective-permute-start.25 = (bf16[2,256,256]{1,2,0:T(8,128)(2,1)S(1)}, bf16[2,256,256]{1,2,0:T(8,128)(2,1)S(1)}, u32[]{:S(2)}, u32[]{:S(2)}) collective-permute-start(bf16[2,256,256]{1,2,0:T(8,128)(2,1)S(1)} %pad_maximum_fusion.4), channel_id=1, source_target_pairs={{0,32},{8,40},{16,48},{24,56},{32,64},{40,72},{48,80},{56,88},{64,... | collective-permute-start | bytes 786440 | tf_op jit(solution)/shard_map/ppermute | solution.py:22
  245.4 31.5 %collective-permute-start.29 = (bf16[256,4,672]{0,2,1:T(8,128)(2,1)S(1)}, bf16[256,4,672]{0,2,1:T(8,128)(2,1)}, u32[]{:S(2)}, u32[]{:S(2)}) collective-permute-start(bf16[256,4,672]{0,2,1:T(8,128)(2,1)S(1)} %dynamic-slice_bitcast_fusion), channel_id=1, source_target_pairs={{0,1},{1,0},{2,3},{3,2},{4,5},{5,4},{6,7},{7,6},{8,9},{9,8},{10,11... | collective-permute-start | bytes 4128776 | tf_op jit(solution)/shard_map/ppermute | solution.py:76
  279.8 27.5 %collective-permute-start.30 = (bf16[256,672]{0,1:T(8,128)(2,1)S(1)}, bf16[256,672]{0,1:T(8,128)(2,1)}, u32[]{:S(2)}, u32[]{:S(2)}) collective-permute-start(bf16[256,672]{0,1:T(8,128)(2,1)S(1)} %get-tuple-element.74), channel_id=1, source_target_pairs={{0,2},{2,4},{4,6},{1,3},{3,5},{5,7},{8,10},{10,12},{12,14},{9,11},... | collective-permute-start | bytes 1032200 | tf_op jit(solution)/shard_map/ppermute | solution.py:87
  (50 other events, 582.6 us)
Sparse Core Ops, SparseCore 0:
  35.3 48.4 all-gather.1

commit v4 on v2

--- a/solution.py
+++ b/solution.py
@@ -51,18 +51,34 @@
     return jnp.stack(whole, axis=0)
 
 
-def ring_pieces(block, axis, n, split_axis):
-    parts = ring(block, axis, n, split_axis)
+def ring_pieces(block, axis, n, split_axis, fold=None, acc=None):
+    fwd = [(i, (i + 1) % n) for i in range(n)]
+    bwd = [(i, (i - 1) % n) for i in range(n)]
     full = block.shape[split_axis]
     pieces = []
-    for d, p in enumerate(parts):
-        if isinstance(p, tuple):
-            k = p[0].shape[split_axis]
-            pieces.append((d, 0, k, p[0]))
-            pieces.append((d, k, full, p[1]))
-        else:
-            pieces.append((d, 0, full, p))
-    return pieces
+
+    def take(new):
+        nonlocal acc
+        pieces.extend(new)
+        if fold is not None:
+            acc = fold(acc, new)
+
+    take([(0, 0, full, block)])
+    left, right = block, block
+    for d in range(1, (n + 1) // 2):
+        if d > 1 and fold is not None:
+            left, right, acc = lax.optimization_barrier((left, right, acc))
+        left = lax.ppermute(left, axis, fwd)
+        right = lax.ppermute(right, axis, bwd)
+        take([(n - d, 0, full, left), (d, 0, full, right)])
+    if n % 2 == 0:
+        if fold is not None:
+            left, right, acc = lax.optimization_barrier((left, right, acc))
+        k = full // 2
+        top = lax.ppermute(lax.slice_in_dim(left, 0, k, axis=split_axis), axis, fwd)
+        bottom = lax.ppermute(lax.slice_in_dim(right, k, None, axis=split_axis), axis, bwd)
+        take([(n // 2, 0, k, top), (n // 2, k, full, bottom)])
+    return pieces, acc
 
 
 def norm_scale(value_matrix, gain):
@@ -109,16 +125,6 @@
     shard_rows = w_query.shape[0]
 
     nz, ny, nx = sizes["zh"], sizes["y"], sizes["x"]
-    packed = jnp.concatenate([w_query, key_weight, value_weight, w_out.T], axis=1)
-    by_zh = stacked_ring(packed, "zh", nz, 0)
-    split = q_cols + k_cols
-    half_a = by_zh[:, :, :split]
-    half_b = by_zh[:, :, split:]
-    a_x = stacked_ring(half_a, "x", nx, 0)
-    a_pieces = ring_pieces(a_x, "y", ny, 0)
-    b_y = stacked_ring(half_b, "y", ny, 0)
-    b_pieces = ring_pieces(b_y, "x", nx, 0)
-
     gathered = lax.all_gather(residual, TP, axis=1, tiled=True)
     normalized_input = norm_scale(gathered.astype(jnp.float32), input_gain).astype(jnp.bfloat16)
     at_zh, at_y, at_x = (lax.axis_index(name) for name in SEQ)
@@ -132,14 +138,27 @@
             lhs, piece, (((1, 2, 3), (0, 1, 2)), ((), ())), preferred_element_type=jnp.float32
         )
 
-    qk = None
-    for dy, lo, hi, piece in a_pieces:
-        term = contract(normed_rel[:, dy, lo:hi], piece)
-        qk = term if qk is None else qk + term
-    projected_values = None
-    for dx, lo, hi, piece in b_pieces:
-        term = contract(normed_rel[:, lo:hi, dx], piece[..., :v_cols])
-        projected_values = term if projected_values is None else projected_values + term
+    def fold_qk(acc, new):
+        for dy, lo, hi, piece in new:
+            term = contract(normed_rel[:, dy, lo:hi], piece)
+            acc = term if acc is None else acc + term
+        return acc
+
+    def fold_v(acc, new):
+        for dx, lo, hi, piece in new:
+            term = contract(normed_rel[:, lo:hi, dx], piece[..., :v_cols])
+            acc = term if acc is None else acc + term
+        return acc
+
+    packed = jnp.concatenate([w_query, key_weight, value_weight, w_out.T], axis=1)
+    by_zh = stacked_ring(packed, "zh", nz, 0)
+    split = q_cols + k_cols
+    half_a = by_zh[:, :, :split]
+    half_b = by_zh[:, :, split:]
+    a_x = stacked_ring(half_a, "x", nx, 0)
+    b_y = stacked_ring(half_b, "y", ny, 0)
+    _, qk = ring_pieces(a_x, "y", ny, 0, fold_qk, None)
+    b_pieces, projected_values = ring_pieces(b_y, "x", nx, 0, fold_v, None)
     queries_raw = qk[:, :q_cols]
     unrotated_keys = qk[:, q_cols:]
     own_places = lax.dynamic_slice_in_dim(positions, seq_at * tok_rows, tok_rows, 0)

time: 360 us -> 355 us (0.986)
  the two profiles are of different devices: /device:TPU:10 before, /device:TPU:2 now
where the time goes in v4:
time: 355 us; the launch traced here: 353 us
  waiting for transfers between devices  114 us (32%)
  starting transfers between devices  109 us (31%)
  local copies, waits for them, and re-layouts  46.3 us (13%)
  matrix products  29 us (8%)
  other arithmetic  24.8 us (7%)
  blocking collectives  15.3 us (4%)
  between operations  14.7 us (4%)
    reduce_scatter x1, waiting for transfers between devices, local(): lax.psum_scatter(partial_out, TP, scatter_dimension=1, tiled=True)  72.2 us
    dot_general x14, matrix products, contract(): lax.dot_general(lhs, piece, (((1, 2, 3), (0, 1, 2)), ((), ())), preferred...  21.2 us
    ppermute x4, starting transfers between devices, ring_pieces(): right = lax.ppermute(right, axis, bwd)  20.2 us
    ppermute x4, starting transfers between devices, ring(): right = lax.ppermute(right, axis, bwd)  18.6 us
    ppermute x4, starting transfers between devices, from_behind(): return lax.ppermute(block, axis, route)  15.7 us
    psum x1, blocking collectives, local(): squares = lax.psum(jnp.sum(summed_cols * summed_cols, axis=1), TP)  15.3 us
    ppermute x2, waiting for transfers between devices, ring(): lax.ppermute(lax.slice_in_dim(right, k, None, axis=split_axis), axis, bwd)  12.4 us
    ppermute x1, starting transfers between devices, ring(): return [block, lax.ppermute(block, axis, fwd)]  10.9 us
  transfers between devices with their start and end apart: 31, of which 9 were waited for; matrix products, arithmetic and copies ran while one was open for 21% of the time, Pallas kernels for 0%

profile of v4, /device:TPU:2, one launch (start us, length us, event | category | flops | bytes accessed | tf_op | source)
XLA Modules:
  0.0 352.8 jit_solution(16186437112524170746)
XLA Ops:
  8.3 10.9 %collective-permute-start = (bf16[84,1536]{1,0:T(8,128)(2,1)S(1)}, bf16[84,1536]{1,0:T(8,128)(2,1)S(1)}, u32[]{:S(2)}, u32[]{:S(2)}) collective-permute-start(bf16[84,1536]{1,0:T(8,128)(2,1)S(1)} %get-tuple-element.105), channel_id=1, source_target_pairs={{0,256},{256,0},{1,257},{257,1},{2,258},{258,2},{3,259},{259,3},{4... | collective-permute-start | bytes 774152 | tf_op jit(solution)/shard_map/ppermute | solution.py:31
  19.3 6.6 %collective-permute-done = bf16[84,1536]{1,0:T(8,128)(2,1)S(1)} collective-permute-done((bf16[84,1536]{1,0:T(8,128)(2,1)S(1)}, bf16[84,1536]{1,0:T(8,128)(2,1)S(1)}, u32[]{:S(2)}, u32[]{:S(2)}) %collective-permute-start) | collective-permute-done | bytes 258080 | tf_op jit(solution)/shard_map/ppermute | solution.py:31
  29.2 3.2 collective-permute-start.14
  33.2 5.4 %collective-permute-start.1 = (bf16[2,84,768]{2,1,0:T(8,128)(2,1)}, bf16[2,84,768]{2,1,0:T(8,128)(2,1)}, u32[]{:S(2)}, u32[]{:S(2)}) collective-permute-start(bf16[2,84,768]{2,1,0:T(8,128)(2,1)} %get-tuple-element.95), channel_id=1, source_target_pairs={{0,224},{32,0},{64,32},{96,64},{128,96},{160,128},{192,160},{224,1... | collective-permute-start | bytes 774152 | tf_op jit(solution)/shard_map/ppermute | solution.py:37
  47.4 5.1 %collective-permute-start.2 = (bf16[2,84,768]{2,1,0:T(8,128)(2,1)}, bf16[2,84,768]{2,1,0:T(8,128)(2,1)S(1)}, u32[]{:S(2)}, u32[]{:S(2)}) collective-permute-start(bf16[2,84,768]{2,1,0:T(8,128)(2,1)} %collective-permute-done.1), channel_id=1, source_target_pairs={{0,224},{32,0},{64,32},{96,64},{128,96},{160,128},{192,160},{224,1... | collective-permute-start | bytes 774152 | tf_op jit(solution)/shard_map/ppermute | solution.py:37
  56.8 5.5 %collective-permute-start.3 = (bf16[2,84,768]{2,1,0:T(8,128)(2,1)S(1)}, bf16[2,84,768]{2,1,0:T(8,128)(2,1)S(1)}, u32[]{:S(2)}, u32[]{:S(2)}) collective-permute-start(bf16[2,84,768]{2,1,0:T(8,128)(2,1)S(1)} %collective-permute-done.2), channel_id=1, source_target_pairs={{0,224},{32,0},{64,32},{96,64},{128,96},{160,128},{192,160},{224,1... | collective-permute-start | bytes 774152 | tf_op jit(solution)/shard_map/ppermute | solution.py:37
  67.0 5.1 %collective-permute-start.18 = (bf16[4,2,84,768]{3,0,2,1:T(4,128)(2,1)}, bf16[4,2,84,768]{3,0,2,1:T(4,128)(2,1)}, u32[]{:S(2)}, u32[]{:S(2)}) collective-permute-start(bf16[4,2,84,768]{3,0,2,1:T(4,128)(2,1)} %copy.137), channel_id=1, source_target_pairs={{0,224},{32,0},{64,32},{96,64},{128,96},{160,128},{192,160},{224,1... | collective-permute-start | bytes 3096584 | tf_op jit(solution)/shard_map/ppermute | solution.py:72
  74.1 5.1 %collective-permute-start.8 = (bf16[1,84,768]{2,1,0:T(8,128)(2,1)S(1)}, bf16[1,84,768]{2,1,0:T(8,128)(2,1)S(1)}, u32[]{:S(2)}, u32[]{:S(2)}) collective-permute-start(bf16[1,84,768]{2,1,0:T(8,128)(2,1)S(1)} %slice.339), channel_id=1, source_target_pairs={{0,224},{32,0},{64,32},{96,64},{128,96},{160,128},{192,160},{224,1... | collective-permute-start | bytes 387080 | tf_op jit(solution)/shard_map/ppermute | solution.py:43
  81.2 12.3 %collective-permute-done.8 = bf16[1,84,768]{2,1,0:T(8,128)(2,1)S(1)} collective-permute-done((bf16[1,84,768]{2,1,0:T(8,128)(2,1)S(1)}, bf16[1,84,768]{2,1,0:T(8,128)(2,1)S(1)}, u32[]{:S(2)}, u32[]{:S(2)}) %collective-permute-start.8) | collective-permute-done | bytes 129056 | tf_op jit(solution)/shard_map/ppermute | solution.py:43
  93.5 5.3 %collective-permute-done.7 = bf16[1,84,768]{2,1,0:T(8,128)(2,1)S(1)} collective-permute-done((bf16[1,84,768]{2,1,0:T(8,128)(2,1)S(1)}, bf16[1,84,768]{2,1,0:T(8,128)(2,1)S(1)}, u32[]{:S(2)}, u32[]{:S(2)}) %collective-permute-start.7) | collective-permute-done | bytes 129056 | tf_op jit(solution)/shard_map/ppermute | solution.py:42
  102.0 4.7 %collective-permute-start.10 = (bf16[8,2,84,768]{3,0,2,1:T(8,128)(2,1)}, bf16[8,2,84,768]{3,0,2,1:T(8,128)(2,1)}, u32[]{:S(2)}, u32[]{:S(2)}) collective-permute-start(bf16[8,2,84,768]{3,0,2,1:T(8,128)(2,1)} %copy.128), channel_id=1, source_target_pairs={{0,24},{8,0},{16,8},{24,16},{1,25},{9,1},{17,9},{25,17},{2,26},{10... | collective-permute-start | bytes 6193160 | tf_op jit(solution)/shard_map/ppermute | solution.py:72
  111.4 3.4 fusion.2
  114.7 3.5 reshape.400
  129.6 5.3 %collective-permute-start.20 = (bf16[4,2,84,768]{3,0,2,1:T(4,128)(2,1)}, bf16[4,2,84,768]{3,0,2,1:T(4,128)(2,1)}, u32[]{:S(2)}, u32[]{:S(2)}) collective-permute-start(bf16[4,2,84,768]{3,0,2,1:T(4,128)(2,1)} %collective-permute-done.18), channel_id=1, source_target_pairs={{0,224},{32,0},{64,32},{96,64},{128,96},{160,128},{192,160},{224,1... | collective-permute-start | bytes 3096584 | tf_op jit(solution)/shard_map/ppermute | solution.py:72
  136.5 10.3 %collective-permute-done.10 = bf16[8,2,84,768]{3,0,2,1:T(8,128)(2,1)} collective-permute-done((bf16[8,2,84,768]{3,0,2,1:T(8,128)(2,1)}, bf16[8,2,84,768]{3,0,2,1:T(8,128)(2,1)}, u32[]{:S(2)}, u32[]{:S(2)}) %collective-permute-start.10) | collective-permute-done | bytes 2064416 | tf_op jit(solution)/shard_map/ppermute | solution.py:72
  148.0 3.8 %collective-permute-done.9 = bf16[8,2,84,768]{3,0,2,1:T(8,128)(2,1)} collective-permute-done((bf16[8,2,84,768]{3,0,2,1:T(8,128)(2,1)}, bf16[8,2,84,768]{3,0,2,1:T(8,128)(2,1)}, u32[]{:S(2)}, u32[]{:S(2)}) %collective-permute-start.9) | collective-permute-done | bytes 2064416 | tf_op jit(solution)/shard_map/ppermute | solution.py:71
  159.6 5.1 %collective-permute-start.22 = (bf16[4,2,84,768]{3,0,2,1:T(4,128)(2,1)}, bf16[4,2,84,768]{3,0,2,1:T(4,128)(2,1)}, u32[]{:S(2)}, u32[]{:S(2)}) collective-permute-start(bf16[4,2,84,768]{3,0,2,1:T(4,128)(2,1)} %collective-permute-done.20), channel_id=1, source_target_pairs={{0,224},{32,0},{64,32},{96,64},{128,96},{160,128},{192,160},{224,1... | collective-permute-start | bytes 3096584 | tf_op jit(solution)/shard_map/ppermute | solution.py:72
  173.4 4.8 %collective-permute-start.12 = (bf16[4,2,84,768]{3,0,2,1:T(4,128)(2,1)}, bf16[4,2,84,768]{3,0,2,1:T(4,128)(2,1)}, u32[]{:S(2)}, u32[]{:S(2)}) collective-permute-start(bf16[4,2,84,768]{3,0,2,1:T(4,128)(2,1)} %slice.305), channel_id=1, source_target_pairs={{0,24},{8,0},{16,8},{24,16},{1,25},{9,1},{17,9},{25,17},{2,26},{10... | collective-permute-start | bytes 3096584 | tf_op jit(solution)/shard_map/ppermute | solution.py:79
  202.5 5.1 %collective-permute-start.24 = (bf16[2,2,84,768]{3,1,2,0:T(2,128)(2,1)}, bf16[2,2,84,768]{3,1,2,0:T(2,128)(2,1)}, u32[]{:S(2)}, u32[]{:S(2)}) collective-permute-start(bf16[2,2,84,768]{3,1,2,0:T(2,128)(2,1)} %copy.147), channel_id=1, source_target_pairs={{0,224},{32,0},{64,32},{96,64},{128,96},{160,128},{192,160},{224,1... | collective-permute-start | bytes 1548296 | tf_op jit(solution)/shard_map/ppermute | solution.py:79
  220.3 5.2 %collective-permute-start.27 = (bf16[2,256,256]{2,1,0:T(8,128)(2,1)S(1)}, bf16[2,256,256]{2,1,0:T(8,128)(2,1)S(1)}, u32[]{:S(2)}, u32[]{:S(2)}) collective-permute-start(bf16[2,256,256]{2,1,0:T(8,128)(2,1)S(1)} %pad_maximum_fusion.4), channel_id=1, source_target_pairs={{0,16},{8,24},{16,32},{24,40},{32,48},{40,56},{48,64},{56,72},{64,... | collective-permute-start | bytes 786440 | tf_op jit(solution)/shard_map/ppermute | solution.py:22
  225.5 4.5 %collective-permute-start.26 = (bf16[2,256,256]{2,1,0:T(8,128)(2,1)S(1)}, bf16[2,256,256]{2,1,0:T(8,128)(2,1)}, u32[]{:S(2)}, u32[]{:S(2)}) collective-permute-start(bf16[2,256,256]{2,1,0:T(8,128)(2,1)S(1)} %pad_maximum_fusion.4), channel_id=1, source_target_pairs={{0,24},{8,32},{16,40},{24,48},{32,56},{40,64},{48,72},{56,80},{64,... | collective-permute-start | bytes 786440 | tf_op jit(solution)/shard_map/ppermute | solution.py:22
  230.0 3.9 %collective-permute-start.25 = (bf16[2,256,256]{2,1,0:T(8,128)(2,1)S(1)}, bf16[2,256,256]{2,1,0:T(8,128)(2,1)}, u32[]{:S(2)}, u32[]{:S(2)}) collective-permute-start(bf16[2,256,256]{2,1,0:T(8,128)(2,1)S(1)} %pad_maximum_fusion.4), channel_id=1, source_target_pairs={{0,32},{8,40},{16,48},{24,56},{32,64},{40,72},{48,80},{56,88},{64,... | collective-permute-start | bytes 786440 | tf_op jit(solution)/shard_map/ppermute | solution.py:22
  255.4 72.2 %reduce-scatter.2.cloned.1.call-done = bf16[256,672]{0,1:T(8,128)(2,1)} async-done(((bf16[256,5376]{0,1:T(8,128)(2,1)}), bf16[256,672]{0,1:T(8,128)(2,1)}) %reduce-scatter.2.cloned.1.call-update) | async-done | bytes 344080 | tf_op jit(solution)/shard_map/reduce_scatter | solution.py:229
  328.7 15.3 %psum.7 = f32[256]{0:T(256)S(1)} all-reduce(f32[256]{0:T(256)S(1)} %fusion.84), channel_id=1, replica_groups=mesh['zh'=2,'y'=8,'x'=4,'zl'=4,'c'=2] {'zl','c'}, use_global_device_ids=true, to_apply=%region_8.12 | all-reduce | flops 256 | bytes 2048 | tf_op jit(solution)/shard_map/psum | solution.py:233
  (202 shorter events, 126.3 us)
Async XLA Ops:
  6.5 102.1 %all-gather.2.cloned.1.call-start = ((), (), s32[]{:S(2)}) async-start(), calls=%async_computation.1 | async-start | bytes 3096576 | tf_op jit(solution)/shard_map/all_gather | solution.py:128
  7.3 320.4 %reduce-scatter.2.cloned.1.call-start = ((), (), s32[]{:S(2)}) async-start(), calls=%async_computation.2 | async-start | bytes 3096576 | tf_op jit(solution)/shard_map/reduce_scatter | solution.py:229
  8.3 17.5 %collective-permute-start = (bf16[84,1536]{1,0:T(8,128)(2,1)S(1)}, bf16[84,1536]{1,0:T(8,128)(2,1)S(1)}, u32[]{:S(2)}, u32[]{:S(2)}) collective-permute-start(bf16[84,1536]{1,0:T(8,128)(2,1)S(1)} %get-tuple-element.105), channel_id=1, source_target_pairs={{0,256},{256,0},{1,257},{257,1},{2,258},{258,2},{3,259},{259,3},{4... | collective-permute-start | bytes 774152 | tf_op jit(solution)/shard_map/ppermute | solution.py:31
  29.2 14.6 %collective-permute-start.14 = (bf16[2,84,768]{2,1,0:T(8,128)(2,1)}, bf16[2,84,768]{2,1,0:T(8,128)(2,1)}, u32[]{:S(2)}, u32[]{:S(2)}) collective-permute-start(bf16[2,84,768]{2,1,0:T(8,128)(2,1)} %pad_maximum_fusion.1), channel_id=1, source_target_pairs={{0,8},{8,16},{16,24},{24,0},{1,9},{9,17},{17,25},{25,1},{2,10},{10... | collective-permute-start | bytes 774152 | tf_op jit(solution)/shard_map/ppermute | solution.py:36
  33.2 14.2 %collective-permute-start.1 = (bf16[2,84,768]{2,1,0:T(8,128)(2,1)}, bf16[2,84,768]{2,1,0:T(8,128)(2,1)}, u32[]{:S(2)}, u32[]{:S(2)}) collective-permute-start(bf16[2,84,768]{2,1,0:T(8,128)(2,1)} %get-tuple-element.95), channel_id=1, source_target_pairs={{0,224},{32,0},{64,32},{96,64},{128,96},{160,128},{192,160},{224,1... | collective-permute-start | bytes 774152 | tf_op jit(solution)/shard_map/ppermute | solution.py:37
  38.6 14.0 %collective-permute-start.4 = (bf16[2,84,768]{2,1,0:T(8,128)(2,1)}, bf16[2,84,768]{2,1,0:T(8,128)(2,1)}, u32[]{:S(2)}, u32[]{:S(2)}) collective-permute-start(bf16[2,84,768]{2,1,0:T(8,128)(2,1)} %get-tuple-element.95), channel_id=1, source_target_pairs={{0,32},{32,64},{64,96},{96,128},{128,160},{160,192},{192,224},{224... | collective-permute-start | bytes 774152 | tf_op jit(solution)/shard_map/ppermute | solution.py:36
  40.6 14.9 %collective-permute-start.16 = (bf16[1,84,768]{2,1,0:T(8,128)(2,1)S(1)}, bf16[1,84,768]{2,1,0:T(8,128)(2,1)S(1)}, u32[]{:S(2)}, u32[]{:S(2)}) collective-permute-start(bf16[1,84,768]{2,1,0:T(8,128)(2,1)S(1)} %slice.351), channel_id=1, source_target_pairs={{0,24},{8,0},{16,8},{24,16},{1,25},{9,1},{17,9},{25,17},{2,26},{10... | collective-permute-start | bytes 387080 | tf_op jit(solution)/shard_map/ppermute | solution.py:43
  56.8 17.2 %collective-permute-start.3 = (bf16[2,84,768]{2,1,0:T(8,128)(2,1)S(1)}, bf16[2,84,768]{2,1,0:T(8,128)(2,1)S(1)}, u32[]{:S(2)}, u32[]{:S(2)}) collective-permute-start(bf16[2,84,768]{2,1,0:T(8,128)(2,1)S(1)} %collective-permute-done.2), channel_id=1, source_target_pairs={{0,224},{32,0},{64,32},{96,64},{128,96},{160,128},{192,160},{224,1... | collective-permute-start | bytes 774152 | tf_op jit(solution)/shard_map/ppermute | solution.py:37
  62.4 16.9 %collective-permute-start.6 = (bf16[2,84,768]{2,1,0:T(8,128)(2,1)S(1)}, bf16[2,84,768]{2,1,0:T(8,128)(2,1)S(1)}, u32[]{:S(2)}, u32[]{:S(2)}) collective-permute-start(bf16[2,84,768]{2,1,0:T(8,128)(2,1)S(1)} %collective-permute-done.5), channel_id=1, source_target_pairs={{0,32},{32,64},{64,96},{96,128},{128,160},{160,192},{192,224},{224... | collective-permute-start | bytes 774152 | tf_op jit(solution)/shard_map/ppermute | solution.py:36
  67.0 54.8 %collective-permute-start.18 = (bf16[4,2,84,768]{3,0,2,1:T(4,128)(2,1)}, bf16[4,2,84,768]{3,0,2,1:T(4,128)(2,1)}, u32[]{:S(2)}, u32[]{:S(2)}) collective-permute-start(bf16[4,2,84,768]{3,0,2,1:T(4,128)(2,1)} %copy.137), channel_id=1, source_target_pairs={{0,224},{32,0},{64,32},{96,64},{128,96},{160,128},{192,160},{224,1... | collective-permute-start | bytes 3096584 | tf_op jit(solution)/shard_map/ppermute | solution.py:72
  72.1 51.5 %collective-permute-start.17 = (bf16[4,2,84,768]{3,0,2,1:T(4,128)(2,1)}, bf16[4,2,84,768]{3,0,2,1:T(4,128)(2,1)}, u32[]{:S(2)}, u32[]{:S(2)}) collective-permute-start(bf16[4,2,84,768]{3,0,2,1:T(4,128)(2,1)} %copy.137), channel_id=1, source_target_pairs={{0,32},{32,64},{64,96},{96,128},{128,160},{160,192},{192,224},{224... | collective-permute-start | bytes 3096584 | tf_op jit(solution)/shard_map/ppermute | solution.py:71
  74.1 19.5 %collective-permute-start.8 = (bf16[1,84,768]{2,1,0:T(8,128)(2,1)S(1)}, bf16[1,84,768]{2,1,0:T(8,128)(2,1)S(1)}, u32[]{:S(2)}, u32[]{:S(2)}) collective-permute-start(bf16[1,84,768]{2,1,0:T(8,128)(2,1)S(1)} %slice.339), channel_id=1, source_target_pairs={{0,224},{32,0},{64,32},{96,64},{128,96},{160,128},{192,160},{224,1... | collective-permute-start | bytes 387080 | tf_op jit(solution)/shard_map/ppermute | solution.py:43
  79.2 19.6 %collective-permute-start.7 = (bf16[1,84,768]{2,1,0:T(8,128)(2,1)S(1)}, bf16[1,84,768]{2,1,0:T(8,128)(2,1)S(1)}, u32[]{:S(2)}, u32[]{:S(2)}) collective-permute-start(bf16[1,84,768]{2,1,0:T(8,128)(2,1)S(1)} %slice.338), channel_id=1, source_target_pairs={{0,32},{32,64},{64,96},{96,128},{128,160},{160,192},{192,224},{224... | collective-permute-start | bytes 387080 | tf_op jit(solution)/shard_map/ppermute | solution.py:42
  102.0 44.8 %collective-permute-start.10 = (bf16[8,2,84,768]{3,0,2,1:T(8,128)(2,1)}, bf16[8,2,84,768]{3,0,2,1:T(8,128)(2,1)}, u32[]{:S(2)}, u32[]{:S(2)}) collective-permute-start(bf16[8,2,84,768]{3,0,2,1:T(8,128)(2,1)} %copy.128), channel_id=1, source_target_pairs={{0,24},{8,0},{16,8},{24,16},{1,25},{9,1},{17,9},{25,17},{2,26},{10... | collective-permute-start | bytes 6193160 | tf_op jit(solution)/shard_map/ppermute | solution.py:72
  106.7 45.0 %collective-permute-start.9 = (bf16[8,2,84,768]{3,0,2,1:T(8,128)(2,1)}, bf16[8,2,84,768]{3,0,2,1:T(8,128)(2,1)}, u32[]{:S(2)}, u32[]{:S(2)}) collective-permute-start(bf16[8,2,84,768]{3,0,2,1:T(8,128)(2,1)} %copy.128), channel_id=1, source_target_pairs={{0,8},{8,16},{16,24},{24,0},{1,9},{9,17},{17,25},{25,1},{2,10},{10... | collective-permute-start | bytes 6193160 | tf_op jit(solution)/shard_map/ppermute | solution.py:71
  127.7 25.1 %collective-permute-start.19 = (bf16[4,2,84,768]{3,0,2,1:T(4,128)(2,1)}, bf16[4,2,84,768]{3,0,2,1:T(4,128)(2,1)}, u32[]{:S(2)}, u32[]{:S(2)}) collective-permute-start(bf16[4,2,84,768]{3,0,2,1:T(4,128)(2,1)} %collective-permute-done.17), channel_id=1, source_target_pairs={{0,32},{32,64},{64,96},{96,128},{128,160},{160,192},{192,224},{224... | collective-permute-start | bytes 3096584 | tf_op jit(solution)/shard_map/ppermute | solution.py:71
  129.6 25.0 %collective-permute-start.20 = (bf16[4,2,84,768]{3,0,2,1:T(4,128)(2,1)}, bf16[4,2,84,768]{3,0,2,1:T(4,128)(2,1)}, u32[]{:S(2)}, u32[]{:S(2)}) collective-permute-start(bf16[4,2,84,768]{3,0,2,1:T(4,128)(2,1)} %collective-permute-done.18), channel_id=1, source_target_pairs={{0,224},{32,0},{64,32},{96,64},{128,96},{160,128},{192,160},{224,1... | collective-permute-start | bytes 3096584 | tf_op jit(solution)/shard_map/ppermute | solution.py:72
  157.3 25.1 %collective-permute-start.21 = (bf16[4,2,84,768]{3,0,2,1:T(4,128)(2,1)}, bf16[4,2,84,768]{3,0,2,1:T(4,128)(2,1)}, u32[]{:S(2)}, u32[]{:S(2)}) collective-permute-start(bf16[4,2,84,768]{3,0,2,1:T(4,128)(2,1)} %collective-permute-done.19), channel_id=1, source_target_pairs={{0,32},{32,64},{64,96},{96,128},{128,160},{160,192},{192,224},{224... | collective-permute-start | bytes 3096584 | tf_op jit(solution)/shard_map/ppermute | solution.py:71
  159.6 24.5 %collective-permute-start.22 = (bf16[4,2,84,768]{3,0,2,1:T(4,128)(2,1)}, bf16[4,2,84,768]{3,0,2,1:T(4,128)(2,1)}, u32[]{:S(2)}, u32[]{:S(2)}) collective-permute-start(bf16[4,2,84,768]{3,0,2,1:T(4,128)(2,1)} %collective-permute-done.20), channel_id=1, source_target_pairs={{0,224},{32,0},{64,32},{96,64},{128,96},{160,128},{192,160},{224,1... | collective-permute-start | bytes 3096584 | tf_op jit(solution)/shard_map/ppermute | solution.py:72
  173.4 23.8 %collective-permute-start.12 = (bf16[4,2,84,768]{3,0,2,1:T(4,128)(2,1)}, bf16[4,2,84,768]{3,0,2,1:T(4,128)(2,1)}, u32[]{:S(2)}, u32[]{:S(2)}) collective-permute-start(bf16[4,2,84,768]{3,0,2,1:T(4,128)(2,1)} %slice.305), channel_id=1, source_target_pairs={{0,24},{8,0},{16,8},{24,16},{1,25},{9,1},{17,9},{25,17},{2,26},{10... | collective-permute-start | bytes 3096584 | tf_op jit(solution)/shard_map/ppermute | solution.py:79
  178.2 20.1 %collective-permute-start.11 = (bf16[4,2,84,768]{3,0,2,1:T(4,128)(2,1)}, bf16[4,2,84,768]{3,0,2,1:T(4,128)(2,1)}, u32[]{:S(2)}, u32[]{:S(2)}) collective-permute-start(bf16[4,2,84,768]{3,0,2,1:T(4,128)(2,1)} %slice.302), channel_id=1, source_target_pairs={{0,8},{8,16},{16,24},{24,0},{1,9},{9,17},{17,25},{25,1},{2,10},{10... | collective-permute-start | bytes 3096584 | tf_op jit(solution)/shard_map/ppermute | solution.py:78
  189.5 23.3 %collective-permute-start.23 = (bf16[2,2,84,768]{3,1,2,0:T(2,128)(2,1)}, bf16[2,2,84,768]{3,1,2,0:T(2,128)(2,1)}, u32[]{:S(2)}, u32[]{:S(2)}) collective-permute-start(bf16[2,2,84,768]{3,1,2,0:T(2,128)(2,1)} %copy.145), channel_id=1, source_target_pairs={{0,32},{32,64},{64,96},{96,128},{128,160},{160,192},{192,224},{224... | collective-permute-start | bytes 1548296 | tf_op jit(solution)/shard_map/ppermute | solution.py:78
  218.2 21.0 %collective-permute-start.28 = (bf16[2,256,256]{2,1,0:T(8,128)(2,1)S(1)}, bf16[2,256,256]{2,1,0:T(8,128)(2,1)S(1)}, u32[]{:S(2)}, u32[]{:S(2)}) collective-permute-start(bf16[2,256,256]{2,1,0:T(8,128)(2,1)S(1)} %pad_maximum_fusion.4), channel_id=1, source_target_pairs={{0,8},{8,16},{16,24},{24,32},{32,40},{40,48},{48,56},{56,64},{64,7... | collective-permute-start | bytes 786440 | tf_op jit(solution)/shard_map/ppermute | solution.py:22
  220.3 18.8 %collective-permute-start.27 = (bf16[2,256,256]{2,1,0:T(8,128)(2,1)S(1)}, bf16[2,256,256]{2,1,0:T(8,128)(2,1)S(1)}, u32[]{:S(2)}, u32[]{:S(2)}) collective-permute-start(bf16[2,256,256]{2,1,0:T(8,128)(2,1)S(1)} %pad_maximum_fusion.4), channel_id=1, source_target_pairs={{0,16},{8,24},{16,32},{24,40},{32,48},{40,56},{48,64},{56,72},{64,... | collective-permute-start | bytes 786440 | tf_op jit(solution)/shard_map/ppermute | solution.py:22
  (32 other events, 342.5 us)
Sparse Core Ops, SparseCore 0:
  9.4 50.1 all-gather.1
  254.7 72.8 reduce-scatter.1

commit v5 on v4

--- a/solution.py
+++ b/solution.py
@@ -79,6 +79,26 @@
         bottom = lax.ppermute(lax.slice_in_dim(right, k, None, axis=split_axis), axis, bwd)
         take([(n // 2, 0, k, top), (n // 2, k, full, bottom)])
     return pieces, acc
+
+
+def reduce_scatter_tp(partial, n_chip):
+    rows = partial.shape[0]
+    block_cols = partial.shape[1] // (2 * n_chip)
+    at_c = lax.axis_index("c")
+    at_z = lax.axis_index("zl")
+    blocks = partial.reshape(rows, n_chip, 2, block_cols)
+    keep = lax.dynamic_index_in_dim(blocks, at_c, axis=2, keepdims=False)
+    give = lax.dynamic_index_in_dim(blocks, 1 - at_c, axis=2, keepdims=False)
+    got = lax.ppermute(give, "c", [(0, 1), (1, 0)])
+    chip_sum = keep.astype(jnp.float32) + got.astype(jnp.float32)
+    total = lax.dynamic_index_in_dim(chip_sum, at_z, axis=1, keepdims=False)
+    for d in range(1, n_chip):
+        for sign in (1, -1):
+            route = [(i, i + sign * d) for i in range(n_chip) if 0 <= i + sign * d < n_chip]
+            target = jnp.clip(at_z + sign * d, 0, n_chip - 1)
+            block = lax.dynamic_index_in_dim(chip_sum, target, axis=1, keepdims=False)
+            total = total + lax.ppermute(block.astype(jnp.bfloat16), "zl", route).astype(jnp.float32)
+    return total
 
 
 def norm_scale(value_matrix, gain):
@@ -226,9 +246,7 @@
     out_abs = jnp.roll(out_abs, at_x, axis=2)
     out_abs = jnp.roll(out_abs, at_zh, axis=3)
     partial_out = out_abs.transpose(0, 3, 1, 2, 4).reshape(tok_rows, n_seq * shard_rows)
-    summed_cols = lax.psum_scatter(
-        partial_out, TP, scatter_dimension=1, tiled=True
-    ).astype(jnp.float32)
+    summed_cols = reduce_scatter_tp(partial_out, dict(TP_PARTS)["zl"])
     full_width = post_gain.shape[0]
     squares = lax.psum(jnp.sum(summed_cols * summed_cols, axis=1), TP)
     inverse_rms = lax.rsqrt(squares / full_width + epsilon)

time: 355 us -> 357 us (level)
  the two profiles are of different devices: /device:TPU:2 before, /device:TPU:263 now
where the time goes in v5:
time: 357 us; the launch traced here: 355 us
  starting transfers between devices  157 us (44%)
  waiting for transfers between devices  62.6 us (18%)
  local copies, waits for them, and re-layouts  49.5 us (14%)
  matrix products  29.1 us (8%)
  other arithmetic  27.6 us (8%)
  between operations  14.8 us (4%)
  blocking collectives  14.1 us (4%)
    ppermute x6, starting transfers between devices, reduce_scatter_tp(): lax.ppermute(block.astype(jnp.bfloat16), 'zl', route).astype(jnp.float32)  39.5 us
    ppermute x1, starting transfers between devices, reduce_scatter_tp(): got = lax.ppermute(give, 'c', [(0, 1), (1, 0)])  24 us
    dot_general x14, matrix products, contract(): lax.dot_general(lhs, piece, (((1, 2, 3), (0, 1, 2)), ((), ())), preferred...  21.2 us
    ppermute x4, starting transfers between devices, ring(): right = lax.ppermute(right, axis, bwd)  17.2 us
    ppermute x6, waiting for transfers between devices, reduce_scatter_tp(): lax.ppermute(block.astype(jnp.bfloat16), 'zl', route).astype(jnp.float32)  16 us
    ppermute x4, starting transfers between devices, ring_pieces(): right = lax.ppermute(right, axis, bwd)  16 us
    psum x1, blocking collectives, local(): squares = lax.psum(jnp.sum(summed_cols * summed_cols, axis=1), TP)  14.1 us
    ppermute x4, starting transfers between devices, from_behind(): return lax.ppermute(block, axis, route)  12.4 us
  transfers between devices with their start and end apart: 37, of which 10 were waited for; matrix products, arithmetic and copies ran while one was open for 21% of the time, Pallas kernels for 0%

profile of v5, /device:TPU:263, one launch (start us, length us, event | category | flops | bytes accessed | tf_op | source)
XLA Modules:
  0.0 354.7 jit_solution(6584301311282227482)
XLA Ops:
  10.2 11.4 %collective-permute-done = bf16[84,1536]{1,0:T(8,128)(2,1)S(1)} collective-permute-done((bf16[84,1536]{1,0:T(8,128)(2,1)S(1)}, bf16[84,1536]{1,0:T(8,128)(2,1)S(1)}, u32[]{:S(2)}, u32[]{:S(2)}) %collective-permute-start) | collective-permute-done | bytes 258080 | tf_op jit(solution)/shard_map/ppermute | solution.py:31
  29.5 5.1 %collective-permute-start.1 = (bf16[2,84,768]{2,1,0:T(8,128)(2,1)}, bf16[2,84,768]{2,1,0:T(8,128)(2,1)}, u32[]{:S(2)}, u32[]{:S(2)}) collective-permute-start(bf16[2,84,768]{2,1,0:T(8,128)(2,1)} %get-tuple-element.97), channel_id=1, source_target_pairs={{0,224},{32,0},{64,32},{96,64},{128,96},{160,128},{192,160},{224,1... | collective-permute-start | bytes 774152 | tf_op jit(solution)/shard_map/ppermute | solution.py:37
  39.6 4.6 %collective-permute-start.15 = (bf16[1,84,768]{2,1,0:T(8,128)(2,1)S(1)}, bf16[1,84,768]{2,1,0:T(8,128)(2,1)S(1)}, u32[]{:S(2)}, u32[]{:S(2)}) collective-permute-start(bf16[1,84,768]{2,1,0:T(8,128)(2,1)S(1)} %slice.350), channel_id=1, source_target_pairs={{0,8},{8,16},{16,24},{24,0},{1,9},{9,17},{17,25},{25,1},{2,10},{10... | collective-permute-start | bytes 387080 | tf_op jit(solution)/shard_map/ppermute | solution.py:42
  44.2 4.6 %collective-permute-start.2 = (bf16[2,84,768]{2,1,0:T(8,128)(2,1)}, bf16[2,84,768]{2,1,0:T(8,128)(2,1)S(1)}, u32[]{:S(2)}, u32[]{:S(2)}) collective-permute-start(bf16[2,84,768]{2,1,0:T(8,128)(2,1)} %collective-permute-done.1), channel_id=1, source_target_pairs={{0,224},{32,0},{64,32},{96,64},{128,96},{160,128},{192,160},{224,1... | collective-permute-start | bytes 774152 | tf_op jit(solution)/shard_map/ppermute | solution.py:37
  52.4 5.1 %collective-permute-start.3 = (bf16[2,84,768]{2,1,0:T(8,128)(2,1)S(1)}, bf16[2,84,768]{2,1,0:T(8,128)(2,1)S(1)}, u32[]{:S(2)}, u32[]{:S(2)}) collective-permute-start(bf16[2,84,768]{2,1,0:T(8,128)(2,1)S(1)} %collective-permute-done.2), channel_id=1, source_target_pairs={{0,224},{32,0},{64,32},{96,64},{128,96},{160,128},{192,160},{224,1... | collective-permute-start | bytes 774152 | tf_op jit(solution)/shard_map/ppermute | solution.py:37
  62.2 4.6 %collective-permute-start.18 = (bf16[4,2,84,768]{3,0,2,1:T(4,128)(2,1)}, bf16[4,2,84,768]{3,0,2,1:T(4,128)(2,1)}, u32[]{:S(2)}, u32[]{:S(2)}) collective-permute-start(bf16[4,2,84,768]{3,0,2,1:T(4,128)(2,1)} %copy.137), channel_id=1, source_target_pairs={{0,224},{32,0},{64,32},{96,64},{128,96},{160,128},{192,160},{224,1... | collective-permute-start | bytes 3096584 | tf_op jit(solution)/shard_map/ppermute | solution.py:72
  68.8 4.6 %collective-permute-start.8 = (bf16[1,84,768]{2,1,0:T(8,128)(2,1)S(1)}, bf16[1,84,768]{2,1,0:T(8,128)(2,1)S(1)}, u32[]{:S(2)}, u32[]{:S(2)}) collective-permute-start(bf16[1,84,768]{2,1,0:T(8,128)(2,1)S(1)} %slice.339), channel_id=1, source_target_pairs={{0,224},{32,0},{64,32},{96,64},{128,96},{160,128},{192,160},{224,1... | collective-permute-start | bytes 387080 | tf_op jit(solution)/shard_map/ppermute | solution.py:43
  75.3 9.9 %collective-permute-done.8 = bf16[1,84,768]{2,1,0:T(8,128)(2,1)S(1)} collective-permute-done((bf16[1,84,768]{2,1,0:T(8,128)(2,1)S(1)}, bf16[1,84,768]{2,1,0:T(8,128)(2,1)S(1)}, u32[]{:S(2)}, u32[]{:S(2)}) %collective-permute-start.8) | collective-permute-done | bytes 129056 | tf_op jit(solution)/shard_map/ppermute | solution.py:43
  85.2 5.2 %collective-permute-done.7 = bf16[1,84,768]{2,1,0:T(8,128)(2,1)S(1)} collective-permute-done((bf16[1,84,768]{2,1,0:T(8,128)(2,1)S(1)}, bf16[1,84,768]{2,1,0:T(8,128)(2,1)S(1)}, u32[]{:S(2)}, u32[]{:S(2)}) %collective-permute-start.7) | collective-permute-done | bytes 129056 | tf_op jit(solution)/shard_map/ppermute | solution.py:42
  95.4 4.6 %collective-permute-start.9 = (bf16[8,2,84,768]{3,0,2,1:T(8,128)(2,1)}, bf16[8,2,84,768]{3,0,2,1:T(8,128)(2,1)}, u32[]{:S(2)}, u32[]{:S(2)}) collective-permute-start(bf16[8,2,84,768]{3,0,2,1:T(8,128)(2,1)} %copy.128), channel_id=1, source_target_pairs={{0,8},{8,16},{16,24},{24,0},{1,9},{9,17},{17,25},{25,1},{2,10},{10... | collective-permute-start | bytes 6193160 | tf_op jit(solution)/shard_map/ppermute | solution.py:71
  121.0 4.8 %collective-permute-start.20 = (bf16[4,2,84,768]{3,0,2,1:T(4,128)(2,1)}, bf16[4,2,84,768]{3,0,2,1:T(4,128)(2,1)}, u32[]{:S(2)}, u32[]{:S(2)}) collective-permute-start(bf16[4,2,84,768]{3,0,2,1:T(4,128)(2,1)} %collective-permute-done.18), channel_id=1, source_target_pairs={{0,224},{32,0},{64,32},{96,64},{128,96},{160,128},{192,160},{224,1... | collective-permute-start | bytes 3096584 | tf_op jit(solution)/shard_map/ppermute | solution.py:72
  127.2 5.3 %collective-permute-done.10 = bf16[8,2,84,768]{3,0,2,1:T(8,128)(2,1)} collective-permute-done((bf16[8,2,84,768]{3,0,2,1:T(8,128)(2,1)}, bf16[8,2,84,768]{3,0,2,1:T(8,128)(2,1)}, u32[]{:S(2)}, u32[]{:S(2)}) %collective-permute-start.10) | collective-permute-done | bytes 2064416 | tf_op jit(solution)/shard_map/ppermute | solution.py:72
  143.0 4.7 %collective-permute-start.22 = (bf16[4,2,84,768]{3,0,2,1:T(4,128)(2,1)}, bf16[4,2,84,768]{3,0,2,1:T(4,128)(2,1)}, u32[]{:S(2)}, u32[]{:S(2)}) collective-permute-start(bf16[4,2,84,768]{3,0,2,1:T(4,128)(2,1)} %collective-permute-done.20), channel_id=1, source_target_pairs={{0,224},{32,0},{64,32},{96,64},{128,96},{160,128},{192,160},{224,1... | collective-permute-start | bytes 3096584 | tf_op jit(solution)/shard_map/ppermute | solution.py:72
  158.3 4.6 %collective-permute-start.11 = (bf16[4,2,84,768]{3,0,2,1:T(4,128)(2,1)}, bf16[4,2,84,768]{3,0,2,1:T(4,128)(2,1)}, u32[]{:S(2)}, u32[]{:S(2)}) collective-permute-start(bf16[4,2,84,768]{3,0,2,1:T(4,128)(2,1)} %slice.302), channel_id=1, source_target_pairs={{0,8},{8,16},{16,24},{24,0},{1,9},{9,17},{17,25},{25,1},{2,10},{10... | collective-permute-start | bytes 3096584 | tf_op jit(solution)/shard_map/ppermute | solution.py:78
  185.2 4.6 %collective-permute-start.24 = (bf16[2,2,84,768]{3,1,2,0:T(2,128)(2,1)}, bf16[2,2,84,768]{3,1,2,0:T(2,128)(2,1)}, u32[]{:S(2)}, u32[]{:S(2)}) collective-permute-start(bf16[2,2,84,768]{3,1,2,0:T(2,128)(2,1)} %copy.147), channel_id=1, source_target_pairs={{0,224},{32,0},{64,32},{96,64},{128,96},{160,128},{192,160},{224,1... | collective-permute-start | bytes 1548296 | tf_op jit(solution)/shard_map/ppermute | solution.py:79
  207.8 4.8 %collective-permute-start.25 = (bf16[2,256,256]{2,1,0:T(8,128)(2,1)S(1)}, bf16[2,256,256]{2,1,0:T(8,128)(2,1)}, u32[]{:S(2)}, u32[]{:S(2)}) collective-permute-start(bf16[2,256,256]{2,1,0:T(8,128)(2,1)S(1)} %pad_maximum_fusion.4), channel_id=1, source_target_pairs={{0,32},{8,40},{16,48},{24,56},{32,64},{40,72},{48,80},{56,88},{64,... | collective-permute-start | bytes 786440 | tf_op jit(solution)/shard_map/ppermute | solution.py:22
  214.9 9.1 %collective-permute-done.25 = bf16[2,256,256]{2,1,0:T(8,128)(2,1)} collective-permute-done((bf16[2,256,256]{2,1,0:T(8,128)(2,1)S(1)}, bf16[2,256,256]{2,1,0:T(8,128)(2,1)}, u32[]{:S(2)}, u32[]{:S(2)}) %collective-permute-start.25) | collective-permute-done | bytes 262176 | tf_op jit(solution)/shard_map/ppermute | solution.py:22
  243.0 24.0 %collective-permute-start.29 = (bf16[256,4,672]{0,2,1:T(8,128)(2,1)S(1)}, bf16[256,4,672]{0,2,1:T(8,128)(2,1)}, u32[]{:S(2)}, u32[]{:S(2)}) collective-permute-start(bf16[256,4,672]{0,2,1:T(8,128)(2,1)S(1)} %dynamic-slice_bitcast_fusion), channel_id=1, source_target_pairs={{0,1},{1,0},{2,3},{3,2},{4,5},{5,4},{6,7},{7,6},{8,9},{9,8},{10,11... | collective-permute-start | bytes 4128776 | tf_op jit(solution)/shard_map/ppermute | solution.py:92
  273.0 22.1 %collective-permute-start.30 = (bf16[256,672]{0,1:T(8,128)(2,1)S(1)}, bf16[256,672]{0,1:T(8,128)(2,1)S(1)}, u32[]{:S(2)}, u32[]{:S(2)}) collective-permute-start(bf16[256,672]{0,1:T(8,128)(2,1)S(1)} %get-tuple-element.98), channel_id=1, source_target_pairs={{0,2},{2,4},{4,6},{1,3},{3,5},{5,7},{8,10},{10,12},{12,14},{9,11},... | collective-permute-start | bytes 1032200 | tf_op jit(solution)/shard_map/ppermute | solution.py:100
  296.3 7.2 %collective-permute-start.34 = (bf16[256,672]{0,1:T(8,128)(2,1)}, bf16[256,672]{0,1:T(8,128)(2,1)}, u32[]{:S(2)}, u32[]{:S(2)}) collective-permute-start(bf16[256,672]{0,1:T(8,128)(2,1)} %get-tuple-element.100), channel_id=1, source_target_pairs={{0,6},{1,7},{8,14},{9,15},{16,22},{17,23},{24,30},{25,31},{32,38},... | collective-permute-start | bytes 1032200 | tf_op jit(solution)/shard_map/ppermute | solution.py:100
  304.9 6.3 %collective-permute-start.32 = (bf16[256,672]{0,1:T(8,128)(2,1)S(1)}, bf16[256,672]{0,1:T(8,128)(2,1)}, u32[]{:S(2)}, u32[]{:S(2)}) collective-permute-start(bf16[256,672]{0,1:T(8,128)(2,1)S(1)} %get-tuple-element.102), channel_id=1, source_target_pairs={{0,4},{2,6},{1,5},{3,7},{8,12},{10,14},{9,13},{11,15},{16,20},{18,... | collective-permute-start | bytes 1032200 | tf_op jit(solution)/shard_map/ppermute | solution.py:100
  314.0 9.8 %collective-permute-done.33 = bf16[256,672]{0,1:T(8,128)(2,1)} collective-permute-done((bf16[256,672]{0,1:T(8,128)(2,1)}, bf16[256,672]{0,1:T(8,128)(2,1)}, u32[]{:S(2)}, u32[]{:S(2)}) %collective-permute-start.33) | collective-permute-done | bytes 344096 | tf_op jit(solution)/shard_map/ppermute | solution.py:100
  323.8 6.2 %collective-permute-done.31 = bf16[256,672]{0,1:T(8,128)(2,1)} collective-permute-done((bf16[256,672]{0,1:T(8,128)(2,1)S(1)}, bf16[256,672]{0,1:T(8,128)(2,1)}, u32[]{:S(2)}, u32[]{:S(2)}) %collective-permute-start.31) | collective-permute-done | bytes 344096 | tf_op jit(solution)/shard_map/ppermute | solution.py:100
  331.9 14.1 %psum.7 = f32[256]{0:T(256)S(1)} all-reduce(f32[256]{0:T(256)S(1)} %get-tuple-element.92), channel_id=1, replica_groups=mesh['zh'=2,'y'=8,'x'=4,'zl'=4,'c'=2] {'zl','c'}, use_global_device_ids=true, to_apply=%region_7.11 | all-reduce | flops 256 | bytes 2048 | tf_op jit(solution)/shard_map/psum | solution.py:251
  (216 shorter events, 152.8 us)
Async XLA Ops:
  6.5 93.4 %all-gather.2.cloned.1.call-start = ((), (), s32[]{:S(2)}) async-start(), calls=%async_computation | async-start | bytes 3096576 | tf_op jit(solution)/shard_map/all_gather | solution.py:148
  62.2 50.9 %collective-permute-start.18 = (bf16[4,2,84,768]{3,0,2,1:T(4,128)(2,1)}, bf16[4,2,84,768]{3,0,2,1:T(4,128)(2,1)}, u32[]{:S(2)}, u32[]{:S(2)}) collective-permute-start(bf16[4,2,84,768]{3,0,2,1:T(4,128)(2,1)} %copy.137), channel_id=1, source_target_pairs={{0,224},{32,0},{64,32},{96,64},{128,96},{160,128},{192,160},{224,1... | collective-permute-start | bytes 3096584 | tf_op jit(solution)/shard_map/ppermute | solution.py:72
  66.8 48.1 %collective-permute-start.17 = (bf16[4,2,84,768]{3,0,2,1:T(4,128)(2,1)}, bf16[4,2,84,768]{3,0,2,1:T(4,128)(2,1)}, u32[]{:S(2)}, u32[]{:S(2)}) collective-permute-start(bf16[4,2,84,768]{3,0,2,1:T(4,128)(2,1)} %copy.137), channel_id=1, source_target_pairs={{0,32},{32,64},{64,96},{96,128},{128,160},{160,192},{192,224},{224... | collective-permute-start | bytes 3096584 | tf_op jit(solution)/shard_map/ppermute | solution.py:71
  68.8 16.4 %collective-permute-start.8 = (bf16[1,84,768]{2,1,0:T(8,128)(2,1)S(1)}, bf16[1,84,768]{2,1,0:T(8,128)(2,1)S(1)}, u32[]{:S(2)}, u32[]{:S(2)}) collective-permute-start(bf16[1,84,768]{2,1,0:T(8,128)(2,1)S(1)} %slice.339), channel_id=1, source_target_pairs={{0,224},{32,0},{64,32},{96,64},{128,96},{160,128},{192,160},{224,1... | collective-permute-start | bytes 387080 | tf_op jit(solution)/shard_map/ppermute | solution.py:43
  73.4 17.0 %collective-permute-start.7 = (bf16[1,84,768]{2,1,0:T(8,128)(2,1)S(1)}, bf16[1,84,768]{2,1,0:T(8,128)(2,1)S(1)}, u32[]{:S(2)}, u32[]{:S(2)}) collective-permute-start(bf16[1,84,768]{2,1,0:T(8,128)(2,1)S(1)} %slice.338), channel_id=1, source_target_pairs={{0,32},{32,64},{64,96},{96,128},{128,160},{160,192},{192,224},{224... | collective-permute-start | bytes 387080 | tf_op jit(solution)/shard_map/ppermute | solution.py:42
  93.4 39.1 %collective-permute-start.10 = (bf16[8,2,84,768]{3,0,2,1:T(8,128)(2,1)}, bf16[8,2,84,768]{3,0,2,1:T(8,128)(2,1)}, u32[]{:S(2)}, u32[]{:S(2)}) collective-permute-start(bf16[8,2,84,768]{3,0,2,1:T(8,128)(2,1)} %copy.128), channel_id=1, source_target_pairs={{0,24},{8,0},{16,8},{24,16},{1,25},{9,1},{17,9},{25,17},{2,26},{10... | collective-permute-start | bytes 6193160 | tf_op jit(solution)/shard_map/ppermute | solution.py:72
  95.4 38.3 %collective-permute-start.9 = (bf16[8,2,84,768]{3,0,2,1:T(8,128)(2,1)}, bf16[8,2,84,768]{3,0,2,1:T(8,128)(2,1)}, u32[]{:S(2)}, u32[]{:S(2)}) collective-permute-start(bf16[8,2,84,768]{3,0,2,1:T(8,128)(2,1)} %copy.128), channel_id=1, source_target_pairs={{0,8},{8,16},{16,24},{24,0},{1,9},{9,17},{17,25},{25,1},{2,10},{10... | collective-permute-start | bytes 6193160 | tf_op jit(solution)/shard_map/ppermute | solution.py:71
  119.0 17.2 %collective-permute-start.19 = (bf16[4,2,84,768]{3,0,2,1:T(4,128)(2,1)}, bf16[4,2,84,768]{3,0,2,1:T(4,128)(2,1)}, u32[]{:S(2)}, u32[]{:S(2)}) collective-permute-start(bf16[4,2,84,768]{3,0,2,1:T(4,128)(2,1)} %collective-permute-done.17), channel_id=1, source_target_pairs={{0,32},{32,64},{64,96},{96,128},{128,160},{160,192},{192,224},{224... | collective-permute-start | bytes 3096584 | tf_op jit(solution)/shard_map/ppermute | solution.py:71
  121.0 17.0 %collective-permute-start.20 = (bf16[4,2,84,768]{3,0,2,1:T(4,128)(2,1)}, bf16[4,2,84,768]{3,0,2,1:T(4,128)(2,1)}, u32[]{:S(2)}, u32[]{:S(2)}) collective-permute-start(bf16[4,2,84,768]{3,0,2,1:T(4,128)(2,1)} %collective-permute-done.18), channel_id=1, source_target_pairs={{0,224},{32,0},{64,32},{96,64},{128,96},{160,128},{192,160},{224,1... | collective-permute-start | bytes 3096584 | tf_op jit(solution)/shard_map/ppermute | solution.py:72
  140.6 24.5 %collective-permute-start.21 = (bf16[4,2,84,768]{3,0,2,1:T(4,128)(2,1)}, bf16[4,2,84,768]{3,0,2,1:T(4,128)(2,1)}, u32[]{:S(2)}, u32[]{:S(2)}) collective-permute-start(bf16[4,2,84,768]{3,0,2,1:T(4,128)(2,1)} %collective-permute-done.19), channel_id=1, source_target_pairs={{0,32},{32,64},{64,96},{96,128},{128,160},{160,192},{192,224},{224... | collective-permute-start | bytes 3096584 | tf_op jit(solution)/shard_map/ppermute | solution.py:71
  143.0 23.9 %collective-permute-start.22 = (bf16[4,2,84,768]{3,0,2,1:T(4,128)(2,1)}, bf16[4,2,84,768]{3,0,2,1:T(4,128)(2,1)}, u32[]{:S(2)}, u32[]{:S(2)}) collective-permute-start(bf16[4,2,84,768]{3,0,2,1:T(4,128)(2,1)} %collective-permute-done.20), channel_id=1, source_target_pairs={{0,224},{32,0},{64,32},{96,64},{128,96},{160,128},{192,160},{224,1... | collective-permute-start | bytes 3096584 | tf_op jit(solution)/shard_map/ppermute | solution.py:72
  156.4 23.6 %collective-permute-start.12 = (bf16[4,2,84,768]{3,0,2,1:T(4,128)(2,1)}, bf16[4,2,84,768]{3,0,2,1:T(4,128)(2,1)}, u32[]{:S(2)}, u32[]{:S(2)}) collective-permute-start(bf16[4,2,84,768]{3,0,2,1:T(4,128)(2,1)} %slice.305), channel_id=1, source_target_pairs={{0,24},{8,0},{16,8},{24,16},{1,25},{9,1},{17,9},{25,17},{2,26},{10... | collective-permute-start | bytes 3096584 | tf_op jit(solution)/shard_map/ppermute | solution.py:79
  158.3 22.8 %collective-permute-start.11 = (bf16[4,2,84,768]{3,0,2,1:T(4,128)(2,1)}, bf16[4,2,84,768]{3,0,2,1:T(4,128)(2,1)}, u32[]{:S(2)}, u32[]{:S(2)}) collective-permute-start(bf16[4,2,84,768]{3,0,2,1:T(4,128)(2,1)} %slice.302), channel_id=1, source_target_pairs={{0,8},{8,16},{16,24},{24,0},{1,9},{9,17},{17,25},{25,1},{2,10},{10... | collective-permute-start | bytes 3096584 | tf_op jit(solution)/shard_map/ppermute | solution.py:78
  172.3 22.7 %collective-permute-start.23 = (bf16[2,2,84,768]{3,1,2,0:T(2,128)(2,1)}, bf16[2,2,84,768]{3,1,2,0:T(2,128)(2,1)}, u32[]{:S(2)}, u32[]{:S(2)}) collective-permute-start(bf16[2,2,84,768]{3,1,2,0:T(2,128)(2,1)} %copy.145), channel_id=1, source_target_pairs={{0,32},{32,64},{64,96},{96,128},{128,160},{160,192},{192,224},{224... | collective-permute-start | bytes 1548296 | tf_op jit(solution)/shard_map/ppermute | solution.py:78
  200.2 25.9 %collective-permute-start.28 = (bf16[2,256,256]{2,1,0:T(8,128)(2,1)S(1)}, bf16[2,256,256]{2,1,0:T(8,128)(2,1)S(1)}, u32[]{:S(2)}, u32[]{:S(2)}) collective-permute-start(bf16[2,256,256]{2,1,0:T(8,128)(2,1)S(1)} %pad_maximum_fusion.4), channel_id=1, source_target_pairs={{0,8},{8,16},{16,24},{24,32},{32,40},{40,48},{48,56},{56,64},{64,7... | collective-permute-start | bytes 786440 | tf_op jit(solution)/shard_map/ppermute | solution.py:22
  202.2 23.8 %collective-permute-start.27 = (bf16[2,256,256]{2,1,0:T(8,128)(2,1)S(1)}, bf16[2,256,256]{2,1,0:T(8,128)(2,1)S(1)}, u32[]{:S(2)}, u32[]{:S(2)}) collective-permute-start(bf16[2,256,256]{2,1,0:T(8,128)(2,1)S(1)} %pad_maximum_fusion.4), channel_id=1, source_target_pairs={{0,16},{8,24},{16,32},{24,40},{32,48},{40,56},{48,64},{56,72},{64,... | collective-permute-start | bytes 786440 | tf_op jit(solution)/shard_map/ppermute | solution.py:22
  204.7 20.3 %collective-permute-start.26 = (bf16[2,256,256]{2,1,0:T(8,128)(2,1)S(1)}, bf16[2,256,256]{2,1,0:T(8,128)(2,1)}, u32[]{:S(2)}, u32[]{:S(2)}) collective-permute-start(bf16[2,256,256]{2,1,0:T(8,128)(2,1)S(1)} %pad_maximum_fusion.4), channel_id=1, source_target_pairs={{0,24},{8,32},{16,40},{24,48},{32,56},{40,64},{48,72},{56,80},{64,... | collective-permute-start | bytes 786440 | tf_op jit(solution)/shard_map/ppermute | solution.py:22
  243.0 26.9 %collective-permute-start.29 = (bf16[256,4,672]{0,2,1:T(8,128)(2,1)S(1)}, bf16[256,4,672]{0,2,1:T(8,128)(2,1)}, u32[]{:S(2)}, u32[]{:S(2)}) collective-permute-start(bf16[256,4,672]{0,2,1:T(8,128)(2,1)S(1)} %dynamic-slice_bitcast_fusion), channel_id=1, source_target_pairs={{0,1},{1,0},{2,3},{3,2},{4,5},{5,4},{6,7},{7,6},{8,9},{9,8},{10,11... | collective-permute-start | bytes 4128776 | tf_op jit(solution)/shard_map/ppermute | solution.py:92
  273.0 38.2 %collective-permute-start.30 = (bf16[256,672]{0,1:T(8,128)(2,1)S(1)}, bf16[256,672]{0,1:T(8,128)(2,1)S(1)}, u32[]{:S(2)}, u32[]{:S(2)}) collective-permute-start(bf16[256,672]{0,1:T(8,128)(2,1)S(1)} %get-tuple-element.98), channel_id=1, source_target_pairs={{0,2},{2,4},{4,6},{1,3},{3,5},{5,7},{8,10},{10,12},{12,14},{9,11},... | collective-permute-start | bytes 1032200 | tf_op jit(solution)/shard_map/ppermute | solution.py:100
  295.0 19.0 %collective-permute-start.35 = (bf16[256,672]{0,1:T(8,128)(2,1)}, bf16[256,672]{0,1:T(8,128)(2,1)}, u32[]{:S(2)}, u32[]{:S(2)}) collective-permute-start(bf16[256,672]{0,1:T(8,128)(2,1)} %get-tuple-element.99), channel_id=1, source_target_pairs={{6,0},{7,1},{14,8},{15,9},{22,16},{23,17},{30,24},{31,25},{38,32},... | collective-permute-start | bytes 1032200 | tf_op jit(solution)/shard_map/ppermute | solution.py:100
  296.3 17.7 %collective-permute-start.34 = (bf16[256,672]{0,1:T(8,128)(2,1)}, bf16[256,672]{0,1:T(8,128)(2,1)}, u32[]{:S(2)}, u32[]{:S(2)}) collective-permute-start(bf16[256,672]{0,1:T(8,128)(2,1)} %get-tuple-element.100), channel_id=1, source_target_pairs={{0,6},{1,7},{8,14},{9,15},{16,22},{17,23},{24,30},{25,31},{32,38},... | collective-permute-start | bytes 1032200 | tf_op jit(solution)/shard_map/ppermute | solution.py:100
  303.6 20.2 %collective-permute-start.33 = (bf16[256,672]{0,1:T(8,128)(2,1)}, bf16[256,672]{0,1:T(8,128)(2,1)}, u32[]{:S(2)}, u32[]{:S(2)}) collective-permute-start(bf16[256,672]{0,1:T(8,128)(2,1)} %get-tuple-element.101), channel_id=1, source_target_pairs={{4,0},{6,2},{5,1},{7,3},{12,8},{14,10},{13,9},{15,11},{20,16},{22,... | collective-permute-start | bytes 1032200 | tf_op jit(solution)/shard_map/ppermute | solution.py:100
  304.9 19.0 %collective-permute-start.32 = (bf16[256,672]{0,1:T(8,128)(2,1)S(1)}, bf16[256,672]{0,1:T(8,128)(2,1)}, u32[]{:S(2)}, u32[]{:S(2)}) collective-permute-start(bf16[256,672]{0,1:T(8,128)(2,1)S(1)} %get-tuple-element.102), channel_id=1, source_target_pairs={{0,4},{2,6},{1,5},{3,7},{8,12},{10,14},{9,13},{11,15},{16,20},{18,... | collective-permute-start | bytes 1032200 | tf_op jit(solution)/shard_map/ppermute | solution.py:100
  311.9 18.1 %collective-permute-start.31 = (bf16[256,672]{0,1:T(8,128)(2,1)S(1)}, bf16[256,672]{0,1:T(8,128)(2,1)}, u32[]{:S(2)}, u32[]{:S(2)}) collective-permute-start(bf16[256,672]{0,1:T(8,128)(2,1)S(1)} %get-tuple-element.103), channel_id=1, source_target_pairs={{2,0},{4,2},{6,4},{3,1},{5,3},{7,5},{10,8},{12,10},{14,12},{11,9},... | collective-permute-start | bytes 1032200 | tf_op jit(solution)/shard_map/ppermute | solution.py:100
  (38 other events, 341.1 us)
Sparse Core Ops, SparseCore 0:
  9.4 45.3 all-gather.1

commit v6 on v5

--- a/solution.py
+++ b/solution.py
@@ -164,23 +164,25 @@
             acc = term if acc is None else acc + term
         return acc
 
-    def fold_v(acc, new):
+    def fold_kv(acc, new):
         for dx, lo, hi, piece in new:
-            term = contract(normed_rel[:, lo:hi, dx], piece[..., :v_cols])
+            term = contract(normed_rel[:, lo:hi, dx], piece)
             acc = term if acc is None else acc + term
         return acc
 
-    packed = jnp.concatenate([w_query, key_weight, value_weight, w_out.T], axis=1)
+    packed = jnp.concatenate([w_query, key_weight, value_weight], axis=1)
     by_zh = stacked_ring(packed, "zh", nz, 0)
-    split = q_cols + k_cols
+    split = q_cols
     half_a = by_zh[:, :, :split]
     half_b = by_zh[:, :, split:]
     a_x = stacked_ring(half_a, "x", nx, 0)
     b_y = stacked_ring(half_b, "y", ny, 0)
-    _, qk = ring_pieces(a_x, "y", ny, 0, fold_qk, None)
-    b_pieces, projected_values = ring_pieces(b_y, "x", nx, 0, fold_v, None)
-    queries_raw = qk[:, :q_cols]
-    unrotated_keys = qk[:, q_cols:]
+    _, queries_raw = ring_pieces(a_x, "y", ny, 0, fold_qk, None)
+    _, kv = ring_pieces(b_y, "x", nx, 0, fold_kv, None)
+    unrotated_keys = kv[:, :k_cols]
+    projected_values = kv[:, k_cols:]
+    _, w_out_after = lax.optimization_barrier((gathered, w_out))
+    w_out_full = lax.all_gather(w_out_after, SEQ, axis=1, tiled=True)
     own_places = lax.dynamic_slice_in_dim(positions, seq_at * tok_rows, tok_rows, 0)
     reach = (LOOKBACK_SPAN - 2) // tok_rows + 1
 
@@ -233,19 +235,9 @@
     total = jnp.transpose(inner_total + outer_total, (2, 0, 1))
     merged = (inner_sum + outer_sum) / total[..., None]
     attended = merged.astype(jnp.bfloat16).reshape(tok_rows, local_kv * query_group * head_dim)
-    out_rel = jnp.zeros((tok_rows, ny, nx, nz, shard_rows), jnp.bfloat16)
-    for dx, lo, hi, piece in b_pieces:
-        cols = lax.dot_general(
-            attended,
-            piece[..., v_cols:],
-            (((1,), (3,)), ((), ())),
-            preferred_element_type=jnp.float32,
-        )
-        out_rel = out_rel.at[:, lo:hi, dx].set(cols.astype(jnp.bfloat16))
-    out_abs = jnp.roll(out_rel, at_y, axis=1)
-    out_abs = jnp.roll(out_abs, at_x, axis=2)
-    out_abs = jnp.roll(out_abs, at_zh, axis=3)
-    partial_out = out_abs.transpose(0, 3, 1, 2, 4).reshape(tok_rows, n_seq * shard_rows)
+    partial_out = jnp.dot(attended, w_out_full, preferred_element_type=jnp.float32).astype(
+        jnp.bfloat16
+    )
     summed_cols = reduce_scatter_tp(partial_out, dict(TP_PARTS)["zl"])
     full_width = post_gain.shape[0]
     squares = lax.psum(jnp.sum(summed_cols * summed_cols, axis=1), TP)

time: 357 us -> 378 us (1.059)
  the two profiles are of different devices: /device:TPU:263 before, /device:TPU:271 now
where the time goes in v6:
time: 378 us; the launch traced here: 375 us
  starting transfers between devices  122 us (32%)
  waiting for transfers between devices  118 us (31%)
  local copies, waits for them, and re-layouts  49.9 us (13%)
  matrix products  29.6 us (8%)
  other arithmetic  27.5 us (7%)
  between operations  14.5 us (4%)
  blocking collectives  13.8 us (4%)
    all_gather x1, waiting for transfers between devices, local(): w_out_full = lax.all_gather(w_out_after, SEQ, axis=1, tiled=True)  54.6 us
    ppermute x6, starting transfers between devices, reduce_scatter_tp(): lax.ppermute(block.astype(jnp.bfloat16), 'zl', route).astype(jnp.float32)  28 us
    dot_general x14, matrix products, contract(): lax.dot_general(lhs, piece, (((1, 2, 3), (0, 1, 2)), ((), ())), preferred...  21 us
    ppermute x6, waiting for transfers between devices, reduce_scatter_tp(): lax.ppermute(block.astype(jnp.bfloat16), 'zl', route).astype(jnp.float32)  17.1 us
    unnamed x51, local copies, waits for them, and re-layouts  15 us
    ppermute x4, starting transfers between devices, ring_pieces(): left = lax.ppermute(left, axis, fwd)  14.6 us
    psum x1, blocking collectives, local(): squares = lax.psum(jnp.sum(summed_cols * summed_cols, axis=1), TP)  13.8 us
    ppermute x4, starting transfers between devices, ring(): right = lax.ppermute(right, axis, bwd)  13.6 us
  transfers between devices with their start and end apart: 38, of which 12 were waited for; matrix products, arithmetic and copies ran while one was open for 21% of the time, Pallas kernels for 0%

profile of v6, /device:TPU:271, one launch (start us, length us, event | category | flops | bytes accessed | tf_op | source)
XLA Modules:
  0.0 375.1 jit_solution(2589447344326248671)
XLA Ops:
  13.7 7.5 %collective-permute-done = bf16[84,1024]{1,0:T(8,128)(2,1)S(1)} collective-permute-done((bf16[84,1024]{1,0:T(8,128)(2,1)S(1)}, bf16[84,1024]{1,0:T(8,128)(2,1)S(1)}, u32[]{:S(2)}, u32[]{:S(2)}) %collective-permute-start) | collective-permute-done | bytes 172064 | tf_op jit(solution)/shard_map/ppermute | solution.py:31
  38.0 3.8 %collective-permute-start.2 = (bf16[2,84,512]{2,1,0:T(8,128)(2,1)S(1)}, bf16[2,84,512]{2,1,0:T(8,128)(2,1)S(1)}, u32[]{:S(2)}, u32[]{:S(2)}) collective-permute-start(bf16[2,84,512]{2,1,0:T(8,128)(2,1)S(1)} %collective-permute-done.1), channel_id=1, source_target_pairs={{0,224},{32,0},{64,32},{96,64},{128,96},{160,128},{192,160},{224,1... | collective-permute-start | bytes 516104 | tf_op jit(solution)/shard_map/ppermute | solution.py:37
  45.3 4.6 %collective-permute-start.18 = (bf16[4,2,84,512]{3,0,2,1:T(4,128)(2,1)}, bf16[4,2,84,512]{3,0,2,1:T(4,128)(2,1)}, u32[]{:S(2)}, u32[]{:S(2)}) collective-permute-start(bf16[4,2,84,512]{3,0,2,1:T(4,128)(2,1)} %copy.99), channel_id=1, source_target_pairs={{0,224},{32,0},{64,32},{96,64},{128,96},{160,128},{192,160},{224,1... | collective-permute-start | bytes 2064392 | tf_op jit(solution)/shard_map/ppermute | solution.py:72
  51.8 4.6 %collective-permute-start.3 = (bf16[2,84,512]{2,1,0:T(8,128)(2,1)S(1)}, bf16[2,84,512]{2,1,0:T(8,128)(2,1)S(1)}, u32[]{:S(2)}, u32[]{:S(2)}) collective-permute-start(bf16[2,84,512]{2,1,0:T(8,128)(2,1)S(1)} %collective-permute-done.2), channel_id=1, source_target_pairs={{0,224},{32,0},{64,32},{96,64},{128,96},{160,128},{192,160},{224,1... | collective-permute-start | bytes 516104 | tf_op jit(solution)/shard_map/ppermute | solution.py:37
  58.4 10.6 %collective-permute-done.6 = bf16[2,84,512]{2,1,0:T(8,128)(2,1)S(1)} collective-permute-done((bf16[2,84,512]{2,1,0:T(8,128)(2,1)S(1)}, bf16[2,84,512]{2,1,0:T(8,128)(2,1)S(1)}, u32[]{:S(2)}, u32[]{:S(2)}) %collective-permute-start.6) | collective-permute-done | bytes 172064 | tf_op jit(solution)/shard_map/ppermute | solution.py:36
  70.9 4.9 %collective-permute-start.8 = (bf16[1,84,512]{2,1,0:T(8,128)(2,1)S(1)}, bf16[1,84,512]{2,1,0:T(8,128)(2,1)S(1)}, u32[]{:S(2)}, u32[]{:S(2)}) collective-permute-start(bf16[1,84,512]{2,1,0:T(8,128)(2,1)S(1)} %slice.134), channel_id=1, source_target_pairs={{0,224},{32,0},{64,32},{96,64},{128,96},{160,128},{192,160},{224,1... | collective-permute-start | bytes 258056 | tf_op jit(solution)/shard_map/ppermute | solution.py:43
  79.3 4.5 %collective-permute-start.9 = (bf16[8,2,84,512]{3,0,2,1:T(8,128)(2,1)}, bf16[8,2,84,512]{3,0,2,1:T(8,128)(2,1)}, u32[]{:S(2)}, u32[]{:S(2)}) collective-permute-start(bf16[8,2,84,512]{3,0,2,1:T(8,128)(2,1)} %copy.90), channel_id=1, source_target_pairs={{0,8},{8,16},{16,24},{24,0},{1,9},{9,17},{17,25},{25,1},{2,10},{10... | collective-permute-start | bytes 4128776 | tf_op jit(solution)/shard_map/ppermute | solution.py:71
  92.1 3.5 reshape.189
  99.1 5.4 %collective-permute-done.9 = bf16[8,2,84,512]{3,0,2,1:T(8,128)(2,1)} collective-permute-done((bf16[8,2,84,512]{3,0,2,1:T(8,128)(2,1)}, bf16[8,2,84,512]{3,0,2,1:T(8,128)(2,1)}, u32[]{:S(2)}, u32[]{:S(2)}) %collective-permute-start.9) | collective-permute-done | bytes 1376288 | tf_op jit(solution)/shard_map/ppermute | solution.py:71
  125.6 3.8 %collective-permute-start.19 = (bf16[4,2,84,512]{3,0,2,1:T(4,128)(2,1)}, bf16[4,2,84,512]{3,0,2,1:T(4,128)(2,1)}, u32[]{:S(2)}, u32[]{:S(2)}) collective-permute-start(bf16[4,2,84,512]{3,0,2,1:T(4,128)(2,1)} %collective-permute-done.17), channel_id=1, source_target_pairs={{0,32},{32,64},{64,96},{96,128},{128,160},{160,192},{192,224},{224... | collective-permute-start | bytes 2064392 | tf_op jit(solution)/shard_map/ppermute | solution.py:71
  145.4 4.0 %collective-permute-start.25 = (bf16[2,256,256]{2,1,0:T(8,128)(2,1)}, bf16[2,256,256]{2,1,0:T(8,128)(2,1)}, u32[]{:S(2)}, u32[]{:S(2)}) collective-permute-start(bf16[2,256,256]{2,1,0:T(8,128)(2,1)} %pad_maximum_fusion.2), channel_id=1, source_target_pairs={{0,32},{8,40},{16,48},{24,56},{32,64},{40,72},{48,80},{56,88},{64,... | collective-permute-start | bytes 786440 | tf_op jit(solution)/shard_map/ppermute | solution.py:22
  153.3 4.4 %collective-permute-start.21 = (bf16[4,2,84,512]{3,0,2,1:T(4,128)(2,1)}, bf16[4,2,84,512]{3,0,2,1:T(4,128)(2,1)}, u32[]{:S(2)}, u32[]{:S(2)}) collective-permute-start(bf16[4,2,84,512]{3,0,2,1:T(4,128)(2,1)} %collective-permute-done.19), channel_id=1, source_target_pairs={{0,32},{32,64},{64,96},{96,128},{128,160},{160,192},{192,224},{224... | collective-permute-start | bytes 2064392 | tf_op jit(solution)/shard_map/ppermute | solution.py:71
  161.1 4.8 %collective-permute-start.27 = (bf16[2,256,256]{2,1,0:T(8,128)(2,1)}, bf16[2,256,256]{2,1,0:T(8,128)(2,1)}, u32[]{:S(2)}, u32[]{:S(2)}) collective-permute-start(bf16[2,256,256]{2,1,0:T(8,128)(2,1)} %pad_maximum_fusion.2), channel_id=1, source_target_pairs={{0,16},{8,24},{16,32},{24,40},{32,48},{40,56},{48,64},{56,72},{64,... | collective-permute-start | bytes 786440 | tf_op jit(solution)/shard_map/ppermute | solution.py:22
  175.3 7.9 %collective-permute-done.26 = bf16[2,256,256]{2,1,0:T(8,128)(2,1)} collective-permute-done((bf16[2,256,256]{2,1,0:T(8,128)(2,1)}, bf16[2,256,256]{2,1,0:T(8,128)(2,1)}, u32[]{:S(2)}, u32[]{:S(2)}) %collective-permute-start.26) | collective-permute-done | bytes 262176 | tf_op jit(solution)/shard_map/ppermute | solution.py:22
  184.1 4.6 %collective-permute-done.27 = bf16[2,256,256]{2,1,0:T(8,128)(2,1)} collective-permute-done((bf16[2,256,256]{2,1,0:T(8,128)(2,1)}, bf16[2,256,256]{2,1,0:T(8,128)(2,1)}, u32[]{:S(2)}, u32[]{:S(2)}) %collective-permute-start.27) | collective-permute-done | bytes 262176 | tf_op jit(solution)/shard_map/ppermute | solution.py:22
  217.6 54.6 %all-gather.6.cloned.1.call-done = bf16[64,84,512]{2,1,0:T(8,128)(2,1)} async-done(((bf16[1,84,512]{2,1,0:T(8,128)(2,1)}), bf16[64,84,512]{2,1,0:T(8,128)(2,1)}) %all-gather.6.cloned.1.call-update) | async-done | bytes 5505040 | tf_op jit(solution)/shard_map/all_gather | solution.py:185
  272.2 8.9 %reshape.196 = bf16[5376,512]{1,0:T(8,128)(2,1)} reshape(bf16[64,84,512]{2,1,0:T(8,128)(2,1)} %all-gather.6.cloned.1.call-done) | data formatting | bytes 11010048
  281.1 5.7 %convolution_convert_fusion = bf16[256,5376]{1,0:T(8,128)(2,1)} fusion(bf16[256,512]{0,1:T(8,128)(2,1)S(1)} %bitcast.267, bf16[5376,512]{1,0:T(8,128)(2,1)} %reshape.196), kind=kOutput, calls=%fused_computation | convolution fusion | flops 1410662400 | bytes 8519680 | tf_op jit(solution)/shard_map/dot_general | solution.py:238
  291.4 6.5 %collective-permute-start.29 = (bf16[256,4,672]{0,2,1:T(8,128)(2,1)}, bf16[256,4,672]{0,2,1:T(8,128)(2,1)}, u32[]{:S(2)}, u32[]{:S(2)}) collective-permute-start(bf16[256,4,672]{0,2,1:T(8,128)(2,1)} %dynamic-slice_bitcast_fusion), channel_id=1, source_target_pairs={{0,1},{1,0},{2,3},{3,2},{4,5},{5,4},{6,7},{7,6},{8,9},{9,8},{10,11... | collective-permute-start | bytes 4128776 | tf_op jit(solution)/shard_map/ppermute | solution.py:92
  304.1 10.7 %collective-permute-start.30 = (bf16[256,672]{0,1:T(8,128)(2,1)S(1)}, bf16[256,672]{0,1:T(8,128)(2,1)S(1)}, u32[]{:S(2)}, u32[]{:S(2)}) collective-permute-start(bf16[256,672]{0,1:T(8,128)(2,1)S(1)} %get-tuple-element.37), channel_id=1, source_target_pairs={{0,2},{2,4},{4,6},{1,3},{3,5},{5,7},{8,10},{10,12},{12,14},{9,11},... | collective-permute-start | bytes 1032200 | tf_op jit(solution)/shard_map/ppermute | solution.py:100
  316.2 6.6 %collective-permute-start.32 = (bf16[256,672]{0,1:T(8,128)(2,1)}, bf16[256,672]{0,1:T(8,128)(2,1)}, u32[]{:S(2)}, u32[]{:S(2)}) collective-permute-start(bf16[256,672]{0,1:T(8,128)(2,1)} %get-tuple-element.41), channel_id=1, source_target_pairs={{0,4},{2,6},{1,5},{3,7},{8,12},{10,14},{9,13},{11,15},{16,20},{18,... | collective-permute-start | bytes 1032200 | tf_op jit(solution)/shard_map/ppermute | solution.py:100
  324.1 6.8 %collective-permute-start.34 = (bf16[256,672]{0,1:T(8,128)(2,1)S(1)}, bf16[256,672]{0,1:T(8,128)(2,1)}, u32[]{:S(2)}, u32[]{:S(2)}) collective-permute-start(bf16[256,672]{0,1:T(8,128)(2,1)S(1)} %get-tuple-element.39), channel_id=1, source_target_pairs={{0,6},{1,7},{8,14},{9,15},{16,22},{17,23},{24,30},{25,31},{32,38},... | collective-permute-start | bytes 1032200 | tf_op jit(solution)/shard_map/ppermute | solution.py:100
  333.7 17.1 %collective-permute-done.33 = bf16[256,672]{0,1:T(8,128)(2,1)} collective-permute-done((bf16[256,672]{0,1:T(8,128)(2,1)}, bf16[256,672]{0,1:T(8,128)(2,1)}, u32[]{:S(2)}, u32[]{:S(2)}) %collective-permute-start.33) | collective-permute-done | bytes 344096 | tf_op jit(solution)/shard_map/ppermute | solution.py:100
  352.6 13.8 %psum.7 = f32[256]{0:T(256)S(1)} all-reduce(f32[256]{0:T(256)S(1)} %get-tuple-element.31), channel_id=1, replica_groups=mesh['zh'=2,'y'=8,'x'=4,'zl'=4,'c'=2] {'zl','c'}, use_global_device_ids=true, to_apply=%region_6.7 | all-reduce | flops 256 | bytes 2048 | tf_op jit(solution)/shard_map/psum | solution.py:243
  (194 shorter events, 151.0 us)
Async XLA Ops:
  6.5 79.4 %all-gather.4.cloned.1.call-start = ((), (), s32[]{:S(2)}) async-start(), calls=%async_computation | async-start | bytes 3096576 | tf_op jit(solution)/shard_map/all_gather | solution.py:148
  7.3 265.0 %all-gather.6.cloned.1.call-start = ((), (), s32[]{:S(2)}) async-start(), calls=%async_computation.1 | async-start | bytes 5857280 | tf_op jit(solution)/shard_map/all_gather | solution.py:185
  38.0 13.8 %collective-permute-start.2 = (bf16[2,84,512]{2,1,0:T(8,128)(2,1)S(1)}, bf16[2,84,512]{2,1,0:T(8,128)(2,1)S(1)}, u32[]{:S(2)}, u32[]{:S(2)}) collective-permute-start(bf16[2,84,512]{2,1,0:T(8,128)(2,1)S(1)} %collective-permute-done.1), channel_id=1, source_target_pairs={{0,224},{32,0},{64,32},{96,64},{128,96},{160,128},{192,160},{224,1... | collective-permute-start | bytes 516104 | tf_op jit(solution)/shard_map/ppermute | solution.py:37
  41.8 14.6 %collective-permute-start.5 = (bf16[2,84,512]{2,1,0:T(8,128)(2,1)S(1)}, bf16[2,84,512]{2,1,0:T(8,128)(2,1)S(1)}, u32[]{:S(2)}, u32[]{:S(2)}) collective-permute-start(bf16[2,84,512]{2,1,0:T(8,128)(2,1)S(1)} %collective-permute-done.4), channel_id=1, source_target_pairs={{0,32},{32,64},{64,96},{96,128},{128,160},{160,192},{192,224},{224... | collective-permute-start | bytes 516104 | tf_op jit(solution)/shard_map/ppermute | solution.py:36
  45.3 76.0 %collective-permute-start.18 = (bf16[4,2,84,512]{3,0,2,1:T(4,128)(2,1)}, bf16[4,2,84,512]{3,0,2,1:T(4,128)(2,1)}, u32[]{:S(2)}, u32[]{:S(2)}) collective-permute-start(bf16[4,2,84,512]{3,0,2,1:T(4,128)(2,1)} %copy.99), channel_id=1, source_target_pairs={{0,224},{32,0},{64,32},{96,64},{128,96},{160,128},{192,160},{224,1... | collective-permute-start | bytes 2064392 | tf_op jit(solution)/shard_map/ppermute | solution.py:72
  49.9 72.9 %collective-permute-start.17 = (bf16[4,2,84,512]{3,0,2,1:T(4,128)(2,1)}, bf16[4,2,84,512]{3,0,2,1:T(4,128)(2,1)}, u32[]{:S(2)}, u32[]{:S(2)}) collective-permute-start(bf16[4,2,84,512]{3,0,2,1:T(4,128)(2,1)} %copy.99), channel_id=1, source_target_pairs={{0,32},{32,64},{64,96},{96,128},{128,160},{160,192},{192,224},{224... | collective-permute-start | bytes 2064392 | tf_op jit(solution)/shard_map/ppermute | solution.py:71
  51.8 19.1 %collective-permute-start.3 = (bf16[2,84,512]{2,1,0:T(8,128)(2,1)S(1)}, bf16[2,84,512]{2,1,0:T(8,128)(2,1)S(1)}, u32[]{:S(2)}, u32[]{:S(2)}) collective-permute-start(bf16[2,84,512]{2,1,0:T(8,128)(2,1)S(1)} %collective-permute-done.2), channel_id=1, source_target_pairs={{0,224},{32,0},{64,32},{96,64},{128,96},{160,128},{192,160},{224,1... | collective-permute-start | bytes 516104 | tf_op jit(solution)/shard_map/ppermute | solution.py:37
  79.3 25.2 %collective-permute-start.9 = (bf16[8,2,84,512]{3,0,2,1:T(8,128)(2,1)}, bf16[8,2,84,512]{3,0,2,1:T(8,128)(2,1)}, u32[]{:S(2)}, u32[]{:S(2)}) collective-permute-start(bf16[8,2,84,512]{3,0,2,1:T(8,128)(2,1)} %copy.90), channel_id=1, source_target_pairs={{0,8},{8,16},{16,24},{24,0},{1,9},{9,17},{17,25},{25,1},{2,10},{10... | collective-permute-start | bytes 4128776 | tf_op jit(solution)/shard_map/ppermute | solution.py:71
  83.8 25.8 %collective-permute-start.10 = (bf16[8,2,84,512]{3,0,2,1:T(8,128)(2,1)}, bf16[8,2,84,512]{3,0,2,1:T(8,128)(2,1)}, u32[]{:S(2)}, u32[]{:S(2)}) collective-permute-start(bf16[8,2,84,512]{3,0,2,1:T(8,128)(2,1)} %copy.90), channel_id=1, source_target_pairs={{0,24},{8,0},{16,8},{24,16},{1,25},{9,1},{17,9},{25,17},{2,26},{10... | collective-permute-start | bytes 4128776 | tf_op jit(solution)/shard_map/ppermute | solution.py:72
  114.1 17.7 %collective-permute-start.11 = (bf16[4,2,84,512]{3,0,2,1:T(4,128)(2,1)S(1)}, bf16[4,2,84,512]{3,0,2,1:T(4,128)(2,1)S(1)}, u32[]{:S(2)}, u32[]{:S(2)}) collective-permute-start(bf16[4,2,84,512]{3,0,2,1:T(4,128)(2,1)S(1)} %slice.106), channel_id=1, source_target_pairs={{0,8},{8,16},{16,24},{24,0},{1,9},{9,17},{17,25},{25,1},{2,10},{10... | collective-permute-start | bytes 2064392 | tf_op jit(solution)/shard_map/ppermute | solution.py:78
  125.6 23.8 %collective-permute-start.19 = (bf16[4,2,84,512]{3,0,2,1:T(4,128)(2,1)}, bf16[4,2,84,512]{3,0,2,1:T(4,128)(2,1)}, u32[]{:S(2)}, u32[]{:S(2)}) collective-permute-start(bf16[4,2,84,512]{3,0,2,1:T(4,128)(2,1)} %collective-permute-done.17), channel_id=1, source_target_pairs={{0,32},{32,64},{64,96},{96,128},{128,160},{160,192},{192,224},{224... | collective-permute-start | bytes 2064392 | tf_op jit(solution)/shard_map/ppermute | solution.py:71
  129.4 21.5 %collective-permute-start.20 = (bf16[4,2,84,512]{3,0,2,1:T(4,128)(2,1)}, bf16[4,2,84,512]{3,0,2,1:T(4,128)(2,1)}, u32[]{:S(2)}, u32[]{:S(2)}) collective-permute-start(bf16[4,2,84,512]{3,0,2,1:T(4,128)(2,1)} %collective-permute-done.18), channel_id=1, source_target_pairs={{0,224},{32,0},{64,32},{96,64},{128,96},{160,128},{192,160},{224,1... | collective-permute-start | bytes 2064392 | tf_op jit(solution)/shard_map/ppermute | solution.py:72
  145.4 27.0 %collective-permute-start.25 = (bf16[2,256,256]{2,1,0:T(8,128)(2,1)}, bf16[2,256,256]{2,1,0:T(8,128)(2,1)}, u32[]{:S(2)}, u32[]{:S(2)}) collective-permute-start(bf16[2,256,256]{2,1,0:T(8,128)(2,1)} %pad_maximum_fusion.2), channel_id=1, source_target_pairs={{0,32},{8,40},{16,48},{24,56},{32,64},{40,72},{48,80},{56,88},{64,... | collective-permute-start | bytes 786440 | tf_op jit(solution)/shard_map/ppermute | solution.py:22
  153.3 36.5 %collective-permute-start.21 = (bf16[4,2,84,512]{3,0,2,1:T(4,128)(2,1)}, bf16[4,2,84,512]{3,0,2,1:T(4,128)(2,1)}, u32[]{:S(2)}, u32[]{:S(2)}) collective-permute-start(bf16[4,2,84,512]{3,0,2,1:T(4,128)(2,1)} %collective-permute-done.19), channel_id=1, source_target_pairs={{0,32},{32,64},{64,96},{96,128},{128,160},{160,192},{192,224},{224... | collective-permute-start | bytes 2064392 | tf_op jit(solution)/shard_map/ppermute | solution.py:71
  159.1 24.0 %collective-permute-start.26 = (bf16[2,256,256]{2,1,0:T(8,128)(2,1)}, bf16[2,256,256]{2,1,0:T(8,128)(2,1)}, u32[]{:S(2)}, u32[]{:S(2)}) collective-permute-start(bf16[2,256,256]{2,1,0:T(8,128)(2,1)} %pad_maximum_fusion.2), channel_id=1, source_target_pairs={{0,24},{8,32},{16,40},{24,48},{32,56},{40,64},{48,72},{56,80},{64,... | collective-permute-start | bytes 786440 | tf_op jit(solution)/shard_map/ppermute | solution.py:22
  161.1 27.7 %collective-permute-start.27 = (bf16[2,256,256]{2,1,0:T(8,128)(2,1)}, bf16[2,256,256]{2,1,0:T(8,128)(2,1)}, u32[]{:S(2)}, u32[]{:S(2)}) collective-permute-start(bf16[2,256,256]{2,1,0:T(8,128)(2,1)} %pad_maximum_fusion.2), channel_id=1, source_target_pairs={{0,16},{8,24},{16,32},{24,40},{32,48},{40,56},{48,64},{56,72},{64,... | collective-permute-start | bytes 786440 | tf_op jit(solution)/shard_map/ppermute | solution.py:22
  165.9 25.4 %collective-permute-start.22 = (bf16[4,2,84,512]{3,0,2,1:T(4,128)(2,1)}, bf16[4,2,84,512]{3,0,2,1:T(4,128)(2,1)}, u32[]{:S(2)}, u32[]{:S(2)}) collective-permute-start(bf16[4,2,84,512]{3,0,2,1:T(4,128)(2,1)} %collective-permute-done.20), channel_id=1, source_target_pairs={{0,224},{32,0},{64,32},{96,64},{128,96},{160,128},{192,160},{224,1... | collective-permute-start | bytes 2064392 | tf_op jit(solution)/shard_map/ppermute | solution.py:72
  172.4 25.2 %collective-permute-start.28 = (bf16[2,256,256]{2,1,0:T(8,128)(2,1)}, bf16[2,256,256]{2,1,0:T(8,128)(2,1)S(1)}, u32[]{:S(2)}, u32[]{:S(2)}) collective-permute-start(bf16[2,256,256]{2,1,0:T(8,128)(2,1)} %pad_maximum_fusion.2), channel_id=1, source_target_pairs={{0,8},{8,16},{16,24},{24,32},{32,40},{40,48},{48,56},{56,64},{64,7... | collective-permute-start | bytes 786440 | tf_op jit(solution)/shard_map/ppermute | solution.py:22
  304.1 26.8 %collective-permute-start.30 = (bf16[256,672]{0,1:T(8,128)(2,1)S(1)}, bf16[256,672]{0,1:T(8,128)(2,1)S(1)}, u32[]{:S(2)}, u32[]{:S(2)}) collective-permute-start(bf16[256,672]{0,1:T(8,128)(2,1)S(1)} %get-tuple-element.37), channel_id=1, source_target_pairs={{0,2},{2,4},{4,6},{1,3},{3,5},{5,7},{8,10},{10,12},{12,14},{9,11},... | collective-permute-start | bytes 1032200 | tf_op jit(solution)/shard_map/ppermute | solution.py:100
  314.9 18.8 %collective-permute-start.31 = (bf16[256,672]{0,1:T(8,128)(2,1)}, bf16[256,672]{0,1:T(8,128)(2,1)}, u32[]{:S(2)}, u32[]{:S(2)}) collective-permute-start(bf16[256,672]{0,1:T(8,128)(2,1)} %get-tuple-element.42), channel_id=1, source_target_pairs={{2,0},{4,2},{6,4},{3,1},{5,3},{7,5},{10,8},{12,10},{14,12},{11,9},... | collective-permute-start | bytes 1032200 | tf_op jit(solution)/shard_map/ppermute | solution.py:100
  316.2 17.5 %collective-permute-start.32 = (bf16[256,672]{0,1:T(8,128)(2,1)}, bf16[256,672]{0,1:T(8,128)(2,1)}, u32[]{:S(2)}, u32[]{:S(2)}) collective-permute-start(bf16[256,672]{0,1:T(8,128)(2,1)} %get-tuple-element.41), channel_id=1, source_target_pairs={{0,4},{2,6},{1,5},{3,7},{8,12},{10,14},{9,13},{11,15},{16,20},{18,... | collective-permute-start | bytes 1032200 | tf_op jit(solution)/shard_map/ppermute | solution.py:100
  322.8 28.0 %collective-permute-start.33 = (bf16[256,672]{0,1:T(8,128)(2,1)}, bf16[256,672]{0,1:T(8,128)(2,1)}, u32[]{:S(2)}, u32[]{:S(2)}) collective-permute-start(bf16[256,672]{0,1:T(8,128)(2,1)} %get-tuple-element.40), channel_id=1, source_target_pairs={{4,0},{6,2},{5,1},{7,3},{12,8},{14,10},{13,9},{15,11},{20,16},{22,... | collective-permute-start | bytes 1032200 | tf_op jit(solution)/shard_map/ppermute | solution.py:100
  324.1 26.7 %collective-permute-start.34 = (bf16[256,672]{0,1:T(8,128)(2,1)S(1)}, bf16[256,672]{0,1:T(8,128)(2,1)}, u32[]{:S(2)}, u32[]{:S(2)}) collective-permute-start(bf16[256,672]{0,1:T(8,128)(2,1)S(1)} %get-tuple-element.39), channel_id=1, source_target_pairs={{0,6},{1,7},{8,14},{9,15},{16,22},{17,23},{24,30},{25,31},{32,38},... | collective-permute-start | bytes 1032200 | tf_op jit(solution)/shard_map/ppermute | solution.py:100
  331.6 19.2 %collective-permute-start.35 = (bf16[256,672]{0,1:T(8,128)(2,1)S(1)}, bf16[256,672]{0,1:T(8,128)(2,1)}, u32[]{:S(2)}, u32[]{:S(2)}) collective-permute-start(bf16[256,672]{0,1:T(8,128)(2,1)S(1)} %get-tuple-element.38), channel_id=1, source_target_pairs={{6,0},{7,1},{14,8},{15,9},{22,16},{23,17},{30,24},{31,25},{38,32},... | collective-permute-start | bytes 1032200 | tf_op jit(solution)/shard_map/ppermute | solution.py:100
  (34 other events, 315.1 us)
Sparse Core Ops, SparseCore 0:
  9.4 42.8 all-gather.3
  86.1 186.0 all-gather.5

commit v7 on v5

--- a/solution.py
+++ b/solution.py
@@ -49,6 +49,13 @@
     parts = ring(block, axis, n, split_axis)
     whole = [jnp.concatenate(p, axis=split_axis) if isinstance(p, tuple) else p for p in parts]
     return jnp.stack(whole, axis=0)
+
+
+def stacked_direct(block, axis, n):
+    parts = [block] + [
+        lax.ppermute(block, axis, [(j, (j - d) % n) for j in range(n)]) for d in range(1, n)
+    ]
+    return jnp.stack(parts, axis=0)
 
 
 def ring_pieces(block, axis, n, split_axis, fold=None, acc=None):
@@ -175,7 +182,7 @@
     split = q_cols + k_cols
     half_a = by_zh[:, :, :split]
     half_b = by_zh[:, :, split:]
-    a_x = stacked_ring(half_a, "x", nx, 0)
+    a_x = stacked_direct(half_a, "x", nx)
     b_y = stacked_ring(half_b, "y", ny, 0)
     _, qk = ring_pieces(a_x, "y", ny, 0, fold_qk, None)
     b_pieces, projected_values = ring_pieces(b_y, "x", nx, 0, fold_v, None)

time: 357 us -> 354 us (level)
  starting transfers between devices: 157 us -> 145 us
  waiting for transfers between devices: 62.6 us -> 73.6 us
    ppermute x4 -> x3, waiting for transfers between devices: 0.73 us -> 15 us  [ring(): right = lax.ppermute(right, axis, bwd)]
    ppermute x0 -> x3, starting transfers between devices: none -> 8.91 us  [stacked_direct(): lax.ppermute(block, axis, [(j, (j - d) % n) for j in range(n)])]
    ppermute x2 -> x1, waiting for transfers between devices: 9.88 us -> 1.03 us  [ring(): lax.ppermute(lax.slice_in_dim(right, k, None, axis=split_axis), axis, bwd)]
    ppermute x1, starting transfers between devices: 24 us -> 17 us  [reduce_scatter_tp(): got = lax.ppermute(give, 'c', [(0, 1), (1, 0)])]
    ppermute x2 -> x1, starting transfers between devices: 6.49 us -> 1.92 us  [ring(): top = lax.ppermute(lax.slice_in_dim(left, 0, k, axis=split_axis), axis, fwd)]
    ppermute x4, waiting for transfers between devices: 9.13 us -> 13.5 us  [from_behind(): return lax.ppermute(block, axis, route)]
    ppermute x4 -> x3, starting transfers between devices: 9.8 us -> 5.76 us  [ring(): left = lax.ppermute(left, axis, fwd)]
    ppermute x4 -> x3, starting transfers between devices: 17.2 us -> 14.2 us  [ring(): right = lax.ppermute(right, axis, bwd)]
  transfers between devices with their start and end apart: 37 -> 36, of which waited for: 10 -> 10; matrix products, arithmetic and copies ran while one was open for 21% -> 21% of each run, Pallas kernels for 0% -> 0%
where the time goes in v7:
time: 354 us; the launch traced here: 352 us
  starting transfers between devices  145 us (41%)
  waiting for transfers between devices  73.6 us (21%)
  local copies, waits for them, and re-layouts  48.6 us (14%)
  matrix products  29 us (8%)
  other arithmetic  26.8 us (8%)
  between operations  14.7 us (4%)
  blocking collectives  14 us (4%)
    ppermute x6, starting transfers between devices, reduce_scatter_tp(): lax.ppermute(block.astype(jnp.bfloat16), 'zl', route).astype(jnp.float32)  37.8 us
    dot_general x14, matrix products, contract(): lax.dot_general(lhs, piece, (((1, 2, 3), (0, 1, 2)), ((), ())), preferred...  21.2 us
    ppermute x1, starting transfers between devices, reduce_scatter_tp(): got = lax.ppermute(give, 'c', [(0, 1), (1, 0)])  17 us
    ppermute x6, waiting for transfers between devices, reduce_scatter_tp(): lax.ppermute(block.astype(jnp.bfloat16), 'zl', route).astype(jnp.float32)  16 us
    ppermute x4, starting transfers between devices, ring_pieces(): right = lax.ppermute(right, axis, bwd)  15.9 us
    ppermute x3, waiting for transfers between devices, ring(): right = lax.ppermute(right, axis, bwd)  15 us
    ppermute x3, starting transfers between devices, ring(): right = lax.ppermute(right, axis, bwd)  14.2 us
    psum x1, blocking collectives, local(): squares = lax.psum(jnp.sum(summed_cols * summed_cols, axis=1), TP)  14 us
  transfers between devices with their start and end apart: 36, of which 10 were waited for; matrix products, arithmetic and copies ran while one was open for 21% of the time, Pallas kernels for 0%

profile of v7, /device:TPU:263, one launch (start us, length us, event | category | flops | bytes accessed | tf_op | source)
XLA Modules:
  0.0 351.6 jit_solution(8499497694895967462)
XLA Ops:
  10.2 11.4 %collective-permute-done = bf16[84,1536]{1,0:T(8,128)(2,1)S(1)} collective-permute-done((bf16[84,1536]{1,0:T(8,128)(2,1)S(1)}, bf16[84,1536]{1,0:T(8,128)(2,1)S(1)}, u32[]{:S(2)}, u32[]{:S(2)}) %collective-permute-start) | collective-permute-done | bytes 258080 | tf_op jit(solution)/shard_map/ppermute | solution.py:31
  21.6 5.1 %collective-permute-start.1 = (bf16[2,84,768]{2,1,0:T(8,128)(2,1)S(1)}, bf16[2,84,768]{2,1,0:T(8,128)(2,1)}, u32[]{:S(2)}, u32[]{:S(2)}) collective-permute-start(bf16[2,84,768]{2,1,0:T(8,128)(2,1)S(1)} %get-tuple-element.97), channel_id=1, source_target_pairs={{0,224},{32,0},{64,32},{96,64},{128,96},{160,128},{192,160},{224,1... | collective-permute-start | bytes 774152 | tf_op jit(solution)/shard_map/ppermute | solution.py:37
  38.4 4.6 %collective-permute-start.2 = (bf16[2,84,768]{2,1,0:T(8,128)(2,1)}, bf16[2,84,768]{2,1,0:T(8,128)(2,1)S(1)}, u32[]{:S(2)}, u32[]{:S(2)}) collective-permute-start(bf16[2,84,768]{2,1,0:T(8,128)(2,1)} %collective-permute-done.1), channel_id=1, source_target_pairs={{0,224},{32,0},{64,32},{96,64},{128,96},{160,128},{192,160},{224,1... | collective-permute-start | bytes 774152 | tf_op jit(solution)/shard_map/ppermute | solution.py:37
  47.7 4.6 %collective-permute-start.17 = (bf16[4,2,84,768]{3,0,2,1:T(4,128)(2,1)}, bf16[4,2,84,768]{3,0,2,1:T(4,128)(2,1)}, u32[]{:S(2)}, u32[]{:S(2)}) collective-permute-start(bf16[4,2,84,768]{3,0,2,1:T(4,128)(2,1)} %copy.137), channel_id=1, source_target_pairs={{0,224},{32,0},{64,32},{96,64},{128,96},{160,128},{192,160},{224,1... | collective-permute-start | bytes 3096584 | tf_op jit(solution)/shard_map/ppermute | solution.py:79
  54.2 4.6 %collective-permute-start.3 = (bf16[2,84,768]{2,1,0:T(8,128)(2,1)S(1)}, bf16[2,84,768]{2,1,0:T(8,128)(2,1)S(1)}, u32[]{:S(2)}, u32[]{:S(2)}) collective-permute-start(bf16[2,84,768]{2,1,0:T(8,128)(2,1)S(1)} %collective-permute-done.2), channel_id=1, source_target_pairs={{0,224},{32,0},{64,32},{96,64},{128,96},{160,128},{192,160},{224,1... | collective-permute-start | bytes 774152 | tf_op jit(solution)/shard_map/ppermute | solution.py:37
  61.7 15.0 %collective-permute-done.3 = bf16[2,84,768]{2,1,0:T(8,128)(2,1)S(1)} collective-permute-done((bf16[2,84,768]{2,1,0:T(8,128)(2,1)S(1)}, bf16[2,84,768]{2,1,0:T(8,128)(2,1)S(1)}, u32[]{:S(2)}, u32[]{:S(2)}) %collective-permute-start.3) | collective-permute-done | bytes 258080 | tf_op jit(solution)/shard_map/ppermute | solution.py:37
  76.8 5.4 %collective-permute-start.8 = (bf16[1,84,768]{2,1,0:T(8,128)(2,1)S(1)}, bf16[1,84,768]{2,1,0:T(8,128)(2,1)S(1)}, u32[]{:S(2)}, u32[]{:S(2)}) collective-permute-start(bf16[1,84,768]{2,1,0:T(8,128)(2,1)S(1)} %slice.331), channel_id=1, source_target_pairs={{0,224},{32,0},{64,32},{96,64},{128,96},{160,128},{192,160},{224,1... | collective-permute-start | bytes 387080 | tf_op jit(solution)/shard_map/ppermute | solution.py:43
  85.2 5.0 %collective-permute-done.7 = bf16[1,84,768]{2,1,0:T(8,128)(2,1)S(1)} collective-permute-done((bf16[1,84,768]{2,1,0:T(8,128)(2,1)S(1)}, bf16[1,84,768]{2,1,0:T(8,128)(2,1)S(1)}, u32[]{:S(2)}, u32[]{:S(2)}) %collective-permute-start.7) | collective-permute-done | bytes 129056 | tf_op jit(solution)/shard_map/ppermute | solution.py:42
  95.3 4.5 %collective-permute-start.9 = (bf16[8,2,84,768]{3,0,2,1:T(8,128)(2,1)}, bf16[8,2,84,768]{3,0,2,1:T(8,128)(2,1)}, u32[]{:S(2)}, u32[]{:S(2)}) collective-permute-start(bf16[8,2,84,768]{3,0,2,1:T(8,128)(2,1)} %copy.128), channel_id=1, source_target_pairs={{0,8},{8,16},{16,24},{24,0},{1,9},{9,17},{17,25},{25,1},{2,10},{10... | collective-permute-start | bytes 6193160 | tf_op jit(solution)/shard_map/ppermute | solution.py:78
  120.9 4.8 %collective-permute-start.19 = (bf16[4,2,84,768]{3,0,2,1:T(4,128)(2,1)}, bf16[4,2,84,768]{3,0,2,1:T(4,128)(2,1)}, u32[]{:S(2)}, u32[]{:S(2)}) collective-permute-start(bf16[4,2,84,768]{3,0,2,1:T(4,128)(2,1)} %collective-permute-done.17), channel_id=1, source_target_pairs={{0,224},{32,0},{64,32},{96,64},{128,96},{160,128},{192,160},{224,1... | collective-permute-start | bytes 3096584 | tf_op jit(solution)/shard_map/ppermute | solution.py:79
  127.2 7.3 %collective-permute-done.10 = bf16[8,2,84,768]{3,0,2,1:T(8,128)(2,1)} collective-permute-done((bf16[8,2,84,768]{3,0,2,1:T(8,128)(2,1)}, bf16[8,2,84,768]{3,0,2,1:T(8,128)(2,1)}, u32[]{:S(2)}, u32[]{:S(2)}) %collective-permute-start.10) | collective-permute-done | bytes 2064416 | tf_op jit(solution)/shard_map/ppermute | solution.py:79
  144.2 4.6 %collective-permute-start.21 = (bf16[4,2,84,768]{3,0,2,1:T(4,128)(2,1)}, bf16[4,2,84,768]{3,0,2,1:T(4,128)(2,1)}, u32[]{:S(2)}, u32[]{:S(2)}) collective-permute-start(bf16[4,2,84,768]{3,0,2,1:T(4,128)(2,1)} %collective-permute-done.19), channel_id=1, source_target_pairs={{0,224},{32,0},{64,32},{96,64},{128,96},{160,128},{192,160},{224,1... | collective-permute-start | bytes 3096584 | tf_op jit(solution)/shard_map/ppermute | solution.py:79
  159.5 4.4 %collective-permute-start.11 = (bf16[4,2,84,768]{3,0,2,1:T(4,128)(2,1)}, bf16[4,2,84,768]{3,0,2,1:T(4,128)(2,1)}, u32[]{:S(2)}, u32[]{:S(2)}) collective-permute-start(bf16[4,2,84,768]{3,0,2,1:T(4,128)(2,1)} %slice.296), channel_id=1, source_target_pairs={{0,8},{8,16},{16,24},{24,0},{1,9},{9,17},{17,25},{25,1},{2,10},{10... | collective-permute-start | bytes 3096584 | tf_op jit(solution)/shard_map/ppermute | solution.py:85
  186.2 4.6 %collective-permute-start.23 = (bf16[2,2,84,768]{3,1,2,0:T(2,128)(2,1)}, bf16[2,2,84,768]{3,1,2,0:T(2,128)(2,1)}, u32[]{:S(2)}, u32[]{:S(2)}) collective-permute-start(bf16[2,2,84,768]{3,1,2,0:T(2,128)(2,1)} %copy.147), channel_id=1, source_target_pairs={{0,224},{32,0},{64,32},{96,64},{128,96},{160,128},{192,160},{224,1... | collective-permute-start | bytes 1548296 | tf_op jit(solution)/shard_map/ppermute | solution.py:86
  205.2 4.0 %collective-permute-start.25 = (bf16[2,256,256]{2,1,0:T(8,128)(2,1)S(1)}, bf16[2,256,256]{2,1,0:T(8,128)(2,1)}, u32[]{:S(2)}, u32[]{:S(2)}) collective-permute-start(bf16[2,256,256]{2,1,0:T(8,128)(2,1)S(1)} %pad_maximum_fusion.4), channel_id=1, source_target_pairs={{0,24},{8,32},{16,40},{24,48},{32,56},{40,64},{48,72},{56,80},{64,... | collective-permute-start | bytes 786440 | tf_op jit(solution)/shard_map/ppermute | solution.py:22
  209.2 4.8 %collective-permute-start.24 = (bf16[2,256,256]{2,1,0:T(8,128)(2,1)S(1)}, bf16[2,256,256]{2,1,0:T(8,128)(2,1)}, u32[]{:S(2)}, u32[]{:S(2)}) collective-permute-start(bf16[2,256,256]{2,1,0:T(8,128)(2,1)S(1)} %pad_maximum_fusion.4), channel_id=1, source_target_pairs={{0,32},{8,40},{16,48},{24,56},{32,64},{40,72},{48,80},{56,88},{64,... | collective-permute-start | bytes 786440 | tf_op jit(solution)/shard_map/ppermute | solution.py:22
  216.3 13.5 %collective-permute-done.24 = bf16[2,256,256]{2,1,0:T(8,128)(2,1)} collective-permute-done((bf16[2,256,256]{2,1,0:T(8,128)(2,1)S(1)}, bf16[2,256,256]{2,1,0:T(8,128)(2,1)}, u32[]{:S(2)}, u32[]{:S(2)}) %collective-permute-start.24) | collective-permute-done | bytes 262176 | tf_op jit(solution)/shard_map/ppermute | solution.py:22
  248.6 17.0 %collective-permute-start.28 = (bf16[256,4,672]{0,2,1:T(8,128)(2,1)S(1)}, bf16[256,4,672]{0,2,1:T(8,128)(2,1)}, u32[]{:S(2)}, u32[]{:S(2)}) collective-permute-start(bf16[256,4,672]{0,2,1:T(8,128)(2,1)S(1)} %dynamic-slice_bitcast_fusion), channel_id=1, source_target_pairs={{0,1},{1,0},{2,3},{3,2},{4,5},{5,4},{6,7},{7,6},{8,9},{9,8},{10,11... | collective-permute-start | bytes 4128776 | tf_op jit(solution)/shard_map/ppermute | solution.py:99
  271.6 20.3 %collective-permute-start.29 = (bf16[256,672]{0,1:T(8,128)(2,1)S(1)}, bf16[256,672]{0,1:T(8,128)(2,1)S(1)}, u32[]{:S(2)}, u32[]{:S(2)}) collective-permute-start(bf16[256,672]{0,1:T(8,128)(2,1)S(1)} %get-tuple-element.98), channel_id=1, source_target_pairs={{0,2},{2,4},{4,6},{1,3},{3,5},{5,7},{8,10},{10,12},{12,14},{9,11},... | collective-permute-start | bytes 1032200 | tf_op jit(solution)/shard_map/ppermute | solution.py:107
  293.2 7.2 %collective-permute-start.33 = (bf16[256,672]{0,1:T(8,128)(2,1)}, bf16[256,672]{0,1:T(8,128)(2,1)}, u32[]{:S(2)}, u32[]{:S(2)}) collective-permute-start(bf16[256,672]{0,1:T(8,128)(2,1)} %get-tuple-element.100), channel_id=1, source_target_pairs={{0,6},{1,7},{8,14},{9,15},{16,22},{17,23},{24,30},{25,31},{32,38},... | collective-permute-start | bytes 1032200 | tf_op jit(solution)/shard_map/ppermute | solution.py:107
  301.8 6.3 %collective-permute-start.31 = (bf16[256,672]{0,1:T(8,128)(2,1)S(1)}, bf16[256,672]{0,1:T(8,128)(2,1)}, u32[]{:S(2)}, u32[]{:S(2)}) collective-permute-start(bf16[256,672]{0,1:T(8,128)(2,1)S(1)} %get-tuple-element.102), channel_id=1, source_target_pairs={{0,4},{2,6},{1,5},{3,7},{8,12},{10,14},{9,13},{11,15},{16,20},{18,... | collective-permute-start | bytes 1032200 | tf_op jit(solution)/shard_map/ppermute | solution.py:107
  310.9 9.8 %collective-permute-done.32 = bf16[256,672]{0,1:T(8,128)(2,1)} collective-permute-done((bf16[256,672]{0,1:T(8,128)(2,1)}, bf16[256,672]{0,1:T(8,128)(2,1)}, u32[]{:S(2)}, u32[]{:S(2)}) %collective-permute-start.32) | collective-permute-done | bytes 344096 | tf_op jit(solution)/shard_map/ppermute | solution.py:107
  320.7 6.2 %collective-permute-done.30 = bf16[256,672]{0,1:T(8,128)(2,1)} collective-permute-done((bf16[256,672]{0,1:T(8,128)(2,1)S(1)}, bf16[256,672]{0,1:T(8,128)(2,1)}, u32[]{:S(2)}, u32[]{:S(2)}) %collective-permute-start.30) | collective-permute-done | bytes 344096 | tf_op jit(solution)/shard_map/ppermute | solution.py:107
  328.8 14.0 %psum.7 = f32[256]{0:T(256)S(1)} all-reduce(f32[256]{0:T(256)S(1)} %get-tuple-element.92), channel_id=1, replica_groups=mesh['zh'=2,'y'=8,'x'=4,'zl'=4,'c'=2] {'zl','c'}, use_global_device_ids=true, to_apply=%region_7.11 | all-reduce | flops 256 | bytes 2048 | tf_op jit(solution)/shard_map/psum | solution.py:258
  (207 shorter events, 147.7 us)
Async XLA Ops:
  6.5 93.4 %all-gather.2.cloned.1.call-start = ((), (), s32[]{:S(2)}) async-start(), calls=%async_computation | async-start | bytes 3096576 | tf_op jit(solution)/shard_map/all_gather | solution.py:155
  47.7 65.3 %collective-permute-start.17 = (bf16[4,2,84,768]{3,0,2,1:T(4,128)(2,1)}, bf16[4,2,84,768]{3,0,2,1:T(4,128)(2,1)}, u32[]{:S(2)}, u32[]{:S(2)}) collective-permute-start(bf16[4,2,84,768]{3,0,2,1:T(4,128)(2,1)} %copy.137), channel_id=1, source_target_pairs={{0,224},{32,0},{64,32},{96,64},{128,96},{160,128},{192,160},{224,1... | collective-permute-start | bytes 3096584 | tf_op jit(solution)/shard_map/ppermute | solution.py:79
  52.3 62.5 %collective-permute-start.16 = (bf16[4,2,84,768]{3,0,2,1:T(4,128)(2,1)}, bf16[4,2,84,768]{3,0,2,1:T(4,128)(2,1)}, u32[]{:S(2)}, u32[]{:S(2)}) collective-permute-start(bf16[4,2,84,768]{3,0,2,1:T(4,128)(2,1)} %copy.137), channel_id=1, source_target_pairs={{0,32},{32,64},{64,96},{96,128},{128,160},{160,192},{192,224},{224... | collective-permute-start | bytes 3096584 | tf_op jit(solution)/shard_map/ppermute | solution.py:78
  54.2 22.5 %collective-permute-start.3 = (bf16[2,84,768]{2,1,0:T(8,128)(2,1)S(1)}, bf16[2,84,768]{2,1,0:T(8,128)(2,1)S(1)}, u32[]{:S(2)}, u32[]{:S(2)}) collective-permute-start(bf16[2,84,768]{2,1,0:T(8,128)(2,1)S(1)} %collective-permute-done.2), channel_id=1, source_target_pairs={{0,224},{32,0},{64,32},{96,64},{128,96},{160,128},{192,160},{224,1... | collective-permute-start | bytes 774152 | tf_op jit(solution)/shard_map/ppermute | solution.py:37
  58.8 23.4 %collective-permute-start.6 = (bf16[2,84,768]{2,1,0:T(8,128)(2,1)S(1)}, bf16[2,84,768]{2,1,0:T(8,128)(2,1)S(1)}, u32[]{:S(2)}, u32[]{:S(2)}) collective-permute-start(bf16[2,84,768]{2,1,0:T(8,128)(2,1)S(1)} %collective-permute-done.5), channel_id=1, source_target_pairs={{0,32},{32,64},{64,96},{96,128},{128,160},{160,192},{192,224},{224... | collective-permute-start | bytes 774152 | tf_op jit(solution)/shard_map/ppermute | solution.py:36
  93.4 41.1 %collective-permute-start.10 = (bf16[8,2,84,768]{3,0,2,1:T(8,128)(2,1)}, bf16[8,2,84,768]{3,0,2,1:T(8,128)(2,1)}, u32[]{:S(2)}, u32[]{:S(2)}) collective-permute-start(bf16[8,2,84,768]{3,0,2,1:T(8,128)(2,1)} %copy.128), channel_id=1, source_target_pairs={{0,24},{8,0},{16,8},{24,16},{1,25},{9,1},{17,9},{25,17},{2,26},{10... | collective-permute-start | bytes 6193160 | tf_op jit(solution)/shard_map/ppermute | solution.py:79
  95.3 40.3 %collective-permute-start.9 = (bf16[8,2,84,768]{3,0,2,1:T(8,128)(2,1)}, bf16[8,2,84,768]{3,0,2,1:T(8,128)(2,1)}, u32[]{:S(2)}, u32[]{:S(2)}) collective-permute-start(bf16[8,2,84,768]{3,0,2,1:T(8,128)(2,1)} %copy.128), channel_id=1, source_target_pairs={{0,8},{8,16},{16,24},{24,0},{1,9},{9,17},{17,25},{25,1},{2,10},{10... | collective-permute-start | bytes 6193160 | tf_op jit(solution)/shard_map/ppermute | solution.py:78
  119.0 18.5 %collective-permute-start.18 = (bf16[4,2,84,768]{3,0,2,1:T(4,128)(2,1)}, bf16[4,2,84,768]{3,0,2,1:T(4,128)(2,1)}, u32[]{:S(2)}, u32[]{:S(2)}) collective-permute-start(bf16[4,2,84,768]{3,0,2,1:T(4,128)(2,1)} %collective-permute-done.16), channel_id=1, source_target_pairs={{0,32},{32,64},{64,96},{96,128},{128,160},{160,192},{192,224},{224... | collective-permute-start | bytes 3096584 | tf_op jit(solution)/shard_map/ppermute | solution.py:78
  120.9 18.3 %collective-permute-start.19 = (bf16[4,2,84,768]{3,0,2,1:T(4,128)(2,1)}, bf16[4,2,84,768]{3,0,2,1:T(4,128)(2,1)}, u32[]{:S(2)}, u32[]{:S(2)}) collective-permute-start(bf16[4,2,84,768]{3,0,2,1:T(4,128)(2,1)} %collective-permute-done.17), channel_id=1, source_target_pairs={{0,224},{32,0},{64,32},{96,64},{128,96},{160,128},{192,160},{224,1... | collective-permute-start | bytes 3096584 | tf_op jit(solution)/shard_map/ppermute | solution.py:79
  141.8 24.3 %collective-permute-start.20 = (bf16[4,2,84,768]{3,0,2,1:T(4,128)(2,1)}, bf16[4,2,84,768]{3,0,2,1:T(4,128)(2,1)}, u32[]{:S(2)}, u32[]{:S(2)}) collective-permute-start(bf16[4,2,84,768]{3,0,2,1:T(4,128)(2,1)} %collective-permute-done.18), channel_id=1, source_target_pairs={{0,32},{32,64},{64,96},{96,128},{128,160},{160,192},{192,224},{224... | collective-permute-start | bytes 3096584 | tf_op jit(solution)/shard_map/ppermute | solution.py:78
  144.2 23.7 %collective-permute-start.21 = (bf16[4,2,84,768]{3,0,2,1:T(4,128)(2,1)}, bf16[4,2,84,768]{3,0,2,1:T(4,128)(2,1)}, u32[]{:S(2)}, u32[]{:S(2)}) collective-permute-start(bf16[4,2,84,768]{3,0,2,1:T(4,128)(2,1)} %collective-permute-done.19), channel_id=1, source_target_pairs={{0,224},{32,0},{64,32},{96,64},{128,96},{160,128},{192,160},{224,1... | collective-permute-start | bytes 3096584 | tf_op jit(solution)/shard_map/ppermute | solution.py:79
  157.4 23.6 %collective-permute-start.12 = (bf16[4,2,84,768]{3,0,2,1:T(4,128)(2,1)}, bf16[4,2,84,768]{3,0,2,1:T(4,128)(2,1)}, u32[]{:S(2)}, u32[]{:S(2)}) collective-permute-start(bf16[4,2,84,768]{3,0,2,1:T(4,128)(2,1)} %slice.299), channel_id=1, source_target_pairs={{0,24},{8,0},{16,8},{24,16},{1,25},{9,1},{17,9},{25,17},{2,26},{10... | collective-permute-start | bytes 3096584 | tf_op jit(solution)/shard_map/ppermute | solution.py:86
  159.5 22.6 %collective-permute-start.11 = (bf16[4,2,84,768]{3,0,2,1:T(4,128)(2,1)}, bf16[4,2,84,768]{3,0,2,1:T(4,128)(2,1)}, u32[]{:S(2)}, u32[]{:S(2)}) collective-permute-start(bf16[4,2,84,768]{3,0,2,1:T(4,128)(2,1)} %slice.296), channel_id=1, source_target_pairs={{0,8},{8,16},{16,24},{24,0},{1,9},{9,17},{17,25},{25,1},{2,10},{10... | collective-permute-start | bytes 3096584 | tf_op jit(solution)/shard_map/ppermute | solution.py:85
  173.3 22.7 %collective-permute-start.22 = (bf16[2,2,84,768]{3,1,2,0:T(2,128)(2,1)}, bf16[2,2,84,768]{3,1,2,0:T(2,128)(2,1)}, u32[]{:S(2)}, u32[]{:S(2)}) collective-permute-start(bf16[2,2,84,768]{3,1,2,0:T(2,128)(2,1)} %copy.145), channel_id=1, source_target_pairs={{0,32},{32,64},{64,96},{96,128},{128,160},{160,192},{192,224},{224... | collective-permute-start | bytes 1548296 | tf_op jit(solution)/shard_map/ppermute | solution.py:85
  201.2 30.6 %collective-permute-start.27 = (bf16[2,256,256]{2,1,0:T(8,128)(2,1)S(1)}, bf16[2,256,256]{2,1,0:T(8,128)(2,1)S(1)}, u32[]{:S(2)}, u32[]{:S(2)}) collective-permute-start(bf16[2,256,256]{2,1,0:T(8,128)(2,1)S(1)} %pad_maximum_fusion.4), channel_id=1, source_target_pairs={{0,8},{8,16},{16,24},{24,32},{32,40},{40,48},{48,56},{56,64},{64,7... | collective-permute-start | bytes 786440 | tf_op jit(solution)/shard_map/ppermute | solution.py:22
  203.2 28.5 %collective-permute-start.26 = (bf16[2,256,256]{2,1,0:T(8,128)(2,1)S(1)}, bf16[2,256,256]{2,1,0:T(8,128)(2,1)S(1)}, u32[]{:S(2)}, u32[]{:S(2)}) collective-permute-start(bf16[2,256,256]{2,1,0:T(8,128)(2,1)S(1)} %pad_maximum_fusion.4), channel_id=1, source_target_pairs={{0,16},{8,24},{16,32},{24,40},{32,48},{40,56},{48,64},{56,72},{64,... | collective-permute-start | bytes 786440 | tf_op jit(solution)/shard_map/ppermute | solution.py:22
  205.2 25.6 %collective-permute-start.25 = (bf16[2,256,256]{2,1,0:T(8,128)(2,1)S(1)}, bf16[2,256,256]{2,1,0:T(8,128)(2,1)}, u32[]{:S(2)}, u32[]{:S(2)}) collective-permute-start(bf16[2,256,256]{2,1,0:T(8,128)(2,1)S(1)} %pad_maximum_fusion.4), channel_id=1, source_target_pairs={{0,24},{8,32},{16,40},{24,48},{32,56},{40,64},{48,72},{56,80},{64,... | collective-permute-start | bytes 786440 | tf_op jit(solution)/shard_map/ppermute | solution.py:22
  209.2 20.6 %collective-permute-start.24 = (bf16[2,256,256]{2,1,0:T(8,128)(2,1)S(1)}, bf16[2,256,256]{2,1,0:T(8,128)(2,1)}, u32[]{:S(2)}, u32[]{:S(2)}) collective-permute-start(bf16[2,256,256]{2,1,0:T(8,128)(2,1)S(1)} %pad_maximum_fusion.4), channel_id=1, source_target_pairs={{0,32},{8,40},{16,48},{24,56},{32,64},{40,72},{48,80},{56,88},{64,... | collective-permute-start | bytes 786440 | tf_op jit(solution)/shard_map/ppermute | solution.py:22
  248.6 19.9 %collective-permute-start.28 = (bf16[256,4,672]{0,2,1:T(8,128)(2,1)S(1)}, bf16[256,4,672]{0,2,1:T(8,128)(2,1)}, u32[]{:S(2)}, u32[]{:S(2)}) collective-permute-start(bf16[256,4,672]{0,2,1:T(8,128)(2,1)S(1)} %dynamic-slice_bitcast_fusion), channel_id=1, source_target_pairs={{0,1},{1,0},{2,3},{3,2},{4,5},{5,4},{6,7},{7,6},{8,9},{9,8},{10,11... | collective-permute-start | bytes 4128776 | tf_op jit(solution)/shard_map/ppermute | solution.py:99
  271.6 36.5 %collective-permute-start.29 = (bf16[256,672]{0,1:T(8,128)(2,1)S(1)}, bf16[256,672]{0,1:T(8,128)(2,1)S(1)}, u32[]{:S(2)}, u32[]{:S(2)}) collective-permute-start(bf16[256,672]{0,1:T(8,128)(2,1)S(1)} %get-tuple-element.98), channel_id=1, source_target_pairs={{0,2},{2,4},{4,6},{1,3},{3,5},{5,7},{8,10},{10,12},{12,14},{9,11},... | collective-permute-start | bytes 1032200 | tf_op jit(solution)/shard_map/ppermute | solution.py:107
  291.9 19.0 %collective-permute-start.34 = (bf16[256,672]{0,1:T(8,128)(2,1)}, bf16[256,672]{0,1:T(8,128)(2,1)}, u32[]{:S(2)}, u32[]{:S(2)}) collective-permute-start(bf16[256,672]{0,1:T(8,128)(2,1)} %get-tuple-element.99), channel_id=1, source_target_pairs={{6,0},{7,1},{14,8},{15,9},{22,16},{23,17},{30,24},{31,25},{38,32},... | collective-permute-start | bytes 1032200 | tf_op jit(solution)/shard_map/ppermute | solution.py:107
  300.5 20.2 %collective-permute-start.32 = (bf16[256,672]{0,1:T(8,128)(2,1)}, bf16[256,672]{0,1:T(8,128)(2,1)}, u32[]{:S(2)}, u32[]{:S(2)}) collective-permute-start(bf16[256,672]{0,1:T(8,128)(2,1)} %get-tuple-element.101), channel_id=1, source_target_pairs={{4,0},{6,2},{5,1},{7,3},{12,8},{14,10},{13,9},{15,11},{20,16},{22,... | collective-permute-start | bytes 1032200 | tf_op jit(solution)/shard_map/ppermute | solution.py:107
  301.8 19.0 %collective-permute-start.31 = (bf16[256,672]{0,1:T(8,128)(2,1)S(1)}, bf16[256,672]{0,1:T(8,128)(2,1)}, u32[]{:S(2)}, u32[]{:S(2)}) collective-permute-start(bf16[256,672]{0,1:T(8,128)(2,1)S(1)} %get-tuple-element.102), channel_id=1, source_target_pairs={{0,4},{2,6},{1,5},{3,7},{8,12},{10,14},{9,13},{11,15},{16,20},{18,... | collective-permute-start | bytes 1032200 | tf_op jit(solution)/shard_map/ppermute | solution.py:107
  308.9 18.1 %collective-permute-start.30 = (bf16[256,672]{0,1:T(8,128)(2,1)S(1)}, bf16[256,672]{0,1:T(8,128)(2,1)}, u32[]{:S(2)}, u32[]{:S(2)}) collective-permute-start(bf16[256,672]{0,1:T(8,128)(2,1)S(1)} %get-tuple-element.103), channel_id=1, source_target_pairs={{2,0},{4,2},{6,4},{3,1},{5,3},{7,5},{10,8},{12,10},{14,12},{11,9},... | collective-permute-start | bytes 1032200 | tf_op jit(solution)/shard_map/ppermute | solution.py:107
  (35 other events, 317.7 us)
Sparse Core Ops, SparseCore 0:
  9.4 45.3 all-gather.1

commit v8 on v7

--- a/solution.py
+++ b/solution.py
@@ -155,10 +155,13 @@
     gathered = lax.all_gather(residual, TP, axis=1, tiled=True)
     normalized_input = norm_scale(gathered.astype(jnp.float32), input_gain).astype(jnp.bfloat16)
     at_zh, at_y, at_x = (lax.axis_index(name) for name in SEQ)
-    normed_rel = normalized_input.reshape(tok_rows, nz, ny, nx, shard_rows).transpose(0, 2, 3, 1, 4)
-    normed_rel = jnp.roll(normed_rel, -at_y, axis=1)
-    normed_rel = jnp.roll(normed_rel, -at_x, axis=2)
-    normed_rel = jnp.roll(normed_rel, -at_zh, axis=3)
+    rel_y = (at_y + jnp.arange(ny)) % ny
+    rel_x = (at_x + jnp.arange(nx)) % nx
+    rel_z = (at_zh + jnp.arange(nz)) % nz
+    rel_shard = ((rel_z[None, None, :] * ny + rel_y[:, None, None]) * nx + rel_x[None, :, None]).reshape(-1)
+    normed_rel = jnp.take(
+        normalized_input.reshape(tok_rows, n_seq, shard_rows), rel_shard, axis=1
+    ).reshape(tok_rows, ny, nx, nz, shard_rows)
 
     def contract(lhs, piece):
         return lax.dot_general(
@@ -249,10 +252,11 @@
             preferred_element_type=jnp.float32,
         )
         out_rel = out_rel.at[:, lo:hi, dx].set(cols.astype(jnp.bfloat16))
-    out_abs = jnp.roll(out_rel, at_y, axis=1)
-    out_abs = jnp.roll(out_abs, at_x, axis=2)
-    out_abs = jnp.roll(out_abs, at_zh, axis=3)
-    partial_out = out_abs.transpose(0, 3, 1, 2, 4).reshape(tok_rows, n_seq * shard_rows)
+    abs_z, abs_y, abs_x = jnp.unravel_index(jnp.arange(n_seq), (nz, ny, nx))
+    abs_rel = (((abs_y - at_y) % ny) * nx + (abs_x - at_x) % nx) * nz + (abs_z - at_zh) % nz
+    partial_out = jnp.take(
+        out_rel.reshape(tok_rows, n_seq, shard_rows), abs_rel, axis=1
+    ).reshape(tok_rows, n_seq * shard_rows)
     summed_cols = reduce_scatter_tp(partial_out, dict(TP_PARTS)["zl"])
     full_width = post_gain.shape[0]
     squares = lax.psum(jnp.sum(summed_cols * summed_cols, axis=1), TP)

time: 354 us -> 356 us (level)
  starting transfers between devices: 145 us -> 154 us
  other arithmetic: 26.8 us -> 20.1 us
  local copies, waits for them, and re-layouts: 48.6 us -> 55.1 us
  waiting for transfers between devices: 73.6 us -> 67.7 us
    ppermute x1, starting transfers between devices: 17 us -> 25 us  [reduce_scatter_tp(): got = lax.ppermute(give, 'c', [(0, 1), (1, 0)])]
    concatenate x5 -> x0, other arithmetic: 5.38 us -> none  [the longest x1 1.08 us: local(): normed_rel = jnp.roll(normed_rel, -at_y, axis=1)]
    gather x0 -> x2, local copies, waits for them, and re-layouts: none -> 5.11 us  [the longest x1 2.56 us: local(): jnp.take(out_rel.reshape(tok_rows, n_seq, shard_rows), abs_rel, axis=1)]
    ppermute x4, waiting for transfers between devices: 13.5 us -> 8.71 us  [from_behind(): return lax.ppermute(block, axis, route)]
    unnamed x52 -> x66, local copies, waits for them, and re-layouts: 6.44 us -> 7.63 us
  transfers between devices with their start and end apart: 36 -> 36, of which waited for: 10 -> 10; matrix products, arithmetic and copies ran while one was open for 21% -> 19% of each run, Pallas kernels for 0% -> 0%
where the time goes in v8:
time: 356 us; the launch traced here: 354 us
  starting transfers between devices  154 us (43%)
  waiting for transfers between devices  67.7 us (19%)
  local copies, waits for them, and re-layouts  55.1 us (15%)
  matrix products  29 us (8%)
  other arithmetic  20.1 us (6%)
  between operations  14.7 us (4%)
  blocking collectives  14 us (4%)
    ppermute x6, starting transfers between devices, reduce_scatter_tp(): lax.ppermute(block.astype(jnp.bfloat16), 'zl', route).astype(jnp.float32)  37 us
    ppermute x1, starting transfers between devices, reduce_scatter_tp(): got = lax.ppermute(give, 'c', [(0, 1), (1, 0)])  25 us
    dot_general x14, matrix products, contract(): lax.dot_general(lhs, piece, (((1, 2, 3), (0, 1, 2)), ((), ())), preferred...  21 us
    ppermute x6, waiting for transfers between devices, reduce_scatter_tp(): lax.ppermute(block.astype(jnp.bfloat16), 'zl', route).astype(jnp.float32)  16 us
    ppermute x4, starting transfers between devices, ring_pieces(): right = lax.ppermute(right, axis, bwd)  16 us
    ppermute x3, starting transfers between devices, ring(): right = lax.ppermute(right, axis, bwd)  15.1 us
    ppermute x3, waiting for transfers between devices, ring(): right = lax.ppermute(right, axis, bwd)  14.4 us
    psum x1, blocking collectives, local(): squares = lax.psum(jnp.sum(summed_cols * summed_cols, axis=1), TP)  14 us
  transfers between devices with their start and end apart: 36, of which 10 were waited for; matrix products, arithmetic and copies ran while one was open for 19% of the time, Pallas kernels for 0%

profile of v8, /device:TPU:263, one launch (start us, length us, event | category | flops | bytes accessed | tf_op | source)
XLA Modules:
  0.0 354.1 jit_solution(15783878639165174692)
XLA Ops:
  10.6 11.0 %collective-permute-done = bf16[84,1536]{1,0:T(8,128)(2,1)S(1)} collective-permute-done((bf16[84,1536]{1,0:T(8,128)(2,1)S(1)}, bf16[84,1536]{1,0:T(8,128)(2,1)S(1)}, u32[]{:S(2)}, u32[]{:S(2)}) %collective-permute-start) | collective-permute-done | bytes 258080 | tf_op jit(solution)/shard_map/ppermute | solution.py:31
  30.6 5.1 %collective-permute-start.1 = (bf16[2,84,768]{2,1,0:T(8,128)(2,1)S(1)}, bf16[2,84,768]{2,1,0:T(8,128)(2,1)S(1)}, u32[]{:S(2)}, u32[]{:S(2)}) collective-permute-start(bf16[2,84,768]{2,1,0:T(8,128)(2,1)S(1)} %get-tuple-element.115), channel_id=1, source_target_pairs={{0,224},{32,0},{64,32},{96,64},{128,96},{160,128},{192,160},{224,1... | collective-permute-start | bytes 774152 | tf_op jit(solution)/shard_map/ppermute | solution.py:37
  39.1 5.4 %collective-permute-start.2 = (bf16[2,84,768]{2,1,0:T(8,128)(2,1)S(1)}, bf16[2,84,768]{2,1,0:T(8,128)(2,1)S(1)}, u32[]{:S(2)}, u32[]{:S(2)}) collective-permute-start(bf16[2,84,768]{2,1,0:T(8,128)(2,1)S(1)} %collective-permute-done.1), channel_id=1, source_target_pairs={{0,224},{32,0},{64,32},{96,64},{128,96},{160,128},{192,160},{224,1... | collective-permute-start | bytes 774152 | tf_op jit(solution)/shard_map/ppermute | solution.py:37
  48.9 4.6 %collective-permute-start.17 = (bf16[4,2,84,768]{3,0,2,1:T(4,128)(2,1)}, bf16[4,2,84,768]{3,0,2,1:T(4,128)(2,1)}, u32[]{:S(2)}, u32[]{:S(2)}) collective-permute-start(bf16[4,2,84,768]{3,0,2,1:T(4,128)(2,1)} %copy.153), channel_id=1, source_target_pairs={{0,224},{32,0},{64,32},{96,64},{128,96},{160,128},{192,160},{224,1... | collective-permute-start | bytes 3096584 | tf_op jit(solution)/shard_map/ppermute | solution.py:79
  55.4 4.6 %collective-permute-start.3 = (bf16[2,84,768]{2,1,0:T(8,128)(2,1)S(1)}, bf16[2,84,768]{2,1,0:T(8,128)(2,1)S(1)}, u32[]{:S(2)}, u32[]{:S(2)}) collective-permute-start(bf16[2,84,768]{2,1,0:T(8,128)(2,1)S(1)} %collective-permute-done.2), channel_id=1, source_target_pairs={{0,224},{32,0},{64,32},{96,64},{128,96},{160,128},{192,160},{224,1... | collective-permute-start | bytes 774152 | tf_op jit(solution)/shard_map/ppermute | solution.py:37
  62.0 12.9 %collective-permute-done.3 = bf16[2,84,768]{2,1,0:T(8,128)(2,1)S(1)} collective-permute-done((bf16[2,84,768]{2,1,0:T(8,128)(2,1)S(1)}, bf16[2,84,768]{2,1,0:T(8,128)(2,1)S(1)}, u32[]{:S(2)}, u32[]{:S(2)}) %collective-permute-start.3) | collective-permute-done | bytes 258080 | tf_op jit(solution)/shard_map/ppermute | solution.py:37
  75.0 5.4 %collective-permute-start.8 = (bf16[1,84,768]{2,1,0:T(8,128)(2,1)S(1)}, bf16[1,84,768]{2,1,0:T(8,128)(2,1)S(1)}, u32[]{:S(2)}, u32[]{:S(2)}) collective-permute-start(bf16[1,84,768]{2,1,0:T(8,128)(2,1)S(1)} %slice.335), channel_id=1, source_target_pairs={{0,224},{32,0},{64,32},{96,64},{128,96},{160,128},{192,160},{224,1... | collective-permute-start | bytes 387080 | tf_op jit(solution)/shard_map/ppermute | solution.py:43
  83.8 5.4 %collective-permute-done.7 = bf16[1,84,768]{2,1,0:T(8,128)(2,1)S(1)} collective-permute-done((bf16[1,84,768]{2,1,0:T(8,128)(2,1)S(1)}, bf16[1,84,768]{2,1,0:T(8,128)(2,1)S(1)}, u32[]{:S(2)}, u32[]{:S(2)}) %collective-permute-start.7) | collective-permute-done | bytes 129056 | tf_op jit(solution)/shard_map/ppermute | solution.py:42
  94.9 4.2 %collective-permute-start.9 = (bf16[8,2,84,768]{3,0,2,1:T(8,128)(2,1)}, bf16[8,2,84,768]{3,0,2,1:T(8,128)(2,1)}, u32[]{:S(2)}, u32[]{:S(2)}) collective-permute-start(bf16[8,2,84,768]{3,0,2,1:T(8,128)(2,1)} %copy.140), channel_id=1, source_target_pairs={{0,8},{8,16},{16,24},{24,0},{1,9},{9,17},{17,25},{25,1},{2,10},{10... | collective-permute-start | bytes 6193160 | tf_op jit(solution)/shard_map/ppermute | solution.py:78
  117.4 4.6 %collective-permute-start.19 = (bf16[4,2,84,768]{3,0,2,1:T(4,128)(2,1)}, bf16[4,2,84,768]{3,0,2,1:T(4,128)(2,1)}, u32[]{:S(2)}, u32[]{:S(2)}) collective-permute-start(bf16[4,2,84,768]{3,0,2,1:T(4,128)(2,1)} %collective-permute-done.17), channel_id=1, source_target_pairs={{0,224},{32,0},{64,32},{96,64},{128,96},{160,128},{192,160},{224,1... | collective-permute-start | bytes 3096584 | tf_op jit(solution)/shard_map/ppermute | solution.py:79
  124.1 6.9 %collective-permute-done.10 = bf16[8,2,84,768]{3,0,2,1:T(8,128)(2,1)} collective-permute-done((bf16[8,2,84,768]{3,0,2,1:T(8,128)(2,1)}, bf16[8,2,84,768]{3,0,2,1:T(8,128)(2,1)}, u32[]{:S(2)}, u32[]{:S(2)}) %collective-permute-start.10) | collective-permute-done | bytes 2064416 | tf_op jit(solution)/shard_map/ppermute | solution.py:79
  140.1 4.6 %collective-permute-start.21 = (bf16[4,2,84,768]{3,0,2,1:T(4,128)(2,1)}, bf16[4,2,84,768]{3,0,2,1:T(4,128)(2,1)}, u32[]{:S(2)}, u32[]{:S(2)}) collective-permute-start(bf16[4,2,84,768]{3,0,2,1:T(4,128)(2,1)} %collective-permute-done.19), channel_id=1, source_target_pairs={{0,224},{32,0},{64,32},{96,64},{128,96},{160,128},{192,160},{224,1... | collective-permute-start | bytes 3096584 | tf_op jit(solution)/shard_map/ppermute | solution.py:79
  156.1 4.2 %collective-permute-start.11 = (bf16[4,2,84,768]{3,0,2,1:T(4,128)(2,1)}, bf16[4,2,84,768]{3,0,2,1:T(4,128)(2,1)}, u32[]{:S(2)}, u32[]{:S(2)}) collective-permute-start(bf16[4,2,84,768]{3,0,2,1:T(4,128)(2,1)} %slice.296), channel_id=1, source_target_pairs={{0,8},{8,16},{16,24},{24,0},{1,9},{9,17},{17,25},{25,1},{2,10},{10... | collective-permute-start | bytes 3096584 | tf_op jit(solution)/shard_map/ppermute | solution.py:85
  182.1 4.6 %collective-permute-start.23 = (bf16[2,2,84,768]{3,1,2,0:T(2,128)(2,1)}, bf16[2,2,84,768]{3,1,2,0:T(2,128)(2,1)}, u32[]{:S(2)}, u32[]{:S(2)}) collective-permute-start(bf16[2,2,84,768]{3,1,2,0:T(2,128)(2,1)} %copy.163), channel_id=1, source_target_pairs={{0,224},{32,0},{64,32},{96,64},{128,96},{160,128},{192,160},{224,1... | collective-permute-start | bytes 1548296 | tf_op jit(solution)/shard_map/ppermute | solution.py:86
  200.9 4.2 %collective-permute-start.25 = (bf16[2,256,256]{2,1,0:T(8,128)(2,1)S(1)}, bf16[2,256,256]{2,1,0:T(8,128)(2,1)}, u32[]{:S(2)}, u32[]{:S(2)}) collective-permute-start(bf16[2,256,256]{2,1,0:T(8,128)(2,1)S(1)} %pad_maximum_fusion.4), channel_id=1, source_target_pairs={{0,24},{8,32},{16,40},{24,48},{32,56},{40,64},{48,72},{56,80},{64,... | collective-permute-start | bytes 786440 | tf_op jit(solution)/shard_map/ppermute | solution.py:22
  205.0 4.8 %collective-permute-start.24 = (bf16[2,256,256]{2,1,0:T(8,128)(2,1)S(1)}, bf16[2,256,256]{2,1,0:T(8,128)(2,1)}, u32[]{:S(2)}, u32[]{:S(2)}) collective-permute-start(bf16[2,256,256]{2,1,0:T(8,128)(2,1)S(1)} %pad_maximum_fusion.4), channel_id=1, source_target_pairs={{0,32},{8,40},{16,48},{24,56},{32,64},{40,72},{48,80},{56,88},{64,... | collective-permute-start | bytes 786440 | tf_op jit(solution)/shard_map/ppermute | solution.py:22
  212.1 8.7 %collective-permute-done.24 = bf16[2,256,256]{2,1,0:T(8,128)(2,1)} collective-permute-done((bf16[2,256,256]{2,1,0:T(8,128)(2,1)S(1)}, bf16[2,256,256]{2,1,0:T(8,128)(2,1)}, u32[]{:S(2)}, u32[]{:S(2)}) %collective-permute-start.24) | collective-permute-done | bytes 262176 | tf_op jit(solution)/shard_map/ppermute | solution.py:22
  243.8 25.0 %collective-permute-start.28 = (bf16[256,4,672]{0,2,1:T(8,128)(2,1)}, bf16[256,4,672]{0,2,1:T(8,128)(2,1)}, u32[]{:S(2)}, u32[]{:S(2)}) collective-permute-start(bf16[256,4,672]{0,2,1:T(8,128)(2,1)} %dynamic-slice_bitcast_fusion), channel_id=1, source_target_pairs={{0,1},{1,0},{2,3},{3,2},{4,5},{5,4},{6,7},{7,6},{8,9},{9,8},{10,11... | collective-permute-start | bytes 4128776 | tf_op jit(solution)/shard_map/ppermute | solution.py:99
  274.9 19.6 %collective-permute-start.29 = (bf16[256,672]{0,1:T(8,128)(2,1)S(1)}, bf16[256,672]{0,1:T(8,128)(2,1)S(1)}, u32[]{:S(2)}, u32[]{:S(2)}) collective-permute-start(bf16[256,672]{0,1:T(8,128)(2,1)S(1)} %get-tuple-element.116), channel_id=1, source_target_pairs={{0,2},{2,4},{4,6},{1,3},{3,5},{5,7},{8,10},{10,12},{12,14},{9,11},... | collective-permute-start | bytes 1032200 | tf_op jit(solution)/shard_map/ppermute | solution.py:107
  295.8 7.3 %collective-permute-start.33 = (bf16[256,672]{0,1:T(8,128)(2,1)}, bf16[256,672]{0,1:T(8,128)(2,1)}, u32[]{:S(2)}, u32[]{:S(2)}) collective-permute-start(bf16[256,672]{0,1:T(8,128)(2,1)} %get-tuple-element.118), channel_id=1, source_target_pairs={{0,6},{1,7},{8,14},{9,15},{16,22},{17,23},{24,30},{25,31},{32,38},... | collective-permute-start | bytes 1032200 | tf_op jit(solution)/shard_map/ppermute | solution.py:107
  304.3 6.3 %collective-permute-start.31 = (bf16[256,672]{0,1:T(8,128)(2,1)S(1)}, bf16[256,672]{0,1:T(8,128)(2,1)}, u32[]{:S(2)}, u32[]{:S(2)}) collective-permute-start(bf16[256,672]{0,1:T(8,128)(2,1)S(1)} %get-tuple-element.120), channel_id=1, source_target_pairs={{0,4},{2,6},{1,5},{3,7},{8,12},{10,14},{9,13},{11,15},{16,20},{18,... | collective-permute-start | bytes 1032200 | tf_op jit(solution)/shard_map/ppermute | solution.py:107
  313.5 9.8 %collective-permute-done.32 = bf16[256,672]{0,1:T(8,128)(2,1)} collective-permute-done((bf16[256,672]{0,1:T(8,128)(2,1)}, bf16[256,672]{0,1:T(8,128)(2,1)}, u32[]{:S(2)}, u32[]{:S(2)}) %collective-permute-start.32) | collective-permute-done | bytes 344096 | tf_op jit(solution)/shard_map/ppermute | solution.py:107
  323.2 6.3 %collective-permute-done.30 = bf16[256,672]{0,1:T(8,128)(2,1)} collective-permute-done((bf16[256,672]{0,1:T(8,128)(2,1)S(1)}, bf16[256,672]{0,1:T(8,128)(2,1)}, u32[]{:S(2)}, u32[]{:S(2)}) %collective-permute-start.30) | collective-permute-done | bytes 344096 | tf_op jit(solution)/shard_map/ppermute | solution.py:107
  331.3 14.0 %psum.7 = f32[256]{0:T(256)S(1)} all-reduce(f32[256]{0:T(256)S(1)} %get-tuple-element.108), channel_id=1, replica_groups=mesh['zh'=2,'y'=8,'x'=4,'zl'=4,'c'=2] {'zl','c'}, use_global_device_ids=true, to_apply=%region_7.12 | all-reduce | flops 256 | bytes 2048 | tf_op jit(solution)/shard_map/psum | solution.py:262
  (228 shorter events, 150.1 us)
Async XLA Ops:
  6.5 92.6 %all-gather.2.cloned.1.call-start = ((), (), s32[]{:S(2)}) async-start(), calls=%async_computation | async-start | bytes 3096576 | tf_op jit(solution)/shard_map/all_gather | solution.py:155
  21.6 24.9 %collective-permute-start.13 = (bf16[2,84,768]{2,1,0:T(8,128)(2,1)S(1)}, bf16[2,84,768]{2,1,0:T(8,128)(2,1)S(1)}, u32[]{:S(2)}, u32[]{:S(2)}) collective-permute-start(bf16[2,84,768]{2,1,0:T(8,128)(2,1)S(1)} %pad_maximum_fusion.1), channel_id=1, source_target_pairs={{0,24},{8,0},{16,8},{24,16},{1,25},{9,1},{17,9},{25,17},{2,26},{10... | collective-permute-start | bytes 774152 | tf_op jit(solution)/shard_map/ppermute | solution.py:56
  24.1 22.4 %collective-permute-start.14 = (bf16[2,84,768]{2,1,0:T(8,128)(2,1)S(1)}, bf16[2,84,768]{2,1,0:T(8,128)(2,1)S(1)}, u32[]{:S(2)}, u32[]{:S(2)}) collective-permute-start(bf16[2,84,768]{2,1,0:T(8,128)(2,1)S(1)} %pad_maximum_fusion.1), channel_id=1, source_target_pairs={{0,16},{8,24},{16,0},{24,8},{1,17},{9,25},{17,1},{25,9},{2,18},{10... | collective-permute-start | bytes 774152 | tf_op jit(solution)/shard_map/ppermute | solution.py:56
  27.0 19.5 %collective-permute-start.15 = (bf16[2,84,768]{2,1,0:T(8,128)(2,1)S(1)}, bf16[2,84,768]{2,1,0:T(8,128)(2,1)S(1)}, u32[]{:S(2)}, u32[]{:S(2)}) collective-permute-start(bf16[2,84,768]{2,1,0:T(8,128)(2,1)S(1)} %pad_maximum_fusion.1), channel_id=1, source_target_pairs={{0,8},{8,16},{16,24},{24,0},{1,9},{9,17},{17,25},{25,1},{2,10},{10... | collective-permute-start | bytes 774152 | tf_op jit(solution)/shard_map/ppermute | solution.py:56
  48.9 60.4 %collective-permute-start.17 = (bf16[4,2,84,768]{3,0,2,1:T(4,128)(2,1)}, bf16[4,2,84,768]{3,0,2,1:T(4,128)(2,1)}, u32[]{:S(2)}, u32[]{:S(2)}) collective-permute-start(bf16[4,2,84,768]{3,0,2,1:T(4,128)(2,1)} %copy.153), channel_id=1, source_target_pairs={{0,224},{32,0},{64,32},{96,64},{128,96},{160,128},{192,160},{224,1... | collective-permute-start | bytes 3096584 | tf_op jit(solution)/shard_map/ppermute | solution.py:79
  53.5 58.5 %collective-permute-start.16 = (bf16[4,2,84,768]{3,0,2,1:T(4,128)(2,1)}, bf16[4,2,84,768]{3,0,2,1:T(4,128)(2,1)}, u32[]{:S(2)}, u32[]{:S(2)}) collective-permute-start(bf16[4,2,84,768]{3,0,2,1:T(4,128)(2,1)} %copy.153), channel_id=1, source_target_pairs={{0,32},{32,64},{64,96},{96,128},{128,160},{160,192},{192,224},{224... | collective-permute-start | bytes 3096584 | tf_op jit(solution)/shard_map/ppermute | solution.py:78
  55.4 19.5 %collective-permute-start.3 = (bf16[2,84,768]{2,1,0:T(8,128)(2,1)S(1)}, bf16[2,84,768]{2,1,0:T(8,128)(2,1)S(1)}, u32[]{:S(2)}, u32[]{:S(2)}) collective-permute-start(bf16[2,84,768]{2,1,0:T(8,128)(2,1)S(1)} %collective-permute-done.2), channel_id=1, source_target_pairs={{0,224},{32,0},{64,32},{96,64},{128,96},{160,128},{192,160},{224,1... | collective-permute-start | bytes 774152 | tf_op jit(solution)/shard_map/ppermute | solution.py:37
  60.0 20.4 %collective-permute-start.6 = (bf16[2,84,768]{2,1,0:T(8,128)(2,1)S(1)}, bf16[2,84,768]{2,1,0:T(8,128)(2,1)S(1)}, u32[]{:S(2)}, u32[]{:S(2)}) collective-permute-start(bf16[2,84,768]{2,1,0:T(8,128)(2,1)S(1)} %collective-permute-done.5), channel_id=1, source_target_pairs={{0,32},{32,64},{64,96},{96,128},{128,160},{160,192},{192,224},{224... | collective-permute-start | bytes 774152 | tf_op jit(solution)/shard_map/ppermute | solution.py:36
  92.6 38.4 %collective-permute-start.10 = (bf16[8,2,84,768]{3,0,2,1:T(8,128)(2,1)}, bf16[8,2,84,768]{3,0,2,1:T(8,128)(2,1)}, u32[]{:S(2)}, u32[]{:S(2)}) collective-permute-start(bf16[8,2,84,768]{3,0,2,1:T(8,128)(2,1)} %copy.140), channel_id=1, source_target_pairs={{0,24},{8,0},{16,8},{24,16},{1,25},{9,1},{17,9},{25,17},{2,26},{10... | collective-permute-start | bytes 6193160 | tf_op jit(solution)/shard_map/ppermute | solution.py:79
  94.9 37.3 %collective-permute-start.9 = (bf16[8,2,84,768]{3,0,2,1:T(8,128)(2,1)}, bf16[8,2,84,768]{3,0,2,1:T(8,128)(2,1)}, u32[]{:S(2)}, u32[]{:S(2)}) collective-permute-start(bf16[8,2,84,768]{3,0,2,1:T(8,128)(2,1)} %copy.140), channel_id=1, source_target_pairs={{0,8},{8,16},{16,24},{24,0},{1,9},{9,17},{17,25},{25,1},{2,10},{10... | collective-permute-start | bytes 6193160 | tf_op jit(solution)/shard_map/ppermute | solution.py:78
  115.2 18.1 %collective-permute-start.18 = (bf16[4,2,84,768]{3,0,2,1:T(4,128)(2,1)}, bf16[4,2,84,768]{3,0,2,1:T(4,128)(2,1)}, u32[]{:S(2)}, u32[]{:S(2)}) collective-permute-start(bf16[4,2,84,768]{3,0,2,1:T(4,128)(2,1)} %collective-permute-done.16), channel_id=1, source_target_pairs={{0,32},{32,64},{64,96},{96,128},{128,160},{160,192},{192,224},{224... | collective-permute-start | bytes 3096584 | tf_op jit(solution)/shard_map/ppermute | solution.py:78
  137.7 24.9 %collective-permute-start.20 = (bf16[4,2,84,768]{3,0,2,1:T(4,128)(2,1)}, bf16[4,2,84,768]{3,0,2,1:T(4,128)(2,1)}, u32[]{:S(2)}, u32[]{:S(2)}) collective-permute-start(bf16[4,2,84,768]{3,0,2,1:T(4,128)(2,1)} %collective-permute-done.18), channel_id=1, source_target_pairs={{0,32},{32,64},{64,96},{96,128},{128,160},{160,192},{192,224},{224... | collective-permute-start | bytes 3096584 | tf_op jit(solution)/shard_map/ppermute | solution.py:78
  140.1 24.3 %collective-permute-start.21 = (bf16[4,2,84,768]{3,0,2,1:T(4,128)(2,1)}, bf16[4,2,84,768]{3,0,2,1:T(4,128)(2,1)}, u32[]{:S(2)}, u32[]{:S(2)}) collective-permute-start(bf16[4,2,84,768]{3,0,2,1:T(4,128)(2,1)} %collective-permute-done.19), channel_id=1, source_target_pairs={{0,224},{32,0},{64,32},{96,64},{128,96},{160,128},{192,160},{224,1... | collective-permute-start | bytes 3096584 | tf_op jit(solution)/shard_map/ppermute | solution.py:79
  153.2 23.6 %collective-permute-start.12 = (bf16[4,2,84,768]{3,0,2,1:T(4,128)(2,1)}, bf16[4,2,84,768]{3,0,2,1:T(4,128)(2,1)}, u32[]{:S(2)}, u32[]{:S(2)}) collective-permute-start(bf16[4,2,84,768]{3,0,2,1:T(4,128)(2,1)} %slice.299), channel_id=1, source_target_pairs={{0,24},{8,0},{16,8},{24,16},{1,25},{9,1},{17,9},{25,17},{2,26},{10... | collective-permute-start | bytes 3096584 | tf_op jit(solution)/shard_map/ppermute | solution.py:86
  156.1 21.8 %collective-permute-start.11 = (bf16[4,2,84,768]{3,0,2,1:T(4,128)(2,1)}, bf16[4,2,84,768]{3,0,2,1:T(4,128)(2,1)}, u32[]{:S(2)}, u32[]{:S(2)}) collective-permute-start(bf16[4,2,84,768]{3,0,2,1:T(4,128)(2,1)} %slice.296), channel_id=1, source_target_pairs={{0,8},{8,16},{16,24},{24,0},{1,9},{9,17},{17,25},{25,1},{2,10},{10... | collective-permute-start | bytes 3096584 | tf_op jit(solution)/shard_map/ppermute | solution.py:85
  169.8 22.0 %collective-permute-start.22 = (bf16[2,2,84,768]{3,1,2,0:T(2,128)(2,1)}, bf16[2,2,84,768]{3,1,2,0:T(2,128)(2,1)}, u32[]{:S(2)}, u32[]{:S(2)}) collective-permute-start(bf16[2,2,84,768]{3,1,2,0:T(2,128)(2,1)} %copy.161), channel_id=1, source_target_pairs={{0,32},{32,64},{64,96},{96,128},{128,160},{160,192},{192,224},{224... | collective-permute-start | bytes 1548296 | tf_op jit(solution)/shard_map/ppermute | solution.py:85
  197.0 25.9 %collective-permute-start.27 = (bf16[2,256,256]{2,1,0:T(8,128)(2,1)S(1)}, bf16[2,256,256]{2,1,0:T(8,128)(2,1)S(1)}, u32[]{:S(2)}, u32[]{:S(2)}) collective-permute-start(bf16[2,256,256]{2,1,0:T(8,128)(2,1)S(1)} %pad_maximum_fusion.4), channel_id=1, source_target_pairs={{0,8},{8,16},{16,24},{24,32},{32,40},{40,48},{48,56},{56,64},{64,7... | collective-permute-start | bytes 786440 | tf_op jit(solution)/shard_map/ppermute | solution.py:22
  198.9 23.9 %collective-permute-start.26 = (bf16[2,256,256]{2,1,0:T(8,128)(2,1)S(1)}, bf16[2,256,256]{2,1,0:T(8,128)(2,1)S(1)}, u32[]{:S(2)}, u32[]{:S(2)}) collective-permute-start(bf16[2,256,256]{2,1,0:T(8,128)(2,1)S(1)} %pad_maximum_fusion.4), channel_id=1, source_target_pairs={{0,16},{8,24},{16,32},{24,40},{32,48},{40,56},{48,64},{56,72},{64,... | collective-permute-start | bytes 786440 | tf_op jit(solution)/shard_map/ppermute | solution.py:22
  200.9 21.0 %collective-permute-start.25 = (bf16[2,256,256]{2,1,0:T(8,128)(2,1)S(1)}, bf16[2,256,256]{2,1,0:T(8,128)(2,1)}, u32[]{:S(2)}, u32[]{:S(2)}) collective-permute-start(bf16[2,256,256]{2,1,0:T(8,128)(2,1)S(1)} %pad_maximum_fusion.4), channel_id=1, source_target_pairs={{0,24},{8,32},{16,40},{24,48},{32,56},{40,64},{48,72},{56,80},{64,... | collective-permute-start | bytes 786440 | tf_op jit(solution)/shard_map/ppermute | solution.py:22
  243.8 28.0 %collective-permute-start.28 = (bf16[256,4,672]{0,2,1:T(8,128)(2,1)}, bf16[256,4,672]{0,2,1:T(8,128)(2,1)}, u32[]{:S(2)}, u32[]{:S(2)}) collective-permute-start(bf16[256,4,672]{0,2,1:T(8,128)(2,1)} %dynamic-slice_bitcast_fusion), channel_id=1, source_target_pairs={{0,1},{1,0},{2,3},{3,2},{4,5},{5,4},{6,7},{7,6},{8,9},{9,8},{10,11... | collective-permute-start | bytes 4128776 | tf_op jit(solution)/shard_map/ppermute | solution.py:99
  274.9 35.8 %collective-permute-start.29 = (bf16[256,672]{0,1:T(8,128)(2,1)S(1)}, bf16[256,672]{0,1:T(8,128)(2,1)S(1)}, u32[]{:S(2)}, u32[]{:S(2)}) collective-permute-start(bf16[256,672]{0,1:T(8,128)(2,1)S(1)} %get-tuple-element.116), channel_id=1, source_target_pairs={{0,2},{2,4},{4,6},{1,3},{3,5},{5,7},{8,10},{10,12},{12,14},{9,11},... | collective-permute-start | bytes 1032200 | tf_op jit(solution)/shard_map/ppermute | solution.py:107
  294.5 19.0 %collective-permute-start.34 = (bf16[256,672]{0,1:T(8,128)(2,1)}, bf16[256,672]{0,1:T(8,128)(2,1)}, u32[]{:S(2)}, u32[]{:S(2)}) collective-permute-start(bf16[256,672]{0,1:T(8,128)(2,1)} %get-tuple-element.117), channel_id=1, source_target_pairs={{6,0},{7,1},{14,8},{15,9},{22,16},{23,17},{30,24},{31,25},{38,32},... | collective-permute-start | bytes 1032200 | tf_op jit(solution)/shard_map/ppermute | solution.py:107
  303.0 20.2 %collective-permute-start.32 = (bf16[256,672]{0,1:T(8,128)(2,1)}, bf16[256,672]{0,1:T(8,128)(2,1)}, u32[]{:S(2)}, u32[]{:S(2)}) collective-permute-start(bf16[256,672]{0,1:T(8,128)(2,1)} %get-tuple-element.119), channel_id=1, source_target_pairs={{4,0},{6,2},{5,1},{7,3},{12,8},{14,10},{13,9},{15,11},{20,16},{22,... | collective-permute-start | bytes 1032200 | tf_op jit(solution)/shard_map/ppermute | solution.py:107
  304.3 18.9 %collective-permute-start.31 = (bf16[256,672]{0,1:T(8,128)(2,1)S(1)}, bf16[256,672]{0,1:T(8,128)(2,1)}, u32[]{:S(2)}, u32[]{:S(2)}) collective-permute-start(bf16[256,672]{0,1:T(8,128)(2,1)S(1)} %get-tuple-element.120), channel_id=1, source_target_pairs={{0,4},{2,6},{1,5},{3,7},{8,12},{10,14},{9,13},{11,15},{16,20},{18,... | collective-permute-start | bytes 1032200 | tf_op jit(solution)/shard_map/ppermute | solution.py:107
  (42 other events, 344.2 us)
Sparse Core Ops, SparseCore 0:
  9.4 45.4 all-gather.1

commit v9 on v8

--- a/solution.py
+++ b/solution.py
@@ -170,13 +170,13 @@
 
     def fold_qk(acc, new):
         for dy, lo, hi, piece in new:
-            term = contract(normed_rel[:, dy, lo:hi], piece)
+            term = contract(normed_rel[:, dy, :, lo:hi], piece)
             acc = term if acc is None else acc + term
         return acc
 
     def fold_v(acc, new):
         for dx, lo, hi, piece in new:
-            term = contract(normed_rel[:, lo:hi, dx], piece[..., :v_cols])
+            term = contract(normed_rel[:, :, dx, lo:hi], piece)
             acc = term if acc is None else acc + term
         return acc
 
@@ -187,8 +187,9 @@
     half_b = by_zh[:, :, split:]
     a_x = stacked_direct(half_a, "x", nx)
     b_y = stacked_ring(half_b, "y", ny, 0)
-    _, qk = ring_pieces(a_x, "y", ny, 0, fold_qk, None)
-    b_pieces, projected_values = ring_pieces(b_y, "x", nx, 0, fold_v, None)
+    _, qk = ring_pieces(a_x, "y", ny, 1, fold_qk, None)
+    b_pieces, b_sum = ring_pieces(b_y, "x", nx, 1, fold_v, None)
+    projected_values = b_sum[:, :v_cols]
     queries_raw = qk[:, :q_cols]
     unrotated_keys = qk[:, q_cols:]
     own_places = lax.dynamic_slice_in_dim(positions, seq_at * tok_rows, tok_rows, 0)
@@ -244,14 +245,17 @@
     merged = (inner_sum + outer_sum) / total[..., None]
     attended = merged.astype(jnp.bfloat16).reshape(tok_rows, local_kv * query_group * head_dim)
     out_rel = jnp.zeros((tok_rows, ny, nx, nz, shard_rows), jnp.bfloat16)
+    attended_wide = jnp.concatenate(
+        [jnp.zeros((tok_rows, v_cols), attended.dtype), attended], axis=1
+    )
     for dx, lo, hi, piece in b_pieces:
         cols = lax.dot_general(
-            attended,
-            piece[..., v_cols:],
+            attended_wide,
+            piece,
             (((1,), (3,)), ((), ())),
             preferred_element_type=jnp.float32,
         )
-        out_rel = out_rel.at[:, lo:hi, dx].set(cols.astype(jnp.bfloat16))
+        out_rel = out_rel.at[:, :, dx, lo:hi].set(cols.astype(jnp.bfloat16))
     abs_z, abs_y, abs_x = jnp.unravel_index(jnp.arange(n_seq), (nz, ny, nx))
     abs_rel = (((abs_y - at_y) % ny) * nx + (abs_x - at_x) % nx) * nz + (abs_z - at_zh) % nz
     partial_out = jnp.take(

time: 356 us -> 355 us (level)
  the two profiles are of different devices: /device:TPU:263 before, /device:TPU:257 now
where the time goes in v9:
time: 355 us; the launch traced here: 353 us
  starting transfers between devices  146 us (41%)
  waiting for transfers between devices  73.9 us (21%)
  local copies, waits for them, and re-layouts  40.5 us (11%)
  matrix products  40.5 us (11%)
  other arithmetic  23.8 us (7%)
  between operations  14.7 us (4%)
  blocking collectives  13.8 us (4%)
    ppermute x6, starting transfers between devices, reduce_scatter_tp(): lax.ppermute(block.astype(jnp.bfloat16), 'zl', route).astype(jnp.float32)  32.1 us
    dot_general x14, matrix products, contract(): lax.dot_general(lhs, piece, (((1, 2, 3), (0, 1, 2)), ((), ())), preferred...  26.6 us
    ppermute x1, starting transfers between devices, reduce_scatter_tp(): got = lax.ppermute(give, 'c', [(0, 1), (1, 0)])  25.5 us
    ppermute x3, waiting for transfers between devices, ring(): left = lax.ppermute(left, axis, fwd)  18.1 us
    ppermute x6, waiting for transfers between devices, reduce_scatter_tp(): lax.ppermute(block.astype(jnp.bfloat16), 'zl', route).astype(jnp.float32)  17.1 us
    ppermute x4, starting transfers between devices, ring_pieces(): right = lax.ppermute(right, axis, bwd)  16.9 us
    ppermute x3, starting transfers between devices, ring(): right = lax.ppermute(right, axis, bwd)  15.1 us
    psum x1, blocking collectives, local(): squares = lax.psum(jnp.sum(summed_cols * summed_cols, axis=1), TP)  13.8 us
  transfers between devices with their start and end apart: 36, of which 12 were waited for; matrix products, arithmetic and copies ran while one was open for 17% of the time, Pallas kernels for 0%

profile of v9, /device:TPU:257, one launch (start us, length us, event | category | flops | bytes accessed | tf_op | source)
XLA Modules:
  0.0 352.7 jit_solution(16158776345368204656)
XLA Ops:
  11.1 10.7 %collective-permute-done = bf16[84,1536]{1,0:T(8,128)(2,1)S(1)} collective-permute-done((bf16[84,1536]{1,0:T(8,128)(2,1)S(1)}, bf16[84,1536]{1,0:T(8,128)(2,1)S(1)}, u32[]{:S(2)}, u32[]{:S(2)}) %collective-permute-start) | collective-permute-done | bytes 258080 | tf_op jit(solution)/shard_map/ppermute | solution.py:31
  21.8 4.2 %collective-permute-start.13 = (bf16[2,84,768]{2,1,0:T(8,128)(2,1)S(1)}, bf16[2,84,768]{2,1,0:T(8,128)(2,1)S(1)}, u32[]{:S(2)}, u32[]{:S(2)}) collective-permute-start(bf16[2,84,768]{2,1,0:T(8,128)(2,1)S(1)} %pad_maximum_fusion.1), channel_id=1, source_target_pairs={{0,24},{8,0},{16,8},{24,16},{1,25},{9,1},{17,9},{25,17},{2,26},{10... | collective-permute-start | bytes 774152 | tf_op jit(solution)/shard_map/ppermute | solution.py:56
  31.0 5.1 %collective-permute-start.1 = (bf16[2,84,768]{2,1,0:T(8,128)(2,1)S(1)}, bf16[2,84,768]{2,1,0:T(8,128)(2,1)S(1)}, u32[]{:S(2)}, u32[]{:S(2)}) collective-permute-start(bf16[2,84,768]{2,1,0:T(8,128)(2,1)S(1)} %get-tuple-element.115), channel_id=1, source_target_pairs={{0,224},{32,0},{64,32},{96,64},{128,96},{160,128},{192,160},{224,1... | collective-permute-start | bytes 774152 | tf_op jit(solution)/shard_map/ppermute | solution.py:37
  39.5 5.4 %collective-permute-start.2 = (bf16[2,84,768]{2,1,0:T(8,128)(2,1)S(1)}, bf16[2,84,768]{2,1,0:T(8,128)(2,1)S(1)}, u32[]{:S(2)}, u32[]{:S(2)}) collective-permute-start(bf16[2,84,768]{2,1,0:T(8,128)(2,1)S(1)} %collective-permute-done.1), channel_id=1, source_target_pairs={{0,224},{32,0},{64,32},{96,64},{128,96},{160,128},{192,160},{224,1... | collective-permute-start | bytes 774152 | tf_op jit(solution)/shard_map/ppermute | solution.py:37
  49.4 4.6 %collective-permute-start.17 = (bf16[4,2,84,768]{3,0,2,1:T(4,128)(2,1)}, bf16[4,2,84,768]{3,0,2,1:T(4,128)(2,1)}, u32[]{:S(2)}, u32[]{:S(2)}) collective-permute-start(bf16[4,2,84,768]{3,0,2,1:T(4,128)(2,1)} %copy.125), channel_id=1, source_target_pairs={{0,224},{32,0},{64,32},{96,64},{128,96},{160,128},{192,160},{224,1... | collective-permute-start | bytes 3096584 | tf_op jit(solution)/shard_map/ppermute | solution.py:79
  55.9 4.6 %collective-permute-start.3 = (bf16[2,84,768]{2,1,0:T(8,128)(2,1)S(1)}, bf16[2,84,768]{2,1,0:T(8,128)(2,1)S(1)}, u32[]{:S(2)}, u32[]{:S(2)}) collective-permute-start(bf16[2,84,768]{2,1,0:T(8,128)(2,1)S(1)} %collective-permute-done.2), channel_id=1, source_target_pairs={{0,224},{32,0},{64,32},{96,64},{128,96},{160,128},{192,160},{224,1... | collective-permute-start | bytes 774152 | tf_op jit(solution)/shard_map/ppermute | solution.py:37
  62.5 18.1 %collective-permute-done.6 = bf16[2,84,768]{2,1,0:T(8,128)(2,1)S(1)} collective-permute-done((bf16[2,84,768]{2,1,0:T(8,128)(2,1)S(1)}, bf16[2,84,768]{2,1,0:T(8,128)(2,1)S(1)}, u32[]{:S(2)}, u32[]{:S(2)}) %collective-permute-start.6) | collective-permute-done | bytes 258080 | tf_op jit(solution)/shard_map/ppermute | solution.py:36
  82.5 4.6 %collective-permute-start.8 = (bf16[1,84,768]{2,1,0:T(8,128)(2,1)S(1)}, bf16[1,84,768]{2,1,0:T(8,128)(2,1)S(1)}, u32[]{:S(2)}, u32[]{:S(2)}) collective-permute-start(bf16[1,84,768]{2,1,0:T(8,128)(2,1)S(1)} %slice.295), channel_id=1, source_target_pairs={{0,224},{32,0},{64,32},{96,64},{128,96},{160,128},{192,160},{224,1... | collective-permute-start | bytes 387080 | tf_op jit(solution)/shard_map/ppermute | solution.py:43
  92.8 3.4 collective-permute-start.9
  116.5 4.6 %collective-permute-start.19 = (bf16[4,2,84,768]{3,0,2,1:T(4,128)(2,1)}, bf16[4,2,84,768]{3,0,2,1:T(4,128)(2,1)}, u32[]{:S(2)}, u32[]{:S(2)}) collective-permute-start(bf16[4,2,84,768]{3,0,2,1:T(4,128)(2,1)} %collective-permute-done.17), channel_id=1, source_target_pairs={{0,224},{32,0},{64,32},{96,64},{128,96},{160,128},{192,160},{224,1... | collective-permute-start | bytes 3096584 | tf_op jit(solution)/shard_map/ppermute | solution.py:79
  121.8 8.0 %collective-permute-done.9 = bf16[8,2,84,768]{3,0,2,1:T(8,128)(2,1)} collective-permute-done((bf16[8,2,84,768]{3,0,2,1:T(8,128)(2,1)}, bf16[8,2,84,768]{3,0,2,1:T(8,128)(2,1)}, u32[]{:S(2)}, u32[]{:S(2)}) %collective-permute-start.9) | collective-permute-done | bytes 2064416 | tf_op jit(solution)/shard_map/ppermute | solution.py:78
  140.7 4.6 %collective-permute-start.21 = (bf16[4,2,84,768]{3,0,2,1:T(4,128)(2,1)}, bf16[4,2,84,768]{3,0,2,1:T(4,128)(2,1)}, u32[]{:S(2)}, u32[]{:S(2)}) collective-permute-start(bf16[4,2,84,768]{3,0,2,1:T(4,128)(2,1)} %collective-permute-done.19), channel_id=1, source_target_pairs={{0,224},{32,0},{64,32},{96,64},{128,96},{160,128},{192,160},{224,1... | collective-permute-start | bytes 3096584 | tf_op jit(solution)/shard_map/ppermute | solution.py:79
  153.9 4.2 %collective-permute-start.12 = (bf16[8,1,84,768]{3,0,2,1:T(8,128)(2,1)}, bf16[8,1,84,768]{3,0,2,1:T(8,128)(2,1)}, u32[]{:S(2)}, u32[]{:S(2)}) collective-permute-start(bf16[8,1,84,768]{3,0,2,1:T(8,128)(2,1)} %slice.266), channel_id=1, source_target_pairs={{0,24},{8,0},{16,8},{24,16},{1,25},{9,1},{17,9},{25,17},{2,26},{10... | collective-permute-start | bytes 3096584 | tf_op jit(solution)/shard_map/ppermute | solution.py:86
  172.1 4.6 %collective-permute-start.23 = (bf16[4,1,84,768]{3,0,2,1:T(4,128)(2,1)}, bf16[4,1,84,768]{3,0,2,1:T(4,128)(2,1)}, u32[]{:S(2)}, u32[]{:S(2)}) collective-permute-start(bf16[4,1,84,768]{3,0,2,1:T(4,128)(2,1)} %slice.279), channel_id=1, source_target_pairs={{0,224},{32,0},{64,32},{96,64},{128,96},{160,128},{192,160},{224,1... | collective-permute-start | bytes 1548296 | tf_op jit(solution)/shard_map/ppermute | solution.py:86
  195.6 3.7 %collective-permute-start.26 = (bf16[2,256,256]{2,1,0:T(8,128)(2,1)}, bf16[2,256,256]{2,1,0:T(8,128)(2,1)}, u32[]{:S(2)}, u32[]{:S(2)}) collective-permute-start(bf16[2,256,256]{2,1,0:T(8,128)(2,1)} %pad_maximum_fusion.4), channel_id=1, source_target_pairs={{0,16},{8,24},{16,32},{24,40},{32,48},{40,56},{48,64},{56,72},{64,... | collective-permute-start | bytes 786440 | tf_op jit(solution)/shard_map/ppermute | solution.py:22
  205.7 4.4 %collective-permute-done.24 = bf16[2,256,256]{2,1,0:T(8,128)(2,1)} collective-permute-done((bf16[2,256,256]{2,1,0:T(8,128)(2,1)}, bf16[2,256,256]{2,1,0:T(8,128)(2,1)}, u32[]{:S(2)}, u32[]{:S(2)}) %collective-permute-start.24) | collective-permute-done | bytes 262176 | tf_op jit(solution)/shard_map/ppermute | solution.py:22
  213.7 4.2 %collective-permute-done.26 = bf16[2,256,256]{2,1,0:T(8,128)(2,1)} collective-permute-done((bf16[2,256,256]{2,1,0:T(8,128)(2,1)}, bf16[2,256,256]{2,1,0:T(8,128)(2,1)}, u32[]{:S(2)}, u32[]{:S(2)}) %collective-permute-start.26) | collective-permute-done | bytes 262176 | tf_op jit(solution)/shard_map/ppermute | solution.py:22
  241.0 3.6 %reshape_reshape.3 = bf16[256,4,2,672]{0,3,2,1:T(8,128)(2,1)S(1)} reshape(bf16[256,64,84]{0,2,1:T(8,128)(2,1)} %select_bitcast_fusion) | data formatting | bytes 5505024 | tf_op jit(solution)/shard_map/reshape;reshape | solution.py:96
  245.9 25.5 %collective-permute-start.28 = (bf16[256,4,672]{0,2,1:T(8,128)(2,1)}, bf16[256,4,672]{0,2,1:T(8,128)(2,1)}, u32[]{:S(2)}, u32[]{:S(2)}) collective-permute-start(bf16[256,4,672]{0,2,1:T(8,128)(2,1)} %dynamic-slice_bitcast_fusion), channel_id=1, source_target_pairs={{0,1},{1,0},{2,3},{3,2},{4,5},{5,4},{6,7},{7,6},{8,9},{9,8},{10,11... | collective-permute-start | bytes 4128776 | tf_op jit(solution)/shard_map/ppermute | solution.py:99
  277.6 16.3 %collective-permute-start.29 = (bf16[256,672]{0,1:T(8,128)(2,1)S(1)}, bf16[256,672]{0,1:T(8,128)(2,1)S(1)}, u32[]{:S(2)}, u32[]{:S(2)}) collective-permute-start(bf16[256,672]{0,1:T(8,128)(2,1)S(1)} %get-tuple-element.116), channel_id=1, source_target_pairs={{0,2},{2,4},{4,6},{1,3},{3,5},{5,7},{8,10},{10,12},{12,14},{9,11},... | collective-permute-start | bytes 1032200 | tf_op jit(solution)/shard_map/ppermute | solution.py:107
  295.2 5.2 %collective-permute-start.31 = (bf16[256,672]{0,1:T(8,128)(2,1)}, bf16[256,672]{0,1:T(8,128)(2,1)}, u32[]{:S(2)}, u32[]{:S(2)}) collective-permute-start(bf16[256,672]{0,1:T(8,128)(2,1)} %get-tuple-element.120), channel_id=1, source_target_pairs={{0,4},{2,6},{1,5},{3,7},{8,12},{10,14},{9,13},{11,15},{16,20},{18,... | collective-permute-start | bytes 1032200 | tf_op jit(solution)/shard_map/ppermute | solution.py:107
  301.6 6.8 %collective-permute-start.33 = (bf16[256,672]{0,1:T(8,128)(2,1)S(1)}, bf16[256,672]{0,1:T(8,128)(2,1)}, u32[]{:S(2)}, u32[]{:S(2)}) collective-permute-start(bf16[256,672]{0,1:T(8,128)(2,1)S(1)} %get-tuple-element.118), channel_id=1, source_target_pairs={{0,6},{1,7},{8,14},{9,15},{16,22},{17,23},{24,30},{25,31},{32,38},... | collective-permute-start | bytes 1032200 | tf_op jit(solution)/shard_map/ppermute | solution.py:107
  311.3 17.1 %collective-permute-done.32 = bf16[256,672]{0,1:T(8,128)(2,1)} collective-permute-done((bf16[256,672]{0,1:T(8,128)(2,1)}, bf16[256,672]{0,1:T(8,128)(2,1)}, u32[]{:S(2)}, u32[]{:S(2)}) %collective-permute-start.32) | collective-permute-done | bytes 344096 | tf_op jit(solution)/shard_map/ppermute | solution.py:107
  330.2 13.8 %psum.7 = f32[256]{0:T(256)S(1)} all-reduce(f32[256]{0:T(256)S(1)} %get-tuple-element.108), channel_id=1, replica_groups=mesh['zh'=2,'y'=8,'x'=4,'zl'=4,'c'=2] {'zl','c'}, use_global_device_ids=true, to_apply=%region_6.11 | all-reduce | flops 256 | bytes 2048 | tf_op jit(solution)/shard_map/psum | solution.py:266
  (210 shorter events, 150.9 us)
Async XLA Ops:
  6.5 92.8 %all-gather.2.cloned.1.call-start = ((), (), s32[]{:S(2)}) async-start(), calls=%async_computation | async-start | bytes 3096576 | tf_op jit(solution)/shard_map/all_gather | solution.py:155
  21.8 25.1 %collective-permute-start.13 = (bf16[2,84,768]{2,1,0:T(8,128)(2,1)S(1)}, bf16[2,84,768]{2,1,0:T(8,128)(2,1)S(1)}, u32[]{:S(2)}, u32[]{:S(2)}) collective-permute-start(bf16[2,84,768]{2,1,0:T(8,128)(2,1)S(1)} %pad_maximum_fusion.1), channel_id=1, source_target_pairs={{0,24},{8,0},{16,8},{24,16},{1,25},{9,1},{17,9},{25,17},{2,26},{10... | collective-permute-start | bytes 774152 | tf_op jit(solution)/shard_map/ppermute | solution.py:56
  26.0 20.9 %collective-permute-start.14 = (bf16[2,84,768]{2,1,0:T(8,128)(2,1)S(1)}, bf16[2,84,768]{2,1,0:T(8,128)(2,1)S(1)}, u32[]{:S(2)}, u32[]{:S(2)}) collective-permute-start(bf16[2,84,768]{2,1,0:T(8,128)(2,1)S(1)} %pad_maximum_fusion.1), channel_id=1, source_target_pairs={{0,16},{8,24},{16,0},{24,8},{1,17},{9,25},{17,1},{25,9},{2,18},{10... | collective-permute-start | bytes 774152 | tf_op jit(solution)/shard_map/ppermute | solution.py:56
  28.4 18.5 %collective-permute-start.15 = (bf16[2,84,768]{2,1,0:T(8,128)(2,1)S(1)}, bf16[2,84,768]{2,1,0:T(8,128)(2,1)S(1)}, u32[]{:S(2)}, u32[]{:S(2)}) collective-permute-start(bf16[2,84,768]{2,1,0:T(8,128)(2,1)S(1)} %pad_maximum_fusion.1), channel_id=1, source_target_pairs={{0,8},{8,16},{16,24},{24,0},{1,9},{9,17},{17,25},{25,1},{2,10},{10... | collective-permute-start | bytes 774152 | tf_op jit(solution)/shard_map/ppermute | solution.py:56
  49.4 60.2 %collective-permute-start.17 = (bf16[4,2,84,768]{3,0,2,1:T(4,128)(2,1)}, bf16[4,2,84,768]{3,0,2,1:T(4,128)(2,1)}, u32[]{:S(2)}, u32[]{:S(2)}) collective-permute-start(bf16[4,2,84,768]{3,0,2,1:T(4,128)(2,1)} %copy.125), channel_id=1, source_target_pairs={{0,224},{32,0},{64,32},{96,64},{128,96},{160,128},{192,160},{224,1... | collective-permute-start | bytes 3096584 | tf_op jit(solution)/shard_map/ppermute | solution.py:79
  53.9 58.1 %collective-permute-start.16 = (bf16[4,2,84,768]{3,0,2,1:T(4,128)(2,1)}, bf16[4,2,84,768]{3,0,2,1:T(4,128)(2,1)}, u32[]{:S(2)}, u32[]{:S(2)}) collective-permute-start(bf16[4,2,84,768]{3,0,2,1:T(4,128)(2,1)} %copy.125), channel_id=1, source_target_pairs={{0,32},{32,64},{64,96},{96,128},{128,160},{160,192},{192,224},{224... | collective-permute-start | bytes 3096584 | tf_op jit(solution)/shard_map/ppermute | solution.py:78
  55.9 26.6 %collective-permute-start.3 = (bf16[2,84,768]{2,1,0:T(8,128)(2,1)S(1)}, bf16[2,84,768]{2,1,0:T(8,128)(2,1)S(1)}, u32[]{:S(2)}, u32[]{:S(2)}) collective-permute-start(bf16[2,84,768]{2,1,0:T(8,128)(2,1)S(1)} %collective-permute-done.2), channel_id=1, source_target_pairs={{0,224},{32,0},{64,32},{96,64},{128,96},{160,128},{192,160},{224,1... | collective-permute-start | bytes 774152 | tf_op jit(solution)/shard_map/ppermute | solution.py:37
  60.5 20.1 %collective-permute-start.6 = (bf16[2,84,768]{2,1,0:T(8,128)(2,1)S(1)}, bf16[2,84,768]{2,1,0:T(8,128)(2,1)S(1)}, u32[]{:S(2)}, u32[]{:S(2)}) collective-permute-start(bf16[2,84,768]{2,1,0:T(8,128)(2,1)S(1)} %collective-permute-done.5), channel_id=1, source_target_pairs={{0,32},{32,64},{64,96},{96,128},{128,160},{160,192},{192,224},{224... | collective-permute-start | bytes 774152 | tf_op jit(solution)/shard_map/ppermute | solution.py:36
  92.8 37.0 %collective-permute-start.9 = (bf16[8,2,84,768]{3,0,2,1:T(8,128)(2,1)}, bf16[8,2,84,768]{3,0,2,1:T(8,128)(2,1)}, u32[]{:S(2)}, u32[]{:S(2)}) collective-permute-start(bf16[8,2,84,768]{3,0,2,1:T(8,128)(2,1)} %copy.114), channel_id=1, source_target_pairs={{0,8},{8,16},{16,24},{24,0},{1,9},{9,17},{17,25},{25,1},{2,10},{10... | collective-permute-start | bytes 6193160 | tf_op jit(solution)/shard_map/ppermute | solution.py:78
  96.2 41.9 %collective-permute-start.10 = (bf16[8,2,84,768]{3,0,2,1:T(8,128)(2,1)}, bf16[8,2,84,768]{3,0,2,1:T(8,128)(2,1)}, u32[]{:S(2)}, u32[]{:S(2)}) collective-permute-start(bf16[8,2,84,768]{3,0,2,1:T(8,128)(2,1)} %copy.114), channel_id=1, source_target_pairs={{0,24},{8,0},{16,8},{24,16},{1,25},{9,1},{17,9},{25,17},{2,26},{10... | collective-permute-start | bytes 6193160 | tf_op jit(solution)/shard_map/ppermute | solution.py:79
  114.4 18.0 %collective-permute-start.18 = (bf16[4,2,84,768]{3,0,2,1:T(4,128)(2,1)}, bf16[4,2,84,768]{3,0,2,1:T(4,128)(2,1)}, u32[]{:S(2)}, u32[]{:S(2)}) collective-permute-start(bf16[4,2,84,768]{3,0,2,1:T(4,128)(2,1)} %collective-permute-done.16), channel_id=1, source_target_pairs={{0,32},{32,64},{64,96},{96,128},{128,160},{160,192},{192,224},{224... | collective-permute-start | bytes 3096584 | tf_op jit(solution)/shard_map/ppermute | solution.py:78
  136.0 23.6 %collective-permute-start.20 = (bf16[4,2,84,768]{3,0,2,1:T(4,128)(2,1)}, bf16[4,2,84,768]{3,0,2,1:T(4,128)(2,1)}, u32[]{:S(2)}, u32[]{:S(2)}) collective-permute-start(bf16[4,2,84,768]{3,0,2,1:T(4,128)(2,1)} %collective-permute-done.18), channel_id=1, source_target_pairs={{0,32},{32,64},{64,96},{96,128},{128,160},{160,192},{192,224},{224... | collective-permute-start | bytes 3096584 | tf_op jit(solution)/shard_map/ppermute | solution.py:78
  140.7 20.8 %collective-permute-start.21 = (bf16[4,2,84,768]{3,0,2,1:T(4,128)(2,1)}, bf16[4,2,84,768]{3,0,2,1:T(4,128)(2,1)}, u32[]{:S(2)}, u32[]{:S(2)}) collective-permute-start(bf16[4,2,84,768]{3,0,2,1:T(4,128)(2,1)} %collective-permute-done.19), channel_id=1, source_target_pairs={{0,224},{32,0},{64,32},{96,64},{128,96},{160,128},{192,160},{224,1... | collective-permute-start | bytes 3096584 | tf_op jit(solution)/shard_map/ppermute | solution.py:79
  149.3 18.9 %collective-permute-start.11 = (bf16[8,1,84,768]{3,0,2,1:T(8,128)(2,1)}, bf16[8,1,84,768]{3,0,2,1:T(8,128)(2,1)}, u32[]{:S(2)}, u32[]{:S(2)}) collective-permute-start(bf16[8,1,84,768]{3,0,2,1:T(8,128)(2,1)} %slice.264), channel_id=1, source_target_pairs={{0,8},{8,16},{16,24},{24,0},{1,9},{9,17},{17,25},{25,1},{2,10},{10... | collective-permute-start | bytes 3096584 | tf_op jit(solution)/shard_map/ppermute | solution.py:85
  153.9 22.8 %collective-permute-start.12 = (bf16[8,1,84,768]{3,0,2,1:T(8,128)(2,1)}, bf16[8,1,84,768]{3,0,2,1:T(8,128)(2,1)}, u32[]{:S(2)}, u32[]{:S(2)}) collective-permute-start(bf16[8,1,84,768]{3,0,2,1:T(8,128)(2,1)} %slice.266), channel_id=1, source_target_pairs={{0,24},{8,0},{16,8},{24,16},{1,25},{9,1},{17,9},{25,17},{2,26},{10... | collective-permute-start | bytes 3096584 | tf_op jit(solution)/shard_map/ppermute | solution.py:86
  191.2 18.9 %collective-permute-start.24 = (bf16[2,256,256]{2,1,0:T(8,128)(2,1)}, bf16[2,256,256]{2,1,0:T(8,128)(2,1)}, u32[]{:S(2)}, u32[]{:S(2)}) collective-permute-start(bf16[2,256,256]{2,1,0:T(8,128)(2,1)} %pad_maximum_fusion.4), channel_id=1, source_target_pairs={{0,32},{8,40},{16,48},{24,56},{32,64},{40,72},{48,80},{56,88},{64,... | collective-permute-start | bytes 786440 | tf_op jit(solution)/shard_map/ppermute | solution.py:22
  193.1 19.6 %collective-permute-start.25 = (bf16[2,256,256]{2,1,0:T(8,128)(2,1)}, bf16[2,256,256]{2,1,0:T(8,128)(2,1)}, u32[]{:S(2)}, u32[]{:S(2)}) collective-permute-start(bf16[2,256,256]{2,1,0:T(8,128)(2,1)} %pad_maximum_fusion.4), channel_id=1, source_target_pairs={{0,24},{8,32},{16,40},{24,48},{32,56},{40,64},{48,72},{56,80},{64,... | collective-permute-start | bytes 786440 | tf_op jit(solution)/shard_map/ppermute | solution.py:22
  195.6 22.2 %collective-permute-start.26 = (bf16[2,256,256]{2,1,0:T(8,128)(2,1)}, bf16[2,256,256]{2,1,0:T(8,128)(2,1)}, u32[]{:S(2)}, u32[]{:S(2)}) collective-permute-start(bf16[2,256,256]{2,1,0:T(8,128)(2,1)} %pad_maximum_fusion.4), channel_id=1, source_target_pairs={{0,16},{8,24},{16,32},{24,40},{32,48},{40,56},{48,64},{56,72},{64,... | collective-permute-start | bytes 786440 | tf_op jit(solution)/shard_map/ppermute | solution.py:22
  199.3 20.5 %collective-permute-start.27 = (bf16[2,256,256]{2,1,0:T(8,128)(2,1)}, bf16[2,256,256]{2,1,0:T(8,128)(2,1)}, u32[]{:S(2)}, u32[]{:S(2)}) collective-permute-start(bf16[2,256,256]{2,1,0:T(8,128)(2,1)} %pad_maximum_fusion.4), channel_id=1, source_target_pairs={{0,8},{8,16},{16,24},{24,32},{32,40},{40,48},{48,56},{56,64},{64,7... | collective-permute-start | bytes 786440 | tf_op jit(solution)/shard_map/ppermute | solution.py:22
  245.9 28.6 %collective-permute-start.28 = (bf16[256,4,672]{0,2,1:T(8,128)(2,1)}, bf16[256,4,672]{0,2,1:T(8,128)(2,1)}, u32[]{:S(2)}, u32[]{:S(2)}) collective-permute-start(bf16[256,4,672]{0,2,1:T(8,128)(2,1)} %dynamic-slice_bitcast_fusion), channel_id=1, source_target_pairs={{0,1},{1,0},{2,3},{3,2},{4,5},{5,4},{6,7},{7,6},{8,9},{9,8},{10,11... | collective-permute-start | bytes 4128776 | tf_op jit(solution)/shard_map/ppermute | solution.py:99
  277.6 30.8 %collective-permute-start.29 = (bf16[256,672]{0,1:T(8,128)(2,1)S(1)}, bf16[256,672]{0,1:T(8,128)(2,1)S(1)}, u32[]{:S(2)}, u32[]{:S(2)}) collective-permute-start(bf16[256,672]{0,1:T(8,128)(2,1)S(1)} %get-tuple-element.116), channel_id=1, source_target_pairs={{0,2},{2,4},{4,6},{1,3},{3,5},{5,7},{8,10},{10,12},{12,14},{9,11},... | collective-permute-start | bytes 1032200 | tf_op jit(solution)/shard_map/ppermute | solution.py:107
  300.3 28.0 %collective-permute-start.32 = (bf16[256,672]{0,1:T(8,128)(2,1)}, bf16[256,672]{0,1:T(8,128)(2,1)}, u32[]{:S(2)}, u32[]{:S(2)}) collective-permute-start(bf16[256,672]{0,1:T(8,128)(2,1)} %get-tuple-element.119), channel_id=1, source_target_pairs={{4,0},{6,2},{5,1},{7,3},{12,8},{14,10},{13,9},{15,11},{20,16},{22,... | collective-permute-start | bytes 1032200 | tf_op jit(solution)/shard_map/ppermute | solution.py:107
  301.6 26.7 %collective-permute-start.33 = (bf16[256,672]{0,1:T(8,128)(2,1)S(1)}, bf16[256,672]{0,1:T(8,128)(2,1)}, u32[]{:S(2)}, u32[]{:S(2)}) collective-permute-start(bf16[256,672]{0,1:T(8,128)(2,1)S(1)} %get-tuple-element.118), channel_id=1, source_target_pairs={{0,6},{1,7},{8,14},{9,15},{16,22},{17,23},{24,30},{25,31},{32,38},... | collective-permute-start | bytes 1032200 | tf_op jit(solution)/shard_map/ppermute | solution.py:107
  309.2 19.1 %collective-permute-start.34 = (bf16[256,672]{0,1:T(8,128)(2,1)S(1)}, bf16[256,672]{0,1:T(8,128)(2,1)}, u32[]{:S(2)}, u32[]{:S(2)}) collective-permute-start(bf16[256,672]{0,1:T(8,128)(2,1)S(1)} %get-tuple-element.117), channel_id=1, source_target_pairs={{6,0},{7,1},{14,8},{15,9},{22,16},{23,17},{30,24},{31,25},{38,32},... | collective-permute-start | bytes 1032200 | tf_op jit(solution)/shard_map/ppermute | solution.py:107
  (38 other events, 439.7 us)
Sparse Core Ops, SparseCore 0:
  9.4 45.2 all-gather.1

commit v10 on v7

--- a/solution.py
+++ b/solution.py
@@ -255,7 +255,9 @@
     partial_out = out_abs.transpose(0, 3, 1, 2, 4).reshape(tok_rows, n_seq * shard_rows)
     summed_cols = reduce_scatter_tp(partial_out, dict(TP_PARTS)["zl"])
     full_width = post_gain.shape[0]
-    squares = lax.psum(jnp.sum(summed_cols * summed_cols, axis=1), TP)
+    own_squares = jnp.sum(summed_cols * summed_cols, axis=1)
+    pair_squares = own_squares + lax.ppermute(own_squares, "c", [(0, 1), (1, 0)])
+    squares = lax.psum(pair_squares, "zl")
     inverse_rms = lax.rsqrt(squares / full_width + epsilon)
     gain_part = lax.dynamic_slice_in_dim(
         post_gain, tp_at * summed_cols.shape[1], summed_cols.shape[1], 0

time: 354 us -> 353 us (level)
  blocking collectives: 14 us -> 7.44 us
    psum x1, blocking collectives: 14 us -> 7.44 us  [local(): squares = lax.psum(pair_squares, 'zl')]
  transfers between devices with their start and end apart: 36 -> 37, of which waited for: 10 -> 10; matrix products, arithmetic and copies ran while one was open for 21% -> 21% of each run, Pallas kernels for 0% -> 0%
where the time goes in v10:
time: 353 us; the launch traced here: 349 us
  starting transfers between devices  148 us (42%)
  waiting for transfers between devices  74.4 us (21%)
  local copies, waits for them, and re-layouts  48.6 us (14%)
  matrix products  29.1 us (8%)
  other arithmetic  26.9 us (8%)
  between operations  14.8 us (4%)
  blocking collectives  7.44 us (2%)
    ppermute x6, starting transfers between devices, reduce_scatter_tp(): lax.ppermute(block.astype(jnp.bfloat16), 'zl', route).astype(jnp.float32)  37.8 us
    dot_general x14, matrix products, contract(): lax.dot_general(lhs, piece, (((1, 2, 3), (0, 1, 2)), ((), ())), preferred...  21.2 us
    ppermute x1, starting transfers between devices, reduce_scatter_tp(): got = lax.ppermute(give, 'c', [(0, 1), (1, 0)])  16.9 us
    ppermute x6, waiting for transfers between devices, reduce_scatter_tp(): lax.ppermute(block.astype(jnp.bfloat16), 'zl', route).astype(jnp.float32)  16.8 us
    ppermute x4, starting transfers between devices, ring_pieces(): right = lax.ppermute(right, axis, bwd)  15.9 us
    ppermute x3, waiting for transfers between devices, ring(): right = lax.ppermute(right, axis, bwd)  15 us
    ppermute x3, starting transfers between devices, ring(): right = lax.ppermute(right, axis, bwd)  14.2 us
    ppermute x4, waiting for transfers between devices, from_behind(): return lax.ppermute(block, axis, route)  13.5 us
  transfers between devices with their start and end apart: 37, of which 10 were waited for; matrix products, arithmetic and copies ran while one was open for 21% of the time, Pallas kernels for 0%

profile of v10, /device:TPU:263, one launch (start us, length us, event | category | flops | bytes accessed | tf_op | source)
XLA Modules:
  0.0 349.0 jit_solution(15290480894422390487)
XLA Ops:
  10.2 11.4 %collective-permute-done = bf16[84,1536]{1,0:T(8,128)(2,1)S(1)} collective-permute-done((bf16[84,1536]{1,0:T(8,128)(2,1)S(1)}, bf16[84,1536]{1,0:T(8,128)(2,1)S(1)}, u32[]{:S(2)}, u32[]{:S(2)}) %collective-permute-start) | collective-permute-done | bytes 258080 | tf_op jit(solution)/shard_map/ppermute | solution.py:31
  21.6 5.1 %collective-permute-start.1 = (bf16[2,84,768]{2,1,0:T(8,128)(2,1)S(1)}, bf16[2,84,768]{2,1,0:T(8,128)(2,1)}, u32[]{:S(2)}, u32[]{:S(2)}) collective-permute-start(bf16[2,84,768]{2,1,0:T(8,128)(2,1)S(1)} %get-tuple-element.97), channel_id=1, source_target_pairs={{0,224},{32,0},{64,32},{96,64},{128,96},{160,128},{192,160},{224,1... | collective-permute-start | bytes 774152 | tf_op jit(solution)/shard_map/ppermute | solution.py:37
  38.4 4.6 %collective-permute-start.2 = (bf16[2,84,768]{2,1,0:T(8,128)(2,1)}, bf16[2,84,768]{2,1,0:T(8,128)(2,1)S(1)}, u32[]{:S(2)}, u32[]{:S(2)}) collective-permute-start(bf16[2,84,768]{2,1,0:T(8,128)(2,1)} %collective-permute-done.1), channel_id=1, source_target_pairs={{0,224},{32,0},{64,32},{96,64},{128,96},{160,128},{192,160},{224,1... | collective-permute-start | bytes 774152 | tf_op jit(solution)/shard_map/ppermute | solution.py:37
  47.7 4.6 %collective-permute-start.17 = (bf16[4,2,84,768]{3,0,2,1:T(4,128)(2,1)}, bf16[4,2,84,768]{3,0,2,1:T(4,128)(2,1)}, u32[]{:S(2)}, u32[]{:S(2)}) collective-permute-start(bf16[4,2,84,768]{3,0,2,1:T(4,128)(2,1)} %copy.137), channel_id=1, source_target_pairs={{0,224},{32,0},{64,32},{96,64},{128,96},{160,128},{192,160},{224,1... | collective-permute-start | bytes 3096584 | tf_op jit(solution)/shard_map/ppermute | solution.py:79
  54.2 4.6 %collective-permute-start.3 = (bf16[2,84,768]{2,1,0:T(8,128)(2,1)S(1)}, bf16[2,84,768]{2,1,0:T(8,128)(2,1)S(1)}, u32[]{:S(2)}, u32[]{:S(2)}) collective-permute-start(bf16[2,84,768]{2,1,0:T(8,128)(2,1)S(1)} %collective-permute-done.2), channel_id=1, source_target_pairs={{0,224},{32,0},{64,32},{96,64},{128,96},{160,128},{192,160},{224,1... | collective-permute-start | bytes 774152 | tf_op jit(solution)/shard_map/ppermute | solution.py:37
  61.7 15.0 %collective-permute-done.3 = bf16[2,84,768]{2,1,0:T(8,128)(2,1)S(1)} collective-permute-done((bf16[2,84,768]{2,1,0:T(8,128)(2,1)S(1)}, bf16[2,84,768]{2,1,0:T(8,128)(2,1)S(1)}, u32[]{:S(2)}, u32[]{:S(2)}) %collective-permute-start.3) | collective-permute-done | bytes 258080 | tf_op jit(solution)/shard_map/ppermute | solution.py:37
  76.8 5.4 %collective-permute-start.8 = (bf16[1,84,768]{2,1,0:T(8,128)(2,1)S(1)}, bf16[1,84,768]{2,1,0:T(8,128)(2,1)S(1)}, u32[]{:S(2)}, u32[]{:S(2)}) collective-permute-start(bf16[1,84,768]{2,1,0:T(8,128)(2,1)S(1)} %slice.331), channel_id=1, source_target_pairs={{0,224},{32,0},{64,32},{96,64},{128,96},{160,128},{192,160},{224,1... | collective-permute-start | bytes 387080 | tf_op jit(solution)/shard_map/ppermute | solution.py:43
  85.2 5.0 %collective-permute-done.7 = bf16[1,84,768]{2,1,0:T(8,128)(2,1)S(1)} collective-permute-done((bf16[1,84,768]{2,1,0:T(8,128)(2,1)S(1)}, bf16[1,84,768]{2,1,0:T(8,128)(2,1)S(1)}, u32[]{:S(2)}, u32[]{:S(2)}) %collective-permute-start.7) | collective-permute-done | bytes 129056 | tf_op jit(solution)/shard_map/ppermute | solution.py:42
  95.3 4.5 %collective-permute-start.9 = (bf16[8,2,84,768]{3,0,2,1:T(8,128)(2,1)}, bf16[8,2,84,768]{3,0,2,1:T(8,128)(2,1)}, u32[]{:S(2)}, u32[]{:S(2)}) collective-permute-start(bf16[8,2,84,768]{3,0,2,1:T(8,128)(2,1)} %copy.128), channel_id=1, source_target_pairs={{0,8},{8,16},{16,24},{24,0},{1,9},{9,17},{17,25},{25,1},{2,10},{10... | collective-permute-start | bytes 6193160 | tf_op jit(solution)/shard_map/ppermute | solution.py:78
  120.9 4.8 %collective-permute-start.19 = (bf16[4,2,84,768]{3,0,2,1:T(4,128)(2,1)}, bf16[4,2,84,768]{3,0,2,1:T(4,128)(2,1)}, u32[]{:S(2)}, u32[]{:S(2)}) collective-permute-start(bf16[4,2,84,768]{3,0,2,1:T(4,128)(2,1)} %collective-permute-done.17), channel_id=1, source_target_pairs={{0,224},{32,0},{64,32},{96,64},{128,96},{160,128},{192,160},{224,1... | collective-permute-start | bytes 3096584 | tf_op jit(solution)/shard_map/ppermute | solution.py:79
  127.2 7.3 %collective-permute-done.10 = bf16[8,2,84,768]{3,0,2,1:T(8,128)(2,1)} collective-permute-done((bf16[8,2,84,768]{3,0,2,1:T(8,128)(2,1)}, bf16[8,2,84,768]{3,0,2,1:T(8,128)(2,1)}, u32[]{:S(2)}, u32[]{:S(2)}) %collective-permute-start.10) | collective-permute-done | bytes 2064416 | tf_op jit(solution)/shard_map/ppermute | solution.py:79
  144.2 4.6 %collective-permute-start.21 = (bf16[4,2,84,768]{3,0,2,1:T(4,128)(2,1)}, bf16[4,2,84,768]{3,0,2,1:T(4,128)(2,1)}, u32[]{:S(2)}, u32[]{:S(2)}) collective-permute-start(bf16[4,2,84,768]{3,0,2,1:T(4,128)(2,1)} %collective-permute-done.19), channel_id=1, source_target_pairs={{0,224},{32,0},{64,32},{96,64},{128,96},{160,128},{192,160},{224,1... | collective-permute-start | bytes 3096584 | tf_op jit(solution)/shard_map/ppermute | solution.py:79
  159.5 4.4 %collective-permute-start.11 = (bf16[4,2,84,768]{3,0,2,1:T(4,128)(2,1)}, bf16[4,2,84,768]{3,0,2,1:T(4,128)(2,1)}, u32[]{:S(2)}, u32[]{:S(2)}) collective-permute-start(bf16[4,2,84,768]{3,0,2,1:T(4,128)(2,1)} %slice.296), channel_id=1, source_target_pairs={{0,8},{8,16},{16,24},{24,0},{1,9},{9,17},{17,25},{25,1},{2,10},{10... | collective-permute-start | bytes 3096584 | tf_op jit(solution)/shard_map/ppermute | solution.py:85
  186.3 4.6 %collective-permute-start.23 = (bf16[2,2,84,768]{3,1,2,0:T(2,128)(2,1)}, bf16[2,2,84,768]{3,1,2,0:T(2,128)(2,1)}, u32[]{:S(2)}, u32[]{:S(2)}) collective-permute-start(bf16[2,2,84,768]{3,1,2,0:T(2,128)(2,1)} %copy.147), channel_id=1, source_target_pairs={{0,224},{32,0},{64,32},{96,64},{128,96},{160,128},{192,160},{224,1... | collective-permute-start | bytes 1548296 | tf_op jit(solution)/shard_map/ppermute | solution.py:86
  205.2 4.0 %collective-permute-start.25 = (bf16[2,256,256]{2,1,0:T(8,128)(2,1)S(1)}, bf16[2,256,256]{2,1,0:T(8,128)(2,1)}, u32[]{:S(2)}, u32[]{:S(2)}) collective-permute-start(bf16[2,256,256]{2,1,0:T(8,128)(2,1)S(1)} %pad_maximum_fusion.4), channel_id=1, source_target_pairs={{0,24},{8,32},{16,40},{24,48},{32,56},{40,64},{48,72},{56,80},{64,... | collective-permute-start | bytes 786440 | tf_op jit(solution)/shard_map/ppermute | solution.py:22
  209.3 4.8 %collective-permute-start.24 = (bf16[2,256,256]{2,1,0:T(8,128)(2,1)S(1)}, bf16[2,256,256]{2,1,0:T(8,128)(2,1)}, u32[]{:S(2)}, u32[]{:S(2)}) collective-permute-start(bf16[2,256,256]{2,1,0:T(8,128)(2,1)S(1)} %pad_maximum_fusion.4), channel_id=1, source_target_pairs={{0,32},{8,40},{16,48},{24,56},{32,64},{40,72},{48,80},{56,88},{64,... | collective-permute-start | bytes 786440 | tf_op jit(solution)/shard_map/ppermute | solution.py:22
  216.4 13.5 %collective-permute-done.24 = bf16[2,256,256]{2,1,0:T(8,128)(2,1)} collective-permute-done((bf16[2,256,256]{2,1,0:T(8,128)(2,1)S(1)}, bf16[2,256,256]{2,1,0:T(8,128)(2,1)}, u32[]{:S(2)}, u32[]{:S(2)}) %collective-permute-start.24) | collective-permute-done | bytes 262176 | tf_op jit(solution)/shard_map/ppermute | solution.py:22
  248.9 16.9 %collective-permute-start.28 = (bf16[256,4,672]{0,2,1:T(8,128)(2,1)S(1)}, bf16[256,4,672]{0,2,1:T(8,128)(2,1)}, u32[]{:S(2)}, u32[]{:S(2)}) collective-permute-start(bf16[256,4,672]{0,2,1:T(8,128)(2,1)S(1)} %dynamic-slice_bitcast_fusion), channel_id=1, source_target_pairs={{0,1},{1,0},{2,3},{3,2},{4,5},{5,4},{6,7},{7,6},{8,9},{9,8},{10,11... | collective-permute-start | bytes 4128776 | tf_op jit(solution)/shard_map/ppermute | solution.py:99
  271.8 20.4 %collective-permute-start.29 = (bf16[256,672]{0,1:T(8,128)(2,1)S(1)}, bf16[256,672]{0,1:T(8,128)(2,1)S(1)}, u32[]{:S(2)}, u32[]{:S(2)}) collective-permute-start(bf16[256,672]{0,1:T(8,128)(2,1)S(1)} %get-tuple-element.98), channel_id=1, source_target_pairs={{0,2},{2,4},{4,6},{1,3},{3,5},{5,7},{8,10},{10,12},{12,14},{9,11},... | collective-permute-start | bytes 1032200 | tf_op jit(solution)/shard_map/ppermute | solution.py:107
  293.5 7.2 %collective-permute-start.33 = (bf16[256,672]{0,1:T(8,128)(2,1)}, bf16[256,672]{0,1:T(8,128)(2,1)}, u32[]{:S(2)}, u32[]{:S(2)}) collective-permute-start(bf16[256,672]{0,1:T(8,128)(2,1)} %get-tuple-element.100), channel_id=1, source_target_pairs={{0,6},{1,7},{8,14},{9,15},{16,22},{17,23},{24,30},{25,31},{32,38},... | collective-permute-start | bytes 1032200 | tf_op jit(solution)/shard_map/ppermute | solution.py:107
  302.1 6.3 %collective-permute-start.31 = (bf16[256,672]{0,1:T(8,128)(2,1)S(1)}, bf16[256,672]{0,1:T(8,128)(2,1)}, u32[]{:S(2)}, u32[]{:S(2)}) collective-permute-start(bf16[256,672]{0,1:T(8,128)(2,1)S(1)} %get-tuple-element.102), channel_id=1, source_target_pairs={{0,4},{2,6},{1,5},{3,7},{8,12},{10,14},{9,13},{11,15},{16,20},{18,... | collective-permute-start | bytes 1032200 | tf_op jit(solution)/shard_map/ppermute | solution.py:107
  310.4 10.6 %collective-permute-done.32 = bf16[256,672]{0,1:T(8,128)(2,1)} collective-permute-done((bf16[256,672]{0,1:T(8,128)(2,1)}, bf16[256,672]{0,1:T(8,128)(2,1)}, u32[]{:S(2)}, u32[]{:S(2)}) %collective-permute-start.32) | collective-permute-done | bytes 344096 | tf_op jit(solution)/shard_map/ppermute | solution.py:107
  321.0 6.2 %collective-permute-done.30 = bf16[256,672]{0,1:T(8,128)(2,1)} collective-permute-done((bf16[256,672]{0,1:T(8,128)(2,1)S(1)}, bf16[256,672]{0,1:T(8,128)(2,1)}, u32[]{:S(2)}, u32[]{:S(2)}) %collective-permute-start.30) | collective-permute-done | bytes 344096 | tf_op jit(solution)/shard_map/ppermute | solution.py:107
  332.9 7.4 %psum.7 = f32[256]{0:T(256)S(1)} all-reduce(f32[256]{0:T(256)S(1)} %add.268), channel_id=1, replica_groups=mesh['zh'=2,'y'=8,'x'=4,'zl'=4,'c'=2] {'zl'}, use_global_device_ids=true, to_apply=%region_7.11 | all-reduce | flops 256 | bytes 2048 | tf_op jit(solution)/shard_map/psum | solution.py:260
  (210 shorter events, 150.9 us)
Async XLA Ops:
  6.5 93.4 %all-gather.2.cloned.1.call-start = ((), (), s32[]{:S(2)}) async-start(), calls=%async_computation | async-start | bytes 3096576 | tf_op jit(solution)/shard_map/all_gather | solution.py:155
  47.7 65.3 %collective-permute-start.17 = (bf16[4,2,84,768]{3,0,2,1:T(4,128)(2,1)}, bf16[4,2,84,768]{3,0,2,1:T(4,128)(2,1)}, u32[]{:S(2)}, u32[]{:S(2)}) collective-permute-start(bf16[4,2,84,768]{3,0,2,1:T(4,128)(2,1)} %copy.137), channel_id=1, source_target_pairs={{0,224},{32,0},{64,32},{96,64},{128,96},{160,128},{192,160},{224,1... | collective-permute-start | bytes 3096584 | tf_op jit(solution)/shard_map/ppermute | solution.py:79
  52.3 62.5 %collective-permute-start.16 = (bf16[4,2,84,768]{3,0,2,1:T(4,128)(2,1)}, bf16[4,2,84,768]{3,0,2,1:T(4,128)(2,1)}, u32[]{:S(2)}, u32[]{:S(2)}) collective-permute-start(bf16[4,2,84,768]{3,0,2,1:T(4,128)(2,1)} %copy.137), channel_id=1, source_target_pairs={{0,32},{32,64},{64,96},{96,128},{128,160},{160,192},{192,224},{224... | collective-permute-start | bytes 3096584 | tf_op jit(solution)/shard_map/ppermute | solution.py:78
  54.2 22.5 %collective-permute-start.3 = (bf16[2,84,768]{2,1,0:T(8,128)(2,1)S(1)}, bf16[2,84,768]{2,1,0:T(8,128)(2,1)S(1)}, u32[]{:S(2)}, u32[]{:S(2)}) collective-permute-start(bf16[2,84,768]{2,1,0:T(8,128)(2,1)S(1)} %collective-permute-done.2), channel_id=1, source_target_pairs={{0,224},{32,0},{64,32},{96,64},{128,96},{160,128},{192,160},{224,1... | collective-permute-start | bytes 774152 | tf_op jit(solution)/shard_map/ppermute | solution.py:37
  58.8 23.4 %collective-permute-start.6 = (bf16[2,84,768]{2,1,0:T(8,128)(2,1)S(1)}, bf16[2,84,768]{2,1,0:T(8,128)(2,1)S(1)}, u32[]{:S(2)}, u32[]{:S(2)}) collective-permute-start(bf16[2,84,768]{2,1,0:T(8,128)(2,1)S(1)} %collective-permute-done.5), channel_id=1, source_target_pairs={{0,32},{32,64},{64,96},{96,128},{128,160},{160,192},{192,224},{224... | collective-permute-start | bytes 774152 | tf_op jit(solution)/shard_map/ppermute | solution.py:36
  93.4 41.1 %collective-permute-start.10 = (bf16[8,2,84,768]{3,0,2,1:T(8,128)(2,1)}, bf16[8,2,84,768]{3,0,2,1:T(8,128)(2,1)}, u32[]{:S(2)}, u32[]{:S(2)}) collective-permute-start(bf16[8,2,84,768]{3,0,2,1:T(8,128)(2,1)} %copy.128), channel_id=1, source_target_pairs={{0,24},{8,0},{16,8},{24,16},{1,25},{9,1},{17,9},{25,17},{2,26},{10... | collective-permute-start | bytes 6193160 | tf_op jit(solution)/shard_map/ppermute | solution.py:79
  95.3 40.3 %collective-permute-start.9 = (bf16[8,2,84,768]{3,0,2,1:T(8,128)(2,1)}, bf16[8,2,84,768]{3,0,2,1:T(8,128)(2,1)}, u32[]{:S(2)}, u32[]{:S(2)}) collective-permute-start(bf16[8,2,84,768]{3,0,2,1:T(8,128)(2,1)} %copy.128), channel_id=1, source_target_pairs={{0,8},{8,16},{16,24},{24,0},{1,9},{9,17},{17,25},{25,1},{2,10},{10... | collective-permute-start | bytes 6193160 | tf_op jit(solution)/shard_map/ppermute | solution.py:78
  119.0 18.5 %collective-permute-start.18 = (bf16[4,2,84,768]{3,0,2,1:T(4,128)(2,1)}, bf16[4,2,84,768]{3,0,2,1:T(4,128)(2,1)}, u32[]{:S(2)}, u32[]{:S(2)}) collective-permute-start(bf16[4,2,84,768]{3,0,2,1:T(4,128)(2,1)} %collective-permute-done.16), channel_id=1, source_target_pairs={{0,32},{32,64},{64,96},{96,128},{128,160},{160,192},{192,224},{224... | collective-permute-start | bytes 3096584 | tf_op jit(solution)/shard_map/ppermute | solution.py:78
  120.9 18.3 %collective-permute-start.19 = (bf16[4,2,84,768]{3,0,2,1:T(4,128)(2,1)}, bf16[4,2,84,768]{3,0,2,1:T(4,128)(2,1)}, u32[]{:S(2)}, u32[]{:S(2)}) collective-permute-start(bf16[4,2,84,768]{3,0,2,1:T(4,128)(2,1)} %collective-permute-done.17), channel_id=1, source_target_pairs={{0,224},{32,0},{64,32},{96,64},{128,96},{160,128},{192,160},{224,1... | collective-permute-start | bytes 3096584 | tf_op jit(solution)/shard_map/ppermute | solution.py:79
  141.8 24.4 %collective-permute-start.20 = (bf16[4,2,84,768]{3,0,2,1:T(4,128)(2,1)}, bf16[4,2,84,768]{3,0,2,1:T(4,128)(2,1)}, u32[]{:S(2)}, u32[]{:S(2)}) collective-permute-start(bf16[4,2,84,768]{3,0,2,1:T(4,128)(2,1)} %collective-permute-done.18), channel_id=1, source_target_pairs={{0,32},{32,64},{64,96},{96,128},{128,160},{160,192},{192,224},{224... | collective-permute-start | bytes 3096584 | tf_op jit(solution)/shard_map/ppermute | solution.py:78
  144.2 23.8 %collective-permute-start.21 = (bf16[4,2,84,768]{3,0,2,1:T(4,128)(2,1)}, bf16[4,2,84,768]{3,0,2,1:T(4,128)(2,1)}, u32[]{:S(2)}, u32[]{:S(2)}) collective-permute-start(bf16[4,2,84,768]{3,0,2,1:T(4,128)(2,1)} %collective-permute-done.19), channel_id=1, source_target_pairs={{0,224},{32,0},{64,32},{96,64},{128,96},{160,128},{192,160},{224,1... | collective-permute-start | bytes 3096584 | tf_op jit(solution)/shard_map/ppermute | solution.py:79
  157.4 23.7 %collective-permute-start.12 = (bf16[4,2,84,768]{3,0,2,1:T(4,128)(2,1)}, bf16[4,2,84,768]{3,0,2,1:T(4,128)(2,1)}, u32[]{:S(2)}, u32[]{:S(2)}) collective-permute-start(bf16[4,2,84,768]{3,0,2,1:T(4,128)(2,1)} %slice.299), channel_id=1, source_target_pairs={{0,24},{8,0},{16,8},{24,16},{1,25},{9,1},{17,9},{25,17},{2,26},{10... | collective-permute-start | bytes 3096584 | tf_op jit(solution)/shard_map/ppermute | solution.py:86
  159.5 22.8 %collective-permute-start.11 = (bf16[4,2,84,768]{3,0,2,1:T(4,128)(2,1)}, bf16[4,2,84,768]{3,0,2,1:T(4,128)(2,1)}, u32[]{:S(2)}, u32[]{:S(2)}) collective-permute-start(bf16[4,2,84,768]{3,0,2,1:T(4,128)(2,1)} %slice.296), channel_id=1, source_target_pairs={{0,8},{8,16},{16,24},{24,0},{1,9},{9,17},{17,25},{25,1},{2,10},{10... | collective-permute-start | bytes 3096584 | tf_op jit(solution)/shard_map/ppermute | solution.py:85
  173.3 22.8 %collective-permute-start.22 = (bf16[2,2,84,768]{3,1,2,0:T(2,128)(2,1)}, bf16[2,2,84,768]{3,1,2,0:T(2,128)(2,1)}, u32[]{:S(2)}, u32[]{:S(2)}) collective-permute-start(bf16[2,2,84,768]{3,1,2,0:T(2,128)(2,1)} %copy.145), channel_id=1, source_target_pairs={{0,32},{32,64},{64,96},{96,128},{128,160},{160,192},{192,224},{224... | collective-permute-start | bytes 1548296 | tf_op jit(solution)/shard_map/ppermute | solution.py:85
  201.3 30.7 %collective-permute-start.27 = (bf16[2,256,256]{2,1,0:T(8,128)(2,1)S(1)}, bf16[2,256,256]{2,1,0:T(8,128)(2,1)S(1)}, u32[]{:S(2)}, u32[]{:S(2)}) collective-permute-start(bf16[2,256,256]{2,1,0:T(8,128)(2,1)S(1)} %pad_maximum_fusion.4), channel_id=1, source_target_pairs={{0,8},{8,16},{16,24},{24,32},{32,40},{40,48},{48,56},{56,64},{64,7... | collective-permute-start | bytes 786440 | tf_op jit(solution)/shard_map/ppermute | solution.py:22
  203.3 28.6 %collective-permute-start.26 = (bf16[2,256,256]{2,1,0:T(8,128)(2,1)S(1)}, bf16[2,256,256]{2,1,0:T(8,128)(2,1)S(1)}, u32[]{:S(2)}, u32[]{:S(2)}) collective-permute-start(bf16[2,256,256]{2,1,0:T(8,128)(2,1)S(1)} %pad_maximum_fusion.4), channel_id=1, source_target_pairs={{0,16},{8,24},{16,32},{24,40},{32,48},{40,56},{48,64},{56,72},{64,... | collective-permute-start | bytes 786440 | tf_op jit(solution)/shard_map/ppermute | solution.py:22
  205.2 25.6 %collective-permute-start.25 = (bf16[2,256,256]{2,1,0:T(8,128)(2,1)S(1)}, bf16[2,256,256]{2,1,0:T(8,128)(2,1)}, u32[]{:S(2)}, u32[]{:S(2)}) collective-permute-start(bf16[2,256,256]{2,1,0:T(8,128)(2,1)S(1)} %pad_maximum_fusion.4), channel_id=1, source_target_pairs={{0,24},{8,32},{16,40},{24,48},{32,56},{40,64},{48,72},{56,80},{64,... | collective-permute-start | bytes 786440 | tf_op jit(solution)/shard_map/ppermute | solution.py:22
  209.3 20.6 %collective-permute-start.24 = (bf16[2,256,256]{2,1,0:T(8,128)(2,1)S(1)}, bf16[2,256,256]{2,1,0:T(8,128)(2,1)}, u32[]{:S(2)}, u32[]{:S(2)}) collective-permute-start(bf16[2,256,256]{2,1,0:T(8,128)(2,1)S(1)} %pad_maximum_fusion.4), channel_id=1, source_target_pairs={{0,32},{8,40},{16,48},{24,56},{32,64},{40,72},{48,80},{56,88},{64,... | collective-permute-start | bytes 786440 | tf_op jit(solution)/shard_map/ppermute | solution.py:22
  248.9 19.8 %collective-permute-start.28 = (bf16[256,4,672]{0,2,1:T(8,128)(2,1)S(1)}, bf16[256,4,672]{0,2,1:T(8,128)(2,1)}, u32[]{:S(2)}, u32[]{:S(2)}) collective-permute-start(bf16[256,4,672]{0,2,1:T(8,128)(2,1)S(1)} %dynamic-slice_bitcast_fusion), channel_id=1, source_target_pairs={{0,1},{1,0},{2,3},{3,2},{4,5},{5,4},{6,7},{7,6},{8,9},{9,8},{10,11... | collective-permute-start | bytes 4128776 | tf_op jit(solution)/shard_map/ppermute | solution.py:99
  271.8 36.6 %collective-permute-start.29 = (bf16[256,672]{0,1:T(8,128)(2,1)S(1)}, bf16[256,672]{0,1:T(8,128)(2,1)S(1)}, u32[]{:S(2)}, u32[]{:S(2)}) collective-permute-start(bf16[256,672]{0,1:T(8,128)(2,1)S(1)} %get-tuple-element.98), channel_id=1, source_target_pairs={{0,2},{2,4},{4,6},{1,3},{3,5},{5,7},{8,10},{10,12},{12,14},{9,11},... | collective-permute-start | bytes 1032200 | tf_op jit(solution)/shard_map/ppermute | solution.py:107
  292.2 18.2 %collective-permute-start.34 = (bf16[256,672]{0,1:T(8,128)(2,1)}, bf16[256,672]{0,1:T(8,128)(2,1)}, u32[]{:S(2)}, u32[]{:S(2)}) collective-permute-start(bf16[256,672]{0,1:T(8,128)(2,1)} %get-tuple-element.99), channel_id=1, source_target_pairs={{6,0},{7,1},{14,8},{15,9},{22,16},{23,17},{30,24},{31,25},{38,32},... | collective-permute-start | bytes 1032200 | tf_op jit(solution)/shard_map/ppermute | solution.py:107
  300.8 20.2 %collective-permute-start.32 = (bf16[256,672]{0,1:T(8,128)(2,1)}, bf16[256,672]{0,1:T(8,128)(2,1)}, u32[]{:S(2)}, u32[]{:S(2)}) collective-permute-start(bf16[256,672]{0,1:T(8,128)(2,1)} %get-tuple-element.101), channel_id=1, source_target_pairs={{4,0},{6,2},{5,1},{7,3},{12,8},{14,10},{13,9},{15,11},{20,16},{22,... | collective-permute-start | bytes 1032200 | tf_op jit(solution)/shard_map/ppermute | solution.py:107
  302.1 18.9 %collective-permute-start.31 = (bf16[256,672]{0,1:T(8,128)(2,1)S(1)}, bf16[256,672]{0,1:T(8,128)(2,1)}, u32[]{:S(2)}, u32[]{:S(2)}) collective-permute-start(bf16[256,672]{0,1:T(8,128)(2,1)S(1)} %get-tuple-element.102), channel_id=1, source_target_pairs={{0,4},{2,6},{1,5},{3,7},{8,12},{10,14},{9,13},{11,15},{16,20},{18,... | collective-permute-start | bytes 1032200 | tf_op jit(solution)/shard_map/ppermute | solution.py:107
  309.1 18.1 %collective-permute-start.30 = (bf16[256,672]{0,1:T(8,128)(2,1)S(1)}, bf16[256,672]{0,1:T(8,128)(2,1)}, u32[]{:S(2)}, u32[]{:S(2)}) collective-permute-start(bf16[256,672]{0,1:T(8,128)(2,1)S(1)} %get-tuple-element.103), channel_id=1, source_target_pairs={{2,0},{4,2},{6,4},{3,1},{5,3},{7,5},{10,8},{12,10},{14,12},{11,9},... | collective-permute-start | bytes 1032200 | tf_op jit(solution)/shard_map/ppermute | solution.py:107
  (36 other events, 321.0 us)
Sparse Core Ops, SparseCore 0:
  9.4 45.3 all-gather.1

commit v11 on v10

--- a/solution.py
+++ b/solution.py
@@ -257,7 +257,12 @@
     full_width = post_gain.shape[0]
     own_squares = jnp.sum(summed_cols * summed_cols, axis=1)
     pair_squares = own_squares + lax.ppermute(own_squares, "c", [(0, 1), (1, 0)])
-    squares = lax.psum(pair_squares, "zl")
+    squares = pair_squares
+    n_zl = dict(TP_PARTS)["zl"]
+    step = 1
+    while step < n_zl:
+        squares = squares + lax.ppermute(squares, "zl", [(i, i ^ step) for i in range(n_zl)])
+        step *= 2
     inverse_rms = lax.rsqrt(squares / full_width + epsilon)
     gain_part = lax.dynamic_slice_in_dim(
         post_gain, tp_at * summed_cols.shape[1], summed_cols.shape[1], 0

time: 353 us -> 355 us (level)
  blocking collectives: 7.44 us -> 0 us
  waiting for transfers between devices: 74.4 us -> 79.3 us
  starting transfers between devices: 148 us -> 152 us
    psum x1 -> x0, blocking collectives: 7.44 us -> none  [local(): squares = lax.psum(pair_squares, 'zl')]
    ppermute x0 -> x2, starting transfers between devices: none -> 4.65 us  [local(): lax.ppermute(squares, 'zl', [(i, i ^ step) for i in range(n_zl)])]
    ppermute x0 -> x2, waiting for transfers between devices: none -> 4.05 us  [local(): lax.ppermute(squares, 'zl', [(i, i ^ step) for i in range(n_zl)])]
  transfers between devices with their start and end apart: 37 -> 39, of which waited for: 10 -> 13; matrix products, arithmetic and copies ran while one was open for 21% -> 21% of each run, Pallas kernels for 0% -> 0%
where the time goes in v11:
time: 355 us; the launch traced here: 351 us
  starting transfers between devices  152 us (43%)
  waiting for transfers between devices  79.3 us (22%)
  local copies, waits for them, and re-layouts  48.5 us (14%)
  matrix products  29.1 us (8%)
  other arithmetic  26.9 us (8%)
  between operations  14.8 us (4%)
    ppermute x6, starting transfers between devices, reduce_scatter_tp(): lax.ppermute(block.astype(jnp.bfloat16), 'zl', route).astype(jnp.float32)  37.8 us
    dot_general x14, matrix products, contract(): lax.dot_general(lhs, piece, (((1, 2, 3), (0, 1, 2)), ((), ())), preferred...  21.2 us
    ppermute x1, starting transfers between devices, reduce_scatter_tp(): got = lax.ppermute(give, 'c', [(0, 1), (1, 0)])  16.9 us
    ppermute x6, waiting for transfers between devices, reduce_scatter_tp(): lax.ppermute(block.astype(jnp.bfloat16), 'zl', route).astype(jnp.float32)  16.8 us
    ppermute x4, starting transfers between devices, ring_pieces(): right = lax.ppermute(right, axis, bwd)  15.9 us
    ppermute x3, waiting for transfers between devices, ring(): right = lax.ppermute(right, axis, bwd)  15 us
    ppermute x3, starting transfers between devices, ring(): right = lax.ppermute(right, axis, bwd)  14.2 us
    ppermute x4, waiting for transfers between devices, from_behind(): return lax.ppermute(block, axis, route)  13.6 us
  transfers between devices with their start and end apart: 39, of which 13 were waited for; matrix products, arithmetic and copies ran while one was open for 21% of the time, Pallas kernels for 0%

profile of v11, /device:TPU:263, one launch (start us, length us, event | category | flops | bytes accessed | tf_op | source)
XLA Modules:
  0.0 350.9 jit_solution(17705175732135647885)
XLA Ops:
  10.2 11.4 %collective-permute-done = bf16[84,1536]{1,0:T(8,128)(2,1)S(1)} collective-permute-done((bf16[84,1536]{1,0:T(8,128)(2,1)S(1)}, bf16[84,1536]{1,0:T(8,128)(2,1)S(1)}, u32[]{:S(2)}, u32[]{:S(2)}) %collective-permute-start) | collective-permute-done | bytes 258080 | tf_op jit(solution)/shard_map/ppermute | solution.py:31
  21.6 5.1 %collective-permute-start.1 = (bf16[2,84,768]{2,1,0:T(8,128)(2,1)S(1)}, bf16[2,84,768]{2,1,0:T(8,128)(2,1)}, u32[]{:S(2)}, u32[]{:S(2)}) collective-permute-start(bf16[2,84,768]{2,1,0:T(8,128)(2,1)S(1)} %get-tuple-element.97), channel_id=1, source_target_pairs={{0,224},{32,0},{64,32},{96,64},{128,96},{160,128},{192,160},{224,1... | collective-permute-start | bytes 774152 | tf_op jit(solution)/shard_map/ppermute | solution.py:37
  34.6 3.7 %collective-permute-start.15 = (bf16[2,84,768]{2,1,0:T(8,128)(2,1)}, bf16[2,84,768]{2,1,0:T(8,128)(2,1)}, u32[]{:S(2)}, u32[]{:S(2)}) collective-permute-start(bf16[2,84,768]{2,1,0:T(8,128)(2,1)} %pad_maximum_fusion.1), channel_id=1, source_target_pairs={{0,8},{8,16},{16,24},{24,0},{1,9},{9,17},{17,25},{25,1},{2,10},{10... | collective-permute-start | bytes 774152 | tf_op jit(solution)/shard_map/ppermute | solution.py:56
  38.4 4.6 %collective-permute-start.2 = (bf16[2,84,768]{2,1,0:T(8,128)(2,1)}, bf16[2,84,768]{2,1,0:T(8,128)(2,1)S(1)}, u32[]{:S(2)}, u32[]{:S(2)}) collective-permute-start(bf16[2,84,768]{2,1,0:T(8,128)(2,1)} %collective-permute-done.1), channel_id=1, source_target_pairs={{0,224},{32,0},{64,32},{96,64},{128,96},{160,128},{192,160},{224,1... | collective-permute-start | bytes 774152 | tf_op jit(solution)/shard_map/ppermute | solution.py:37
  47.7 4.6 %collective-permute-start.17 = (bf16[4,2,84,768]{3,0,2,1:T(4,128)(2,1)}, bf16[4,2,84,768]{3,0,2,1:T(4,128)(2,1)}, u32[]{:S(2)}, u32[]{:S(2)}) collective-permute-start(bf16[4,2,84,768]{3,0,2,1:T(4,128)(2,1)} %copy.137), channel_id=1, source_target_pairs={{0,224},{32,0},{64,32},{96,64},{128,96},{160,128},{192,160},{224,1... | collective-permute-start | bytes 3096584 | tf_op jit(solution)/shard_map/ppermute | solution.py:79
  54.2 4.6 %collective-permute-start.3 = (bf16[2,84,768]{2,1,0:T(8,128)(2,1)S(1)}, bf16[2,84,768]{2,1,0:T(8,128)(2,1)S(1)}, u32[]{:S(2)}, u32[]{:S(2)}) collective-permute-start(bf16[2,84,768]{2,1,0:T(8,128)(2,1)S(1)} %collective-permute-done.2), channel_id=1, source_target_pairs={{0,224},{32,0},{64,32},{96,64},{128,96},{160,128},{192,160},{224,1... | collective-permute-start | bytes 774152 | tf_op jit(solution)/shard_map/ppermute | solution.py:37
  61.7 15.0 %collective-permute-done.3 = bf16[2,84,768]{2,1,0:T(8,128)(2,1)S(1)} collective-permute-done((bf16[2,84,768]{2,1,0:T(8,128)(2,1)S(1)}, bf16[2,84,768]{2,1,0:T(8,128)(2,1)S(1)}, u32[]{:S(2)}, u32[]{:S(2)}) %collective-permute-start.3) | collective-permute-done | bytes 258080 | tf_op jit(solution)/shard_map/ppermute | solution.py:37
  76.8 5.4 %collective-permute-start.8 = (bf16[1,84,768]{2,1,0:T(8,128)(2,1)S(1)}, bf16[1,84,768]{2,1,0:T(8,128)(2,1)S(1)}, u32[]{:S(2)}, u32[]{:S(2)}) collective-permute-start(bf16[1,84,768]{2,1,0:T(8,128)(2,1)S(1)} %slice.331), channel_id=1, source_target_pairs={{0,224},{32,0},{64,32},{96,64},{128,96},{160,128},{192,160},{224,1... | collective-permute-start | bytes 387080 | tf_op jit(solution)/shard_map/ppermute | solution.py:43
  85.2 5.0 %collective-permute-done.7 = bf16[1,84,768]{2,1,0:T(8,128)(2,1)S(1)} collective-permute-done((bf16[1,84,768]{2,1,0:T(8,128)(2,1)S(1)}, bf16[1,84,768]{2,1,0:T(8,128)(2,1)S(1)}, u32[]{:S(2)}, u32[]{:S(2)}) %collective-permute-start.7) | collective-permute-done | bytes 129056 | tf_op jit(solution)/shard_map/ppermute | solution.py:42
  95.3 4.5 %collective-permute-start.9 = (bf16[8,2,84,768]{3,0,2,1:T(8,128)(2,1)}, bf16[8,2,84,768]{3,0,2,1:T(8,128)(2,1)}, u32[]{:S(2)}, u32[]{:S(2)}) collective-permute-start(bf16[8,2,84,768]{3,0,2,1:T(8,128)(2,1)} %copy.128), channel_id=1, source_target_pairs={{0,8},{8,16},{16,24},{24,0},{1,9},{9,17},{17,25},{25,1},{2,10},{10... | collective-permute-start | bytes 6193160 | tf_op jit(solution)/shard_map/ppermute | solution.py:78
  120.9 4.8 %collective-permute-start.19 = (bf16[4,2,84,768]{3,0,2,1:T(4,128)(2,1)}, bf16[4,2,84,768]{3,0,2,1:T(4,128)(2,1)}, u32[]{:S(2)}, u32[]{:S(2)}) collective-permute-start(bf16[4,2,84,768]{3,0,2,1:T(4,128)(2,1)} %collective-permute-done.17), channel_id=1, source_target_pairs={{0,224},{32,0},{64,32},{96,64},{128,96},{160,128},{192,160},{224,1... | collective-permute-start | bytes 3096584 | tf_op jit(solution)/shard_map/ppermute | solution.py:79
  127.2 7.3 %collective-permute-done.10 = bf16[8,2,84,768]{3,0,2,1:T(8,128)(2,1)} collective-permute-done((bf16[8,2,84,768]{3,0,2,1:T(8,128)(2,1)}, bf16[8,2,84,768]{3,0,2,1:T(8,128)(2,1)}, u32[]{:S(2)}, u32[]{:S(2)}) %collective-permute-start.10) | collective-permute-done | bytes 2064416 | tf_op jit(solution)/shard_map/ppermute | solution.py:79
  144.2 4.6 %collective-permute-start.21 = (bf16[4,2,84,768]{3,0,2,1:T(4,128)(2,1)}, bf16[4,2,84,768]{3,0,2,1:T(4,128)(2,1)}, u32[]{:S(2)}, u32[]{:S(2)}) collective-permute-start(bf16[4,2,84,768]{3,0,2,1:T(4,128)(2,1)} %collective-permute-done.19), channel_id=1, source_target_pairs={{0,224},{32,0},{64,32},{96,64},{128,96},{160,128},{192,160},{224,1... | collective-permute-start | bytes 3096584 | tf_op jit(solution)/shard_map/ppermute | solution.py:79
  159.4 4.4 %collective-permute-start.11 = (bf16[4,2,84,768]{3,0,2,1:T(4,128)(2,1)}, bf16[4,2,84,768]{3,0,2,1:T(4,128)(2,1)}, u32[]{:S(2)}, u32[]{:S(2)}) collective-permute-start(bf16[4,2,84,768]{3,0,2,1:T(4,128)(2,1)} %slice.296), channel_id=1, source_target_pairs={{0,8},{8,16},{16,24},{24,0},{1,9},{9,17},{17,25},{25,1},{2,10},{10... | collective-permute-start | bytes 3096584 | tf_op jit(solution)/shard_map/ppermute | solution.py:85
  186.2 4.6 %collective-permute-start.23 = (bf16[2,2,84,768]{3,1,2,0:T(2,128)(2,1)}, bf16[2,2,84,768]{3,1,2,0:T(2,128)(2,1)}, u32[]{:S(2)}, u32[]{:S(2)}) collective-permute-start(bf16[2,2,84,768]{3,1,2,0:T(2,128)(2,1)} %copy.147), channel_id=1, source_target_pairs={{0,224},{32,0},{64,32},{96,64},{128,96},{160,128},{192,160},{224,1... | collective-permute-start | bytes 1548296 | tf_op jit(solution)/shard_map/ppermute | solution.py:86
  205.2 4.0 %collective-permute-start.25 = (bf16[2,256,256]{2,1,0:T(8,128)(2,1)S(1)}, bf16[2,256,256]{2,1,0:T(8,128)(2,1)}, u32[]{:S(2)}, u32[]{:S(2)}) collective-permute-start(bf16[2,256,256]{2,1,0:T(8,128)(2,1)S(1)} %pad_maximum_fusion.4), channel_id=1, source_target_pairs={{0,24},{8,32},{16,40},{24,48},{32,56},{40,64},{48,72},{56,80},{64,... | collective-permute-start | bytes 786440 | tf_op jit(solution)/shard_map/ppermute | solution.py:22
  209.2 4.8 %collective-permute-start.24 = (bf16[2,256,256]{2,1,0:T(8,128)(2,1)S(1)}, bf16[2,256,256]{2,1,0:T(8,128)(2,1)}, u32[]{:S(2)}, u32[]{:S(2)}) collective-permute-start(bf16[2,256,256]{2,1,0:T(8,128)(2,1)S(1)} %pad_maximum_fusion.4), channel_id=1, source_target_pairs={{0,32},{8,40},{16,48},{24,56},{32,64},{40,72},{48,80},{56,88},{64,... | collective-permute-start | bytes 786440 | tf_op jit(solution)/shard_map/ppermute | solution.py:22
  216.2 13.6 %collective-permute-done.24 = bf16[2,256,256]{2,1,0:T(8,128)(2,1)} collective-permute-done((bf16[2,256,256]{2,1,0:T(8,128)(2,1)S(1)}, bf16[2,256,256]{2,1,0:T(8,128)(2,1)}, u32[]{:S(2)}, u32[]{:S(2)}) %collective-permute-start.24) | collective-permute-done | bytes 262176 | tf_op jit(solution)/shard_map/ppermute | solution.py:22
  248.7 16.9 %collective-permute-start.28 = (bf16[256,4,672]{0,2,1:T(8,128)(2,1)S(1)}, bf16[256,4,672]{0,2,1:T(8,128)(2,1)}, u32[]{:S(2)}, u32[]{:S(2)}) collective-permute-start(bf16[256,4,672]{0,2,1:T(8,128)(2,1)S(1)} %dynamic-slice_bitcast_fusion), channel_id=1, source_target_pairs={{0,1},{1,0},{2,3},{3,2},{4,5},{5,4},{6,7},{7,6},{8,9},{9,8},{10,11... | collective-permute-start | bytes 4128776 | tf_op jit(solution)/shard_map/ppermute | solution.py:99
  271.7 20.4 %collective-permute-start.29 = (bf16[256,672]{0,1:T(8,128)(2,1)S(1)}, bf16[256,672]{0,1:T(8,128)(2,1)S(1)}, u32[]{:S(2)}, u32[]{:S(2)}) collective-permute-start(bf16[256,672]{0,1:T(8,128)(2,1)S(1)} %get-tuple-element.98), channel_id=1, source_target_pairs={{0,2},{2,4},{4,6},{1,3},{3,5},{5,7},{8,10},{10,12},{12,14},{9,11},... | collective-permute-start | bytes 1032200 | tf_op jit(solution)/shard_map/ppermute | solution.py:107
  293.3 7.2 %collective-permute-start.33 = (bf16[256,672]{0,1:T(8,128)(2,1)}, bf16[256,672]{0,1:T(8,128)(2,1)}, u32[]{:S(2)}, u32[]{:S(2)}) collective-permute-start(bf16[256,672]{0,1:T(8,128)(2,1)} %get-tuple-element.100), channel_id=1, source_target_pairs={{0,6},{1,7},{8,14},{9,15},{16,22},{17,23},{24,30},{25,31},{32,38},... | collective-permute-start | bytes 1032200 | tf_op jit(solution)/shard_map/ppermute | solution.py:107
  301.9 6.3 %collective-permute-start.31 = (bf16[256,672]{0,1:T(8,128)(2,1)S(1)}, bf16[256,672]{0,1:T(8,128)(2,1)}, u32[]{:S(2)}, u32[]{:S(2)}) collective-permute-start(bf16[256,672]{0,1:T(8,128)(2,1)S(1)} %get-tuple-element.102), channel_id=1, source_target_pairs={{0,4},{2,6},{1,5},{3,7},{8,12},{10,14},{9,13},{11,15},{16,20},{18,... | collective-permute-start | bytes 1032200 | tf_op jit(solution)/shard_map/ppermute | solution.py:107
  310.3 10.6 %collective-permute-done.32 = bf16[256,672]{0,1:T(8,128)(2,1)} collective-permute-done((bf16[256,672]{0,1:T(8,128)(2,1)}, bf16[256,672]{0,1:T(8,128)(2,1)}, u32[]{:S(2)}, u32[]{:S(2)}) %collective-permute-start.32) | collective-permute-done | bytes 344096 | tf_op jit(solution)/shard_map/ppermute | solution.py:107
  320.8 6.2 %collective-permute-done.30 = bf16[256,672]{0,1:T(8,128)(2,1)} collective-permute-done((bf16[256,672]{0,1:T(8,128)(2,1)S(1)}, bf16[256,672]{0,1:T(8,128)(2,1)}, u32[]{:S(2)}, u32[]{:S(2)}) %collective-permute-start.30) | collective-permute-done | bytes 344096 | tf_op jit(solution)/shard_map/ppermute | solution.py:107
  (214 shorter events, 156.6 us)
Async XLA Ops:
  6.5 93.3 %all-gather.2.cloned.1.call-start = ((), (), s32[]{:S(2)}) async-start(), calls=%async_computation | async-start | bytes 3096576 | tf_op jit(solution)/shard_map/all_gather | solution.py:155
  47.7 65.3 %collective-permute-start.17 = (bf16[4,2,84,768]{3,0,2,1:T(4,128)(2,1)}, bf16[4,2,84,768]{3,0,2,1:T(4,128)(2,1)}, u32[]{:S(2)}, u32[]{:S(2)}) collective-permute-start(bf16[4,2,84,768]{3,0,2,1:T(4,128)(2,1)} %copy.137), channel_id=1, source_target_pairs={{0,224},{32,0},{64,32},{96,64},{128,96},{160,128},{192,160},{224,1... | collective-permute-start | bytes 3096584 | tf_op jit(solution)/shard_map/ppermute | solution.py:79
  52.3 62.5 %collective-permute-start.16 = (bf16[4,2,84,768]{3,0,2,1:T(4,128)(2,1)}, bf16[4,2,84,768]{3,0,2,1:T(4,128)(2,1)}, u32[]{:S(2)}, u32[]{:S(2)}) collective-permute-start(bf16[4,2,84,768]{3,0,2,1:T(4,128)(2,1)} %copy.137), channel_id=1, source_target_pairs={{0,32},{32,64},{64,96},{96,128},{128,160},{160,192},{192,224},{224... | collective-permute-start | bytes 3096584 | tf_op jit(solution)/shard_map/ppermute | solution.py:78
  54.2 22.5 %collective-permute-start.3 = (bf16[2,84,768]{2,1,0:T(8,128)(2,1)S(1)}, bf16[2,84,768]{2,1,0:T(8,128)(2,1)S(1)}, u32[]{:S(2)}, u32[]{:S(2)}) collective-permute-start(bf16[2,84,768]{2,1,0:T(8,128)(2,1)S(1)} %collective-permute-done.2), channel_id=1, source_target_pairs={{0,224},{32,0},{64,32},{96,64},{128,96},{160,128},{192,160},{224,1... | collective-permute-start | bytes 774152 | tf_op jit(solution)/shard_map/ppermute | solution.py:37
  58.8 23.4 %collective-permute-start.6 = (bf16[2,84,768]{2,1,0:T(8,128)(2,1)S(1)}, bf16[2,84,768]{2,1,0:T(8,128)(2,1)S(1)}, u32[]{:S(2)}, u32[]{:S(2)}) collective-permute-start(bf16[2,84,768]{2,1,0:T(8,128)(2,1)S(1)} %collective-permute-done.5), channel_id=1, source_target_pairs={{0,32},{32,64},{64,96},{96,128},{128,160},{160,192},{192,224},{224... | collective-permute-start | bytes 774152 | tf_op jit(solution)/shard_map/ppermute | solution.py:36
  93.4 41.1 %collective-permute-start.10 = (bf16[8,2,84,768]{3,0,2,1:T(8,128)(2,1)}, bf16[8,2,84,768]{3,0,2,1:T(8,128)(2,1)}, u32[]{:S(2)}, u32[]{:S(2)}) collective-permute-start(bf16[8,2,84,768]{3,0,2,1:T(8,128)(2,1)} %copy.128), channel_id=1, source_target_pairs={{0,24},{8,0},{16,8},{24,16},{1,25},{9,1},{17,9},{25,17},{2,26},{10... | collective-permute-start | bytes 6193160 | tf_op jit(solution)/shard_map/ppermute | solution.py:79
  95.3 40.3 %collective-permute-start.9 = (bf16[8,2,84,768]{3,0,2,1:T(8,128)(2,1)}, bf16[8,2,84,768]{3,0,2,1:T(8,128)(2,1)}, u32[]{:S(2)}, u32[]{:S(2)}) collective-permute-start(bf16[8,2,84,768]{3,0,2,1:T(8,128)(2,1)} %copy.128), channel_id=1, source_target_pairs={{0,8},{8,16},{16,24},{24,0},{1,9},{9,17},{17,25},{25,1},{2,10},{10... | collective-permute-start | bytes 6193160 | tf_op jit(solution)/shard_map/ppermute | solution.py:78
  119.0 18.5 %collective-permute-start.18 = (bf16[4,2,84,768]{3,0,2,1:T(4,128)(2,1)}, bf16[4,2,84,768]{3,0,2,1:T(4,128)(2,1)}, u32[]{:S(2)}, u32[]{:S(2)}) collective-permute-start(bf16[4,2,84,768]{3,0,2,1:T(4,128)(2,1)} %collective-permute-done.16), channel_id=1, source_target_pairs={{0,32},{32,64},{64,96},{96,128},{128,160},{160,192},{192,224},{224... | collective-permute-start | bytes 3096584 | tf_op jit(solution)/shard_map/ppermute | solution.py:78
  120.9 18.3 %collective-permute-start.19 = (bf16[4,2,84,768]{3,0,2,1:T(4,128)(2,1)}, bf16[4,2,84,768]{3,0,2,1:T(4,128)(2,1)}, u32[]{:S(2)}, u32[]{:S(2)}) collective-permute-start(bf16[4,2,84,768]{3,0,2,1:T(4,128)(2,1)} %collective-permute-done.17), channel_id=1, source_target_pairs={{0,224},{32,0},{64,32},{96,64},{128,96},{160,128},{192,160},{224,1... | collective-permute-start | bytes 3096584 | tf_op jit(solution)/shard_map/ppermute | solution.py:79
  141.8 24.4 %collective-permute-start.20 = (bf16[4,2,84,768]{3,0,2,1:T(4,128)(2,1)}, bf16[4,2,84,768]{3,0,2,1:T(4,128)(2,1)}, u32[]{:S(2)}, u32[]{:S(2)}) collective-permute-start(bf16[4,2,84,768]{3,0,2,1:T(4,128)(2,1)} %collective-permute-done.18), channel_id=1, source_target_pairs={{0,32},{32,64},{64,96},{96,128},{128,160},{160,192},{192,224},{224... | collective-permute-start | bytes 3096584 | tf_op jit(solution)/shard_map/ppermute | solution.py:78
  144.2 23.7 %collective-permute-start.21 = (bf16[4,2,84,768]{3,0,2,1:T(4,128)(2,1)}, bf16[4,2,84,768]{3,0,2,1:T(4,128)(2,1)}, u32[]{:S(2)}, u32[]{:S(2)}) collective-permute-start(bf16[4,2,84,768]{3,0,2,1:T(4,128)(2,1)} %collective-permute-done.19), channel_id=1, source_target_pairs={{0,224},{32,0},{64,32},{96,64},{128,96},{160,128},{192,160},{224,1... | collective-permute-start | bytes 3096584 | tf_op jit(solution)/shard_map/ppermute | solution.py:79
  157.4 23.6 %collective-permute-start.12 = (bf16[4,2,84,768]{3,0,2,1:T(4,128)(2,1)}, bf16[4,2,84,768]{3,0,2,1:T(4,128)(2,1)}, u32[]{:S(2)}, u32[]{:S(2)}) collective-permute-start(bf16[4,2,84,768]{3,0,2,1:T(4,128)(2,1)} %slice.299), channel_id=1, source_target_pairs={{0,24},{8,0},{16,8},{24,16},{1,25},{9,1},{17,9},{25,17},{2,26},{10... | collective-permute-start | bytes 3096584 | tf_op jit(solution)/shard_map/ppermute | solution.py:86
  159.4 22.7 %collective-permute-start.11 = (bf16[4,2,84,768]{3,0,2,1:T(4,128)(2,1)}, bf16[4,2,84,768]{3,0,2,1:T(4,128)(2,1)}, u32[]{:S(2)}, u32[]{:S(2)}) collective-permute-start(bf16[4,2,84,768]{3,0,2,1:T(4,128)(2,1)} %slice.296), channel_id=1, source_target_pairs={{0,8},{8,16},{16,24},{24,0},{1,9},{9,17},{17,25},{25,1},{2,10},{10... | collective-permute-start | bytes 3096584 | tf_op jit(solution)/shard_map/ppermute | solution.py:85
  173.3 22.8 %collective-permute-start.22 = (bf16[2,2,84,768]{3,1,2,0:T(2,128)(2,1)}, bf16[2,2,84,768]{3,1,2,0:T(2,128)(2,1)}, u32[]{:S(2)}, u32[]{:S(2)}) collective-permute-start(bf16[2,2,84,768]{3,1,2,0:T(2,128)(2,1)} %copy.145), channel_id=1, source_target_pairs={{0,32},{32,64},{64,96},{96,128},{128,160},{160,192},{192,224},{224... | collective-permute-start | bytes 1548296 | tf_op jit(solution)/shard_map/ppermute | solution.py:85
  201.2 30.7 %collective-permute-start.27 = (bf16[2,256,256]{2,1,0:T(8,128)(2,1)S(1)}, bf16[2,256,256]{2,1,0:T(8,128)(2,1)S(1)}, u32[]{:S(2)}, u32[]{:S(2)}) collective-permute-start(bf16[2,256,256]{2,1,0:T(8,128)(2,1)S(1)} %pad_maximum_fusion.4), channel_id=1, source_target_pairs={{0,8},{8,16},{16,24},{24,32},{32,40},{40,48},{48,56},{56,64},{64,7... | collective-permute-start | bytes 786440 | tf_op jit(solution)/shard_map/ppermute | solution.py:22
  203.3 28.5 %collective-permute-start.26 = (bf16[2,256,256]{2,1,0:T(8,128)(2,1)S(1)}, bf16[2,256,256]{2,1,0:T(8,128)(2,1)S(1)}, u32[]{:S(2)}, u32[]{:S(2)}) collective-permute-start(bf16[2,256,256]{2,1,0:T(8,128)(2,1)S(1)} %pad_maximum_fusion.4), channel_id=1, source_target_pairs={{0,16},{8,24},{16,32},{24,40},{32,48},{40,56},{48,64},{56,72},{64,... | collective-permute-start | bytes 786440 | tf_op jit(solution)/shard_map/ppermute | solution.py:22
  205.2 25.6 %collective-permute-start.25 = (bf16[2,256,256]{2,1,0:T(8,128)(2,1)S(1)}, bf16[2,256,256]{2,1,0:T(8,128)(2,1)}, u32[]{:S(2)}, u32[]{:S(2)}) collective-permute-start(bf16[2,256,256]{2,1,0:T(8,128)(2,1)S(1)} %pad_maximum_fusion.4), channel_id=1, source_target_pairs={{0,24},{8,32},{16,40},{24,48},{32,56},{40,64},{48,72},{56,80},{64,... | collective-permute-start | bytes 786440 | tf_op jit(solution)/shard_map/ppermute | solution.py:22
  209.2 20.6 %collective-permute-start.24 = (bf16[2,256,256]{2,1,0:T(8,128)(2,1)S(1)}, bf16[2,256,256]{2,1,0:T(8,128)(2,1)}, u32[]{:S(2)}, u32[]{:S(2)}) collective-permute-start(bf16[2,256,256]{2,1,0:T(8,128)(2,1)S(1)} %pad_maximum_fusion.4), channel_id=1, source_target_pairs={{0,32},{8,40},{16,48},{24,56},{32,64},{40,72},{48,80},{56,88},{64,... | collective-permute-start | bytes 786440 | tf_op jit(solution)/shard_map/ppermute | solution.py:22
  248.7 19.8 %collective-permute-start.28 = (bf16[256,4,672]{0,2,1:T(8,128)(2,1)S(1)}, bf16[256,4,672]{0,2,1:T(8,128)(2,1)}, u32[]{:S(2)}, u32[]{:S(2)}) collective-permute-start(bf16[256,4,672]{0,2,1:T(8,128)(2,1)S(1)} %dynamic-slice_bitcast_fusion), channel_id=1, source_target_pairs={{0,1},{1,0},{2,3},{3,2},{4,5},{5,4},{6,7},{7,6},{8,9},{9,8},{10,11... | collective-permute-start | bytes 4128776 | tf_op jit(solution)/shard_map/ppermute | solution.py:99
  271.7 36.5 %collective-permute-start.29 = (bf16[256,672]{0,1:T(8,128)(2,1)S(1)}, bf16[256,672]{0,1:T(8,128)(2,1)S(1)}, u32[]{:S(2)}, u32[]{:S(2)}) collective-permute-start(bf16[256,672]{0,1:T(8,128)(2,1)S(1)} %get-tuple-element.98), channel_id=1, source_target_pairs={{0,2},{2,4},{4,6},{1,3},{3,5},{5,7},{8,10},{10,12},{12,14},{9,11},... | collective-permute-start | bytes 1032200 | tf_op jit(solution)/shard_map/ppermute | solution.py:107
  292.0 18.2 %collective-permute-start.34 = (bf16[256,672]{0,1:T(8,128)(2,1)}, bf16[256,672]{0,1:T(8,128)(2,1)}, u32[]{:S(2)}, u32[]{:S(2)}) collective-permute-start(bf16[256,672]{0,1:T(8,128)(2,1)} %get-tuple-element.99), channel_id=1, source_target_pairs={{6,0},{7,1},{14,8},{15,9},{22,16},{23,17},{30,24},{31,25},{38,32},... | collective-permute-start | bytes 1032200 | tf_op jit(solution)/shard_map/ppermute | solution.py:107
  300.6 20.2 %collective-permute-start.32 = (bf16[256,672]{0,1:T(8,128)(2,1)}, bf16[256,672]{0,1:T(8,128)(2,1)}, u32[]{:S(2)}, u32[]{:S(2)}) collective-permute-start(bf16[256,672]{0,1:T(8,128)(2,1)} %get-tuple-element.101), channel_id=1, source_target_pairs={{4,0},{6,2},{5,1},{7,3},{12,8},{14,10},{13,9},{15,11},{20,16},{22,... | collective-permute-start | bytes 1032200 | tf_op jit(solution)/shard_map/ppermute | solution.py:107
  301.9 18.9 %collective-permute-start.31 = (bf16[256,672]{0,1:T(8,128)(2,1)S(1)}, bf16[256,672]{0,1:T(8,128)(2,1)}, u32[]{:S(2)}, u32[]{:S(2)}) collective-permute-start(bf16[256,672]{0,1:T(8,128)(2,1)S(1)} %get-tuple-element.102), channel_id=1, source_target_pairs={{0,4},{2,6},{1,5},{3,7},{8,12},{10,14},{9,13},{11,15},{16,20},{18,... | collective-permute-start | bytes 1032200 | tf_op jit(solution)/shard_map/ppermute | solution.py:107
  308.9 18.1 %collective-permute-start.30 = (bf16[256,672]{0,1:T(8,128)(2,1)S(1)}, bf16[256,672]{0,1:T(8,128)(2,1)}, u32[]{:S(2)}, u32[]{:S(2)}) collective-permute-start(bf16[256,672]{0,1:T(8,128)(2,1)S(1)} %get-tuple-element.103), channel_id=1, source_target_pairs={{2,0},{4,2},{6,4},{3,1},{5,3},{7,5},{10,8},{12,10},{14,12},{11,9},... | collective-permute-start | bytes 1032200 | tf_op jit(solution)/shard_map/ppermute | solution.py:107
  (38 other events, 330.3 us)
Sparse Core Ops, SparseCore 0:
  9.4 45.3 all-gather.1

commit v12 on v10

--- a/solution.py
+++ b/solution.py
@@ -167,13 +167,13 @@
 
     def fold_qk(acc, new):
         for dy, lo, hi, piece in new:
-            term = contract(normed_rel[:, dy, lo:hi], piece)
+            term = contract(normed_rel[:, dy, :, lo:hi], piece)
             acc = term if acc is None else acc + term
         return acc
 
     def fold_v(acc, new):
         for dx, lo, hi, piece in new:
-            term = contract(normed_rel[:, lo:hi, dx], piece[..., :v_cols])
+            term = contract(normed_rel[:, :, dx, lo:hi], piece)
             acc = term if acc is None else acc + term
         return acc
 
@@ -184,8 +184,9 @@
     half_b = by_zh[:, :, split:]
     a_x = stacked_direct(half_a, "x", nx)
     b_y = stacked_ring(half_b, "y", ny, 0)
-    _, qk = ring_pieces(a_x, "y", ny, 0, fold_qk, None)
-    b_pieces, projected_values = ring_pieces(b_y, "x", nx, 0, fold_v, None)
+    _, qk = ring_pieces(a_x, "y", ny, 1, fold_qk, None)
+    b_pieces, b_sum = ring_pieces(b_y, "x", nx, 1, fold_v, None)
+    projected_values = b_sum[:, :v_cols]
     queries_raw = qk[:, :q_cols]
     unrotated_keys = qk[:, q_cols:]
     own_places = lax.dynamic_slice_in_dim(positions, seq_at * tok_rows, tok_rows, 0)
@@ -241,14 +242,17 @@
     merged = (inner_sum + outer_sum) / total[..., None]
     attended = merged.astype(jnp.bfloat16).reshape(tok_rows, local_kv * query_group * head_dim)
     out_rel = jnp.zeros((tok_rows, ny, nx, nz, shard_rows), jnp.bfloat16)
+    attended_wide = jnp.concatenate(
+        [jnp.zeros((tok_rows, v_cols), attended.dtype), attended], axis=1
+    )
     for dx, lo, hi, piece in b_pieces:
         cols = lax.dot_general(
-            attended,
-            piece[..., v_cols:],
+            attended_wide,
+            piece,
             (((1,), (3,)), ((), ())),
             preferred_element_type=jnp.float32,
         )
-        out_rel = out_rel.at[:, lo:hi, dx].set(cols.astype(jnp.bfloat16))
+        out_rel = out_rel.at[:, :, dx, lo:hi].set(cols.astype(jnp.bfloat16))
     out_abs = jnp.roll(out_rel, at_y, axis=1)
     out_abs = jnp.roll(out_abs, at_x, axis=2)
     out_abs = jnp.roll(out_abs, at_zh, axis=3)

time: 353 us -> 357 us (1.011)
  the two profiles are of different devices: /device:TPU:263 before, /device:TPU:320 now
where the time goes in v12:
time: 357 us; the launch traced here: 354 us
  starting transfers between devices  116 us (32%)
  waiting for transfers between devices  102 us (29%)
  matrix products  43.6 us (12%)
  local copies, waits for them, and re-layouts  34 us (10%)
  other arithmetic  30.1 us (8%)
  between operations  14.7 us (4%)
  blocking collectives  14.1 us (4%)
    dot_general x14, matrix products, contract(): lax.dot_general(lhs, piece, (((1, 2, 3), (0, 1, 2)), ((), ())), preferred...  29.7 us
    ppermute x4, waiting for transfers between devices, from_behind(): return lax.ppermute(block, axis, route)  28.4 us
    ppermute x1, waiting for transfers between devices, ring(): return [block, lax.ppermute(block, axis, fwd)]  20.8 us
    ppermute x4, starting transfers between devices, ring_pieces(): right = lax.ppermute(right, axis, bwd)  19 us
    ppermute x3, waiting for transfers between devices, ring(): left = lax.ppermute(left, axis, fwd)  18.8 us
    ppermute x6, waiting for transfers between devices, reduce_scatter_tp(): lax.ppermute(block.astype(jnp.bfloat16), 'zl', route).astype(jnp.float32)  18.3 us
    ppermute x6, starting transfers between devices, reduce_scatter_tp(): lax.ppermute(block.astype(jnp.bfloat16), 'zl', route).astype(jnp.float32)  16.9 us
    ppermute x3, starting transfers between devices, ring(): right = lax.ppermute(right, axis, bwd)  15.6 us
  transfers between devices with their start and end apart: 37, of which 15 were waited for; matrix products, arithmetic and copies ran while one was open for 19% of the time, Pallas kernels for 0%

profile of v12, /device:TPU:320, one launch (start us, length us, event | category | flops | bytes accessed | tf_op | source)
XLA Modules:
  0.0 354.5 jit_solution(14276365021480558379)
XLA Ops:
  10.2 20.8 %collective-permute-done = bf16[84,1536]{1,0:T(8,128)(2,1)S(1)} collective-permute-done((bf16[84,1536]{1,0:T(8,128)(2,1)S(1)}, bf16[84,1536]{1,0:T(8,128)(2,1)S(1)}, u32[]{:S(2)}, u32[]{:S(2)}) %collective-permute-start) | collective-permute-done | bytes 258080 | tf_op jit(solution)/shard_map/ppermute | solution.py:31
  31.1 5.4 %collective-permute-start.1 = (bf16[2,84,768]{2,1,0:T(8,128)(2,1)S(1)}, bf16[2,84,768]{2,1,0:T(8,128)(2,1)}, u32[]{:S(2)}, u32[]{:S(2)}) collective-permute-start(bf16[2,84,768]{2,1,0:T(8,128)(2,1)S(1)} %get-tuple-element.97), channel_id=1, source_target_pairs={{0,224},{32,0},{64,32},{96,64},{128,96},{160,128},{192,160},{224,1... | collective-permute-start | bytes 774152 | tf_op jit(solution)/shard_map/ppermute | solution.py:37
  39.1 4.7 %collective-permute-start.13 = (bf16[2,84,768]{2,1,0:T(8,128)(2,1)}, bf16[2,84,768]{2,1,0:T(8,128)(2,1)S(1)}, u32[]{:S(2)}, u32[]{:S(2)}) collective-permute-start(bf16[2,84,768]{2,1,0:T(8,128)(2,1)} %pad_maximum_fusion.1), channel_id=1, source_target_pairs={{0,24},{8,0},{16,8},{24,16},{1,25},{9,1},{17,9},{25,17},{2,26},{10... | collective-permute-start | bytes 774152 | tf_op jit(solution)/shard_map/ppermute | solution.py:56
  49.4 5.1 %collective-permute-start.2 = (bf16[2,84,768]{2,1,0:T(8,128)(2,1)}, bf16[2,84,768]{2,1,0:T(8,128)(2,1)S(1)}, u32[]{:S(2)}, u32[]{:S(2)}) collective-permute-start(bf16[2,84,768]{2,1,0:T(8,128)(2,1)} %collective-permute-done.1), channel_id=1, source_target_pairs={{0,224},{32,0},{64,32},{96,64},{128,96},{160,128},{192,160},{224,1... | collective-permute-start | bytes 774152 | tf_op jit(solution)/shard_map/ppermute | solution.py:37
  60.0 4.8 %collective-permute-start.17 = (bf16[4,2,84,768]{3,0,2,1:T(4,128)(2,1)}, bf16[4,2,84,768]{3,0,2,1:T(4,128)(2,1)}, u32[]{:S(2)}, u32[]{:S(2)}) collective-permute-start(bf16[4,2,84,768]{3,0,2,1:T(4,128)(2,1)} %copy.103), channel_id=1, source_target_pairs={{0,224},{32,0},{64,32},{96,64},{128,96},{160,128},{192,160},{224,1... | collective-permute-start | bytes 3096584 | tf_op jit(solution)/shard_map/ppermute | solution.py:79
  66.8 5.1 %collective-permute-start.3 = (bf16[2,84,768]{2,1,0:T(8,128)(2,1)S(1)}, bf16[2,84,768]{2,1,0:T(8,128)(2,1)S(1)}, u32[]{:S(2)}, u32[]{:S(2)}) collective-permute-start(bf16[2,84,768]{2,1,0:T(8,128)(2,1)S(1)} %collective-permute-done.2), channel_id=1, source_target_pairs={{0,224},{32,0},{64,32},{96,64},{128,96},{160,128},{192,160},{224,1... | collective-permute-start | bytes 774152 | tf_op jit(solution)/shard_map/ppermute | solution.py:37
  74.9 18.8 %collective-permute-done.6 = bf16[2,84,768]{2,1,0:T(8,128)(2,1)S(1)} collective-permute-done((bf16[2,84,768]{2,1,0:T(8,128)(2,1)S(1)}, bf16[2,84,768]{2,1,0:T(8,128)(2,1)S(1)}, u32[]{:S(2)}, u32[]{:S(2)}) %collective-permute-start.6) | collective-permute-done | bytes 258080 | tf_op jit(solution)/shard_map/ppermute | solution.py:36
  95.7 5.1 %collective-permute-start.8 = (bf16[1,84,768]{2,1,0:T(8,128)(2,1)S(1)}, bf16[1,84,768]{2,1,0:T(8,128)(2,1)S(1)}, u32[]{:S(2)}, u32[]{:S(2)}) collective-permute-start(bf16[1,84,768]{2,1,0:T(8,128)(2,1)S(1)} %slice.291), channel_id=1, source_target_pairs={{0,224},{32,0},{64,32},{96,64},{128,96},{160,128},{192,160},{224,1... | collective-permute-start | bytes 387080 | tf_op jit(solution)/shard_map/ppermute | solution.py:43
  109.6 3.8 %collective-permute-start.10 = (bf16[8,2,84,768]{3,0,2,1:T(8,128)(2,1)}, bf16[8,2,84,768]{3,0,2,1:T(8,128)(2,1)}, u32[]{:S(2)}, u32[]{:S(2)}) collective-permute-start(bf16[8,2,84,768]{3,0,2,1:T(8,128)(2,1)} %copy.96), channel_id=1, source_target_pairs={{0,24},{8,0},{16,8},{24,16},{1,25},{9,1},{17,9},{25,17},{2,26},{10... | collective-permute-start | bytes 6193160 | tf_op jit(solution)/shard_map/ppermute | solution.py:79
  116.2 3.4 fusion.2
  119.6 3.5 reshape.439
  135.4 5.7 %collective-permute-start.19 = (bf16[4,2,84,768]{3,0,2,1:T(4,128)(2,1)}, bf16[4,2,84,768]{3,0,2,1:T(4,128)(2,1)}, u32[]{:S(2)}, u32[]{:S(2)}) collective-permute-start(bf16[4,2,84,768]{3,0,2,1:T(4,128)(2,1)} %collective-permute-done.17), channel_id=1, source_target_pairs={{0,224},{32,0},{64,32},{96,64},{128,96},{160,128},{192,160},{224,1... | collective-permute-start | bytes 3096584 | tf_op jit(solution)/shard_map/ppermute | solution.py:79
  141.7 6.3 %collective-permute-done.9 = bf16[8,2,84,768]{3,0,2,1:T(8,128)(2,1)} collective-permute-done((bf16[8,2,84,768]{3,0,2,1:T(8,128)(2,1)}, bf16[8,2,84,768]{3,0,2,1:T(8,128)(2,1)}, u32[]{:S(2)}, u32[]{:S(2)}) %collective-permute-start.9) | collective-permute-done | bytes 2064416 | tf_op jit(solution)/shard_map/ppermute | solution.py:78
  159.5 4.6 %collective-permute-start.21 = (bf16[4,2,84,768]{3,0,2,1:T(4,128)(2,1)}, bf16[4,2,84,768]{3,0,2,1:T(4,128)(2,1)}, u32[]{:S(2)}, u32[]{:S(2)}) collective-permute-start(bf16[4,2,84,768]{3,0,2,1:T(4,128)(2,1)} %collective-permute-done.19), channel_id=1, source_target_pairs={{0,224},{32,0},{64,32},{96,64},{128,96},{160,128},{192,160},{224,1... | collective-permute-start | bytes 3096584 | tf_op jit(solution)/shard_map/ppermute | solution.py:79
  173.6 5.1 %collective-permute-start.12 = (bf16[8,1,84,768]{3,0,2,1:T(8,128)(2,1)}, bf16[8,1,84,768]{3,0,2,1:T(8,128)(2,1)}, u32[]{:S(2)}, u32[]{:S(2)}) collective-permute-start(bf16[8,1,84,768]{3,0,2,1:T(8,128)(2,1)} %slice.266), channel_id=1, source_target_pairs={{0,24},{8,0},{16,8},{24,16},{1,25},{9,1},{17,9},{25,17},{2,26},{10... | collective-permute-start | bytes 3096584 | tf_op jit(solution)/shard_map/ppermute | solution.py:86
  192.7 5.1 %collective-permute-start.23 = (bf16[4,1,84,768]{3,0,2,1:T(4,128)(2,1)}, bf16[4,1,84,768]{3,0,2,1:T(4,128)(2,1)}, u32[]{:S(2)}, u32[]{:S(2)}) collective-permute-start(bf16[4,1,84,768]{3,0,2,1:T(4,128)(2,1)} %slice.279), channel_id=1, source_target_pairs={{0,224},{32,0},{64,32},{96,64},{128,96},{160,128},{192,160},{224,1... | collective-permute-start | bytes 1548296 | tf_op jit(solution)/shard_map/ppermute | solution.py:86
  231.3 6.1 %collective-permute-done.25 = bf16[2,256,256]{2,1,0:T(8,128)(2,1)} collective-permute-done((bf16[2,256,256]{2,1,0:T(8,128)(2,1)}, bf16[2,256,256]{2,1,0:T(8,128)(2,1)}, u32[]{:S(2)}, u32[]{:S(2)}) %collective-permute-start.25) | collective-permute-done | bytes 262176 | tf_op jit(solution)/shard_map/ppermute | solution.py:22
  238.3 10.1 %collective-permute-done.26 = bf16[2,256,256]{2,1,0:T(8,128)(2,1)} collective-permute-done((bf16[2,256,256]{2,1,0:T(8,128)(2,1)}, bf16[2,256,256]{2,1,0:T(8,128)(2,1)}, u32[]{:S(2)}, u32[]{:S(2)}) %collective-permute-start.26) | collective-permute-done | bytes 262176 | tf_op jit(solution)/shard_map/ppermute | solution.py:22
  249.3 11.0 %collective-permute-done.27 = bf16[2,256,256]{2,1,0:T(8,128)(2,1)} collective-permute-done((bf16[2,256,256]{2,1,0:T(8,128)(2,1)}, bf16[2,256,256]{2,1,0:T(8,128)(2,1)}, u32[]{:S(2)}, u32[]{:S(2)}) %collective-permute-start.27) | collective-permute-done | bytes 262176 | tf_op jit(solution)/shard_map/ppermute | solution.py:22
  290.9 6.1 %collective-permute-start.29 = (bf16[256,672]{0,1:T(8,128)(2,1)S(1)}, bf16[256,672]{0,1:T(8,128)(2,1)S(1)}, u32[]{:S(2)}, u32[]{:S(2)}) collective-permute-start(bf16[256,672]{0,1:T(8,128)(2,1)S(1)} %get-tuple-element.98), channel_id=1, source_target_pairs={{0,2},{2,4},{4,6},{1,3},{3,5},{5,7},{8,10},{10,12},{12,14},{9,11},... | collective-permute-start | bytes 1032200 | tf_op jit(solution)/shard_map/ppermute | solution.py:107
  298.9 4.8 %collective-permute-start.31 = (bf16[256,672]{0,1:T(8,128)(2,1)}, bf16[256,672]{0,1:T(8,128)(2,1)}, u32[]{:S(2)}, u32[]{:S(2)}) collective-permute-start(bf16[256,672]{0,1:T(8,128)(2,1)} %get-tuple-element.102), channel_id=1, source_target_pairs={{0,4},{2,6},{1,5},{3,7},{8,12},{10,14},{9,13},{11,15},{16,20},{18,... | collective-permute-start | bytes 1032200 | tf_op jit(solution)/shard_map/ppermute | solution.py:107
  306.4 13.7 %collective-permute-done.29 = bf16[256,672]{0,1:T(8,128)(2,1)S(1)} collective-permute-done((bf16[256,672]{0,1:T(8,128)(2,1)S(1)}, bf16[256,672]{0,1:T(8,128)(2,1)S(1)}, u32[]{:S(2)}, u32[]{:S(2)}) %collective-permute-start.29) | collective-permute-done | bytes 344096 | tf_op jit(solution)/shard_map/ppermute | solution.py:107
  322.2 4.6 %collective-permute-done.31 = bf16[256,672]{0,1:T(8,128)(2,1)} collective-permute-done((bf16[256,672]{0,1:T(8,128)(2,1)}, bf16[256,672]{0,1:T(8,128)(2,1)}, u32[]{:S(2)}, u32[]{:S(2)}) %collective-permute-start.31) | collective-permute-done | bytes 344096 | tf_op jit(solution)/shard_map/ppermute | solution.py:107
  331.7 14.1 %psum.7 = f32[256]{0:T(256)S(1)} all-reduce(f32[256]{0:T(256)S(1)} %add.270), channel_id=1, replica_groups=mesh['zh'=2,'y'=8,'x'=4,'zl'=4,'c'=2] {'zl'}, use_global_device_ids=true, to_apply=%region_6.10 | all-reduce | flops 256 | bytes 2048 | tf_op jit(solution)/shard_map/psum | solution.py:264
  (192 shorter events, 161.9 us)
Async XLA Ops:
  6.5 106.9 %all-gather.2.cloned.1.call-start = ((), (), s32[]{:S(2)}) async-start(), calls=%async_computation | async-start | bytes 3096576 | tf_op jit(solution)/shard_map/all_gather | solution.py:155
  8.3 22.8 %collective-permute-start = (bf16[84,1536]{1,0:T(8,128)(2,1)S(1)}, bf16[84,1536]{1,0:T(8,128)(2,1)S(1)}, u32[]{:S(2)}, u32[]{:S(2)}) collective-permute-start(bf16[84,1536]{1,0:T(8,128)(2,1)S(1)} %get-tuple-element.113), channel_id=1, source_target_pairs={{0,256},{256,0},{1,257},{257,1},{2,258},{258,2},{3,259},{259,3},{4... | collective-permute-start | bytes 774152 | tf_op jit(solution)/shard_map/ppermute | solution.py:31
  31.1 18.3 %collective-permute-start.1 = (bf16[2,84,768]{2,1,0:T(8,128)(2,1)S(1)}, bf16[2,84,768]{2,1,0:T(8,128)(2,1)}, u32[]{:S(2)}, u32[]{:S(2)}) collective-permute-start(bf16[2,84,768]{2,1,0:T(8,128)(2,1)S(1)} %get-tuple-element.97), channel_id=1, source_target_pairs={{0,224},{32,0},{64,32},{96,64},{128,96},{160,128},{192,160},{224,1... | collective-permute-start | bytes 774152 | tf_op jit(solution)/shard_map/ppermute | solution.py:37
  36.5 18.1 %collective-permute-start.4 = (bf16[2,84,768]{2,1,0:T(8,128)(2,1)S(1)}, bf16[2,84,768]{2,1,0:T(8,128)(2,1)}, u32[]{:S(2)}, u32[]{:S(2)}) collective-permute-start(bf16[2,84,768]{2,1,0:T(8,128)(2,1)S(1)} %get-tuple-element.97), channel_id=1, source_target_pairs={{0,32},{32,64},{64,96},{96,128},{128,160},{160,192},{192,224},{224... | collective-permute-start | bytes 774152 | tf_op jit(solution)/shard_map/ppermute | solution.py:36
  60.0 66.6 %collective-permute-start.17 = (bf16[4,2,84,768]{3,0,2,1:T(4,128)(2,1)}, bf16[4,2,84,768]{3,0,2,1:T(4,128)(2,1)}, u32[]{:S(2)}, u32[]{:S(2)}) collective-permute-start(bf16[4,2,84,768]{3,0,2,1:T(4,128)(2,1)} %copy.103), channel_id=1, source_target_pairs={{0,224},{32,0},{64,32},{96,64},{128,96},{160,128},{192,160},{224,1... | collective-permute-start | bytes 3096584 | tf_op jit(solution)/shard_map/ppermute | solution.py:79
  64.9 64.3 %collective-permute-start.16 = (bf16[4,2,84,768]{3,0,2,1:T(4,128)(2,1)}, bf16[4,2,84,768]{3,0,2,1:T(4,128)(2,1)}, u32[]{:S(2)}, u32[]{:S(2)}) collective-permute-start(bf16[4,2,84,768]{3,0,2,1:T(4,128)(2,1)} %copy.103), channel_id=1, source_target_pairs={{0,32},{32,64},{64,96},{96,128},{128,160},{160,192},{192,224},{224... | collective-permute-start | bytes 3096584 | tf_op jit(solution)/shard_map/ppermute | solution.py:78
  66.8 28.9 %collective-permute-start.3 = (bf16[2,84,768]{2,1,0:T(8,128)(2,1)S(1)}, bf16[2,84,768]{2,1,0:T(8,128)(2,1)S(1)}, u32[]{:S(2)}, u32[]{:S(2)}) collective-permute-start(bf16[2,84,768]{2,1,0:T(8,128)(2,1)S(1)} %collective-permute-done.2), channel_id=1, source_target_pairs={{0,224},{32,0},{64,32},{96,64},{128,96},{160,128},{192,160},{224,1... | collective-permute-start | bytes 774152 | tf_op jit(solution)/shard_map/ppermute | solution.py:37
  72.0 21.8 %collective-permute-start.6 = (bf16[2,84,768]{2,1,0:T(8,128)(2,1)S(1)}, bf16[2,84,768]{2,1,0:T(8,128)(2,1)S(1)}, u32[]{:S(2)}, u32[]{:S(2)}) collective-permute-start(bf16[2,84,768]{2,1,0:T(8,128)(2,1)S(1)} %collective-permute-done.5), channel_id=1, source_target_pairs={{0,32},{32,64},{64,96},{96,128},{128,160},{160,192},{192,224},{224... | collective-permute-start | bytes 774152 | tf_op jit(solution)/shard_map/ppermute | solution.py:36
  106.4 41.6 %collective-permute-start.9 = (bf16[8,2,84,768]{3,0,2,1:T(8,128)(2,1)}, bf16[8,2,84,768]{3,0,2,1:T(8,128)(2,1)}, u32[]{:S(2)}, u32[]{:S(2)}) collective-permute-start(bf16[8,2,84,768]{3,0,2,1:T(8,128)(2,1)} %copy.96), channel_id=1, source_target_pairs={{0,8},{8,16},{16,24},{24,0},{1,9},{9,17},{17,25},{25,1},{2,10},{10... | collective-permute-start | bytes 6193160 | tf_op jit(solution)/shard_map/ppermute | solution.py:78
  109.6 40.8 %collective-permute-start.10 = (bf16[8,2,84,768]{3,0,2,1:T(8,128)(2,1)}, bf16[8,2,84,768]{3,0,2,1:T(8,128)(2,1)}, u32[]{:S(2)}, u32[]{:S(2)}) collective-permute-start(bf16[8,2,84,768]{3,0,2,1:T(8,128)(2,1)} %copy.96), channel_id=1, source_target_pairs={{0,24},{8,0},{16,8},{24,16},{1,25},{9,1},{17,9},{25,17},{2,26},{10... | collective-permute-start | bytes 6193160 | tf_op jit(solution)/shard_map/ppermute | solution.py:79
  133.4 19.6 %collective-permute-start.18 = (bf16[4,2,84,768]{3,0,2,1:T(4,128)(2,1)}, bf16[4,2,84,768]{3,0,2,1:T(4,128)(2,1)}, u32[]{:S(2)}, u32[]{:S(2)}) collective-permute-start(bf16[4,2,84,768]{3,0,2,1:T(4,128)(2,1)} %collective-permute-done.16), channel_id=1, source_target_pairs={{0,32},{32,64},{64,96},{96,128},{128,160},{160,192},{192,224},{224... | collective-permute-start | bytes 3096584 | tf_op jit(solution)/shard_map/ppermute | solution.py:78
  135.4 19.6 %collective-permute-start.19 = (bf16[4,2,84,768]{3,0,2,1:T(4,128)(2,1)}, bf16[4,2,84,768]{3,0,2,1:T(4,128)(2,1)}, u32[]{:S(2)}, u32[]{:S(2)}) collective-permute-start(bf16[4,2,84,768]{3,0,2,1:T(4,128)(2,1)} %collective-permute-done.17), channel_id=1, source_target_pairs={{0,224},{32,0},{64,32},{96,64},{128,96},{160,128},{192,160},{224,1... | collective-permute-start | bytes 3096584 | tf_op jit(solution)/shard_map/ppermute | solution.py:79
  156.9 23.4 %collective-permute-start.20 = (bf16[4,2,84,768]{3,0,2,1:T(4,128)(2,1)}, bf16[4,2,84,768]{3,0,2,1:T(4,128)(2,1)}, u32[]{:S(2)}, u32[]{:S(2)}) collective-permute-start(bf16[4,2,84,768]{3,0,2,1:T(4,128)(2,1)} %collective-permute-done.18), channel_id=1, source_target_pairs={{0,32},{32,64},{64,96},{96,128},{128,160},{160,192},{192,224},{224... | collective-permute-start | bytes 3096584 | tf_op jit(solution)/shard_map/ppermute | solution.py:78
  159.5 22.7 %collective-permute-start.21 = (bf16[4,2,84,768]{3,0,2,1:T(4,128)(2,1)}, bf16[4,2,84,768]{3,0,2,1:T(4,128)(2,1)}, u32[]{:S(2)}, u32[]{:S(2)}) collective-permute-start(bf16[4,2,84,768]{3,0,2,1:T(4,128)(2,1)} %collective-permute-done.19), channel_id=1, source_target_pairs={{0,224},{32,0},{64,32},{96,64},{128,96},{160,128},{192,160},{224,1... | collective-permute-start | bytes 3096584 | tf_op jit(solution)/shard_map/ppermute | solution.py:79
  169.2 19.6 %collective-permute-start.11 = (bf16[8,1,84,768]{3,0,2,1:T(8,128)(2,1)}, bf16[8,1,84,768]{3,0,2,1:T(8,128)(2,1)}, u32[]{:S(2)}, u32[]{:S(2)}) collective-permute-start(bf16[8,1,84,768]{3,0,2,1:T(8,128)(2,1)} %slice.264), channel_id=1, source_target_pairs={{0,8},{8,16},{16,24},{24,0},{1,9},{9,17},{17,25},{25,1},{2,10},{10... | collective-permute-start | bytes 3096584 | tf_op jit(solution)/shard_map/ppermute | solution.py:85
  173.6 24.2 %collective-permute-start.12 = (bf16[8,1,84,768]{3,0,2,1:T(8,128)(2,1)}, bf16[8,1,84,768]{3,0,2,1:T(8,128)(2,1)}, u32[]{:S(2)}, u32[]{:S(2)}) collective-permute-start(bf16[8,1,84,768]{3,0,2,1:T(8,128)(2,1)} %slice.266), channel_id=1, source_target_pairs={{0,24},{8,0},{16,8},{24,16},{1,25},{9,1},{17,9},{25,17},{2,26},{10... | collective-permute-start | bytes 3096584 | tf_op jit(solution)/shard_map/ppermute | solution.py:86
  215.3 22.0 %collective-permute-start.25 = (bf16[2,256,256]{2,1,0:T(8,128)(2,1)}, bf16[2,256,256]{2,1,0:T(8,128)(2,1)}, u32[]{:S(2)}, u32[]{:S(2)}) collective-permute-start(bf16[2,256,256]{2,1,0:T(8,128)(2,1)} %pad_maximum_fusion.4), channel_id=1, source_target_pairs={{0,24},{8,32},{16,40},{24,48},{32,56},{40,64},{48,72},{56,80},{64,... | collective-permute-start | bytes 786440 | tf_op jit(solution)/shard_map/ppermute | solution.py:22
  218.5 29.9 %collective-permute-start.26 = (bf16[2,256,256]{2,1,0:T(8,128)(2,1)}, bf16[2,256,256]{2,1,0:T(8,128)(2,1)}, u32[]{:S(2)}, u32[]{:S(2)}) collective-permute-start(bf16[2,256,256]{2,1,0:T(8,128)(2,1)} %pad_maximum_fusion.4), channel_id=1, source_target_pairs={{0,16},{8,24},{16,32},{24,40},{32,48},{40,56},{48,64},{56,72},{64,... | collective-permute-start | bytes 786440 | tf_op jit(solution)/shard_map/ppermute | solution.py:22
  221.5 38.8 %collective-permute-start.27 = (bf16[2,256,256]{2,1,0:T(8,128)(2,1)}, bf16[2,256,256]{2,1,0:T(8,128)(2,1)}, u32[]{:S(2)}, u32[]{:S(2)}) collective-permute-start(bf16[2,256,256]{2,1,0:T(8,128)(2,1)} %pad_maximum_fusion.4), channel_id=1, source_target_pairs={{0,8},{8,16},{16,24},{24,32},{32,40},{40,48},{48,56},{56,64},{64,7... | collective-permute-start | bytes 786440 | tf_op jit(solution)/shard_map/ppermute | solution.py:22
  290.9 29.3 %collective-permute-start.29 = (bf16[256,672]{0,1:T(8,128)(2,1)S(1)}, bf16[256,672]{0,1:T(8,128)(2,1)S(1)}, u32[]{:S(2)}, u32[]{:S(2)}) collective-permute-start(bf16[256,672]{0,1:T(8,128)(2,1)S(1)} %get-tuple-element.98), channel_id=1, source_target_pairs={{0,2},{2,4},{4,6},{1,3},{3,5},{5,7},{8,10},{10,12},{12,14},{9,11},... | collective-permute-start | bytes 1032200 | tf_op jit(solution)/shard_map/ppermute | solution.py:107
  297.0 25.3 %collective-permute-start.30 = (bf16[256,672]{0,1:T(8,128)(2,1)}, bf16[256,672]{0,1:T(8,128)(2,1)}, u32[]{:S(2)}, u32[]{:S(2)}) collective-permute-start(bf16[256,672]{0,1:T(8,128)(2,1)} %get-tuple-element.103), channel_id=1, source_target_pairs={{2,0},{4,2},{6,4},{3,1},{5,3},{7,5},{10,8},{12,10},{14,12},{11,9},... | collective-permute-start | bytes 1032200 | tf_op jit(solution)/shard_map/ppermute | solution.py:107
  298.9 27.9 %collective-permute-start.31 = (bf16[256,672]{0,1:T(8,128)(2,1)}, bf16[256,672]{0,1:T(8,128)(2,1)}, u32[]{:S(2)}, u32[]{:S(2)}) collective-permute-start(bf16[256,672]{0,1:T(8,128)(2,1)} %get-tuple-element.102), channel_id=1, source_target_pairs={{0,4},{2,6},{1,5},{3,7},{8,12},{10,14},{9,13},{11,15},{16,20},{18,... | collective-permute-start | bytes 1032200 | tf_op jit(solution)/shard_map/ppermute | solution.py:107
  303.7 23.1 %collective-permute-start.32 = (bf16[256,672]{0,1:T(8,128)(2,1)}, bf16[256,672]{0,1:T(8,128)(2,1)}, u32[]{:S(2)}, u32[]{:S(2)}) collective-permute-start(bf16[256,672]{0,1:T(8,128)(2,1)} %get-tuple-element.101), channel_id=1, source_target_pairs={{4,0},{6,2},{5,1},{7,3},{12,8},{14,10},{13,9},{15,11},{20,16},{22,... | collective-permute-start | bytes 1032200 | tf_op jit(solution)/shard_map/ppermute | solution.py:107
  305.0 21.8 %collective-permute-start.33 = (bf16[256,672]{0,1:T(8,128)(2,1)S(1)}, bf16[256,672]{0,1:T(8,128)(2,1)}, u32[]{:S(2)}, u32[]{:S(2)}) collective-permute-start(bf16[256,672]{0,1:T(8,128)(2,1)S(1)} %get-tuple-element.100), channel_id=1, source_target_pairs={{0,6},{1,7},{8,14},{9,15},{16,22},{17,23},{24,30},{25,31},{32,38},... | collective-permute-start | bytes 1032200 | tf_op jit(solution)/shard_map/ppermute | solution.py:107
  (32 other events, 490.0 us)
Sparse Core Ops, SparseCore 0:
  9.4 44.3 all-gather.1
